TPU v7x, 32 devices: a whole 2x2x4 slice. The times are simulated.
32 devices in a mesh: dp: 8 (over y, x, core), expert: 4 (over z).
Axes of the slice: x: 2, y: 2, z: 4, core: 2. Of those that a mesh axis runs over, the one named last changes fastest.
Arguments:
- tokens: bfloat16 [4096, 1024], P(('dp', 'expert')), may hold values from -6 to 6
- expert_ids: int32 [4096, 2], P(('dp', 'expert')), may hold values from 0 to 3, all different within a row; in each aligned block of 128 rows (0 to 127, 128 to 255, ...) at most 96 rows name the same one
- routing: float32 [4096, 2], P(('dp', 'expert')), may hold values from 0.2 to 1
- w_gate: bfloat16 [4, 1024, 384], P('expert', 'dp'), may hold values from -0.1875 to 0.1875
- w_up: bfloat16 [4, 1024, 384], P('expert', 'dp'), may hold values from -0.1875 to 0.1875
- w_down: bfloat16 [4, 1024, 384], P('expert', 'dp'), may hold values from -0.3125 to 0.3125
- grad_out: bfloat16 [4096, 1024], P(('dp', 'expert')), may hold values from -6 to 6
Outputs:
- output: bfloat16 [4096, 1024], P(('dp', 'expert'))
- token_grad: bfloat16 [4096, 1024], P(('dp', 'expert'))
- down_grad: float32 [4, 1024, 384], P('expert', 'dp')
Inputs may be any that keep to these rules, and one draw needn't show every extreme that they name: `expert_ids`: the 2 experts of a token differ. Among the 128 tokens of one device no expert is named by more than 96 (token, choice) pairs, and in every draw some device names some expert exactly 96 times.
All inputs are finite; a program needn't handle non-finite values.
Results may differ from a plain program's by a relative error of at most 0.0065.
Values may be sent and summed in bfloat16 or wider, within the bound.
No kernel may reach another device: no remote copies, remote signals or barrier semaphores. Data moves between devices by JAX's collectives and lax.ppermute only.
A program may use at most 64 MiB of HBM per device.

v0:
```python
import jax
import jax.numpy as jnp
from jax import lax
from jax.sharding import PartitionSpec as P

contract_last = (((1,), (1,)), ((), ()))
contract_first = (((0,), (0,)), ((), ()))


def forward_rows(row_data, gate_w, up_w, down_w):
    gate_pre = jnp.dot(row_data, gate_w, preferred_element_type=jnp.float32)
    up_pre = jnp.dot(row_data, up_w, preferred_element_type=jnp.float32)
    sigmoid_val = jax.nn.sigmoid(gate_pre)
    hidden = (gate_pre * sigmoid_val * up_pre).astype(jnp.bfloat16)
    expert_out = lax.dot_general(
        hidden, down_w, contract_last, preferred_element_type=jnp.float32
    ).astype(jnp.bfloat16)
    return (gate_pre, up_pre, hidden, expert_out)


def backward_rows(grad_rows, gate_pre, up_pre, gate_w, up_w, down_w):
    hidden_grad = jnp.dot(grad_rows, down_w, preferred_element_type=jnp.float32)
    sigmoid_val = jax.nn.sigmoid(gate_pre)
    slope_val = sigmoid_val * (1.0 + gate_pre * (1.0 - sigmoid_val))
    gate_grad = (hidden_grad * up_pre * slope_val).astype(jnp.bfloat16)
    up_grad = (hidden_grad * gate_pre * sigmoid_val).astype(jnp.bfloat16)
    summed = lax.dot_general(gate_grad, gate_w, contract_last, preferred_element_type=jnp.float32)
    summed = summed + lax.dot_general(
        up_grad, up_w, contract_last, preferred_element_type=jnp.float32
    )
    return summed.astype(jnp.bfloat16)


def local(tokens, expert_ids, routing, w_gate, w_up, w_down, grad_out):
    tok_rows, width = tokens.shape
    groups = lax.axis_size("expert")
    local_count = w_gate.shape[0]
    ff_width = w_gate.shape[2]
    experts_all = local_count * groups
    top_count = expert_ids.shape[1]
    capacity = 3 * tok_rows * top_count // (2 * experts_all)
    pair_count = tok_rows * top_count
    chosen = expert_ids.reshape(pair_count)
    onehot = (chosen[:, None] == jnp.arange(experts_all, dtype=jnp.int32)[None, :]).astype(
        jnp.int32
    )
    before = jnp.cumsum(onehot, axis=0) - onehot
    slot_index = jnp.sum(before * onehot, axis=1)
    flat_index = chosen * capacity + slot_index
    owner_row = jnp.arange(pair_count, dtype=jnp.int32) // top_count
    slot_owner = (
        jnp.full((experts_all * capacity,), tok_rows, jnp.int32).at[flat_index].set(owner_row)
    )
    weight_slot = (
        jnp.zeros((experts_all * capacity,), jnp.float32)
        .at[flat_index]
        .set(routing.reshape(pair_count))
    )
    zero_row = jnp.zeros((1, width), jnp.bfloat16)
    send_rows = jnp.concatenate([tokens, zero_row], axis=0)[slot_owner].reshape(
        experts_all, capacity, width
    )
    grads_picked = jnp.concatenate([grad_out, zero_row], axis=0)[slot_owner].astype(jnp.float32)
    send_grads = (
        (weight_slot[:, None] * grads_picked)
        .astype(jnp.bfloat16)
        .reshape(experts_all, capacity, width)
    )
    gate_full, up_full, down_full = (
        lax.all_gather(w_gate, "dp", axis=1, tiled=True),
        lax.all_gather(w_up, "dp", axis=1, tiled=True),
        lax.all_gather(w_down, "dp", axis=1, tiled=True),
    )
    recv_rows, recv_grads = (
        lax.all_to_all(send_rows, "expert", split_axis=0, concat_axis=0, tiled=True),
        lax.all_to_all(send_grads, "expert", split_axis=0, concat_axis=0, tiled=True),
    )
    rows_x = recv_rows.reshape(groups, local_count, capacity, width)
    rows_g = recv_grads.reshape(groups, local_count, capacity, width)
    slab_rows = groups * capacity
    expert_index = 0
    x_rows = rows_x[:, expert_index].reshape(slab_rows, width)
    g_rows = rows_g[:, expert_index].reshape(slab_rows, width)
    gate_w = gate_full[expert_index]
    up_w = up_full[expert_index]
    down_w = down_full[expert_index]
    is_valid = None
    position = None
    live_rows = None
    g_used = g_rows
    gate_pre, up_pre, hidden, expert_out = forward_rows(x_rows, gate_w, up_w, down_w)
    out_parts = [expert_out]
    forward_parts = [(gate_pre, up_pre, hidden, g_used, is_valid, position, live_rows)]
    out_send = jnp.stack(out_parts, axis=1).reshape(groups * local_count, capacity, width)
    back_out = lax.all_to_all(out_send, "expert", split_axis=0, concat_axis=0, tiled=True)
    expert_index = 0
    gate_pre, up_pre, hidden, g_used, is_valid, position, live_rows = forward_parts[expert_index]
    gate_w = gate_full[expert_index]
    up_w = up_full[expert_index]
    down_w = down_full[expert_index]
    grad_parts = [backward_rows(g_used, gate_pre, up_pre, gate_w, up_w, down_w)]
    grad_send = jnp.stack(grad_parts, axis=1).reshape(groups * local_count, capacity, width)
    back_grad = lax.all_to_all(grad_send, "expert", split_axis=0, concat_axis=0, tiled=True)
    out_rows = back_out.reshape(experts_all * capacity, width)[flat_index].reshape(
        tok_rows, top_count, width
    )
    output = jnp.sum(routing[:, :, None] * out_rows.astype(jnp.float32), axis=1).astype(
        jnp.bfloat16
    )
    grad_rows = back_grad.reshape(experts_all * capacity, width)[flat_index].reshape(
        tok_rows, top_count, width
    )
    token_grad = jnp.sum(grad_rows.astype(jnp.float32), axis=1).astype(jnp.bfloat16)
    shard_rows = w_gate.shape[1]
    saved = forward_parts[0]
    grad_cols = saved[3]
    pieces = lax.dot_general(
        grad_cols, saved[2], contract_first, preferred_element_type=jnp.float32
    )
    summed = lax.psum_scatter(pieces, "dp", scatter_dimension=0, tiled=True)
    down_grad = jnp.transpose(
        (summed / lax.axis_size("dp")).reshape(shard_rows, local_count, ff_width), (1, 0, 2)
    )
    return (output, token_grad, down_grad)


def solution(mesh):
    return jax.shard_map(
        local,
        mesh=mesh,
        in_specs=(
            P(("dp", "expert"), None),
            P(("dp", "expert"), None),
            P(("dp", "expert"), None),
            P("expert", "dp", None),
            P("expert", "dp", None),
            P("expert", "dp", None),
            P(("dp", "expert"), None),
        ),
        out_specs=(P(("dp", "expert"), None), P(("dp", "expert"), None), P("expert", "dp", None)),
        check_vma=False,
    )
```

profile of v0, /device:TPU:0, one launch (start us, length us, event | category | flops | bytes accessed | tf_op | source)
XLA Modules:
  0.0 133.2 jit_solution(17261941709889650081)
XLA Ops:
  7.2 0.7 broadcast_multiply_fusion
  7.8 0.8 copy.15
  8.6 0.1 eq.29
  8.8 0.1 eq.25
  8.9 0.1 copy.14
  9.0 0.1 mul.65
  9.2 1.2 reduce-window.6
  10.4 0.1 slice.16
  10.5 0.1 copy.17
  10.6 0.1 copy.18
  10.7 0.1 add_bitcast_fusion
  10.8 1.4 %scatter_custom_fusion = s32[384]{0:T(512)S(1)} fusion(s32[256]{0:T(256)S(1)} %bitcast.62, s32[256]{0:T(256)S(1)} %and_select_fusion, s32[]{:T(128)} %constant.32.clone.1), kind=kCustom, calls=%fused_computation.45 | custom fusion | bytes 1540 | tf_op jit(solution)/shard_map/scatter | solution.py:52
  12.3 1.0 concatenate.6
  13.2 2.7 %gather_fusion = bf16[384,1024]{1,0:T(8,128)(2,1)} fusion(bf16[129,1024]{1,0:T(8,128)(2,1)S(1)} %concatenate.6, s32[1024]{0:T(1024)S(1)} %pad_clamp_fusion.1), kind=kCustom, calls=%fused_computation | custom fusion | bytes 1574400 | tf_op jit(solution)/shard_map/gather | solution.py:60
  16.0 6.5 %all-to-all-start = ((bf16[4,96,1024]{2,1,0:T(8,128)(2,1)}), bf16[4,96,1024]{2,1,0:T(8,128)(2,1)S(1)}, u32[]{:S(2)}, u32[]{:S(2)}) async-start(bf16[4,96,1024]{2,1,0:T(8,128)(2,1)} %bitcast.4), calls=%async_computation | async-start | bytes 1572864 | tf_op jit(solution)/shard_map/all_to_all | solution.py:75
  22.4 0.1 copy.13
  22.6 2.1 %gather_fusion.2 = bf16[384,1024]{1,0:T(8,128)(2,1)S(1)} fusion(bf16[129,1024]{1,0:T(8,128)(2,1)S(1)} %concatenate.7, s32[1024]{0:T(1024)S(1)} %pad_clamp_fusion.1), kind=kCustom, calls=%fused_computation.2 | custom fusion | bytes 1574400 | tf_op jit(solution)/shard_map/gather | solution.py:63
  24.7 0.1 reshape.133
  24.8 1.4 %scatter_custom_fusion.1 = f32[384]{0:T(512)S(1)} fusion(s32[256]{0:T(256)S(1)} %bitcast.63, f32[256]{0:T(256)S(1)} %reshape.133, f32[]{:T(128)} %constant.40.clone.1), kind=kCustom, calls=%fused_computation.43 | custom fusion | bytes 1540 | tf_op jit(solution)/shard_map/scatter | solution.py:57
  26.2 0.1 mul.70
  26.3 10.4 %all_gather.9 = bf16[1,1024,384]{2,1,0:T(8,128)(2,1)S(1)} all-gather(bf16[1,128,384]{2,1,0:T(8,128)(2,1)S(1)} %copy-done.5), channel_id=1, replica_groups=mesh['dp'=8,'expert'=4] {'dp'}, dimensions={1}, use_global_device_ids=true | all-gather | bytes 884736 | tf_op jit(solution)/shard_map/all_gather | solution.py:70
  36.7 1.1 fusion
  37.8 4.8 %all-to-all-done = bf16[4,96,1024]{2,1,0:T(8,128)(2,1)S(1)} async-done(((bf16[4,96,1024]{2,1,0:T(8,128)(2,1)}), bf16[4,96,1024]{2,1,0:T(8,128)(2,1)S(1)}, u32[]{:S(2)}, u32[]{:S(2)}) %all-to-all-start) | async-done | bytes 786464 | tf_op jit(solution)/shard_map/all_to_all | solution.py:75
  42.5 3.5 %all-to-all-start.2 = ((bf16[4,96,1024]{2,1,0:T(8,128)(2,1)}), bf16[4,96,1024]{2,1,0:T(8,128)(2,1)S(1)}, u32[]{:S(2)}, u32[]{:S(2)}) async-start(bf16[4,96,1024]{2,1,0:T(8,128)(2,1)} %fusion), calls=%async_computation.2 | async-start | bytes 1572864 | tf_op jit(solution)/shard_map/all_to_all | solution.py:76
  46.1 10.4 %all_gather.10 = bf16[1,1024,384]{2,1,0:T(8,128)(2,1)S(1)} all-gather(bf16[1,128,384]{2,1,0:T(8,128)(2,1)S(1)} %copy-done.6), channel_id=1, replica_groups=mesh['dp'=8,'expert'=4] {'dp'}, dimensions={1}, use_global_device_ids=true | all-gather | bytes 884736 | tf_op jit(solution)/shard_map/all_gather | solution.py:71
  56.5 10.4 %all_gather.11 = bf16[1,1024,384]{2,1,0:T(8,128)(2,1)S(1)} all-gather(bf16[1,128,384]{2,1,0:T(8,128)(2,1)S(1)} %copy-done.7), channel_id=1, replica_groups=mesh['dp'=8,'expert'=4] {'dp'}, dimensions={1}, use_global_device_ids=true | all-gather | bytes 884736 | tf_op jit(solution)/shard_map/all_gather | solution.py:72
  66.8 0.6 fusion.9
  67.4 1.4 %multiply_convert_fusion.2 = (bf16[384,384]{1,0:T(8,128)(2,1)S(1)}, f32[384,384]{1,0:T(8,128)}) fusion(f32[384,384]{1,0:T(8,128)S(1)} %fusion.9, bf16[384,1024]{1,0:T(8,128)(2,1)S(1)} %bitcast.60, bf16[1,1024,384]{2,1,0:T(8,128)(2,1)S(1)} %all_gather.10), kind=kOutput, calls=%fused_computation.23 | convolution fusion | flops 302874624 | bytes 3047424 | tf_op jit(solution)/shard_map/dot_general | solution.py:12
  68.8 1.5 %convolution_convert_fusion = bf16[384,1024]{1,0:T(8,128)(2,1)} fusion(bf16[384,384]{1,0:T(8,128)(2,1)S(1)} %get-tuple-element.3, bf16[1,1024,384]{2,1,0:T(8,128)(2,1)S(1)} %all_gather.11), kind=kOutput, calls=%fused_computation.9 | convolution fusion | flops 302383104 | bytes 1867776 | tf_op jit(solution)/shard_map/dot_general | solution.py:15
  70.3 5.0 %all-to-all-start.1 = ((bf16[4,96,1024]{2,1,0:T(8,128)(2,1)}), bf16[4,96,1024]{2,1,0:T(8,128)(2,1)S(1)}, u32[]{:S(2)}, u32[]{:S(2)}) async-start(bf16[4,96,1024]{2,1,0:T(8,128)(2,1)} %bitcast.9), calls=%async_computation.1 | async-start | bytes 1572864 | tf_op jit(solution)/shard_map/all_to_all | solution.py:95
  75.3 1.8 %fusion.22 = f32[1024,384]{1,0:T(8,128)} fusion(bf16[384,1024]{1,0:T(8,128)(2,1)S(1)} %bitcast.57, bf16[384,384]{1,0:T(8,128)(2,1)S(1)} %get-tuple-element.3), kind=kOutput, calls=%fused_computation.50 | convolution fusion | flops 301989888 | bytes 2654208 | tf_op jit(solution)/shard_map/dot_general | solution.py:117
  77.2 0.0 reduce-scatter.2.cloned.1.call-update
  77.2 0.6 fusion.1
  77.8 0.5 copy-done.3
  78.3 0.2 copy-done.9
  78.5 0.7 fusion.7
  79.1 0.5 copy-done.1
  79.6 1.5 %add_convert_fusion = bf16[384,1024]{1,0:T(8,128)(2,1)} fusion(f32[384,1024]{1,0:T(8,128)S(1)} %fusion.7, bf16[1,1024,384]{2,1,0:T(8,128)(2,1)S(1)} %copy-done.1, f32[384,384]{1,0:T(8,128)S(1)} %fusion.1, f32[384,384]{1,0:T(8,128)S(1)} %copy-done.3), kind=kOutput, calls=%fused_computation.8 | convolution fusion | flops 303661056 | bytes 4325376 | tf_op jit(solution)/shard_map/dot_general | solution.py:28
  81.1 14.8 %all-to-all-done.1 = bf16[4,96,1024]{2,1,0:T(8,128)(2,1)S(1)} async-done(((bf16[4,96,1024]{2,1,0:T(8,128)(2,1)}), bf16[4,96,1024]{2,1,0:T(8,128)(2,1)S(1)}, u32[]{:S(2)}, u32[]{:S(2)}) %all-to-all-start.1) | async-done | bytes 786464 | tf_op jit(solution)/shard_map/all_to_all | solution.py:95
  96.0 3.7 %all-to-all-start.3 = ((bf16[4,96,1024]{2,1,0:T(8,128)(2,1)}), bf16[4,96,1024]{2,1,0:T(8,128)(2,1)S(1)}, u32[]{:S(2)}, u32[]{:S(2)}) async-start(bf16[4,96,1024]{2,1,0:T(8,128)(2,1)} %bitcast.13), calls=%async_computation.3 | async-start | bytes 1572864 | tf_op jit(solution)/shard_map/all_to_all | solution.py:103
  99.7 1.2 gather_fusion.1
  100.8 0.7 reshape.87
  101.5 17.7 %all-to-all-done.3 = bf16[4,96,1024]{2,1,0:T(8,128)(2,1)S(1)} async-done(((bf16[4,96,1024]{2,1,0:T(8,128)(2,1)}), bf16[4,96,1024]{2,1,0:T(8,128)(2,1)S(1)}, u32[]{:S(2)}, u32[]{:S(2)}) %all-to-all-start.3) | async-done | bytes 786464 | tf_op jit(solution)/shard_map/all_to_all | solution.py:103
  119.2 1.2 gather_fusion.3
  120.4 0.2 reshape.86
  120.6 2.1 %reduce_sum.35 = bf16[128,1024]{1,0:T(8,128)(2,1)} reduce(bf16[128,2,1024]{2,1,0:T(2,128)(2,1)S(1)} %reshape.86, bf16[]{:T(256)} %constant.16.clone.1), dimensions={1}, to_apply=%region_6.7 | reduce | flops 131072 | bytes 786434 | tf_op jit(solution)/shard_map/reduce_sum | solution.py:113
  122.7 2.1 %multiply_reduce_fusion = bf16[128,1024]{1,0:T(8,128)(2,1)} fusion(f32[128,2,1024]{2,1,0:T(2,128)S(1)} %reshape.87, f32[128,2]{1,0:T(8,128)S(1)} %copy.13), kind=kLoop, calls=%fused_computation.10 | loop fusion | flops 393216 | bytes 1311744 | tf_op jit(solution)/shard_map/reduce_sum | solution.py:107
  124.7 1.6 %multiply_bitcast_fusion = f32[1,128,384]{2,1,0:T(8,128)} fusion(f32[128,384]{1,0:T(8,128)} %reduce-scatter.2.cloned.1.call-done), kind=kLoop, calls=%fused_computation.27 | loop fusion | flops 49152 | bytes 393216 | tf_op jit(solution)/shard_map/transpose;reshape | solution.py:121
  (30 shorter events, 0.2 us)
Async XLA Ops:
  16.0 6.5 %copy-start.8 = (f32[128,2]{0,1:T(2,128)S(1)}, f32[128,2]{0,1:T(2,128)}, u32[]{:S(2)}) copy-start(f32[128,2]{0,1:T(2,128)} %param.9) | copy-start | bytes 3076
  16.0 6.6 %copy-start.4 = (bf16[128,1024]{1,0:T(8,128)(2,1)S(1)}, bf16[128,1024]{1,0:T(8,128)(2,1)}, u32[]{:S(2)}) copy-start(bf16[128,1024]{1,0:T(8,128)(2,1)} %param.13) | copy-start | bytes 786436
  16.0 26.6 %all-to-all-start = ((bf16[4,96,1024]{2,1,0:T(8,128)(2,1)}), bf16[4,96,1024]{2,1,0:T(8,128)(2,1)S(1)}, u32[]{:S(2)}, u32[]{:S(2)}) async-start(bf16[4,96,1024]{2,1,0:T(8,128)(2,1)} %bitcast.4), calls=%async_computation | async-start | bytes 1572864 | tf_op jit(solution)/shard_map/all_to_all | solution.py:75
  22.6 3.7 %copy-start.5 = (bf16[1,128,384]{2,1,0:T(8,128)(2,1)S(1)}, bf16[1,128,384]{2,1,0:T(8,128)(2,1)}, u32[]{:S(2)}) copy-start(bf16[1,128,384]{2,1,0:T(8,128)(2,1)} %param.10) | copy-start | bytes 294916
  36.7 9.3 %copy-start.6 = (bf16[1,128,384]{2,1,0:T(8,128)(2,1)S(1)}, bf16[1,128,384]{2,1,0:T(8,128)(2,1)}, u32[]{:S(2)}) copy-start(bf16[1,128,384]{2,1,0:T(8,128)(2,1)} %param.11) | copy-start | bytes 294916
  37.8 18.7 %copy-start.7 = (bf16[1,128,384]{2,1,0:T(8,128)(2,1)S(1)}, bf16[1,128,384]{2,1,0:T(8,128)(2,1)}, u32[]{:S(2)}) copy-start(bf16[1,128,384]{2,1,0:T(8,128)(2,1)} %param.12) | copy-start | bytes 294916
  42.5 27.8 %all-to-all-start.2 = ((bf16[4,96,1024]{2,1,0:T(8,128)(2,1)}), bf16[4,96,1024]{2,1,0:T(8,128)(2,1)S(1)}, u32[]{:S(2)}, u32[]{:S(2)}) async-start(bf16[4,96,1024]{2,1,0:T(8,128)(2,1)} %fusion), calls=%async_computation.2 | async-start | bytes 1572864 | tf_op jit(solution)/shard_map/all_to_all | solution.py:76
  56.5 12.3 %copy-start = (bf16[1,1024,384]{2,1,0:T(8,128)(2,1)}, bf16[1,1024,384]{2,1,0:T(8,128)(2,1)S(1)}, u32[]{:S(2)}) copy-start(bf16[1,1024,384]{2,1,0:T(8,128)(2,1)S(1)} %all_gather.10) | copy-start | bytes 2359300
  67.4 1.4 %copy-start.2 = (f32[384,384]{1,0:T(8,128)}, f32[384,384]{1,0:T(8,128)S(1)}, u32[]{:S(2)}) copy-start(f32[384,384]{1,0:T(8,128)S(1)} %fusion.9) | copy-start | bytes 1769476
  70.3 25.7 %all-to-all-start.1 = ((bf16[4,96,1024]{2,1,0:T(8,128)(2,1)}), bf16[4,96,1024]{2,1,0:T(8,128)(2,1)S(1)}, u32[]{:S(2)}, u32[]{:S(2)}) async-start(bf16[4,96,1024]{2,1,0:T(8,128)(2,1)} %bitcast.9), calls=%async_computation.1 | async-start | bytes 1572864 | tf_op jit(solution)/shard_map/all_to_all | solution.py:95
  75.3 49.4 %reduce-scatter.2.cloned.1.call-start = ((), (), s32[]{:S(2)}) async-start(), calls=%async_computation.5 | async-start | bytes 1769472 | tf_op jit(solution)/shard_map/reduce_scatter | solution.py:120
  77.2 1.1 copy-start.3
  77.2 1.2 copy-start.9
  78.5 1.1 copy-start.1
  96.0 23.2 %all-to-all-start.3 = ((bf16[4,96,1024]{2,1,0:T(8,128)(2,1)}), bf16[4,96,1024]{2,1,0:T(8,128)(2,1)S(1)}, u32[]{:S(2)}, u32[]{:S(2)}) async-start(bf16[4,96,1024]{2,1,0:T(8,128)(2,1)} %bitcast.13), calls=%async_computation.3 | async-start | bytes 1572864 | tf_op jit(solution)/shard_map/all_to_all | solution.py:103
Sparse Core Ops, SparseCore 0:
  79.4 38.8 reduce-scatter.1
where the time goes:
time: 134 us; the launch traced here: 133 us
  waiting for transfers between devices  37.3 us (28%)
  blocking collectives  31.2 us (23%)
  starting transfers between devices  18.7 us (14%)
  local copies, waits for them, and re-layouts  14.8 us (11%)
  between operations  14.2 us (11%)
  other arithmetic  8.93 us (7%)
  matrix products  8.06 us (6%)
    all_to_all x1, waiting for transfers between devices, local(): lax.all_to_all(grad_send, 'expert', split_axis=0, concat_axis=0, tiled=True)  17.7 us
    all_to_all x1, waiting for transfers between devices, local(): lax.all_to_all(out_send, 'expert', split_axis=0, concat_axis=0, tiled=True)  14.8 us
    all_gather x1, blocking collectives, local(): lax.all_gather(w_up, 'dp', axis=1, tiled=True)  10.4 us
    all_gather x1, blocking collectives, local(): lax.all_gather(w_gate, 'dp', axis=1, tiled=True)  10.4 us
    all_gather x1, blocking collectives, local(): lax.all_gather(w_down, 'dp', axis=1, tiled=True)  10.4 us
    all_to_all x1, starting transfers between devices, local(): lax.all_to_all(send_rows, 'expert', split_axis=0, concat_axis=0, tiled=True)  6.48 us
    all_to_all x1, starting transfers between devices, local(): lax.all_to_all(out_send, 'expert', split_axis=0, concat_axis=0, tiled=True)  5.03 us
    all_to_all x1, waiting for transfers between devices, local(): lax.all_to_all(send_rows, 'expert', split_axis=0, concat_axis=0, tiled=True)  4.76 us
  transfers between devices with their start and end apart: 5, of which 3 were waited for; matrix products, arithmetic and copies ran while one was open for 15% of the time, Pallas kernels for 0%

commit v1 on v0

--- a/solution.py
+++ b/solution.py
@@ -66,11 +66,14 @@
         .astype(jnp.bfloat16)
         .reshape(experts_all, capacity, width)
     )
-    gate_full, up_full, down_full = (
-        lax.all_gather(w_gate, "dp", axis=1, tiled=True),
-        lax.all_gather(w_up, "dp", axis=1, tiled=True),
-        lax.all_gather(w_down, "dp", axis=1, tiled=True),
-    )
+    shard_d = w_gate.shape[1]
+    packed = jnp.concatenate([w_gate, w_up, w_down], axis=2)
+    packed = jnp.transpose(packed, (1, 0, 2)).reshape(shard_d, local_count * 3 * ff_width)
+    full = lax.all_gather(packed, "dp", axis=0, tiled=True)
+    full = jnp.transpose(full.reshape(width, local_count, 3 * ff_width), (1, 0, 2))
+    gate_full = full[:, :, :ff_width]
+    up_full = full[:, :, ff_width : 2 * ff_width]
+    down_full = full[:, :, 2 * ff_width :]
     recv_rows, recv_grads = (
         lax.all_to_all(send_rows, "expert", split_axis=0, concat_axis=0, tiled=True),
         lax.all_to_all(send_grads, "expert", split_axis=0, concat_axis=0, tiled=True),

time: 134 us -> 128 us (0.955)
  blocking collectives: 31.2 us -> 0 us
  waiting for transfers between devices: 37.3 us -> 57.9 us
  matrix products: 8.06 us -> 14.1 us
  other arithmetic: 8.93 us -> 10.7 us
  starting transfers between devices: 18.7 us -> 17.1 us
    all_gather x3 -> x0, blocking collectives: 31.2 us -> none  [the longest x1 10.4 us: local(): lax.all_gather(w_up, 'dp', axis=1, tiled=True)]
    all_to_all x1, waiting for transfers between devices: 0.01 us -> 13.6 us  [local(): lax.all_to_all(send_grads, 'expert', split_axis=0, concat_axis=0, tiled=T...]
    all_to_all x1, waiting for transfers between devices: 4.76 us -> 15.2 us  [local(): lax.all_to_all(send_rows, 'expert', split_axis=0, concat_axis=0, tiled=True)]
    all_to_all x1, waiting for transfers between devices: 14.8 us -> 11.5 us  [local(): lax.all_to_all(out_send, 'expert', split_axis=0, concat_axis=0, tiled=True)]
    concatenate x0 -> x1, other arithmetic: none -> 1.72 us  [local(): packed = jnp.concatenate([w_gate, w_up, w_down], axis=2)]
    all_to_all x1, starting transfers between devices: 5.03 us -> 3.49 us  [local(): lax.all_to_all(out_send, 'expert', split_axis=0, concat_axis=0, tiled=True)]
  transfers between devices with their start and end apart: 5 -> 6, of which waited for: 3 -> 4; matrix products, arithmetic and copies ran while one was open for 15% -> 27% of each run, Pallas kernels for 0% -> 0%
where the time goes in v1:
time: 128 us
  waiting for transfers between devices  57.9 us (45%)
  starting transfers between devices  17.1 us (13%)
  between operations  14.2 us (11%)
  matrix products  14.1 us (11%)
  local copies, waits for them, and re-layouts  13.7 us (11%)
  other arithmetic  10.7 us (8%)
    all_to_all x1, waiting for transfers between devices, local(): lax.all_to_all(grad_send, 'expert', split_axis=0, concat_axis=0, tiled=True)  17.6 us
    all_to_all x1, waiting for transfers between devices, local(): lax.all_to_all(send_rows, 'expert', split_axis=0, concat_axis=0, tiled=True)  15.2 us
    all_to_all x1, waiting for transfers between devices, local(): lax.all_to_all(send_grads, 'expert', split_axis=0, concat_axis=0, tiled=T...  13.6 us
    all_to_all x1, waiting for transfers between devices, local(): lax.all_to_all(out_send, 'expert', split_axis=0, concat_axis=0, tiled=True)  11.5 us
    all_to_all x1, starting transfers between devices, local(): lax.all_to_all(send_rows, 'expert', split_axis=0, concat_axis=0, tiled=True)  6.35 us
    all_to_all x1, starting transfers between devices, local(): lax.all_to_all(grad_send, 'expert', split_axis=0, concat_axis=0, tiled=True)  3.67 us
    all_to_all x1, starting transfers between devices, local(): lax.all_to_all(send_grads, 'expert', split_axis=0, concat_axis=0, tiled=T...  3.49 us
    all_to_all x1, starting transfers between devices, local(): lax.all_to_all(out_send, 'expert', split_axis=0, concat_axis=0, tiled=True)  3.49 us
  transfers between devices with their start and end apart: 6, of which 4 were waited for; matrix products, arithmetic and copies ran while one was open for 27% of the time, Pallas kernels for 0%

profile of v1, /device:TPU:0, one launch (start us, length us, event | category | flops | bytes accessed | tf_op | source)
XLA Modules:
  0.0 127.7 jit_solution(5773724412011694440)
XLA Ops:
  7.2 0.0 all-gather.3.cloned.1.call-start
  7.2 1.7 %pad_maximum_fusion = bf16[1,128,1152]{2,1,0:T(8,128)(2,1)} fusion(bf16[1,128,384]{2,1,0:T(8,128)(2,1)} %param.12, bf16[1,128,384]{2,1,0:T(8,128)(2,1)} %param.11, bf16[1,128,384]{2,1,0:T(8,128)(2,1)} %param.10), kind=kLoop, calls=%fused_computation.22 | loop fusion | flops 884736 | bytes 589824 | tf_op jit(solution)/shard_map/concatenate | solution.py:70
  8.9 0.0 all-gather.3.cloned.1.call-update
  9.0 0.8 copy.15
  9.7 0.1 eq.29
  9.9 0.1 eq.25
  10.0 0.7 broadcast_multiply_fusion
  10.7 0.1 copy.14
  10.8 0.1 mul.65
  11.0 1.2 reduce-window.6
  12.2 0.1 slice.28
  12.3 0.1 copy.17
  12.4 0.1 copy.18
  12.5 1.0 concatenate.9
  13.5 0.1 add_bitcast_fusion
  13.6 1.4 %scatter_custom_fusion = s32[384]{0:T(512)S(1)} fusion(s32[256]{0:T(256)S(1)} %bitcast.61, s32[256]{0:T(256)S(1)} %and_select_fusion, s32[]{:T(128)} %constant.32.clone.1), kind=kCustom, calls=%fused_computation.43 | custom fusion | bytes 1540 | tf_op jit(solution)/shard_map/scatter | solution.py:52
  15.1 2.7 %gather_fusion = bf16[384,1024]{1,0:T(8,128)(2,1)} fusion(bf16[129,1024]{1,0:T(8,128)(2,1)S(1)} %concatenate.9, s32[1024]{0:T(1024)S(1)} %pad_clamp_fusion.1), kind=kCustom, calls=%fused_computation | custom fusion | bytes 1574400 | tf_op jit(solution)/shard_map/gather | solution.py:60
  17.8 6.3 %all-to-all-start = ((bf16[4,96,1024]{2,1,0:T(8,128)(2,1)}), bf16[4,96,1024]{2,1,0:T(8,128)(2,1)S(1)}, u32[]{:S(2)}, u32[]{:S(2)}) async-start(bf16[4,96,1024]{2,1,0:T(8,128)(2,1)} %bitcast.4), calls=%async_computation | async-start | bytes 1572864 | tf_op jit(solution)/shard_map/all_to_all | solution.py:78
  24.1 0.1 copy.13
  24.2 0.1 reshape.133
  24.4 1.4 %scatter_custom_fusion.1 = f32[384]{0:T(512)S(1)} fusion(s32[256]{0:T(256)S(1)} %bitcast.62, f32[256]{0:T(256)S(1)} %reshape.133, f32[]{:T(128)} %constant.40.clone.1), kind=kCustom, calls=%fused_computation.41 | custom fusion | bytes 1540 | tf_op jit(solution)/shard_map/scatter | solution.py:57
  25.8 0.1 mul.70
  25.9 2.1 %gather_fusion.2 = bf16[384,1024]{1,0:T(8,128)(2,1)S(1)} fusion(bf16[129,1024]{1,0:T(8,128)(2,1)S(1)} %concatenate.11, s32[1024]{0:T(1024)S(1)} %pad_clamp_fusion.1), kind=kCustom, calls=%fused_computation.2 | custom fusion | bytes 1574400 | tf_op jit(solution)/shard_map/gather | solution.py:63
  28.0 1.1 fusion
  29.0 15.2 %all-to-all-done = bf16[4,96,1024]{2,1,0:T(8,128)(2,1)S(1)} async-done(((bf16[4,96,1024]{2,1,0:T(8,128)(2,1)}), bf16[4,96,1024]{2,1,0:T(8,128)(2,1)S(1)}, u32[]{:S(2)}, u32[]{:S(2)}) %all-to-all-start) | async-done | bytes 786464 | tf_op jit(solution)/shard_map/all_to_all | solution.py:78
  44.2 3.5 %all-to-all-start.2 = ((bf16[4,96,1024]{2,1,0:T(8,128)(2,1)}), bf16[4,96,1024]{2,1,0:T(8,128)(2,1)S(1)}, u32[]{:S(2)}, u32[]{:S(2)}) async-start(bf16[4,96,1024]{2,1,0:T(8,128)(2,1)} %fusion), calls=%async_computation.2 | async-start | bytes 1572864 | tf_op jit(solution)/shard_map/all_to_all | solution.py:79
  47.7 0.0 all-gather.3.cloned.1.call-done
  47.7 1.7 %fusion.2 = f32[384,384]{1,0:T(8,128)S(1)} fusion(bf16[384,1024]{1,0:T(8,128)(2,1)S(1)} %bitcast.59, bf16[1,1024,1152]{2,1,0:T(8,128)(2,1)} %all-gather.3.cloned.1.call-done), kind=kOutput, calls=%fused_computation.15 | convolution fusion | flops 301989888 | bytes 2162688 | tf_op jit(solution)/shard_map/dot_general | solution.py:11
  49.4 1.7 %multiply_convert_fusion.2 = (bf16[384,384]{1,0:T(8,128)(2,1)S(1)}, f32[384,384]{1,0:T(8,128)S(1)}) fusion(f32[384,384]{1,0:T(8,128)S(1)} %fusion.2, bf16[384,1024]{1,0:T(8,128)(2,1)S(1)} %bitcast.60, bf16[1,1024,1152]{2,1,0:T(8,128)(2,1)} %all-gather.3.cloned.1.call-done), kind=kOutput, calls=%fused_computation.20 | convolution fusion | flops 302874624 | bytes 3047424 | tf_op jit(solution)/shard_map/dot_general | solution.py:12
  51.2 2.6 %convolution_convert_fusion = bf16[384,1024]{1,0:T(8,128)(2,1)} fusion(bf16[384,384]{1,0:T(8,128)(2,1)S(1)} %get-tuple-element.3, bf16[1,1024,1152]{2,1,0:T(8,128)(2,1)} %all-gather.3.cloned.1.call-done), kind=kOutput, calls=%fused_computation.9 | convolution fusion | flops 302383104 | bytes 1867776 | tf_op jit(solution)/shard_map/dot_general | solution.py:15
  53.8 13.6 %all-to-all-done.2 = bf16[4,96,1024]{2,1,0:T(8,128)(2,1)S(1)} async-done(((bf16[4,96,1024]{2,1,0:T(8,128)(2,1)}), bf16[4,96,1024]{2,1,0:T(8,128)(2,1)S(1)}, u32[]{:S(2)}, u32[]{:S(2)}) %all-to-all-start.2) | async-done | bytes 786464 | tf_op jit(solution)/shard_map/all_to_all | solution.py:79
  67.3 3.5 %all-to-all-start.1 = ((bf16[4,96,1024]{2,1,0:T(8,128)(2,1)}), bf16[4,96,1024]{2,1,0:T(8,128)(2,1)S(1)}, u32[]{:S(2)}, u32[]{:S(2)}) async-start(bf16[4,96,1024]{2,1,0:T(8,128)(2,1)} %bitcast.9), calls=%async_computation.1 | async-start | bytes 1572864 | tf_op jit(solution)/shard_map/all_to_all | solution.py:98
  70.8 0.0 reduce-scatter.2.cloned.1.call-start
  70.9 1.9 %fusion.16 = f32[1024,384]{1,0:T(8,128)} fusion(bf16[384,1024]{1,0:T(8,128)(2,1)S(1)} %bitcast.56, bf16[384,384]{1,0:T(8,128)(2,1)S(1)} %get-tuple-element.3), kind=kOutput, calls=%fused_computation.48 | convolution fusion | flops 301989888 | bytes 2654208 | tf_op jit(solution)/shard_map/dot_general | solution.py:120
  72.8 0.0 reduce-scatter.2.cloned.1.call-update
  72.8 1.7 %fusion.4 = f32[384,384]{1,0:T(8,128)S(1)} fusion(bf16[384,1024]{1,0:T(8,128)(2,1)S(1)} %bitcast.57, bf16[1,1024,1152]{2,1,0:T(8,128)(2,1)} %all-gather.3.cloned.1.call-done), kind=kOutput, calls=%fused_computation.17 | convolution fusion | flops 301989888 | bytes 2162688 | tf_op jit(solution)/shard_map/dot_general | solution.py:22
  74.5 1.8 %fusion.1 = f32[384,1024]{1,0:T(8,128)S(1)} fusion(bf16[1,1024,1152]{2,1,0:T(8,128)(2,1)} %all-gather.3.cloned.1.call-done, f32[384,384]{1,0:T(8,128)S(1)} %fusion.2, f32[384,384]{1,0:T(8,128)S(1)} %fusion.4, f32[384,384]{1,0:T(8,128)S(1)} %get-tuple-element.4), kind=kOutput, calls=%fused_computation.14 | convolution fusion | flops 303464448 | bytes 4128768 | tf_op jit(solution)/shard_map/dot_general | solution.py:27
  76.3 2.7 %add_convert_fusion = bf16[384,1024]{1,0:T(8,128)(2,1)} fusion(f32[384,1024]{1,0:T(8,128)S(1)} %fusion.1, bf16[1,1024,1152]{2,1,0:T(8,128)(2,1)} %all-gather.3.cloned.1.call-done, f32[384,384]{1,0:T(8,128)S(1)} %fusion.4, f32[384,384]{1,0:T(8,128)S(1)} %fusion.2), kind=kOutput, calls=%fused_computation.8 | convolution fusion | flops 303661056 | bytes 4325376 | tf_op jit(solution)/shard_map/dot_general | solution.py:28
  79.0 11.5 %all-to-all-done.1 = bf16[4,96,1024]{2,1,0:T(8,128)(2,1)S(1)} async-done(((bf16[4,96,1024]{2,1,0:T(8,128)(2,1)}), bf16[4,96,1024]{2,1,0:T(8,128)(2,1)S(1)}, u32[]{:S(2)}, u32[]{:S(2)}) %all-to-all-start.1) | async-done | bytes 786464 | tf_op jit(solution)/shard_map/all_to_all | solution.py:98
  90.5 3.7 %all-to-all-start.3 = ((bf16[4,96,1024]{2,1,0:T(8,128)(2,1)}), bf16[4,96,1024]{2,1,0:T(8,128)(2,1)S(1)}, u32[]{:S(2)}, u32[]{:S(2)}) async-start(bf16[4,96,1024]{2,1,0:T(8,128)(2,1)} %bitcast.13), calls=%async_computation.3 | async-start | bytes 1572864 | tf_op jit(solution)/shard_map/all_to_all | solution.py:106
  94.2 1.2 gather_fusion.1
  95.3 0.7 reshape.87
  96.0 17.6 %all-to-all-done.3 = bf16[4,96,1024]{2,1,0:T(8,128)(2,1)S(1)} async-done(((bf16[4,96,1024]{2,1,0:T(8,128)(2,1)}), bf16[4,96,1024]{2,1,0:T(8,128)(2,1)S(1)}, u32[]{:S(2)}, u32[]{:S(2)}) %all-to-all-start.3) | async-done | bytes 786464 | tf_op jit(solution)/shard_map/all_to_all | solution.py:106
  113.6 1.2 gather_fusion.3
  114.8 0.2 reshape.86
  115.0 2.1 %reduce_sum.35 = bf16[128,1024]{1,0:T(8,128)(2,1)} reduce(bf16[128,2,1024]{2,1,0:T(2,128)(2,1)S(1)} %reshape.86, bf16[]{:T(256)} %constant.16.clone.1), dimensions={1}, to_apply=%region_6.7 | reduce | flops 131072 | bytes 786434 | tf_op jit(solution)/shard_map/reduce_sum | solution.py:116
  117.1 2.1 %multiply_reduce_fusion = bf16[128,1024]{1,0:T(8,128)(2,1)} fusion(f32[128,2,1024]{2,1,0:T(2,128)S(1)} %reshape.87, f32[128,2]{1,0:T(8,128)S(1)} %copy.13), kind=kLoop, calls=%fused_computation.10 | loop fusion | flops 393216 | bytes 1311744 | tf_op jit(solution)/shard_map/reduce_sum | solution.py:110
  119.2 1.6 %multiply_bitcast_fusion = f32[1,128,384]{2,1,0:T(8,128)} fusion(f32[128,384]{1,0:T(8,128)} %reduce-scatter.2.cloned.1.call-done), kind=kLoop, calls=%fused_computation.25 | loop fusion | flops 49152 | bytes 393216 | tf_op jit(solution)/shard_map/transpose;reshape | solution.py:124
  (15 shorter events, 0.1 us)
Async XLA Ops:
  7.2 40.6 %all-gather.3.cloned.1.call-start = ((), (), s32[]{:S(2)}) async-start(), calls=%async_computation.6 | async-start | bytes 2654208 | tf_op jit(solution)/shard_map/all_gather | solution.py:72
  15.0 9.1 %copy-start.1 = (f32[128,2]{0,1:T(2,128)S(1)}, f32[128,2]{0,1:T(2,128)}, u32[]{:S(2)}) copy-start(f32[128,2]{0,1:T(2,128)} %param.9) | copy-start | bytes 3076
  15.1 10.8 %copy-start = (bf16[128,1024]{1,0:T(8,128)(2,1)S(1)}, bf16[128,1024]{1,0:T(8,128)(2,1)}, u32[]{:S(2)}) copy-start(bf16[128,1024]{1,0:T(8,128)(2,1)} %param.13) | copy-start | bytes 786436
  17.8 26.5 %all-to-all-start = ((bf16[4,96,1024]{2,1,0:T(8,128)(2,1)}), bf16[4,96,1024]{2,1,0:T(8,128)(2,1)S(1)}, u32[]{:S(2)}, u32[]{:S(2)}) async-start(bf16[4,96,1024]{2,1,0:T(8,128)(2,1)} %bitcast.4), calls=%async_computation | async-start | bytes 1572864 | tf_op jit(solution)/shard_map/all_to_all | solution.py:78
  44.2 23.1 %all-to-all-start.2 = ((bf16[4,96,1024]{2,1,0:T(8,128)(2,1)}), bf16[4,96,1024]{2,1,0:T(8,128)(2,1)S(1)}, u32[]{:S(2)}, u32[]{:S(2)}) async-start(bf16[4,96,1024]{2,1,0:T(8,128)(2,1)} %fusion), calls=%async_computation.2 | async-start | bytes 1572864 | tf_op jit(solution)/shard_map/all_to_all | solution.py:79
  67.3 23.1 %all-to-all-start.1 = ((bf16[4,96,1024]{2,1,0:T(8,128)(2,1)}), bf16[4,96,1024]{2,1,0:T(8,128)(2,1)S(1)}, u32[]{:S(2)}, u32[]{:S(2)}) async-start(bf16[4,96,1024]{2,1,0:T(8,128)(2,1)} %bitcast.9), calls=%async_computation.1 | async-start | bytes 1572864 | tf_op jit(solution)/shard_map/all_to_all | solution.py:98
  70.8 48.4 %reduce-scatter.2.cloned.1.call-start = ((), (), s32[]{:S(2)}) async-start(), calls=%async_computation.5 | async-start | bytes 1769472 | tf_op jit(solution)/shard_map/reduce_scatter | solution.py:123
  90.5 23.1 %all-to-all-start.3 = ((bf16[4,96,1024]{2,1,0:T(8,128)(2,1)}), bf16[4,96,1024]{2,1,0:T(8,128)(2,1)S(1)}, u32[]{:S(2)}, u32[]{:S(2)}) async-start(bf16[4,96,1024]{2,1,0:T(8,128)(2,1)} %bitcast.13), calls=%async_computation.3 | async-start | bytes 1572864 | tf_op jit(solution)/shard_map/all_to_all | solution.py:106
Sparse Core Ops, SparseCore 0:
  9.9 31.6 all-gather.2
  75.0 39.7 reduce-scatter.1

commit v2 on v1

--- a/solution.py
+++ b/solution.py
@@ -44,23 +44,28 @@
     onehot = (chosen[:, None] == jnp.arange(experts_all, dtype=jnp.int32)[None, :]).astype(
         jnp.int32
     )
-    before = jnp.cumsum(onehot, axis=0) - onehot
+    earlier = (
+        jnp.arange(pair_count, dtype=jnp.int32)[:, None]
+        > jnp.arange(pair_count, dtype=jnp.int32)[None, :]
+    ).astype(jnp.bfloat16)
+    before = jnp.dot(
+        earlier, onehot.astype(jnp.bfloat16), preferred_element_type=jnp.float32
+    ).astype(jnp.int32)
     slot_index = jnp.sum(before * onehot, axis=1)
     flat_index = chosen * capacity + slot_index
-    owner_row = jnp.arange(pair_count, dtype=jnp.int32) // top_count
-    slot_owner = (
-        jnp.full((experts_all * capacity,), tok_rows, jnp.int32).at[flat_index].set(owner_row)
+    slots = experts_all * capacity
+    hit = flat_index[:, None] == jnp.arange(slots, dtype=jnp.int32)[None, :]
+    hit3 = hit.reshape(tok_rows, top_count, slots)
+    dispatch = jnp.any(hit3, axis=1).astype(jnp.bfloat16)
+    send_rows = (
+        lax.dot_general(dispatch, tokens, contract_first, preferred_element_type=jnp.float32)
+        .astype(jnp.bfloat16)
+        .reshape(experts_all, capacity, width)
     )
-    weight_slot = (
-        jnp.zeros((experts_all * capacity,), jnp.float32)
-        .at[flat_index]
-        .set(routing.reshape(pair_count))
+    weight_slot = jnp.sum(jnp.where(hit, routing.reshape(pair_count)[:, None], 0.0), axis=0)
+    grads_picked = lax.dot_general(
+        dispatch, grad_out, contract_first, preferred_element_type=jnp.float32
     )
-    zero_row = jnp.zeros((1, width), jnp.bfloat16)
-    send_rows = jnp.concatenate([tokens, zero_row], axis=0)[slot_owner].reshape(
-        experts_all, capacity, width
-    )
-    grads_picked = jnp.concatenate([grad_out, zero_row], axis=0)[slot_owner].astype(jnp.float32)
     send_grads = (
         (weight_slot[:, None] * grads_picked)
         .astype(jnp.bfloat16)
@@ -104,16 +109,19 @@
     grad_parts = [backward_rows(g_used, gate_pre, up_pre, gate_w, up_w, down_w)]
     grad_send = jnp.stack(grad_parts, axis=1).reshape(groups * local_count, capacity, width)
     back_grad = lax.all_to_all(grad_send, "expert", split_axis=0, concat_axis=0, tiled=True)
-    out_rows = back_out.reshape(experts_all * capacity, width)[flat_index].reshape(
-        tok_rows, top_count, width
-    )
-    output = jnp.sum(routing[:, :, None] * out_rows.astype(jnp.float32), axis=1).astype(
-        jnp.bfloat16
-    )
-    grad_rows = back_grad.reshape(experts_all * capacity, width)[flat_index].reshape(
-        tok_rows, top_count, width
-    )
-    token_grad = jnp.sum(grad_rows.astype(jnp.float32), axis=1).astype(jnp.bfloat16)
+    back_out_flat = back_out.reshape(slots, width)
+    output = None
+    for choice in range(top_count):
+        pick = hit3[:, choice, :].astype(jnp.bfloat16)
+        part = routing[:, choice][:, None] * jnp.dot(
+            pick, back_out_flat, preferred_element_type=jnp.float32
+        )
+        output = part if output is None else output + part
+    output = output.astype(jnp.bfloat16)
+    gather_both = jnp.sum(hit3.astype(jnp.int32), axis=1).astype(jnp.bfloat16)
+    token_grad = jnp.dot(
+        gather_both, back_grad.reshape(slots, width), preferred_element_type=jnp.float32
+    ).astype(jnp.bfloat16)
     shard_rows = w_gate.shape[1]
     saved = forward_parts[0]
     grad_cols = saved[3]

time: 128 us -> 126 us (0.984)
  waiting for transfers between devices: 57.9 us -> 70.3 us
  local copies, waits for them, and re-layouts: 13.7 us -> 2.12 us
  other arithmetic: 10.7 us -> 4.46 us
  matrix products: 14.1 us -> 17.1 us
    gather x4 -> x0, local copies, waits for them, and re-layouts: 7.09 us -> none  [the longest x1 2.68 us: local(): jnp.concatenate([tokens, zero_row], axis=0)[slot_owner]]
    all_to_all x1, waiting for transfers between devices: 11.5 us -> 18.5 us  [local(): lax.all_to_all(out_send, 'expert', split_axis=0, concat_axis=0, tiled=True)]
    all_to_all x1, waiting for transfers between devices: 13.6 us -> 18.8 us  [local(): lax.all_to_all(send_grads, 'expert', split_axis=0, concat_axis=0, tiled=T...]
    dot_general x0 -> x6, matrix products: none -> 5.15 us  [the longest x2 1.32 us: local(): jnp.dot(pick, back_out_flat, preferred_element_type=jnp.float32)]
    reduce_sum x3 -> x2, other arithmetic: 4.24 us -> 0.25 us  [the longest x1 0.15 us: local(): jnp.sum(jnp.where(hit, routing.reshape(pair_count)[:, None], 0.0), axis=0)]
    all_to_all x1, starting transfers between devices: 6.35 us -> 3.49 us  [local(): lax.all_to_all(send_rows, 'expert', split_axis=0, concat_axis=0, tiled=True)]
    all_to_all x1, starting transfers between devices: 3.49 us -> 6.35 us  [local(): lax.all_to_all(send_grads, 'expert', split_axis=0, concat_axis=0, tiled=T...]
    scatter x2 -> x0, local copies, waits for them, and re-layouts: 2.79 us -> none  [the longest x1 1.4 us: local(): jnp.full((experts_all * capacity,), tok_rows, jnp.int32).at[flat_index]]
  transfers between devices with their start and end apart: 6 -> 6, of which waited for: 4 -> 4; matrix products, arithmetic and copies ran while one was open for 27% -> 12% of each run, Pallas kernels for 0% -> 0%
where the time goes in v2:
time: 126 us; the launch traced here: 125 us
  waiting for transfers between devices  70.3 us (56%)
  matrix products  17.1 us (14%)
  starting transfers between devices  16.9 us (13%)
  between operations  14.2 us (11%)
  other arithmetic  4.46 us (4%)
  local copies, waits for them, and re-layouts  2.12 us (2%)
    all_to_all x1, waiting for transfers between devices, local(): lax.all_to_all(send_grads, 'expert', split_axis=0, concat_axis=0, tiled=T...  18.8 us
    all_to_all x1, waiting for transfers between devices, local(): lax.all_to_all(out_send, 'expert', split_axis=0, concat_axis=0, tiled=True)  18.5 us
    all_to_all x1, waiting for transfers between devices, local(): lax.all_to_all(send_rows, 'expert', split_axis=0, concat_axis=0, tiled=True)  17.9 us
    all_to_all x1, waiting for transfers between devices, local(): lax.all_to_all(grad_send, 'expert', split_axis=0, concat_axis=0, tiled=True)  15.1 us
    all_to_all x1, starting transfers between devices, local(): lax.all_to_all(send_grads, 'expert', split_axis=0, concat_axis=0, tiled=T...  6.35 us
    all_to_all x1, starting transfers between devices, local(): lax.all_to_all(send_rows, 'expert', split_axis=0, concat_axis=0, tiled=True)  3.49 us
    all_to_all x1, starting transfers between devices, local(): lax.all_to_all(out_send, 'expert', split_axis=0, concat_axis=0, tiled=True)  3.49 us
    all_to_all x1, starting transfers between devices, local(): lax.all_to_all(grad_send, 'expert', split_axis=0, concat_axis=0, tiled=True)  3.49 us
  transfers between devices with their start and end apart: 6, of which 4 were waited for; matrix products, arithmetic and copies ran while one was open for 12% of the time, Pallas kernels for 0%

profile of v2, /device:TPU:0, one launch (start us, length us, event | category | flops | bytes accessed | tf_op | source)
XLA Modules:
  0.0 125.1 jit_solution(9355336804597339415)
XLA Ops:
  7.2 0.0 copy-start
  7.2 0.0 copy-start.1
  7.2 0.0 all-gather.3.cloned.1.call-start
  7.2 1.8 %pad_maximum_fusion = bf16[1,128,1152]{2,1,0:T(8,128)(2,1)} fusion(bf16[1,128,384]{2,1,0:T(8,128)(2,1)} %param.12, bf16[1,128,384]{2,1,0:T(8,128)(2,1)} %param.11, bf16[1,128,384]{2,1,0:T(8,128)(2,1)} %param.10), kind=kLoop, calls=%fused_computation.27 | loop fusion | flops 884736 | bytes 589824 | tf_op jit(solution)/shard_map/concatenate | solution.py:75
  9.0 0.0 all-gather.3.cloned.1.call-update
  9.0 0.8 copy.21
  9.8 0.1 eq.35
  9.9 0.2 fusion.3
  10.2 0.1 reduce_sum.30
  10.3 0.1 copy.22
  10.4 0.8 copy.23
  11.2 0.1 broadcast_in_dim.20
  11.3 0.2 select_reduce_fusion
  11.5 0.7 multiply_add_fusion.1
  12.2 0.1 iota_compare_fusion.1
  12.3 0.0 copy-done
  12.3 1.3 %multiply_convert_fusion = bf16[384,1024]{1,0:T(8,128)(2,1)} fusion(pred[128,384]{1,0:T(8,128)(4,1)S(1)} %get-tuple-element.6, bf16[128,1024]{1,0:T(8,128)(2,1)S(1)} %copy-done, f32[384]{0:T(512)S(1)} %select_reduce_fusion), kind=kOutput, calls=%fused_computation.1 | convolution fusion | flops 101449728 | bytes 1099264 | tf_op jit(solution)/shard_map/dot_general | solution.py:66
  13.6 6.3 %all-to-all-start.2 = ((bf16[4,96,1024]{2,1,0:T(8,128)(2,1)}), bf16[4,96,1024]{2,1,0:T(8,128)(2,1)S(1)}, u32[]{:S(2)}, u32[]{:S(2)}) async-start(bf16[4,96,1024]{2,1,0:T(8,128)(2,1)} %bitcast.11), calls=%async_computation.2 | async-start | bytes 1572864 | tf_op jit(solution)/shard_map/all_to_all | solution.py:84
  20.0 0.0 copy-done.1
  20.0 1.3 %convolution_convert_fusion = bf16[384,1024]{1,0:T(8,128)(2,1)} fusion(pred[128,384]{1,0:T(8,128)(4,1)S(1)} %get-tuple-element.6, bf16[128,1024]{1,0:T(8,128)(2,1)S(1)} %copy-done.1), kind=kOutput, calls=%fused_computation.2 | convolution fusion | flops 101056512 | bytes 1097728 | tf_op jit(solution)/shard_map/dot_general | solution.py:61
  21.3 18.8 %all-to-all-done.2 = bf16[4,96,1024]{2,1,0:T(8,128)(2,1)S(1)} async-done(((bf16[4,96,1024]{2,1,0:T(8,128)(2,1)}), bf16[4,96,1024]{2,1,0:T(8,128)(2,1)S(1)}, u32[]{:S(2)}, u32[]{:S(2)}) %all-to-all-start.2) | async-done | bytes 786464 | tf_op jit(solution)/shard_map/all_to_all | solution.py:84
  40.1 3.5 %all-to-all-start = ((bf16[4,96,1024]{2,1,0:T(8,128)(2,1)}), bf16[4,96,1024]{2,1,0:T(8,128)(2,1)S(1)}, u32[]{:S(2)}, u32[]{:S(2)}) async-start(bf16[4,96,1024]{2,1,0:T(8,128)(2,1)} %bitcast.2), calls=%async_computation | async-start | bytes 1572864 | tf_op jit(solution)/shard_map/all_to_all | solution.py:83
  43.6 0.0 all-gather.3.cloned.1.call-done
  43.6 1.7 %fusion.7 = f32[384,384]{1,0:T(8,128)S(1)} fusion(bf16[384,1024]{1,0:T(8,128)(2,1)S(1)} %bitcast.50, bf16[1,1024,1152]{2,1,0:T(8,128)(2,1)} %all-gather.3.cloned.1.call-done), kind=kOutput, calls=%fused_computation.18 | convolution fusion | flops 301989888 | bytes 2162688 | tf_op jit(solution)/shard_map/dot_general | solution.py:22
  45.3 17.9 %all-to-all-done = bf16[4,96,1024]{2,1,0:T(8,128)(2,1)S(1)} async-done(((bf16[4,96,1024]{2,1,0:T(8,128)(2,1)}), bf16[4,96,1024]{2,1,0:T(8,128)(2,1)S(1)}, u32[]{:S(2)}, u32[]{:S(2)}) %all-to-all-start) | async-done | bytes 786464 | tf_op jit(solution)/shard_map/all_to_all | solution.py:83
  63.2 1.7 %fusion.5 = f32[384,384]{1,0:T(8,128)S(1)} fusion(bf16[384,1024]{1,0:T(8,128)(2,1)S(1)} %bitcast.52, bf16[1,1024,1152]{2,1,0:T(8,128)(2,1)} %all-gather.3.cloned.1.call-done), kind=kOutput, calls=%fused_computation.16 | convolution fusion | flops 301989888 | bytes 2162688 | tf_op jit(solution)/shard_map/dot_general | solution.py:11
  64.9 0.0 copy-start.3
  64.9 1.9 %multiply_convert_fusion.3 = (bf16[384,384]{1,0:T(8,128)(2,1)S(1)}, f32[384,384]{1,0:T(8,128)S(1)}) fusion(f32[384,384]{1,0:T(8,128)S(1)} %fusion.5, bf16[384,1024]{1,0:T(8,128)(2,1)S(1)} %bitcast.53, bf16[1,1024,1152]{2,1,0:T(8,128)(2,1)} %all-gather.3.cloned.1.call-done), kind=kOutput, calls=%fused_computation.21 | convolution fusion | flops 302874624 | bytes 3047424 | tf_op jit(solution)/shard_map/dot_general | solution.py:12
  66.8 0.0 copy-done.3
  66.8 0.7 fusion.4
  67.5 1.5 %add_convert_fusion = bf16[384,1024]{1,0:T(8,128)(2,1)} fusion(f32[384,1024]{1,0:T(8,128)S(1)} %fusion.4, bf16[1,1024,1152]{2,1,0:T(8,128)(2,1)S(1)} %copy-done.3, f32[384,384]{1,0:T(8,128)S(1)} %fusion.7, f32[384,384]{1,0:T(8,128)S(1)} %fusion.5), kind=kOutput, calls=%fused_computation | convolution fusion | flops 303661056 | bytes 4325376 | tf_op jit(solution)/shard_map/dot_general | solution.py:28
  69.0 3.5 %all-to-all-start.3 = ((bf16[4,96,1024]{2,1,0:T(8,128)(2,1)}), bf16[4,96,1024]{2,1,0:T(8,128)(2,1)S(1)}, u32[]{:S(2)}, u32[]{:S(2)}) async-start(bf16[4,96,1024]{2,1,0:T(8,128)(2,1)} %bitcast.13), calls=%async_computation.3 | async-start | bytes 1572864 | tf_op jit(solution)/shard_map/all_to_all | solution.py:111
  72.5 0.0 reduce-scatter.2.cloned.1.call-start
  72.6 1.8 %fusion.15 = f32[1024,384]{1,0:T(8,128)} fusion(bf16[384,1024]{1,0:T(8,128)(2,1)S(1)} %bitcast.51, bf16[384,384]{1,0:T(8,128)(2,1)S(1)} %get-tuple-element.7), kind=kOutput, calls=%fused_computation.45 | convolution fusion | flops 301989888 | bytes 2654208 | tf_op jit(solution)/shard_map/dot_general | solution.py:128
  74.4 0.0 copy-start.2
  74.4 0.0 reduce-scatter.2.cloned.1.call-update
  74.4 2.7 %convolution_convert_fusion.1 = bf16[384,1024]{1,0:T(8,128)(2,1)} fusion(bf16[384,384]{1,0:T(8,128)(2,1)S(1)} %get-tuple-element.7, bf16[1,1024,1152]{2,1,0:T(8,128)(2,1)} %all-gather.3.cloned.1.call-done), kind=kOutput, calls=%fused_computation.3 | convolution fusion | flops 302383104 | bytes 1867776 | tf_op jit(solution)/shard_map/dot_general | solution.py:15
  77.1 15.1 %all-to-all-done.3 = bf16[4,96,1024]{2,1,0:T(8,128)(2,1)S(1)} async-done(((bf16[4,96,1024]{2,1,0:T(8,128)(2,1)}), bf16[4,96,1024]{2,1,0:T(8,128)(2,1)S(1)}, u32[]{:S(2)}, u32[]{:S(2)}) %all-to-all-start.3) | async-done | bytes 786464 | tf_op jit(solution)/shard_map/all_to_all | solution.py:111
  92.2 3.5 %all-to-all-start.1 = ((bf16[4,96,1024]{2,1,0:T(8,128)(2,1)}), bf16[4,96,1024]{2,1,0:T(8,128)(2,1)S(1)}, u32[]{:S(2)}, u32[]{:S(2)}) async-start(bf16[4,96,1024]{2,1,0:T(8,128)(2,1)} %bitcast.7), calls=%async_computation.1 | async-start | bytes 1572864 | tf_op jit(solution)/shard_map/all_to_all | solution.py:103
  95.7 0.1 convert_reduce_fusion
  95.8 0.0 copy-done.2
  95.8 1.0 convolution_convert_fusion.2
  96.8 18.5 %all-to-all-done.1 = bf16[4,96,1024]{2,1,0:T(8,128)(2,1)S(1)} async-done(((bf16[4,96,1024]{2,1,0:T(8,128)(2,1)}), bf16[4,96,1024]{2,1,0:T(8,128)(2,1)S(1)}, u32[]{:S(2)}, u32[]{:S(2)}) %all-to-all-start.1) | async-done | bytes 786464 | tf_op jit(solution)/shard_map/all_to_all | solution.py:103
  115.3 0.3 convolution_multiply_fusion.1
  115.6 1.0 fusion.1
  116.6 0.0 reduce-scatter.2.cloned.1.call-done
  116.6 1.6 %multiply_bitcast_fusion = f32[1,128,384]{2,1,0:T(8,128)} fusion(f32[128,384]{1,0:T(8,128)} %reduce-scatter.2.cloned.1.call-done), kind=kLoop, calls=%fused_computation.32 | loop fusion | flops 49152 | bytes 393216 | tf_op jit(solution)/shard_map/transpose;reshape | solution.py:132
  (2 shorter events, 0.0 us)
Async XLA Ops:
  7.2 5.1 %copy-start = (bf16[128,1024]{1,0:T(8,128)(2,1)S(1)}, bf16[128,1024]{1,0:T(8,128)(2,1)}, u32[]{:S(2)}) copy-start(bf16[128,1024]{1,0:T(8,128)(2,1)} %param.13) | copy-start | bytes 786436
  7.2 12.8 %copy-start.1 = (bf16[128,1024]{1,0:T(8,128)(2,1)S(1)}, bf16[128,1024]{1,0:T(8,128)(2,1)}, u32[]{:S(2)}) copy-start(bf16[128,1024]{1,0:T(8,128)(2,1)} %param.7) | copy-start | bytes 786436
  7.2 36.4 %all-gather.3.cloned.1.call-start = ((), (), s32[]{:S(2)}) async-start(), calls=%async_computation.6 | async-start | bytes 2654208 | tf_op jit(solution)/shard_map/all_gather | solution.py:77
  13.6 26.5 %all-to-all-start.2 = ((bf16[4,96,1024]{2,1,0:T(8,128)(2,1)}), bf16[4,96,1024]{2,1,0:T(8,128)(2,1)S(1)}, u32[]{:S(2)}, u32[]{:S(2)}) async-start(bf16[4,96,1024]{2,1,0:T(8,128)(2,1)} %bitcast.11), calls=%async_computation.2 | async-start | bytes 1572864 | tf_op jit(solution)/shard_map/all_to_all | solution.py:84
  40.1 23.1 %all-to-all-start = ((bf16[4,96,1024]{2,1,0:T(8,128)(2,1)}), bf16[4,96,1024]{2,1,0:T(8,128)(2,1)S(1)}, u32[]{:S(2)}, u32[]{:S(2)}) async-start(bf16[4,96,1024]{2,1,0:T(8,128)(2,1)} %bitcast.2), calls=%async_computation | async-start | bytes 1572864 | tf_op jit(solution)/shard_map/all_to_all | solution.py:83
  64.9 1.9 %copy-start.3 = (bf16[1,1024,1152]{2,1,0:T(8,128)(2,1)S(1)}, bf16[1,1024,1152]{2,1,0:T(8,128)(2,1)}, u32[]{:S(2)}) copy-start(bf16[1,1024,1152]{2,1,0:T(8,128)(2,1)} %all-gather.3.cloned.1.call-done) | copy-start | bytes 7077892
  69.0 23.1 %all-to-all-start.3 = ((bf16[4,96,1024]{2,1,0:T(8,128)(2,1)}), bf16[4,96,1024]{2,1,0:T(8,128)(2,1)S(1)}, u32[]{:S(2)}, u32[]{:S(2)}) async-start(bf16[4,96,1024]{2,1,0:T(8,128)(2,1)} %bitcast.13), calls=%async_computation.3 | async-start | bytes 1572864 | tf_op jit(solution)/shard_map/all_to_all | solution.py:111
  72.5 44.1 %reduce-scatter.2.cloned.1.call-start = ((), (), s32[]{:S(2)}) async-start(), calls=%async_computation.5 | async-start | bytes 1769472 | tf_op jit(solution)/shard_map/reduce_scatter | solution.py:131
  74.4 21.4 %copy-start.2 = (f32[128,2]{0,1:T(2,128)S(1)}, f32[128,2]{0,1:T(2,128)}, u32[]{:S(2)}) copy-start(f32[128,2]{0,1:T(2,128)} %param.9) | copy-start | bytes 3076
  92.2 23.1 %all-to-all-start.1 = ((bf16[4,96,1024]{2,1,0:T(8,128)(2,1)}), bf16[4,96,1024]{2,1,0:T(8,128)(2,1)S(1)}, u32[]{:S(2)}, u32[]{:S(2)}) async-start(bf16[4,96,1024]{2,1,0:T(8,128)(2,1)} %bitcast.7), calls=%async_computation.1 | async-start | bytes 1572864 | tf_op jit(solution)/shard_map/all_to_all | solution.py:103
Sparse Core Ops, SparseCore 0:
  9.9 31.5 all-gather.2
  76.6 39.7 reduce-scatter.1

commit v3 on v2

v3 whole, which is shorter than its diff:
```python
import jax
import jax.numpy as jnp
from jax import lax
from jax.sharding import PartitionSpec as P

contract_last = (((1,), (1,)), ((), ()))
contract_first = (((0,), (0,)), ((), ()))


def forward_rows(row_data, gate_w, up_w, down_w):
    gate_pre = jnp.dot(row_data, gate_w, preferred_element_type=jnp.float32)
    up_pre = jnp.dot(row_data, up_w, preferred_element_type=jnp.float32)
    sigmoid_val = jax.nn.sigmoid(gate_pre)
    hidden = (gate_pre * sigmoid_val * up_pre).astype(jnp.bfloat16)
    expert_out = lax.dot_general(
        hidden, down_w, contract_last, preferred_element_type=jnp.float32
    ).astype(jnp.bfloat16)
    return (gate_pre, up_pre, hidden, expert_out)


def backward_rows(grad_rows, gate_pre, up_pre, gate_w, up_w, down_w):
    hidden_grad = jnp.dot(grad_rows, down_w, preferred_element_type=jnp.float32)
    sigmoid_val = jax.nn.sigmoid(gate_pre)
    slope_val = sigmoid_val * (1.0 + gate_pre * (1.0 - sigmoid_val))
    gate_grad = (hidden_grad * up_pre * slope_val).astype(jnp.bfloat16)
    up_grad = (hidden_grad * gate_pre * sigmoid_val).astype(jnp.bfloat16)
    summed = lax.dot_general(gate_grad, gate_w, contract_last, preferred_element_type=jnp.float32)
    summed = summed + lax.dot_general(
        up_grad, up_w, contract_last, preferred_element_type=jnp.float32
    )
    return summed.astype(jnp.bfloat16)


def shift_send(blocks, groups, sign):
    got = [blocks[0]]
    for step in range(1, groups):
        pairs = [(i, (i + sign * step) % groups) for i in range(groups)]
        got.append(lax.ppermute(blocks[step], "expert", pairs))
    return got


def reduce_scatter_dp(pieces, n_dp):
    me = lax.axis_index("dp")
    work = pieces
    bit = 1
    while bit < n_dp:
        halves = work.reshape((work.shape[0] // 2, 2) + work.shape[1:])
        mine = (me // bit) % 2
        keep = jnp.take(halves, mine, axis=1)
        give = jnp.take(halves, 1 - mine, axis=1)
        pairs = [(i, i ^ bit) for i in range(n_dp)]
        work = keep + lax.ppermute(give, "dp", pairs)
        bit *= 2
    return work[0]


def local(tokens, expert_ids, routing, w_gate, w_up, w_down, grad_out):
    tok_rows, width = tokens.shape
    groups = lax.axis_size("expert")
    n_dp = lax.axis_size("dp")
    me = lax.axis_index("expert")
    local_count = w_gate.shape[0]
    ff_width = w_gate.shape[2]
    shard_d = w_gate.shape[1]
    experts_all = local_count * groups
    top_count = expert_ids.shape[1]
    capacity = 3 * tok_rows * top_count // (2 * experts_all)
    pair_count = tok_rows * top_count
    chosen = expert_ids.reshape(pair_count)
    home = chosen // local_count
    rotated = ((home - me) % groups) * local_count + chosen % local_count
    onehot = (rotated[:, None] == jnp.arange(experts_all, dtype=jnp.int32)[None, :]).astype(
        jnp.bfloat16
    )
    earlier = (
        jnp.arange(pair_count, dtype=jnp.int32)[:, None]
        > jnp.arange(pair_count, dtype=jnp.int32)[None, :]
    ).astype(jnp.bfloat16)
    before = jnp.dot(earlier, onehot, preferred_element_type=jnp.float32)
    slot_index = jnp.sum(before * onehot.astype(jnp.float32), axis=1).astype(jnp.int32)
    flat_index = rotated * capacity + slot_index
    slots = experts_all * capacity
    hit = flat_index[:, None] == jnp.arange(slots, dtype=jnp.int32)[None, :]
    hit3 = hit.reshape(tok_rows, top_count, slots)
    dispatch = jnp.any(hit3, axis=1).astype(jnp.bfloat16)
    send_rows = (
        lax.dot_general(dispatch, tokens, contract_first, preferred_element_type=jnp.float32)
        .astype(jnp.bfloat16)
        .reshape(groups, local_count * capacity, width)
    )
    weight_slot = jnp.sum(jnp.where(hit, routing.reshape(pair_count)[:, None], 0.0), axis=0)
    grads_picked = lax.dot_general(
        dispatch, grad_out, contract_first, preferred_element_type=jnp.float32
    )
    send_grads = (
        (weight_slot[:, None] * grads_picked)
        .astype(jnp.bfloat16)
        .reshape(groups, local_count * capacity, width)
    )
    packed = jnp.concatenate([w_gate, w_up, w_down], axis=2)
    packed = jnp.transpose(packed, (1, 0, 2)).reshape(shard_d, local_count * 3 * ff_width)
    full = lax.all_gather(packed, "dp", axis=0, tiled=True)
    full = jnp.transpose(full.reshape(width, local_count, 3 * ff_width), (1, 0, 2))
    gate_full = full[:, :, :ff_width]
    up_full = full[:, :, ff_width : 2 * ff_width]
    down_full = full[:, :, 2 * ff_width :]
    recv_rows = shift_send([send_rows[s] for s in range(groups)], groups, 1)
    recv_grads = shift_send([send_grads[s] for s in range(groups)], groups, 1)
    gate_w = gate_full[0]
    up_w = up_full[0]
    down_w = down_full[0]
    out_blocks = []
    grad_blocks = []
    hidden_blocks = []
    for s in range(groups):
        gate_pre, up_pre, hidden, expert_out = forward_rows(recv_rows[s], gate_w, up_w, down_w)
        out_blocks.append(expert_out)
        hidden_blocks.append(hidden)
        grad_blocks.append(
            backward_rows(recv_grads[s], gate_pre, up_pre, gate_w, up_w, down_w)
        )
    pieces = lax.dot_general(
        jnp.concatenate(recv_grads, axis=0),
        jnp.concatenate(hidden_blocks, axis=0),
        contract_first,
        preferred_element_type=jnp.float32,
    )
    back_out = jnp.concatenate(shift_send(out_blocks, groups, -1), axis=0)
    back_grad = jnp.concatenate(shift_send(grad_blocks, groups, -1), axis=0)
    output = None
    for choice in range(top_count):
        pick = hit3[:, choice, :].astype(jnp.bfloat16)
        part = routing[:, choice][:, None] * jnp.dot(
            pick, back_out, preferred_element_type=jnp.float32
        )
        output = part if output is None else output + part
    output = output.astype(jnp.bfloat16)
    gather_both = jnp.sum(hit3.astype(jnp.int32), axis=1).astype(jnp.bfloat16)
    token_grad = jnp.dot(
        gather_both, back_grad, preferred_element_type=jnp.float32
    ).astype(jnp.bfloat16)
    summed = reduce_scatter_dp(pieces.reshape(n_dp, shard_d, ff_width), n_dp)
    down_grad = (summed / n_dp).reshape(local_count, shard_d, ff_width)
    return (output, token_grad, down_grad)


def solution(mesh):
    return jax.shard_map(
        local,
        mesh=mesh,
        in_specs=(
            P(("dp", "expert"), None),
            P(("dp", "expert"), None),
            P(("dp", "expert"), None),
            P("expert", "dp", None),
            P("expert", "dp", None),
            P("expert", "dp", None),
            P(("dp", "expert"), None),
        ),
        out_specs=(P(("dp", "expert"), None), P(("dp", "expert"), None), P("expert", "dp", None)),
        check_vma=False,
    )
```

time: 126 us -> 97.6 us (0.77)
  waiting for transfers between devices: 70.3 us -> 31.5 us
  starting transfers between devices: 16.9 us -> 24.2 us
  matrix products: 17.1 us -> 22.5 us
    all_to_all x4 -> x0, waiting for transfers between devices: 70.2 us -> none  [the longest x1 18.8 us: local(): lax.all_to_all(send_grads, 'expert', split_axis=0, concat_axis=0, tiled=T...]
    ppermute x0 -> x15, starting transfers between devices: none -> 24.2 us  [the longest x12 21.2 us: shift_send(): got.append(lax.ppermute(blocks[step], 'expert', pairs))]
    all_gather x1, waiting for transfers between devices: 0.02 us -> 19.2 us  [local(): full = lax.all_gather(packed, 'dp', axis=0, tiled=True)]
    all_to_all x4 -> x0, starting transfers between devices: 16.8 us -> none  [the longest x1 6.35 us: local(): lax.all_to_all(send_grads, 'expert', split_axis=0, concat_axis=0, tiled=T...]
    ppermute x0 -> x15, waiting for transfers between devices: none -> 12.2 us  [the longest x3 12.2 us: reduce_scatter_dp(): work = keep + lax.ppermute(give, 'dp', pairs)]
    dot_general x1 -> x4, matrix products: 1.7 us -> 5.55 us  [forward_rows(): gate_pre = jnp.dot(row_data, gate_w, preferred_element_type=jnp.float32)]
    dot_general x1 -> x4, matrix products: 1.86 us -> 4.28 us  [forward_rows(): up_pre = jnp.dot(row_data, up_w, preferred_element_type=jnp.float32)]
    another operation x1 -> x0, other arithmetic: 1.62 us -> none  [local(): jnp.transpose((summed / lax.axis_size('dp')).reshape(shard_rows, local_co...]
  transfers between devices with their start and end apart: 6 -> 16, of which waited for: 4 -> 3; matrix products, arithmetic and copies ran while one was open for 12% -> 25% of each run, Pallas kernels for 0% -> 0%
where the time goes in v3:
time: 97.6 us; the launch traced here: 97.3 us
  waiting for transfers between devices  31.5 us (32%)
  starting transfers between devices  24.2 us (25%)
  matrix products  22.5 us (23%)
  between operations  14.4 us (15%)
  other arithmetic  3.21 us (3%)
  local copies, waits for them, and re-layouts  1.49 us (2%)
    ppermute x12, starting transfers between devices, shift_send(): got.append(lax.ppermute(blocks[step], 'expert', pairs))  21.2 us
    all_gather x1, waiting for transfers between devices, local(): full = lax.all_gather(packed, 'dp', axis=0, tiled=True)  19.2 us
    ppermute x3, waiting for transfers between devices, reduce_scatter_dp(): work = keep + lax.ppermute(give, 'dp', pairs)  12.2 us
    dot_general x4, matrix products, forward_rows(): gate_pre = jnp.dot(row_data, gate_w, preferred_element_type=jnp.float32)  5.55 us
    dot_general x4, matrix products, forward_rows(): up_pre = jnp.dot(row_data, up_w, preferred_element_type=jnp.float32)  4.28 us
    dot_general x4, matrix products, backward_rows(): hidden_grad = jnp.dot(grad_rows, down_w, preferred_element_type=jnp.float32)  3.02 us
    ppermute x3, starting transfers between devices, reduce_scatter_dp(): work = keep + lax.ppermute(give, 'dp', pairs)  2.99 us
  transfers between devices with their start and end apart: 16, of which 3 were waited for; matrix products, arithmetic and copies ran while one was open for 25% of the time, Pallas kernels for 0%

profile of v3, /device:TPU:0, one launch (start us, length us, event | category | flops | bytes accessed | tf_op | source)
XLA Modules:
  0.0 97.3 jit_solution(2908152394560533456)
XLA Ops:
  7.2 1.8 %pad_maximum_fusion.1 = bf16[1,128,1152]{2,1,0:T(8,128)(2,1)} fusion(bf16[1,128,384]{2,1,0:T(8,128)(2,1)} %param.18, bf16[1,128,384]{2,1,0:T(8,128)(2,1)} %param.17, bf16[1,128,384]{2,1,0:T(8,128)(2,1)} %param.16), kind=kLoop, calls=%fused_computation.54 | loop fusion | flops 884736 | bytes 589824 | tf_op jit(solution)/shard_map/concatenate | solution.py:100
  9.1 0.8 copy.18
  10.7 0.4 convolution_convert_fusion
  11.1 5.1 %collective-permute-start.4 = (bf16[96,1024]{1,0:T(8,128)(2,1)S(1)}, bf16[96,1024]{1,0:T(8,128)(2,1)}, u32[]{:S(2)}, u32[]{:S(2)}) collective-permute-start(bf16[96,1024]{1,0:T(8,128)(2,1)S(1)} %get-tuple-element.44), channel_id=1, source_target_pairs={{0,3},{1,0},{2,1},{3,2},{4,7},{5,4},{6,5},{7,6},{8,11},{9,8},{10,9... | collective-permute-start | bytes 589832 | tf_op jit(solution)/shard_map/ppermute | solution.py:38
  16.3 1.0 %collective-permute-start = (bf16[96,1024]{1,0:T(8,128)(2,1)S(1)}, bf16[96,1024]{1,0:T(8,128)(2,1)}, u32[]{:S(2)}, u32[]{:S(2)}) collective-permute-start(bf16[96,1024]{1,0:T(8,128)(2,1)S(1)} %get-tuple-element.43), channel_id=1, source_target_pairs={{0,1},{1,2},{2,3},{3,0},{4,5},{5,6},{6,7},{7,4},{8,9},{9,10},{10,1... | collective-permute-start | bytes 589832 | tf_op jit(solution)/shard_map/ppermute | solution.py:38
  17.7 0.4 multiply_convert_fusion
  18.2 2.9 %collective-permute-start.10 = (bf16[96,1024]{1,0:T(8,128)(2,1)S(1)}, bf16[96,1024]{1,0:T(8,128)(2,1)}, u32[]{:S(2)}, u32[]{:S(2)}) collective-permute-start(bf16[96,1024]{1,0:T(8,128)(2,1)S(1)} %get-tuple-element.40), channel_id=1, source_target_pairs={{0,3},{1,0},{2,1},{3,2},{4,7},{5,4},{6,5},{7,6},{8,11},{9,8},{10,9... | collective-permute-start | bytes 589832 | tf_op jit(solution)/shard_map/ppermute | solution.py:38
  21.0 1.1 %collective-permute-start.8 = (bf16[96,1024]{1,0:T(8,128)(2,1)S(1)}, bf16[96,1024]{1,0:T(8,128)(2,1)}, u32[]{:S(2)}, u32[]{:S(2)}) collective-permute-start(bf16[96,1024]{1,0:T(8,128)(2,1)S(1)} %get-tuple-element.41), channel_id=1, source_target_pairs={{0,2},{1,3},{2,0},{3,1},{4,6},{5,7},{6,4},{7,5},{8,10},{9,11},{10,... | collective-permute-start | bytes 589832 | tf_op jit(solution)/shard_map/ppermute | solution.py:38
  22.3 19.2 %all-gather.3.cloned.1.call-done = bf16[1,1024,1152]{2,1,0:T(8,128)(2,1)} async-done(((bf16[1,128,1152]{2,1,0:T(8,128)(2,1)}), bf16[1,1024,1152]{2,1,0:T(8,128)(2,1)}) %all-gather.3.cloned.1.call-update) | async-done | bytes 2359312 | tf_op jit(solution)/shard_map/all_gather | solution.py:102
  41.5 1.6 %fusion.39 = f32[96,384]{1,0:T(8,128)S(1)} fusion(bf16[384,1024]{1,0:T(8,128)(2,1)S(1)} %convolution_convert_fusion, bf16[1,1024,1152]{2,1,0:T(8,128)(2,1)} %all-gather.3.cloned.1.call-done), kind=kOutput, calls=%fused_computation.71 | convolution fusion | flops 75497472 | bytes 1130496 | tf_op jit(solution)/shard_map/dot_general | solution.py:11
  43.1 1.5 %collective-permute-start.6 = (bf16[96,1024]{1,0:T(8,128)(2,1)S(1)}, bf16[96,1024]{1,0:T(8,128)(2,1)S(1)}, u32[]{:S(2)}, u32[]{:S(2)}) collective-permute-start(bf16[96,1024]{1,0:T(8,128)(2,1)S(1)} %get-tuple-element.42), channel_id=1, source_target_pairs={{0,1},{1,2},{2,3},{3,0},{4,5},{5,6},{6,7},{7,4},{8,9},{9,10},{10,1... | collective-permute-start | bytes 589832 | tf_op jit(solution)/shard_map/ppermute | solution.py:38
  44.7 1.5 %fusion.45 = f32[96,384]{1,0:T(8,128)S(1)} fusion(bf16[96,1024]{1,0:T(8,128)(2,1)} %collective-permute-done.4, bf16[1,1024,1152]{2,1,0:T(8,128)(2,1)} %all-gather.3.cloned.1.call-done), kind=kOutput, calls=%fused_computation.93 | convolution fusion | flops 75497472 | bytes 1130496 | tf_op jit(solution)/shard_map/dot_general | solution.py:11
  46.2 1.5 %multiply_convert_fusion.9 = (bf16[96,384]{1,0:T(8,128)(2,1)S(1)}, f32[96,384]{1,0:T(8,128)S(1)}) fusion(f32[96,384]{1,0:T(8,128)S(1)} %fusion.45, bf16[96,1024]{1,0:T(8,128)(2,1)} %collective-permute-done.4, bf16[1,1024,1152]{2,1,0:T(8,128)(2,1)} %all-gather.3.cloned.1.call-done), kind=kOutput, calls=%fused_computation.81 | convolution fusion | flops 75718656 | bytes 1351680 | tf_op jit(solution)/shard_map/dot_general | solution.py:12
  47.8 0.4 convolution_convert_fusion.2
  48.2 1.5 %collective-permute-start.5 = (bf16[96,1024]{1,0:T(8,128)(2,1)S(1)}, bf16[96,1024]{1,0:T(8,128)(2,1)S(1)}, u32[]{:S(2)}, u32[]{:S(2)}) collective-permute-start(bf16[96,1024]{1,0:T(8,128)(2,1)S(1)} %convolution_convert_fusion.2), channel_id=1, source_target_pairs={{0,1},{1,2},{2,3},{3,0},{4,5},{5,6},{6,7},{7,4},{8,9},{9,10},{10,1... | collective-permute-start | bytes 589832 | tf_op jit(solution)/shard_map/ppermute | solution.py:38
  49.7 1.2 %fusion.46 = f32[96,384]{1,0:T(8,128)S(1)} fusion(bf16[96,1024]{1,0:T(8,128)(2,1)} %collective-permute-done.2, bf16[1,1024,1152]{2,1,0:T(8,128)(2,1)S(1)} %copy-done.1), kind=kOutput, calls=%fused_computation.94 | convolution fusion | flops 75497472 | bytes 1130496 | tf_op jit(solution)/shard_map/dot_general | solution.py:11
  50.9 1.2 %multiply_convert_fusion.10 = (bf16[96,384]{1,0:T(8,128)(2,1)S(1)}, f32[96,384]{1,0:T(8,128)S(1)}) fusion(f32[96,384]{1,0:T(8,128)S(1)} %fusion.46, bf16[96,1024]{1,0:T(8,128)(2,1)} %collective-permute-done.2, bf16[1,1024,1152]{2,1,0:T(8,128)(2,1)S(1)} %copy-done.1), kind=kOutput, calls=%fused_computation.83 | convolution fusion | flops 75718656 | bytes 1351680 | tf_op jit(solution)/shard_map/dot_general | solution.py:12
  52.1 0.4 convolution_convert_fusion.3
  52.5 1.5 %collective-permute-start.3 = (bf16[96,1024]{1,0:T(8,128)(2,1)S(1)}, bf16[96,1024]{1,0:T(8,128)(2,1)S(1)}, u32[]{:S(2)}, u32[]{:S(2)}) collective-permute-start(bf16[96,1024]{1,0:T(8,128)(2,1)S(1)} %convolution_convert_fusion.3), channel_id=1, source_target_pairs={{0,2},{1,3},{2,0},{3,1},{4,6},{5,7},{6,4},{7,5},{8,10},{9,11},{10,... | collective-permute-start | bytes 589832 | tf_op jit(solution)/shard_map/ppermute | solution.py:38
  54.0 1.2 %fusion.47 = f32[96,384]{1,0:T(8,128)S(1)} fusion(bf16[96,1024]{1,0:T(8,128)(2,1)} %collective-permute-done, bf16[1,1024,1152]{2,1,0:T(8,128)(2,1)S(1)} %copy-done.1), kind=kOutput, calls=%fused_computation.95 | convolution fusion | flops 75497472 | bytes 1130496 | tf_op jit(solution)/shard_map/dot_general | solution.py:11
  55.2 1.2 %multiply_convert_fusion.11 = (bf16[96,384]{1,0:T(8,128)(2,1)S(1)}, f32[96,384]{1,0:T(8,128)S(1)}) fusion(f32[96,384]{1,0:T(8,128)S(1)} %fusion.47, bf16[96,1024]{1,0:T(8,128)(2,1)} %collective-permute-done, bf16[1,1024,1152]{2,1,0:T(8,128)(2,1)S(1)} %copy-done.1), kind=kOutput, calls=%fused_computation.85 | convolution fusion | flops 75718656 | bytes 1351680 | tf_op jit(solution)/shard_map/dot_general | solution.py:12
  56.5 0.4 convolution_convert_fusion.4
  56.8 2.5 %collective-permute-start.1 = (bf16[96,1024]{1,0:T(8,128)(2,1)S(1)}, bf16[96,1024]{1,0:T(8,128)(2,1)S(1)}, u32[]{:S(2)}, u32[]{:S(2)}) collective-permute-start(bf16[96,1024]{1,0:T(8,128)(2,1)S(1)} %convolution_convert_fusion.4), channel_id=1, source_target_pairs={{0,3},{1,0},{2,1},{3,2},{4,7},{5,4},{6,5},{7,6},{8,11},{9,8},{10,9... | collective-permute-start | bytes 589832 | tf_op jit(solution)/shard_map/ppermute | solution.py:38
  59.3 1.2 %fusion.51 = f32[96,384]{1,0:T(8,128)S(1)} fusion(bf16[96,1024]{1,0:T(8,128)(2,1)} %collective-permute-done.10, bf16[1,1024,1152]{2,1,0:T(8,128)(2,1)S(1)} %copy-done.1), kind=kOutput, calls=%fused_computation.99 | convolution fusion | flops 75497472 | bytes 1130496 | tf_op jit(solution)/shard_map/dot_general | solution.py:22
  60.5 0.4 fusion.41
  60.9 0.4 fusion.5
  61.3 0.3 multiply_convert_fusion.12
  61.7 1.7 %fusion.14 = f32[1024,384]{1,0:T(8,128)S(1)} fusion(bf16[96,1024]{1,0:T(8,128)(2,1)} %collective-permute-done.10, bf16[96,1024]{1,0:T(8,128)(2,1)} %collective-permute-done.8, bf16[96,1024]{1,0:T(8,128)(2,1)S(1)} %collective-permute-done.6, bf16[96,1024]{1,0:T(8,128)(2,1)S(1)} %get-tuple-element.39, bf16[96,384]{1,0:T(8,128)(2,1)S(1)} %get-tuple-element.50, ...), kind=kOutput, calls=%fused_computation.32 | convolution fusion | flops 306315264 | bytes 2654208 | tf_op jit(solution)/shard_map/dot_general | solution.py:122
  63.6 1.2 %fusion.52 = f32[96,384]{1,0:T(8,128)S(1)} fusion(bf16[96,1024]{1,0:T(8,128)(2,1)} %collective-permute-done.8, bf16[1,1024,1152]{2,1,0:T(8,128)(2,1)S(1)} %copy-done.1), kind=kOutput, calls=%fused_computation.100 | convolution fusion | flops 75497472 | bytes 1130496 | tf_op jit(solution)/shard_map/dot_general | solution.py:22
  64.8 0.3 fusion.53
  65.1 0.3 fusion.54
  65.4 0.4 fusion.42
  65.8 0.4 fusion.4
  66.2 0.4 fusion.43
  66.5 0.4 fusion.44
  66.9 0.4 convolution_convert_fusion.5
  67.3 0.4 fusion.3
  67.7 0.4 fusion.2
  68.1 1.1 %collective-permute-start.9 = (bf16[96,1024]{1,0:T(8,128)(2,1)S(1)}, bf16[96,1024]{1,0:T(8,128)(2,1)S(1)}, u32[]{:S(2)}, u32[]{:S(2)}) collective-permute-start(bf16[96,1024]{1,0:T(8,128)(2,1)S(1)} %fusion.4), channel_id=1, source_target_pairs={{0,2},{1,3},{2,0},{3,1},{4,6},{5,7},{6,4},{7,5},{8,10},{9,11},{10,... | collective-permute-start | bytes 589832 | tf_op jit(solution)/shard_map/ppermute | solution.py:38
  69.4 2.8 %collective-permute-start.7 = (bf16[96,1024]{1,0:T(8,128)(2,1)S(1)}, bf16[96,1024]{1,0:T(8,128)(2,1)S(1)}, u32[]{:S(2)}, u32[]{:S(2)}) collective-permute-start(bf16[96,1024]{1,0:T(8,128)(2,1)S(1)} %fusion.3), channel_id=1, source_target_pairs={{0,3},{1,0},{2,1},{3,2},{4,7},{5,4},{6,5},{7,6},{8,11},{9,8},{10,9... | collective-permute-start | bytes 589832 | tf_op jit(solution)/shard_map/ppermute | solution.py:38
  72.2 1.5 %collective-permute-start.13 = (f32[2,128,384]{2,1,0:T(8,128)S(1)}, f32[2,128,384]{2,1,0:T(8,128)S(1)}, u32[]{:S(2)}, u32[]{:S(2)}) collective-permute-start(f32[2,128,384]{2,1,0:T(8,128)S(1)} %select_bitcast_fusion), channel_id=1, source_target_pairs={{0,8},{4,12},{8,0},{12,4},{16,24},{20,28},{24,16},{28,20},{1,9},{5... | collective-permute-start | bytes 1179656 | tf_op jit(solution)/shard_map/ppermute | solution.py:52
  73.6 0.3 convolution_multiply_fusion
  73.9 1.0 %fusion.1 = bf16[128,1024]{1,0:T(8,128)(2,1)} fusion(f32[128,1024]{1,0:T(8,128)S(1)} %convolution_multiply_fusion, f32[128]{0:T(128)S(1)} %get-tuple-element.46, pred[128,2,384]{2,0,1:T(32,128)(4,1)S(1)} %get-tuple-element.49, bf16[96,1024]{1,0:T(8,128)(2,1)S(1)} %collective-permute-done.5, bf16[96,1024]{1,0:T(8,128)(2,1)S(1)} %collective-permute-done.3, ...), kind=kOutput, calls=%fused_computation.5 | convolution fusion | flops 104202240 | bytes 1622528 | tf_op jit(solution)/shard_map/dot_general | solution.py:133
  75.0 8.4 %collective-permute-done.13 = f32[2,128,384]{2,1,0:T(8,128)S(1)} collective-permute-done((f32[2,128,384]{2,1,0:T(8,128)S(1)}, f32[2,128,384]{2,1,0:T(8,128)S(1)}, u32[]{:S(2)}, u32[]{:S(2)}) %collective-permute-start.13) | collective-permute-done | bytes 393248 | tf_op jit(solution)/shard_map/ppermute | solution.py:52
  83.5 1.5 %collective-permute-start.14 = (f32[1,128,384]{2,1,0:T(8,128)S(1)}, f32[1,128,384]{2,1,0:T(8,128)S(1)}, u32[]{:S(2)}, u32[]{:S(2)}) collective-permute-start(f32[1,128,384]{2,1,0:T(8,128)S(1)} %select_bitcast_fusion.1), channel_id=1, source_target_pairs={{0,16},{4,20},{8,24},{12,28},{16,0},{20,4},{24,8},{28,12},{1,17},{... | collective-permute-start | bytes 589832 | tf_op jit(solution)/shard_map/ppermute | solution.py:52
  84.9 1.0 %convolution_convert_fusion.1 = bf16[128,1024]{1,0:T(8,128)(2,1)} fusion(bf16[96,1024]{1,0:T(8,128)(2,1)S(1)} %collective-permute-done.11, bf16[96,1024]{1,0:T(8,128)(2,1)S(1)} %collective-permute-done.9, bf16[96,1024]{1,0:T(8,128)(2,1)S(1)} %collective-permute-done.7, bf16[96,1024]{1,0:T(8,128)(2,1)S(1)} %fusion.2, s32[128,384]{1,0:T(8,128)S(1)} %convert_reduce_fusion), kind=kOutput, calls=%fused_computation.6 | convolution fusion | flops 103989248 | bytes 1245184 | tf_op jit(solution)/shard_map/dot_general | solution.py:139
  86.0 3.8 %collective-permute-done.14 = f32[1,128,384]{2,1,0:T(8,128)S(1)} collective-permute-done((f32[1,128,384]{2,1,0:T(8,128)S(1)}, f32[1,128,384]{2,1,0:T(8,128)S(1)}, u32[]{:S(2)}, u32[]{:S(2)}) %collective-permute-start.14) | collective-permute-done | bytes 196640 | tf_op jit(solution)/shard_map/ppermute | solution.py:52
  89.7 0.7 fusion.36
  (48 shorter events, 1.9 us)
Async XLA Ops:
  7.2 3.5 %copy-start = (bf16[128,1024]{1,0:T(8,128)(2,1)S(1)}, bf16[128,1024]{1,0:T(8,128)(2,1)}, u32[]{:S(2)}) copy-start(bf16[128,1024]{1,0:T(8,128)(2,1)} %param.13) | copy-start | bytes 786436
  7.2 10.1 %copy-start.3 = (f32[128,2]{0,1:T(2,128)S(1)}, f32[128,2]{0,1:T(2,128)}, u32[]{:S(2)}) copy-start(f32[128,2]{0,1:T(2,128)} %param.15) | copy-start | bytes 3076
  7.2 10.5 %copy-start.2 = (bf16[128,1024]{1,0:T(8,128)(2,1)S(1)}, bf16[128,1024]{1,0:T(8,128)(2,1)}, u32[]{:S(2)}) copy-start(bf16[128,1024]{1,0:T(8,128)(2,1)} %param.19) | copy-start | bytes 786436
  7.2 34.3 %all-gather.3.cloned.1.call-start = ((), (), s32[]{:S(2)}) async-start(), calls=%async_computation | async-start | bytes 2654208 | tf_op jit(solution)/shard_map/all_gather | solution.py:102
  11.1 32.0 %collective-permute-start.4 = (bf16[96,1024]{1,0:T(8,128)(2,1)S(1)}, bf16[96,1024]{1,0:T(8,128)(2,1)}, u32[]{:S(2)}, u32[]{:S(2)}) collective-permute-start(bf16[96,1024]{1,0:T(8,128)(2,1)S(1)} %get-tuple-element.44), channel_id=1, source_target_pairs={{0,3},{1,0},{2,1},{3,2},{4,7},{5,4},{6,5},{7,6},{8,11},{9,8},{10,9... | collective-permute-start | bytes 589832 | tf_op jit(solution)/shard_map/ppermute | solution.py:38
  16.3 31.9 %collective-permute-start.2 = (bf16[96,1024]{1,0:T(8,128)(2,1)S(1)}, bf16[96,1024]{1,0:T(8,128)(2,1)}, u32[]{:S(2)}, u32[]{:S(2)}) collective-permute-start(bf16[96,1024]{1,0:T(8,128)(2,1)S(1)} %get-tuple-element.45), channel_id=1, source_target_pairs={{0,2},{1,3},{2,0},{3,1},{4,6},{5,7},{6,4},{7,5},{8,10},{9,11},{10,... | collective-permute-start | bytes 589832 | tf_op jit(solution)/shard_map/ppermute | solution.py:38
  16.3 36.3 %collective-permute-start = (bf16[96,1024]{1,0:T(8,128)(2,1)S(1)}, bf16[96,1024]{1,0:T(8,128)(2,1)}, u32[]{:S(2)}, u32[]{:S(2)}) collective-permute-start(bf16[96,1024]{1,0:T(8,128)(2,1)S(1)} %get-tuple-element.43), channel_id=1, source_target_pairs={{0,1},{1,2},{2,3},{3,0},{4,5},{5,6},{6,7},{7,4},{8,9},{9,10},{10,1... | collective-permute-start | bytes 589832 | tf_op jit(solution)/shard_map/ppermute | solution.py:38
  18.2 38.6 %collective-permute-start.10 = (bf16[96,1024]{1,0:T(8,128)(2,1)S(1)}, bf16[96,1024]{1,0:T(8,128)(2,1)}, u32[]{:S(2)}, u32[]{:S(2)}) collective-permute-start(bf16[96,1024]{1,0:T(8,128)(2,1)S(1)} %get-tuple-element.40), channel_id=1, source_target_pairs={{0,3},{1,0},{2,1},{3,2},{4,7},{5,4},{6,5},{7,6},{8,11},{9,8},{10,9... | collective-permute-start | bytes 589832 | tf_op jit(solution)/shard_map/ppermute | solution.py:38
  21.0 40.6 %collective-permute-start.8 = (bf16[96,1024]{1,0:T(8,128)(2,1)S(1)}, bf16[96,1024]{1,0:T(8,128)(2,1)}, u32[]{:S(2)}, u32[]{:S(2)}) collective-permute-start(bf16[96,1024]{1,0:T(8,128)(2,1)S(1)} %get-tuple-element.41), channel_id=1, source_target_pairs={{0,2},{1,3},{2,0},{3,1},{4,6},{5,7},{6,4},{7,5},{8,10},{9,11},{10,... | collective-permute-start | bytes 589832 | tf_op jit(solution)/shard_map/ppermute | solution.py:38
  41.5 6.2 %copy-start.1 = (bf16[1,1024,1152]{2,1,0:T(8,128)(2,1)S(1)}, bf16[1,1024,1152]{2,1,0:T(8,128)(2,1)}, u32[]{:S(2)}) copy-start(bf16[1,1024,1152]{2,1,0:T(8,128)(2,1)} %all-gather.3.cloned.1.call-done) | copy-start | bytes 7077892
  43.1 18.6 %collective-permute-start.6 = (bf16[96,1024]{1,0:T(8,128)(2,1)S(1)}, bf16[96,1024]{1,0:T(8,128)(2,1)S(1)}, u32[]{:S(2)}, u32[]{:S(2)}) collective-permute-start(bf16[96,1024]{1,0:T(8,128)(2,1)S(1)} %get-tuple-element.42), channel_id=1, source_target_pairs={{0,1},{1,2},{2,3},{3,0},{4,5},{5,6},{6,7},{7,4},{8,9},{9,10},{10,1... | collective-permute-start | bytes 589832 | tf_op jit(solution)/shard_map/ppermute | solution.py:38
  48.2 21.2 %collective-permute-start.5 = (bf16[96,1024]{1,0:T(8,128)(2,1)S(1)}, bf16[96,1024]{1,0:T(8,128)(2,1)S(1)}, u32[]{:S(2)}, u32[]{:S(2)}) collective-permute-start(bf16[96,1024]{1,0:T(8,128)(2,1)S(1)} %convolution_convert_fusion.2), channel_id=1, source_target_pairs={{0,1},{1,2},{2,3},{3,0},{4,5},{5,6},{6,7},{7,4},{8,9},{9,10},{10,1... | collective-permute-start | bytes 589832 | tf_op jit(solution)/shard_map/ppermute | solution.py:38
  52.5 19.6 %collective-permute-start.3 = (bf16[96,1024]{1,0:T(8,128)(2,1)S(1)}, bf16[96,1024]{1,0:T(8,128)(2,1)S(1)}, u32[]{:S(2)}, u32[]{:S(2)}) collective-permute-start(bf16[96,1024]{1,0:T(8,128)(2,1)S(1)} %convolution_convert_fusion.3), channel_id=1, source_target_pairs={{0,2},{1,3},{2,0},{3,1},{4,6},{5,7},{6,4},{7,5},{8,10},{9,11},{10,... | collective-permute-start | bytes 589832 | tf_op jit(solution)/shard_map/ppermute | solution.py:38
  56.8 16.8 %collective-permute-start.1 = (bf16[96,1024]{1,0:T(8,128)(2,1)S(1)}, bf16[96,1024]{1,0:T(8,128)(2,1)S(1)}, u32[]{:S(2)}, u32[]{:S(2)}) collective-permute-start(bf16[96,1024]{1,0:T(8,128)(2,1)S(1)} %convolution_convert_fusion.4), channel_id=1, source_target_pairs={{0,3},{1,0},{2,1},{3,2},{4,7},{5,4},{6,5},{7,6},{8,11},{9,8},{10,9... | collective-permute-start | bytes 589832 | tf_op jit(solution)/shard_map/ppermute | solution.py:38
  61.6 23.3 %collective-permute-start.11 = (bf16[96,1024]{1,0:T(8,128)(2,1)S(1)}, bf16[96,1024]{1,0:T(8,128)(2,1)S(1)}, u32[]{:S(2)}, u32[]{:S(2)}) collective-permute-start(bf16[96,1024]{1,0:T(8,128)(2,1)S(1)} %fusion.5), channel_id=1, source_target_pairs={{0,1},{1,2},{2,3},{3,0},{4,5},{5,6},{6,7},{7,4},{8,9},{9,10},{10,1... | collective-permute-start | bytes 589832 | tf_op jit(solution)/shard_map/ppermute | solution.py:38
  63.5 4.6 %collective-permute-start.12 = (f32[4,128,384]{2,1,0:T(8,128)S(1)}, f32[4,128,384]{2,1,0:T(8,128)S(1)}, u32[]{:S(2)}, u32[]{:S(2)}) collective-permute-start(f32[4,128,384]{2,1,0:T(8,128)S(1)} %fusion.22), channel_id=1, source_target_pairs={{0,4},{4,0},{8,12},{12,8},{16,20},{20,16},{24,28},{28,24},{1,5},{5... | collective-permute-start | bytes 2359304 | tf_op jit(solution)/shard_map/ppermute | solution.py:52
  68.1 16.9 %collective-permute-start.9 = (bf16[96,1024]{1,0:T(8,128)(2,1)S(1)}, bf16[96,1024]{1,0:T(8,128)(2,1)S(1)}, u32[]{:S(2)}, u32[]{:S(2)}) collective-permute-start(bf16[96,1024]{1,0:T(8,128)(2,1)S(1)} %fusion.4), channel_id=1, source_target_pairs={{0,2},{1,3},{2,0},{3,1},{4,6},{5,7},{6,4},{7,5},{8,10},{9,11},{10,... | collective-permute-start | bytes 589832 | tf_op jit(solution)/shard_map/ppermute | solution.py:38
  69.4 15.6 %collective-permute-start.7 = (bf16[96,1024]{1,0:T(8,128)(2,1)S(1)}, bf16[96,1024]{1,0:T(8,128)(2,1)S(1)}, u32[]{:S(2)}, u32[]{:S(2)}) collective-permute-start(bf16[96,1024]{1,0:T(8,128)(2,1)S(1)} %fusion.3), channel_id=1, source_target_pairs={{0,3},{1,0},{2,1},{3,2},{4,7},{5,4},{6,5},{7,6},{8,11},{9,8},{10,9... | collective-permute-start | bytes 589832 | tf_op jit(solution)/shard_map/ppermute | solution.py:38
  72.2 11.2 %collective-permute-start.13 = (f32[2,128,384]{2,1,0:T(8,128)S(1)}, f32[2,128,384]{2,1,0:T(8,128)S(1)}, u32[]{:S(2)}, u32[]{:S(2)}) collective-permute-start(f32[2,128,384]{2,1,0:T(8,128)S(1)} %select_bitcast_fusion), channel_id=1, source_target_pairs={{0,8},{4,12},{8,0},{12,4},{16,24},{20,28},{24,16},{28,20},{1,9},{5... | collective-permute-start | bytes 1179656 | tf_op jit(solution)/shard_map/ppermute | solution.py:52
  83.5 6.2 %collective-permute-start.14 = (f32[1,128,384]{2,1,0:T(8,128)S(1)}, f32[1,128,384]{2,1,0:T(8,128)S(1)}, u32[]{:S(2)}, u32[]{:S(2)}) collective-permute-start(f32[1,128,384]{2,1,0:T(8,128)S(1)} %select_bitcast_fusion.1), channel_id=1, source_target_pairs={{0,16},{4,20},{8,24},{12,28},{16,0},{20,4},{24,8},{28,12},{1,17},{... | collective-permute-start | bytes 589832 | tf_op jit(solution)/shard_map/ppermute | solution.py:52
Sparse Core Ops, SparseCore 0:
  9.9 31.5 all-gather.2

commit v4 on v3

--- a/solution.py
+++ b/solution.py
@@ -37,6 +37,20 @@
         pairs = [(i, (i + sign * step) % groups) for i in range(groups)]
         got.append(lax.ppermute(blocks[step], "expert", pairs))
     return got
+
+
+def all_gather_dp(block, n_dp):
+    me = lax.axis_index("dp")
+    work = block[None]
+    bit = n_dp // 2
+    while bit >= 1:
+        recv = lax.ppermute(work, "dp", [(i, i ^ bit) for i in range(n_dp)])
+        upper = (me // bit) % 2 == 1
+        low = jnp.where(upper, recv, work)
+        high = jnp.where(upper, work, recv)
+        work = jnp.stack([low, high], axis=1).reshape((2 * work.shape[0],) + work.shape[1:])
+        bit //= 2
+    return work
 
 
 def reduce_scatter_dp(pieces, n_dp):
@@ -99,7 +113,7 @@
     )
     packed = jnp.concatenate([w_gate, w_up, w_down], axis=2)
     packed = jnp.transpose(packed, (1, 0, 2)).reshape(shard_d, local_count * 3 * ff_width)
-    full = lax.all_gather(packed, "dp", axis=0, tiled=True)
+    full = all_gather_dp(packed, n_dp).reshape(width, local_count * 3 * ff_width)
     full = jnp.transpose(full.reshape(width, local_count, 3 * ff_width), (1, 0, 2))
     gate_full = full[:, :, :ff_width]
     up_full = full[:, :, ff_width : 2 * ff_width]
@@ -109,22 +123,14 @@
     gate_w = gate_full[0]
     up_w = up_full[0]
     down_w = down_full[0]
-    out_blocks = []
-    grad_blocks = []
-    hidden_blocks = []
-    for s in range(groups):
-        gate_pre, up_pre, hidden, expert_out = forward_rows(recv_rows[s], gate_w, up_w, down_w)
-        out_blocks.append(expert_out)
-        hidden_blocks.append(hidden)
-        grad_blocks.append(
-            backward_rows(recv_grads[s], gate_pre, up_pre, gate_w, up_w, down_w)
-        )
-    pieces = lax.dot_general(
-        jnp.concatenate(recv_grads, axis=0),
-        jnp.concatenate(hidden_blocks, axis=0),
-        contract_first,
-        preferred_element_type=jnp.float32,
-    )
+    x_rows = jnp.concatenate(recv_rows, axis=0)
+    g_rows = jnp.concatenate(recv_grads, axis=0)
+    gate_pre, up_pre, hidden, expert_out = forward_rows(x_rows, gate_w, up_w, down_w)
+    pair_grad = backward_rows(g_rows, gate_pre, up_pre, gate_w, up_w, down_w)
+    pieces = lax.dot_general(g_rows, hidden, contract_first, preferred_element_type=jnp.float32)
+    block_rows = local_count * capacity
+    out_blocks = [expert_out[s * block_rows : (s + 1) * block_rows] for s in range(groups)]
+    grad_blocks = [pair_grad[s * block_rows : (s + 1) * block_rows] for s in range(groups)]
     back_out = jnp.concatenate(shift_send(out_blocks, groups, -1), axis=0)
     back_grad = jnp.concatenate(shift_send(grad_blocks, groups, -1), axis=0)
     output = None

time: 97.6 us -> 89 us (0.912)
  between operations: 14.4 us -> 1.06 us
  matrix products: 22.5 us -> 11.8 us
  starting transfers between devices: 24.2 us -> 31.6 us
  local copies, waits for them, and re-layouts: 1.49 us -> 8.04 us
  waiting for transfers between devices: 31.5 us -> 33.2 us
    all_gather x1 -> x0, waiting for transfers between devices: 19.2 us -> none  [local(): full = lax.all_gather(packed, 'dp', axis=0, tiled=True)]
    ppermute x0 -> x3, waiting for transfers between devices: none -> 12.2 us  [all_gather_dp(): recv = lax.ppermute(work, 'dp', [(i, i ^ bit) for i in range(n_dp)])]
    ppermute x12, waiting for transfers between devices: 0.03 us -> 8.49 us  [shift_send(): got.append(lax.ppermute(blocks[step], 'expert', pairs))]
    ppermute x0 -> x3, starting transfers between devices: none -> 4.91 us  [all_gather_dp(): recv = lax.ppermute(work, 'dp', [(i, i ^ bit) for i in range(n_dp)])]
    dot_general x4 -> x1, matrix products: 5.55 us -> 1.69 us  [forward_rows(): gate_pre = jnp.dot(row_data, gate_w, preferred_element_type=jnp.float32)]
    ppermute x12, starting transfers between devices: 21.2 us -> 25 us  [shift_send(): got.append(lax.ppermute(blocks[step], 'expert', pairs))]
    unnamed x10 -> x26, local copies, waits for them, and re-layouts: 0.92 us -> 4.09 us
    dot_general x4 -> x1, matrix products: 4.28 us -> 1.7 us  [forward_rows(): up_pre = jnp.dot(row_data, up_w, preferred_element_type=jnp.float32)]
  transfers between devices with their start and end apart: 16 -> 18, of which waited for: 3 -> 5; matrix products, arithmetic and copies ran while one was open for 25% -> 20% of each run, Pallas kernels for 0% -> 0%
where the time goes in v4:
time: 89 us; the launch traced here: 88.6 us
  waiting for transfers between devices  33.2 us (37%)
  starting transfers between devices  31.6 us (36%)
  matrix products  11.8 us (13%)
  local copies, waits for them, and re-layouts  8.04 us (9%)
  other arithmetic  3.01 us (3%)
  between operations  1.06 us (1%)
    ppermute x12, starting transfers between devices, shift_send(): got.append(lax.ppermute(blocks[step], 'expert', pairs))  25 us
    ppermute x3, waiting for transfers between devices, reduce_scatter_dp(): work = keep + lax.ppermute(give, 'dp', pairs)  12.4 us
    ppermute x3, waiting for transfers between devices, all_gather_dp(): recv = lax.ppermute(work, 'dp', [(i, i ^ bit) for i in range(n_dp)])  12.2 us
    ppermute x12, waiting for transfers between devices, shift_send(): got.append(lax.ppermute(blocks[step], 'expert', pairs))  8.49 us
    ppermute x3, starting transfers between devices, all_gather_dp(): recv = lax.ppermute(work, 'dp', [(i, i ^ bit) for i in range(n_dp)])  4.91 us
    unnamed x26, local copies, waits for them, and re-layouts  4.09 us
  transfers between devices with their start and end apart: 18, of which 5 were waited for; matrix products, arithmetic and copies ran while one was open for 20% of the time, Pallas kernels for 0%

profile of v4, /device:TPU:0, one launch (start us, length us, event | category | flops | bytes accessed | tf_op | source)
XLA Modules:
  0.0 88.6 jit_solution(17844151069113276616)
XLA Ops:
  0.6 0.9 %constant_dynamic-update-slice_fusion.2 = bf16[1,128,1152]{2,1,0:T(8,128)(2,1)S(1)} fusion(bf16[1,128,384]{2,1,0:T(8,128)(2,1)} %param.16), kind=kLoop, calls=%fused_computation.75 | loop fusion | bytes 196608
  1.6 0.9 %constant_dynamic-update-slice_fusion.1 = bf16[1,128,1152]{2,1,0:T(8,128)(2,1)S(1)} fusion(bf16[1,128,1152]{2,1,0:T(8,128)(2,1)S(1)} %constant_dynamic-update-slice_fusion.2, bf16[1,128,384]{2,1,0:T(8,128)(2,1)} %param.17), kind=kLoop, calls=%fused_computation.74 | loop fusion | bytes 196608
  2.5 0.9 %constant_dynamic-update-slice_fusion = bf16[1,128,1152]{2,1,0:T(8,128)(2,1)S(1)} fusion(bf16[1,128,1152]{2,1,0:T(8,128)(2,1)S(1)} %constant_dynamic-update-slice_fusion.1, bf16[1,128,384]{2,1,0:T(8,128)(2,1)} %param.18), kind=kLoop, calls=%fused_computation.73 | loop fusion | bytes 196608 | tf_op jit(solution)/shard_map/concatenate | solution.py:114
  3.4 3.1 %collective-permute-start.3 = (bf16[1,128,1152]{2,1,0:T(8,128)(2,1)S(1)}, bf16[1,128,1152]{2,1,0:T(8,128)(2,1)S(1)}, u32[]{:S(2)}, u32[]{:S(2)}) collective-permute-start(bf16[1,128,1152]{2,1,0:T(8,128)(2,1)S(1)} %constant_dynamic-update-slice_fusion), channel_id=1, source_target_pairs={{0,16},{4,20},{8,24},{12,28},{16,0},{20,4},{24,8},{28,12},{1,17},{... | collective-permute-start | bytes 884744 | tf_op jit(solution)/shard_map/ppermute | solution.py:47
  6.5 0.8 copy.20
  7.3 0.1 sub.46
  7.4 0.2 fusion.2
  7.7 0.1 convert_element_type.57
  7.9 5.6 %collective-permute-done.3 = bf16[1,128,1152]{2,1,0:T(8,128)(2,1)S(1)} collective-permute-done((bf16[1,128,1152]{2,1,0:T(8,128)(2,1)S(1)}, bf16[1,128,1152]{2,1,0:T(8,128)(2,1)S(1)}, u32[]{:S(2)}, u32[]{:S(2)}) %collective-permute-start.3) | collective-permute-done | bytes 294944 | tf_op jit(solution)/shard_map/ppermute | solution.py:47
  13.7 1.8 %collective-permute-start.4 = (bf16[2,128,1152]{2,1,0:T(8,128)(2,1)S(1)}, bf16[2,128,1152]{2,1,0:T(8,128)(2,1)S(1)}, u32[]{:S(2)}, u32[]{:S(2)}) collective-permute-start(bf16[2,128,1152]{2,1,0:T(8,128)(2,1)S(1)} %maximum_bitcast_fusion), channel_id=1, source_target_pairs={{0,8},{4,12},{8,0},{12,4},{16,24},{20,28},{24,16},{28,20},{1,9},{5... | collective-permute-start | bytes 1769480 | tf_op jit(solution)/shard_map/ppermute | solution.py:47
  15.4 0.1 fusion.22
  15.6 0.4 convolution_convert_fusion
  16.1 3.7 %collective-permute-start.2 = (bf16[96,1024]{1,0:T(8,128)(2,1)S(1)}, bf16[96,1024]{1,0:T(8,128)(2,1)}, u32[]{:S(2)}, u32[]{:S(2)}) collective-permute-start(bf16[96,1024]{1,0:T(8,128)(2,1)S(1)} %get-tuple-element.56), channel_id=1, source_target_pairs={{0,3},{1,0},{2,1},{3,2},{4,7},{5,4},{6,5},{7,6},{8,11},{9,8},{10,9... | collective-permute-start | bytes 589832 | tf_op jit(solution)/shard_map/ppermute | solution.py:38
  19.7 1.0 %collective-permute-start = (bf16[96,1024]{1,0:T(8,128)(2,1)S(1)}, bf16[96,1024]{1,0:T(8,128)(2,1)}, u32[]{:S(2)}, u32[]{:S(2)}) collective-permute-start(bf16[96,1024]{1,0:T(8,128)(2,1)S(1)} %get-tuple-element.58), channel_id=1, source_target_pairs={{0,1},{1,2},{2,3},{3,0},{4,5},{5,6},{6,7},{7,4},{8,9},{9,10},{10,1... | collective-permute-start | bytes 589832 | tf_op jit(solution)/shard_map/ppermute | solution.py:38
  20.9 0.7 broadcast_in_dim.48
  21.6 6.6 %collective-permute-done.4 = bf16[2,128,1152]{2,1,0:T(8,128)(2,1)S(1)} collective-permute-done((bf16[2,128,1152]{2,1,0:T(8,128)(2,1)S(1)}, bf16[2,128,1152]{2,1,0:T(8,128)(2,1)S(1)}, u32[]{:S(2)}, u32[]{:S(2)}) %collective-permute-start.4) | collective-permute-done | bytes 589856 | tf_op jit(solution)/shard_map/ppermute | solution.py:47
  28.6 0.4 copy-done.6
  29.1 0.1 select_reduce_fusion
  29.3 0.4 multiply_convert_fusion
  29.8 0.9 fusion.42
  30.6 3.5 %collective-permute-start.11 = (bf16[96,1024]{1,0:T(8,128)(2,1)}, bf16[96,1024]{1,0:T(8,128)(2,1)}, u32[]{:S(2)}, u32[]{:S(2)}) collective-permute-start(bf16[96,1024]{1,0:T(8,128)(2,1)} %get-tuple-element.48), channel_id=1, source_target_pairs={{0,3},{1,0},{2,1},{3,2},{4,7},{5,4},{6,5},{7,6},{8,11},{9,8},{10,9... | collective-permute-start | bytes 589832 | tf_op jit(solution)/shard_map/ppermute | solution.py:38
  34.2 0.8 convert_reduce_fusion
  35.0 0.8 slice_bitcast_fusion.14
  35.7 0.3 select_bitcast_fusion.1
  36.1 0.2 pad_maximum_fusion
  36.3 0.2 copy.23
  36.5 0.7 copy-done.3
  37.2 1.0 %collective-permute-start.9 = (bf16[96,1024]{1,0:T(8,128)(2,1)S(1)}, bf16[96,1024]{1,0:T(8,128)(2,1)S(1)}, u32[]{:S(2)}, u32[]{:S(2)}) collective-permute-start(bf16[96,1024]{1,0:T(8,128)(2,1)S(1)} %copy-done.3), channel_id=1, source_target_pairs={{0,1},{1,2},{2,3},{3,0},{4,5},{5,6},{6,7},{7,4},{8,9},{9,10},{10,1... | collective-permute-start | bytes 589832 | tf_op jit(solution)/shard_map/ppermute | solution.py:38
  38.2 1.7 %fusion.14 = f32[384,384]{1,0:T(8,128)S(1)} fusion(bf16[1,1024,1152]{2,1,0:T(8,128)(2,1)S(1)} %bitcast.99, bf16[96,1024]{1,0:T(8,128)(2,1)} %collective-permute-done.2, bf16[96,1024]{1,0:T(8,128)(2,1)} %collective-permute-done.1, bf16[96,1024]{1,0:T(8,128)(2,1)} %collective-permute-done, bf16[96,1024]{1,0:T(8,128)(2,1)S(1)} %get-tuple-element.55), kind=kOutput, calls=%fused_computation.34 | convolution fusion | flops 305135616 | bytes 2162688 | tf_op jit(solution)/shard_map/dot_general | solution.py:11
  39.9 1.7 %multiply_convert_fusion.3 = (bf16[384,384]{1,0:T(8,128)(2,1)S(1)}, f32[384,384]{1,0:T(8,128)S(1)}) fusion(f32[384,384]{1,0:T(8,128)S(1)} %fusion.14, bf16[1,1024,1152]{2,1,0:T(8,128)(2,1)S(1)} %bitcast.100, bf16[96,1024]{1,0:T(8,128)(2,1)} %collective-permute-done.2, bf16[96,1024]{1,0:T(8,128)(2,1)} %collective-permute-done.1, ...), kind=kOutput, calls=%fused_computation.40 | convolution fusion | flops 306020352 | bytes 3047424 | tf_op jit(solution)/shard_map/dot_general | solution.py:12
  41.7 0.6 convolution_convert_fusion.1
  42.3 2.5 %collective-permute-start.8 = (bf16[96,1024]{1,0:T(8,128)(2,1)S(1)}, bf16[96,1024]{1,0:T(8,128)(2,1)S(1)}, u32[]{:S(2)}, u32[]{:S(2)}) collective-permute-start(bf16[96,1024]{1,0:T(8,128)(2,1)S(1)} %get-tuple-element.52), channel_id=1, source_target_pairs={{0,1},{1,2},{2,3},{3,0},{4,5},{5,6},{6,7},{7,4},{8,9},{9,10},{10,1... | collective-permute-start | bytes 589832 | tf_op jit(solution)/shard_map/ppermute | solution.py:38
  44.9 5.6 %collective-permute-start.7 = (bf16[96,1024]{1,0:T(8,128)(2,1)S(1)}, bf16[96,1024]{1,0:T(8,128)(2,1)S(1)}, u32[]{:S(2)}, u32[]{:S(2)}) collective-permute-start(bf16[96,1024]{1,0:T(8,128)(2,1)S(1)} %get-tuple-element.53), channel_id=1, source_target_pairs={{0,2},{1,3},{2,0},{3,1},{4,6},{5,7},{6,4},{7,5},{8,10},{9,11},{10,... | collective-permute-start | bytes 589832 | tf_op jit(solution)/shard_map/ppermute | solution.py:38
  50.4 2.8 %collective-permute-start.6 = (bf16[96,1024]{1,0:T(8,128)(2,1)S(1)}, bf16[96,1024]{1,0:T(8,128)(2,1)S(1)}, u32[]{:S(2)}, u32[]{:S(2)}) collective-permute-start(bf16[96,1024]{1,0:T(8,128)(2,1)S(1)} %get-tuple-element.54), channel_id=1, source_target_pairs={{0,3},{1,0},{2,1},{3,2},{4,7},{5,4},{6,5},{7,6},{8,11},{9,8},{10,9... | collective-permute-start | bytes 589832 | tf_op jit(solution)/shard_map/ppermute | solution.py:38
  53.3 8.5 %collective-permute-done.10 = bf16[96,1024]{1,0:T(8,128)(2,1)S(1)} collective-permute-done((bf16[96,1024]{1,0:T(8,128)(2,1)}, bf16[96,1024]{1,0:T(8,128)(2,1)S(1)}, u32[]{:S(2)}, u32[]{:S(2)}) %collective-permute-start.10) | collective-permute-done | bytes 196640 | tf_op jit(solution)/shard_map/ppermute | solution.py:38
  61.7 1.6 %fusion.24 = f32[1024,384]{1,0:T(8,128)S(1)} fusion(bf16[384,384]{1,0:T(8,128)(2,1)S(1)} %get-tuple-element.65, bf16[96,1024]{1,0:T(8,128)(2,1)} %collective-permute-done.11, bf16[96,1024]{1,0:T(8,128)(2,1)S(1)} %collective-permute-done.10, bf16[96,1024]{1,0:T(8,128)(2,1)S(1)} %collective-permute-done.9, bf16[96,1024]{1,0:T(8,128)(2,1)S(1)} %copy-done.2), kind=kOutput, calls=%fused_computation.64 | convolution fusion | flops 305135616 | bytes 2654208 | tf_op jit(solution)/shard_map/dot_general | solution.py:130
  63.5 1.5 %fusion.16 = f32[384,384]{1,0:T(8,128)S(1)} fusion(bf16[1,1024,1152]{2,1,0:T(8,128)(2,1)S(1)} %bitcast.102, bf16[96,1024]{1,0:T(8,128)(2,1)} %collective-permute-done.11, bf16[96,1024]{1,0:T(8,128)(2,1)S(1)} %collective-permute-done.10, bf16[96,1024]{1,0:T(8,128)(2,1)S(1)} %collective-permute-done.9, bf16[96,1024]{1,0:T(8,128)(2,1)S(1)} %copy-done.2), kind=kOutput, calls=%fused_computation.36 | convolution fusion | flops 305135616 | bytes 2162688 | tf_op jit(solution)/shard_map/dot_general | solution.py:22
  65.0 0.7 fusion.13
  65.7 0.6 add_convert_fusion
  66.5 1.9 %collective-permute-start.13 = (bf16[96,1024]{1,0:T(8,128)(2,1)S(1)}, bf16[96,1024]{1,0:T(8,128)(2,1)S(1)}, u32[]{:S(2)}, u32[]{:S(2)}) collective-permute-start(bf16[96,1024]{1,0:T(8,128)(2,1)S(1)} %get-tuple-element.45), channel_id=1, source_target_pairs={{0,2},{1,3},{2,0},{3,1},{4,6},{5,7},{6,4},{7,5},{8,10},{9,11},{10,... | collective-permute-start | bytes 589832 | tf_op jit(solution)/shard_map/ppermute | solution.py:38
  68.5 2.9 %collective-permute-start.12 = (bf16[96,1024]{1,0:T(8,128)(2,1)S(1)}, bf16[96,1024]{1,0:T(8,128)(2,1)S(1)}, u32[]{:S(2)}, u32[]{:S(2)}) collective-permute-start(bf16[96,1024]{1,0:T(8,128)(2,1)S(1)} %get-tuple-element.46), channel_id=1, source_target_pairs={{0,3},{1,0},{2,1},{3,2},{4,7},{5,4},{6,5},{7,6},{8,11},{9,8},{10,9... | collective-permute-start | bytes 589832 | tf_op jit(solution)/shard_map/ppermute | solution.py:38
  71.4 0.3 convolution_multiply_fusion
  71.8 1.0 %fusion.1 = bf16[128,1024]{1,0:T(8,128)(2,1)} fusion(f32[128,1024]{1,0:T(8,128)S(1)} %convolution_multiply_fusion, f32[128]{0:T(128)S(1)} %get-tuple-element.61, pred[128,2,384]{2,0,1:T(32,128)(4,1)S(1)} %get-tuple-element.64, bf16[96,1024]{1,0:T(8,128)(2,1)S(1)} %collective-permute-done.8, bf16[96,1024]{1,0:T(8,128)(2,1)S(1)} %collective-permute-done.7, ...), kind=kOutput, calls=%fused_computation.8 | convolution fusion | flops 104202240 | bytes 1622528 | tf_op jit(solution)/shard_map/dot_general | solution.py:139
  72.8 9.3 %collective-permute-done.16 = f32[2,128,384]{2,1,0:T(8,128)S(1)} collective-permute-done((f32[2,128,384]{2,1,0:T(8,128)S(1)}, f32[2,128,384]{2,1,0:T(8,128)S(1)}, u32[]{:S(2)}, u32[]{:S(2)}) %collective-permute-start.16) | collective-permute-done | bytes 393248 | tf_op jit(solution)/shard_map/ppermute | solution.py:66
  82.2 1.6 %collective-permute-start.17 = (f32[1,128,384]{2,1,0:T(8,128)S(1)}, f32[1,128,384]{2,1,0:T(8,128)S(1)}, u32[]{:S(2)}, u32[]{:S(2)}) collective-permute-start(f32[1,128,384]{2,1,0:T(8,128)S(1)} %select_bitcast_fusion.7), channel_id=1, source_target_pairs={{0,16},{4,20},{8,24},{12,28},{16,0},{20,4},{24,8},{28,12},{1,17},{... | collective-permute-start | bytes 589832 | tf_op jit(solution)/shard_map/ppermute | solution.py:66
  83.8 1.0 %convolution_convert_fusion.2 = bf16[128,1024]{1,0:T(8,128)(2,1)} fusion(bf16[96,1024]{1,0:T(8,128)(2,1)S(1)} %collective-permute-done.14, bf16[96,1024]{1,0:T(8,128)(2,1)S(1)} %collective-permute-done.13, bf16[96,1024]{1,0:T(8,128)(2,1)S(1)} %collective-permute-done.12, bf16[96,1024]{1,0:T(8,128)(2,1)S(1)} %get-tuple-element.43, ...), kind=kOutput, calls=%fused_computation.9 | convolution fusion | flops 103989248 | bytes 1245184 | tf_op jit(solution)/shard_map/dot_general | solution.py:145
  84.8 3.1 %collective-permute-done.17 = f32[1,128,384]{2,1,0:T(8,128)S(1)} collective-permute-done((f32[1,128,384]{2,1,0:T(8,128)S(1)}, f32[1,128,384]{2,1,0:T(8,128)S(1)}, u32[]{:S(2)}, u32[]{:S(2)}) %collective-permute-start.17) | collective-permute-done | bytes 196640 | tf_op jit(solution)/shard_map/ppermute | solution.py:66
  87.9 0.7 fusion.23
  (58 shorter events, 1.5 us)
Async XLA Ops:
  0.6 15.0 %copy-start = (bf16[128,1024]{1,0:T(8,128)(2,1)S(1)}, bf16[128,1024]{1,0:T(8,128)(2,1)}, u32[]{:S(2)}) copy-start(bf16[128,1024]{1,0:T(8,128)(2,1)} %param.13) | copy-start | bytes 786436
  3.4 10.1 %collective-permute-start.3 = (bf16[1,128,1152]{2,1,0:T(8,128)(2,1)S(1)}, bf16[1,128,1152]{2,1,0:T(8,128)(2,1)S(1)}, u32[]{:S(2)}, u32[]{:S(2)}) collective-permute-start(bf16[1,128,1152]{2,1,0:T(8,128)(2,1)S(1)} %constant_dynamic-update-slice_fusion), channel_id=1, source_target_pairs={{0,16},{4,20},{8,24},{12,28},{16,0},{20,4},{24,8},{28,12},{1,17},{... | collective-permute-start | bytes 884744 | tf_op jit(solution)/shard_map/ppermute | solution.py:47
  7.4 6.2 %copy-start.5 = (s32[256]{0:T(256)}, s32[256]{0:T(256)S(1)}, u32[]{:S(2)}) copy-start(s32[256]{0:T(256)S(1)} %sub.46) | copy-start | bytes 3076
  7.6 6.0 %copy-start.9 = (f32[256]{0:T(256)}, f32[256]{0:T(256)S(1)}, u32[]{:S(2)}) copy-start(f32[256]{0:T(256)S(1)} %fusion.2) | copy-start | bytes 3076
  7.9 7.7 %copy-start.4 = (s32[128,2]{0,1:T(2,128)}, s32[128,2]{0,1:T(2,128)S(1)}, u32[]{:S(2)}) copy-start(s32[128,2]{0,1:T(2,128)S(1)} %copy.21) | copy-start | bytes 3076
  13.6 7.1 %copy-start.7 = (f32[128,2]{0,1:T(2,128)S(1)}, f32[128,2]{0,1:T(2,128)}, u32[]{:S(2)}) copy-start(f32[128,2]{0,1:T(2,128)} %param.15) | copy-start | bytes 3076
  13.7 14.6 %collective-permute-start.4 = (bf16[2,128,1152]{2,1,0:T(8,128)(2,1)S(1)}, bf16[2,128,1152]{2,1,0:T(8,128)(2,1)S(1)}, u32[]{:S(2)}, u32[]{:S(2)}) collective-permute-start(bf16[2,128,1152]{2,1,0:T(8,128)(2,1)S(1)} %maximum_bitcast_fusion), channel_id=1, source_target_pairs={{0,8},{4,12},{8,0},{12,4},{16,24},{20,28},{24,16},{28,20},{1,9},{5... | collective-permute-start | bytes 1769480 | tf_op jit(solution)/shard_map/ppermute | solution.py:47
  16.1 20.4 %collective-permute-start.2 = (bf16[96,1024]{1,0:T(8,128)(2,1)S(1)}, bf16[96,1024]{1,0:T(8,128)(2,1)}, u32[]{:S(2)}, u32[]{:S(2)}) collective-permute-start(bf16[96,1024]{1,0:T(8,128)(2,1)S(1)} %get-tuple-element.56), channel_id=1, source_target_pairs={{0,3},{1,0},{2,1},{3,2},{4,7},{5,4},{6,5},{7,6},{8,11},{9,8},{10,9... | collective-permute-start | bytes 589832 | tf_op jit(solution)/shard_map/ppermute | solution.py:38
  19.7 18.5 %collective-permute-start.1 = (bf16[96,1024]{1,0:T(8,128)(2,1)S(1)}, bf16[96,1024]{1,0:T(8,128)(2,1)}, u32[]{:S(2)}, u32[]{:S(2)}) collective-permute-start(bf16[96,1024]{1,0:T(8,128)(2,1)S(1)} %get-tuple-element.57), channel_id=1, source_target_pairs={{0,2},{1,3},{2,0},{3,1},{4,6},{5,7},{6,4},{7,5},{8,10},{9,11},{10,... | collective-permute-start | bytes 589832 | tf_op jit(solution)/shard_map/ppermute | solution.py:38
  19.7 18.5 %collective-permute-start = (bf16[96,1024]{1,0:T(8,128)(2,1)S(1)}, bf16[96,1024]{1,0:T(8,128)(2,1)}, u32[]{:S(2)}, u32[]{:S(2)}) collective-permute-start(bf16[96,1024]{1,0:T(8,128)(2,1)S(1)} %get-tuple-element.58), channel_id=1, source_target_pairs={{0,1},{1,2},{2,3},{3,0},{4,5},{5,6},{6,7},{7,4},{8,9},{9,10},{10,1... | collective-permute-start | bytes 589832 | tf_op jit(solution)/shard_map/ppermute | solution.py:38
  28.3 0.7 copy-start.6
  28.4 0.7 copy-start.10
  28.4 0.7 copy-start.8
  28.4 1.0 %copy-start.1 = (bf16[128,1024]{1,0:T(8,128)(2,1)S(1)}, bf16[128,1024]{1,0:T(8,128)(2,1)}, u32[]{:S(2)}) copy-start(bf16[128,1024]{1,0:T(8,128)(2,1)} %param.19) | copy-start | bytes 786436
  28.5 7.2 %collective-permute-start.5 = (bf16[4,128,1152]{2,1,0:T(8,128)(2,1)S(1)}, bf16[4,128,1152]{2,1,0:T(8,128)(2,1)S(1)}, u32[]{:S(2)}, u32[]{:S(2)}) collective-permute-start(bf16[4,128,1152]{2,1,0:T(8,128)(2,1)S(1)} %bitcast.96), channel_id=1, source_target_pairs={{0,4},{4,0},{8,12},{12,8},{16,20},{20,16},{24,28},{28,24},{1,5},{5... | collective-permute-start | bytes 3538952 | tf_op jit(solution)/shard_map/ppermute | solution.py:47
  30.6 19.8 %collective-permute-start.11 = (bf16[96,1024]{1,0:T(8,128)(2,1)}, bf16[96,1024]{1,0:T(8,128)(2,1)}, u32[]{:S(2)}, u32[]{:S(2)}) collective-permute-start(bf16[96,1024]{1,0:T(8,128)(2,1)} %get-tuple-element.48), channel_id=1, source_target_pairs={{0,3},{1,0},{2,1},{3,2},{4,7},{5,4},{6,5},{7,6},{8,11},{9,8},{10,9... | collective-permute-start | bytes 589832 | tf_op jit(solution)/shard_map/ppermute | solution.py:38
  35.7 26.0 %collective-permute-start.10 = (bf16[96,1024]{1,0:T(8,128)(2,1)}, bf16[96,1024]{1,0:T(8,128)(2,1)S(1)}, u32[]{:S(2)}, u32[]{:S(2)}) collective-permute-start(bf16[96,1024]{1,0:T(8,128)(2,1)} %get-tuple-element.49), channel_id=1, source_target_pairs={{0,2},{1,3},{2,0},{3,1},{4,6},{5,7},{6,4},{7,5},{8,10},{9,11},{10,... | collective-permute-start | bytes 589832 | tf_op jit(solution)/shard_map/ppermute | solution.py:38
  36.3 0.9 %copy-start.3 = (bf16[96,1024]{1,0:T(8,128)(2,1)S(1)}, bf16[96,1024]{1,0:T(8,128)(2,1)}, u32[]{:S(2)}) copy-start(bf16[96,1024]{1,0:T(8,128)(2,1)} %get-tuple-element.50) | copy-start | bytes 589828
  37.2 24.5 %collective-permute-start.9 = (bf16[96,1024]{1,0:T(8,128)(2,1)S(1)}, bf16[96,1024]{1,0:T(8,128)(2,1)S(1)}, u32[]{:S(2)}, u32[]{:S(2)}) collective-permute-start(bf16[96,1024]{1,0:T(8,128)(2,1)S(1)} %copy-done.3), channel_id=1, source_target_pairs={{0,1},{1,2},{2,3},{3,0},{4,5},{5,6},{6,7},{7,4},{8,9},{9,10},{10,1... | collective-permute-start | bytes 589832 | tf_op jit(solution)/shard_map/ppermute | solution.py:38
  41.6 20.1 %copy-start.2 = (bf16[96,1024]{1,0:T(8,128)(2,1)S(1)}, bf16[96,1024]{1,0:T(8,128)(2,1)}, u32[]{:S(2)}) copy-start(bf16[96,1024]{1,0:T(8,128)(2,1)} %get-tuple-element.47) | copy-start | bytes 589828
  42.3 26.2 %collective-permute-start.8 = (bf16[96,1024]{1,0:T(8,128)(2,1)S(1)}, bf16[96,1024]{1,0:T(8,128)(2,1)S(1)}, u32[]{:S(2)}, u32[]{:S(2)}) collective-permute-start(bf16[96,1024]{1,0:T(8,128)(2,1)S(1)} %get-tuple-element.52), channel_id=1, source_target_pairs={{0,1},{1,2},{2,3},{3,0},{4,5},{5,6},{6,7},{7,4},{8,9},{9,10},{10,1... | collective-permute-start | bytes 589832 | tf_op jit(solution)/shard_map/ppermute | solution.py:38
  44.9 26.6 %collective-permute-start.7 = (bf16[96,1024]{1,0:T(8,128)(2,1)S(1)}, bf16[96,1024]{1,0:T(8,128)(2,1)S(1)}, u32[]{:S(2)}, u32[]{:S(2)}) collective-permute-start(bf16[96,1024]{1,0:T(8,128)(2,1)S(1)} %get-tuple-element.53), channel_id=1, source_target_pairs={{0,2},{1,3},{2,0},{3,1},{4,6},{5,7},{6,4},{7,5},{8,10},{9,11},{10,... | collective-permute-start | bytes 589832 | tf_op jit(solution)/shard_map/ppermute | solution.py:38
  50.4 21.0 %collective-permute-start.6 = (bf16[96,1024]{1,0:T(8,128)(2,1)S(1)}, bf16[96,1024]{1,0:T(8,128)(2,1)S(1)}, u32[]{:S(2)}, u32[]{:S(2)}) collective-permute-start(bf16[96,1024]{1,0:T(8,128)(2,1)S(1)} %get-tuple-element.54), channel_id=1, source_target_pairs={{0,3},{1,0},{2,1},{3,2},{4,7},{5,4},{6,5},{7,6},{8,11},{9,8},{10,9... | collective-permute-start | bytes 589832 | tf_op jit(solution)/shard_map/ppermute | solution.py:38
  63.4 3.0 %collective-permute-start.15 = (f32[4,128,384]{2,1,0:T(8,128)S(1)}, f32[4,128,384]{2,1,0:T(8,128)S(1)}, u32[]{:S(2)}, u32[]{:S(2)}) collective-permute-start(f32[4,128,384]{2,1,0:T(8,128)S(1)} %fusion.10), channel_id=1, source_target_pairs={{0,4},{4,0},{8,12},{12,8},{16,20},{20,16},{24,28},{28,24},{1,5},{5... | collective-permute-start | bytes 2359304 | tf_op jit(solution)/shard_map/ppermute | solution.py:66
  66.4 17.4 %collective-permute-start.14 = (bf16[96,1024]{1,0:T(8,128)(2,1)S(1)}, bf16[96,1024]{1,0:T(8,128)(2,1)S(1)}, u32[]{:S(2)}, u32[]{:S(2)}) collective-permute-start(bf16[96,1024]{1,0:T(8,128)(2,1)S(1)} %get-tuple-element.44), channel_id=1, source_target_pairs={{0,1},{1,2},{2,3},{3,0},{4,5},{5,6},{6,7},{7,4},{8,9},{9,10},{10,1... | collective-permute-start | bytes 589832 | tf_op jit(solution)/shard_map/ppermute | solution.py:38
  66.5 17.3 %collective-permute-start.13 = (bf16[96,1024]{1,0:T(8,128)(2,1)S(1)}, bf16[96,1024]{1,0:T(8,128)(2,1)S(1)}, u32[]{:S(2)}, u32[]{:S(2)}) collective-permute-start(bf16[96,1024]{1,0:T(8,128)(2,1)S(1)} %get-tuple-element.45), channel_id=1, source_target_pairs={{0,2},{1,3},{2,0},{3,1},{4,6},{5,7},{6,4},{7,5},{8,10},{9,11},{10,... | collective-permute-start | bytes 589832 | tf_op jit(solution)/shard_map/ppermute | solution.py:38
  68.5 15.2 %collective-permute-start.12 = (bf16[96,1024]{1,0:T(8,128)(2,1)S(1)}, bf16[96,1024]{1,0:T(8,128)(2,1)S(1)}, u32[]{:S(2)}, u32[]{:S(2)}) collective-permute-start(bf16[96,1024]{1,0:T(8,128)(2,1)S(1)} %get-tuple-element.46), channel_id=1, source_target_pairs={{0,3},{1,0},{2,1},{3,2},{4,7},{5,4},{6,5},{7,6},{8,11},{9,8},{10,9... | collective-permute-start | bytes 589832 | tf_op jit(solution)/shard_map/ppermute | solution.py:38
  71.4 10.7 %collective-permute-start.16 = (f32[2,128,384]{2,1,0:T(8,128)S(1)}, f32[2,128,384]{2,1,0:T(8,128)S(1)}, u32[]{:S(2)}, u32[]{:S(2)}) collective-permute-start(f32[2,128,384]{2,1,0:T(8,128)S(1)} %select_bitcast_fusion.4), channel_id=1, source_target_pairs={{0,8},{4,12},{8,0},{12,4},{16,24},{20,28},{24,16},{28,20},{1,9},{5... | collective-permute-start | bytes 1179656 | tf_op jit(solution)/shard_map/ppermute | solution.py:66
  82.2 5.7 %collective-permute-start.17 = (f32[1,128,384]{2,1,0:T(8,128)S(1)}, f32[1,128,384]{2,1,0:T(8,128)S(1)}, u32[]{:S(2)}, u32[]{:S(2)}) collective-permute-start(f32[1,128,384]{2,1,0:T(8,128)S(1)} %select_bitcast_fusion.7), channel_id=1, source_target_pairs={{0,16},{4,20},{8,24},{12,28},{16,0},{20,4},{24,8},{28,12},{1,17},{... | collective-permute-start | bytes 589832 | tf_op jit(solution)/shard_map/ppermute | solution.py:66

commit v5 on v4

--- a/solution.py
+++ b/solution.py
@@ -113,13 +113,14 @@
     )
     packed = jnp.concatenate([w_gate, w_up, w_down], axis=2)
     packed = jnp.transpose(packed, (1, 0, 2)).reshape(shard_d, local_count * 3 * ff_width)
+    recv_rows = shift_send([send_rows[s] for s in range(groups)], groups, 1)
+    recv_grads = shift_send([send_grads[s] for s in range(groups)], groups, 1)
+    packed, _ = lax.optimization_barrier((packed, recv_rows[1:]))
     full = all_gather_dp(packed, n_dp).reshape(width, local_count * 3 * ff_width)
     full = jnp.transpose(full.reshape(width, local_count, 3 * ff_width), (1, 0, 2))
     gate_full = full[:, :, :ff_width]
     up_full = full[:, :, ff_width : 2 * ff_width]
     down_full = full[:, :, 2 * ff_width :]
-    recv_rows = shift_send([send_rows[s] for s in range(groups)], groups, 1)
-    recv_grads = shift_send([send_grads[s] for s in range(groups)], groups, 1)
     gate_w = gate_full[0]
     up_w = up_full[0]
     down_w = down_full[0]

time: 89 us -> 108 us (1.21)
  waiting for transfers between devices: 33.2 us -> 62.1 us
  starting transfers between devices: 31.6 us -> 27.8 us
  local copies, waits for them, and re-layouts: 8.04 us -> 4.77 us
  matrix products: 11.8 us -> 9.96 us
    ppermute x12, waiting for transfers between devices: 8.49 us -> 31.3 us  [shift_send(): got.append(lax.ppermute(blocks[step], 'expert', pairs))]
    ppermute x3, waiting for transfers between devices: 12.2 us -> 19.9 us  [all_gather_dp(): recv = lax.ppermute(work, 'dp', [(i, i ^ bit) for i in range(n_dp)])]
    ppermute x12, starting transfers between devices: 25 us -> 21.7 us  [shift_send(): got.append(lax.ppermute(blocks[step], 'expert', pairs))]
    ppermute x3, starting transfers between devices: 4.91 us -> 3.09 us  [all_gather_dp(): recv = lax.ppermute(work, 'dp', [(i, i ^ bit) for i in range(n_dp)])]
    ppermute x3, waiting for transfers between devices: 12.4 us -> 10.9 us  [reduce_scatter_dp(): work = keep + lax.ppermute(give, 'dp', pairs)]
    ppermute x3, starting transfers between devices: 1.65 us -> 3.09 us  [reduce_scatter_dp(): work = keep + lax.ppermute(give, 'dp', pairs)]
    dot_general x1, matrix products: 1.69 us -> 0.57 us  [forward_rows(): gate_pre = jnp.dot(row_data, gate_w, preferred_element_type=jnp.float32)]
    dot_general x1, matrix products: 1.7 us -> 0.58 us  [forward_rows(): up_pre = jnp.dot(row_data, up_w, preferred_element_type=jnp.float32)]
  transfers between devices with their start and end apart: 18 -> 18, of which waited for: 5 -> 8; matrix products, arithmetic and copies ran while one was open for 20% -> 11% of each run, Pallas kernels for 0% -> 0%
where the time goes in v5:
time: 108 us
  waiting for transfers between devices  62.1 us (58%)
  starting transfers between devices  27.8 us (26%)
  matrix products  9.96 us (9%)
  local copies, waits for them, and re-layouts  4.77 us (4%)
  other arithmetic  2.39 us (2%)
    ppermute x12, waiting for transfers between devices, shift_send(): got.append(lax.ppermute(blocks[step], 'expert', pairs))  31.3 us
    ppermute x12, starting transfers between devices, shift_send(): got.append(lax.ppermute(blocks[step], 'expert', pairs))  21.7 us
    ppermute x3, waiting for transfers between devices, all_gather_dp(): recv = lax.ppermute(work, 'dp', [(i, i ^ bit) for i in range(n_dp)])  19.9 us
    ppermute x3, waiting for transfers between devices, reduce_scatter_dp(): work = keep + lax.ppermute(give, 'dp', pairs)  10.9 us
    unnamed x26, local copies, waits for them, and re-layouts  3.16 us
    ppermute x3, starting transfers between devices, all_gather_dp(): recv = lax.ppermute(work, 'dp', [(i, i ^ bit) for i in range(n_dp)])  3.09 us
    ppermute x3, starting transfers between devices, reduce_scatter_dp(): work = keep + lax.ppermute(give, 'dp', pairs)  3.09 us
  transfers between devices with their start and end apart: 18, of which 8 were waited for; matrix products, arithmetic and copies ran while one was open for 11% of the time, Pallas kernels for 0%

profile of v5, /device:TPU:0, one launch (start us, length us, event | category | flops | bytes accessed | tf_op | source)
XLA Modules:
  0.0 108.1 jit_solution(16680620807615007548)
XLA Ops:
  0.6 0.8 copy.20
  1.5 0.1 sub.46
  1.6 0.2 fusion.2
  1.9 0.1 convert_element_type.57
  2.1 0.2 fusion.22
  2.3 0.4 convolution_convert_fusion
  2.8 3.1 %collective-permute-start = (bf16[96,1024]{1,0:T(8,128)(2,1)S(1)}, bf16[96,1024]{1,0:T(8,128)(2,1)S(1)}, u32[]{:S(2)}, u32[]{:S(2)}) collective-permute-start(bf16[96,1024]{1,0:T(8,128)(2,1)S(1)} %get-tuple-element.60), channel_id=1, source_target_pairs={{0,1},{1,2},{2,3},{3,0},{4,5},{5,6},{6,7},{7,4},{8,9},{9,10},{10,1... | collective-permute-start | bytes 589832 | tf_op jit(solution)/shard_map/ppermute | solution.py:38
  5.9 2.6 %collective-permute-start.1 = (bf16[96,1024]{1,0:T(8,128)(2,1)S(1)}, bf16[96,1024]{1,0:T(8,128)(2,1)S(1)}, u32[]{:S(2)}, u32[]{:S(2)}) collective-permute-start(bf16[96,1024]{1,0:T(8,128)(2,1)S(1)} %get-tuple-element.59), channel_id=1, source_target_pairs={{0,2},{1,3},{2,0},{3,1},{4,6},{5,7},{6,4},{7,5},{8,10},{9,11},{10,... | collective-permute-start | bytes 589832 | tf_op jit(solution)/shard_map/ppermute | solution.py:38
  8.5 1.3 %collective-permute-start.2 = (bf16[96,1024]{1,0:T(8,128)(2,1)S(1)}, bf16[96,1024]{1,0:T(8,128)(2,1)S(1)}, u32[]{:S(2)}, u32[]{:S(2)}) collective-permute-start(bf16[96,1024]{1,0:T(8,128)(2,1)S(1)} %get-tuple-element.58), channel_id=1, source_target_pairs={{0,3},{1,0},{2,1},{3,2},{4,7},{5,4},{6,5},{7,6},{8,11},{9,8},{10,9... | collective-permute-start | bytes 589832 | tf_op jit(solution)/shard_map/ppermute | solution.py:38
  9.9 3.9 %collective-permute-done = bf16[96,1024]{1,0:T(8,128)(2,1)S(1)} collective-permute-done((bf16[96,1024]{1,0:T(8,128)(2,1)S(1)}, bf16[96,1024]{1,0:T(8,128)(2,1)S(1)}, u32[]{:S(2)}, u32[]{:S(2)}) %collective-permute-start) | collective-permute-done | bytes 196640 | tf_op jit(solution)/shard_map/ppermute | solution.py:38
  13.8 7.6 %collective-permute-done.1 = bf16[96,1024]{1,0:T(8,128)(2,1)S(1)} collective-permute-done((bf16[96,1024]{1,0:T(8,128)(2,1)S(1)}, bf16[96,1024]{1,0:T(8,128)(2,1)S(1)}, u32[]{:S(2)}, u32[]{:S(2)}) %collective-permute-start.1) | collective-permute-done | bytes 196640 | tf_op jit(solution)/shard_map/ppermute | solution.py:38
  21.4 0.7 copy-done.8
  22.1 1.5 %collective-permute-start.3 = (bf16[1,128,1152]{2,1,0:T(8,128)(2,1)S(1)}, bf16[1,128,1152]{2,1,0:T(8,128)(2,1)S(1)}, u32[]{:S(2)}, u32[]{:S(2)}) collective-permute-start(bf16[1,128,1152]{2,1,0:T(8,128)(2,1)S(1)} %bitcast.112), channel_id=1, source_target_pairs={{0,16},{4,20},{8,24},{12,28},{16,0},{20,4},{24,8},{28,12},{1,17},{... | collective-permute-start | bytes 884744 | tf_op jit(solution)/shard_map/ppermute | solution.py:47
  23.6 7.3 %collective-permute-done.3 = bf16[1,128,1152]{2,1,0:T(8,128)(2,1)S(1)} collective-permute-done((bf16[1,128,1152]{2,1,0:T(8,128)(2,1)S(1)}, bf16[1,128,1152]{2,1,0:T(8,128)(2,1)S(1)}, u32[]{:S(2)}, u32[]{:S(2)}) %collective-permute-start.3) | collective-permute-done | bytes 294944 | tf_op jit(solution)/shard_map/ppermute | solution.py:47
  31.1 1.5 %collective-permute-start.4 = (bf16[2,128,1152]{2,1,0:T(8,128)(2,1)S(1)}, bf16[2,128,1152]{2,1,0:T(8,128)(2,1)S(1)}, u32[]{:S(2)}, u32[]{:S(2)}) collective-permute-start(bf16[2,128,1152]{2,1,0:T(8,128)(2,1)S(1)} %maximum_bitcast_fusion), channel_id=1, source_target_pairs={{0,8},{4,12},{8,0},{12,4},{16,24},{20,28},{24,16},{28,20},{1,9},{5... | collective-permute-start | bytes 1769480 | tf_op jit(solution)/shard_map/ppermute | solution.py:47
  32.8 0.1 broadcast_in_dim.52
  32.9 12.6 %collective-permute-done.4 = bf16[2,128,1152]{2,1,0:T(8,128)(2,1)S(1)} collective-permute-done((bf16[2,128,1152]{2,1,0:T(8,128)(2,1)S(1)}, bf16[2,128,1152]{2,1,0:T(8,128)(2,1)S(1)}, u32[]{:S(2)}, u32[]{:S(2)}) %collective-permute-start.4) | collective-permute-done | bytes 589856 | tf_op jit(solution)/shard_map/ppermute | solution.py:47
  45.5 0.1 select_bitcast_fusion.3
  45.8 0.1 select_reduce_fusion
  46.0 0.6 copy-done.1
  46.6 0.4 multiply_convert_fusion
  47.0 0.8 fusion.42
  47.8 3.8 %collective-permute-start.11 = (bf16[96,1024]{1,0:T(8,128)(2,1)}, bf16[96,1024]{1,0:T(8,128)(2,1)}, u32[]{:S(2)}, u32[]{:S(2)}) collective-permute-start(bf16[96,1024]{1,0:T(8,128)(2,1)} %get-tuple-element.50), channel_id=1, source_target_pairs={{0,3},{1,0},{2,1},{3,2},{4,7},{5,4},{6,5},{7,6},{8,11},{9,8},{10,9... | collective-permute-start | bytes 589832 | tf_op jit(solution)/shard_map/ppermute | solution.py:38
  51.6 2.4 %collective-permute-start.10 = (bf16[96,1024]{1,0:T(8,128)(2,1)S(1)}, bf16[96,1024]{1,0:T(8,128)(2,1)}, u32[]{:S(2)}, u32[]{:S(2)}) collective-permute-start(bf16[96,1024]{1,0:T(8,128)(2,1)S(1)} %get-tuple-element.51), channel_id=1, source_target_pairs={{0,2},{1,3},{2,0},{3,1},{4,6},{5,7},{6,4},{7,5},{8,10},{9,11},{10,... | collective-permute-start | bytes 589832 | tf_op jit(solution)/shard_map/ppermute | solution.py:38
  54.2 0.3 select_bitcast_fusion.1
  54.5 0.2 pad_maximum_fusion
  54.8 0.2 copy.23
  55.0 0.7 copy-done.7
  55.8 0.6 fusion.14
  56.4 0.6 multiply_convert_fusion.3
  57.0 0.6 convolution_convert_fusion.1
  57.7 1.1 %collective-permute-start.8 = (bf16[96,1024]{1,0:T(8,128)(2,1)S(1)}, bf16[96,1024]{1,0:T(8,128)(2,1)S(1)}, u32[]{:S(2)}, u32[]{:S(2)}) collective-permute-start(bf16[96,1024]{1,0:T(8,128)(2,1)S(1)} %get-tuple-element.54), channel_id=1, source_target_pairs={{0,1},{1,2},{2,3},{3,0},{4,5},{5,6},{6,7},{7,4},{8,9},{9,10},{10,1... | collective-permute-start | bytes 589832 | tf_op jit(solution)/shard_map/ppermute | solution.py:38
  58.8 3.3 %collective-permute-start.7 = (bf16[96,1024]{1,0:T(8,128)(2,1)S(1)}, bf16[96,1024]{1,0:T(8,128)(2,1)S(1)}, u32[]{:S(2)}, u32[]{:S(2)}) collective-permute-start(bf16[96,1024]{1,0:T(8,128)(2,1)S(1)} %get-tuple-element.55), channel_id=1, source_target_pairs={{0,2},{1,3},{2,0},{3,1},{4,6},{5,7},{6,4},{7,5},{8,10},{9,11},{10,... | collective-permute-start | bytes 589832 | tf_op jit(solution)/shard_map/ppermute | solution.py:38
  62.1 19.1 %collective-permute-done.10 = bf16[96,1024]{1,0:T(8,128)(2,1)} collective-permute-done((bf16[96,1024]{1,0:T(8,128)(2,1)S(1)}, bf16[96,1024]{1,0:T(8,128)(2,1)}, u32[]{:S(2)}, u32[]{:S(2)}) %collective-permute-start.10) | collective-permute-done | bytes 196640 | tf_op jit(solution)/shard_map/ppermute | solution.py:38
  81.3 1.8 %fusion.24 = f32[1024,384]{1,0:T(8,128)S(1)} fusion(bf16[384,384]{1,0:T(8,128)(2,1)S(1)} %get-tuple-element.67, bf16[96,1024]{1,0:T(8,128)(2,1)} %collective-permute-done.11, bf16[96,1024]{1,0:T(8,128)(2,1)} %collective-permute-done.10, bf16[96,1024]{1,0:T(8,128)(2,1)} %collective-permute-done.9, bf16[96,1024]{1,0:T(8,128)(2,1)S(1)} %get-tuple-element.49), kind=kOutput, calls=%fused_computation.65 | convolution fusion | flops 305135616 | bytes 2654208 | tf_op jit(solution)/shard_map/dot_general | solution.py:131
  83.3 1.7 %fusion.16 = f32[384,384]{1,0:T(8,128)S(1)} fusion(bf16[1,1024,1152]{2,1,0:T(8,128)(2,1)S(1)} %bitcast.107, bf16[96,1024]{1,0:T(8,128)(2,1)} %collective-permute-done.11, bf16[96,1024]{1,0:T(8,128)(2,1)} %collective-permute-done.10, bf16[96,1024]{1,0:T(8,128)(2,1)} %collective-permute-done.9, bf16[96,1024]{1,0:T(8,128)(2,1)S(1)} %get-tuple-element.49), kind=kOutput, calls=%fused_computation.36 | convolution fusion | flops 305135616 | bytes 2162688 | tf_op jit(solution)/shard_map/dot_general | solution.py:22
  84.9 0.7 fusion.13
  85.6 0.6 add_convert_fusion
  86.6 3.8 %collective-permute-start.12 = (bf16[96,1024]{1,0:T(8,128)(2,1)S(1)}, bf16[96,1024]{1,0:T(8,128)(2,1)S(1)}, u32[]{:S(2)}, u32[]{:S(2)}) collective-permute-start(bf16[96,1024]{1,0:T(8,128)(2,1)S(1)} %get-tuple-element.48), channel_id=1, source_target_pairs={{0,3},{1,0},{2,1},{3,2},{4,7},{5,4},{6,5},{7,6},{8,11},{9,8},{10,9... | collective-permute-start | bytes 589832 | tf_op jit(solution)/shard_map/ppermute | solution.py:38
  90.4 1.5 %collective-permute-start.16 = (f32[2,128,384]{2,1,0:T(8,128)S(1)}, f32[2,128,384]{2,1,0:T(8,128)S(1)}, u32[]{:S(2)}, u32[]{:S(2)}) collective-permute-start(f32[2,128,384]{2,1,0:T(8,128)S(1)} %select_bitcast_fusion.4), channel_id=1, source_target_pairs={{0,8},{4,12},{8,0},{12,4},{16,24},{20,28},{24,16},{28,20},{1,9},{5... | collective-permute-start | bytes 1179656 | tf_op jit(solution)/shard_map/ppermute | solution.py:66
  91.9 0.3 convolution_multiply_fusion
  92.2 1.0 fusion.1
  93.2 8.1 %collective-permute-done.16 = f32[2,128,384]{2,1,0:T(8,128)S(1)} collective-permute-done((f32[2,128,384]{2,1,0:T(8,128)S(1)}, f32[2,128,384]{2,1,0:T(8,128)S(1)}, u32[]{:S(2)}, u32[]{:S(2)}) %collective-permute-start.16) | collective-permute-done | bytes 393248 | tf_op jit(solution)/shard_map/ppermute | solution.py:66
  101.5 1.6 %collective-permute-start.17 = (f32[1,128,384]{2,1,0:T(8,128)S(1)}, f32[1,128,384]{2,1,0:T(8,128)S(1)}, u32[]{:S(2)}, u32[]{:S(2)}) collective-permute-start(f32[1,128,384]{2,1,0:T(8,128)S(1)} %select_bitcast_fusion.7), channel_id=1, source_target_pairs={{0,16},{4,20},{8,24},{12,28},{16,0},{20,4},{24,8},{28,12},{1,17},{... | collective-permute-start | bytes 589832 | tf_op jit(solution)/shard_map/ppermute | solution.py:66
  103.0 0.6 collective-permute-done.13
  103.6 1.0 convolution_convert_fusion.2
  104.6 2.8 %collective-permute-done.17 = f32[1,128,384]{2,1,0:T(8,128)S(1)} collective-permute-done((f32[1,128,384]{2,1,0:T(8,128)S(1)}, f32[1,128,384]{2,1,0:T(8,128)S(1)}, u32[]{:S(2)}, u32[]{:S(2)}) %collective-permute-start.17) | collective-permute-done | bytes 196640 | tf_op jit(solution)/shard_map/ppermute | solution.py:66
  107.4 0.7 fusion.23
  (58 shorter events, 1.7 us)
Async XLA Ops:
  0.6 1.7 %copy-start = (bf16[128,1024]{1,0:T(8,128)(2,1)S(1)}, bf16[128,1024]{1,0:T(8,128)(2,1)}, u32[]{:S(2)}) copy-start(bf16[128,1024]{1,0:T(8,128)(2,1)} %param.13) | copy-start | bytes 786436
  1.9 8.0 %copy-start.2 = (bf16[1,128,384]{2,1,0:T(8,128)(2,1)S(1)}, bf16[1,128,384]{2,1,0:T(8,128)(2,1)}, u32[]{:S(2)}) copy-start(bf16[1,128,384]{2,1,0:T(8,128)(2,1)} %param.18) | copy-start | bytes 294916
  1.9 8.0 %copy-start.3 = (bf16[1,128,384]{2,1,0:T(8,128)(2,1)S(1)}, bf16[1,128,384]{2,1,0:T(8,128)(2,1)}, u32[]{:S(2)}) copy-start(bf16[1,128,384]{2,1,0:T(8,128)(2,1)} %param.17) | copy-start | bytes 294916
  1.9 8.0 %copy-start.4 = (bf16[1,128,384]{2,1,0:T(8,128)(2,1)S(1)}, bf16[1,128,384]{2,1,0:T(8,128)(2,1)}, u32[]{:S(2)}) copy-start(bf16[1,128,384]{2,1,0:T(8,128)(2,1)} %param.16) | copy-start | bytes 294916
  2.8 29.8 %copy-start.5 = (f32[128,2]{0,1:T(2,128)S(1)}, f32[128,2]{0,1:T(2,128)}, u32[]{:S(2)}) copy-start(f32[128,2]{0,1:T(2,128)} %param.15) | copy-start | bytes 3076
  2.8 11.0 %collective-permute-start = (bf16[96,1024]{1,0:T(8,128)(2,1)S(1)}, bf16[96,1024]{1,0:T(8,128)(2,1)S(1)}, u32[]{:S(2)}, u32[]{:S(2)}) collective-permute-start(bf16[96,1024]{1,0:T(8,128)(2,1)S(1)} %get-tuple-element.60), channel_id=1, source_target_pairs={{0,1},{1,2},{2,3},{3,0},{4,5},{5,6},{6,7},{7,4},{8,9},{9,10},{10,1... | collective-permute-start | bytes 589832 | tf_op jit(solution)/shard_map/ppermute | solution.py:38
  5.9 15.5 %collective-permute-start.1 = (bf16[96,1024]{1,0:T(8,128)(2,1)S(1)}, bf16[96,1024]{1,0:T(8,128)(2,1)S(1)}, u32[]{:S(2)}, u32[]{:S(2)}) collective-permute-start(bf16[96,1024]{1,0:T(8,128)(2,1)S(1)} %get-tuple-element.59), channel_id=1, source_target_pairs={{0,2},{1,3},{2,0},{3,1},{4,6},{5,7},{6,4},{7,5},{8,10},{9,11},{10,... | collective-permute-start | bytes 589832 | tf_op jit(solution)/shard_map/ppermute | solution.py:38
  8.5 12.9 %collective-permute-start.2 = (bf16[96,1024]{1,0:T(8,128)(2,1)S(1)}, bf16[96,1024]{1,0:T(8,128)(2,1)S(1)}, u32[]{:S(2)}, u32[]{:S(2)}) collective-permute-start(bf16[96,1024]{1,0:T(8,128)(2,1)S(1)} %get-tuple-element.58), channel_id=1, source_target_pairs={{0,3},{1,0},{2,1},{3,2},{4,7},{5,4},{6,5},{7,6},{8,11},{9,8},{10,9... | collective-permute-start | bytes 589832 | tf_op jit(solution)/shard_map/ppermute | solution.py:38
  13.8 7.6 %copy-start.6 = (bf16[96,1024]{1,0:T(8,128)(2,1)}, bf16[96,1024]{1,0:T(8,128)(2,1)S(1)}, u32[]{:S(2)}) copy-start(bf16[96,1024]{1,0:T(8,128)(2,1)S(1)} %collective-permute-done) | copy-start | bytes 589828
  21.4 0.7 copy-start.8
  21.4 0.7 copy-start.10
  22.1 8.8 %collective-permute-start.3 = (bf16[1,128,1152]{2,1,0:T(8,128)(2,1)S(1)}, bf16[1,128,1152]{2,1,0:T(8,128)(2,1)S(1)}, u32[]{:S(2)}, u32[]{:S(2)}) collective-permute-start(bf16[1,128,1152]{2,1,0:T(8,128)(2,1)S(1)} %bitcast.112), channel_id=1, source_target_pairs={{0,16},{4,20},{8,24},{12,28},{16,0},{20,4},{24,8},{28,12},{1,17},{... | collective-permute-start | bytes 884744 | tf_op jit(solution)/shard_map/ppermute | solution.py:47
  31.1 14.4 %collective-permute-start.4 = (bf16[2,128,1152]{2,1,0:T(8,128)(2,1)S(1)}, bf16[2,128,1152]{2,1,0:T(8,128)(2,1)S(1)}, u32[]{:S(2)}, u32[]{:S(2)}) collective-permute-start(bf16[2,128,1152]{2,1,0:T(8,128)(2,1)S(1)} %maximum_bitcast_fusion), channel_id=1, source_target_pairs={{0,8},{4,12},{8,0},{12,4},{16,24},{20,28},{24,16},{28,20},{1,9},{5... | collective-permute-start | bytes 1769480 | tf_op jit(solution)/shard_map/ppermute | solution.py:47
  45.6 1.0 copy-start.1
  45.7 8.4 %collective-permute-start.5 = (bf16[4,128,1152]{2,1,0:T(8,128)(2,1)S(1)}, bf16[4,128,1152]{2,1,0:T(8,128)(2,1)S(1)}, u32[]{:S(2)}, u32[]{:S(2)}) collective-permute-start(bf16[4,128,1152]{2,1,0:T(8,128)(2,1)S(1)} %bitcast.101), channel_id=1, source_target_pairs={{0,4},{4,0},{8,12},{12,8},{16,20},{20,16},{24,28},{28,24},{1,5},{5... | collective-permute-start | bytes 3538952 | tf_op jit(solution)/shard_map/ppermute | solution.py:47
  47.8 14.4 %collective-permute-start.11 = (bf16[96,1024]{1,0:T(8,128)(2,1)}, bf16[96,1024]{1,0:T(8,128)(2,1)}, u32[]{:S(2)}, u32[]{:S(2)}) collective-permute-start(bf16[96,1024]{1,0:T(8,128)(2,1)} %get-tuple-element.50), channel_id=1, source_target_pairs={{0,3},{1,0},{2,1},{3,2},{4,7},{5,4},{6,5},{7,6},{8,11},{9,8},{10,9... | collective-permute-start | bytes 589832 | tf_op jit(solution)/shard_map/ppermute | solution.py:38
  51.6 29.7 %collective-permute-start.10 = (bf16[96,1024]{1,0:T(8,128)(2,1)S(1)}, bf16[96,1024]{1,0:T(8,128)(2,1)}, u32[]{:S(2)}, u32[]{:S(2)}) collective-permute-start(bf16[96,1024]{1,0:T(8,128)(2,1)S(1)} %get-tuple-element.51), channel_id=1, source_target_pairs={{0,2},{1,3},{2,0},{3,1},{4,6},{5,7},{6,4},{7,5},{8,10},{9,11},{10,... | collective-permute-start | bytes 589832 | tf_op jit(solution)/shard_map/ppermute | solution.py:38
  54.0 27.3 %collective-permute-start.9 = (bf16[96,1024]{1,0:T(8,128)(2,1)S(1)}, bf16[96,1024]{1,0:T(8,128)(2,1)}, u32[]{:S(2)}, u32[]{:S(2)}) collective-permute-start(bf16[96,1024]{1,0:T(8,128)(2,1)S(1)} %get-tuple-element.52), channel_id=1, source_target_pairs={{0,1},{1,2},{2,3},{3,0},{4,5},{5,6},{6,7},{7,4},{8,9},{9,10},{10,1... | collective-permute-start | bytes 589832 | tf_op jit(solution)/shard_map/ppermute | solution.py:38
  54.7 0.9 copy-start.7
  54.7 1.0 copy-start.9
  54.7 1.1 %copy-start.11 = (bf16[96,1024]{1,0:T(8,128)(2,1)S(1)}, bf16[96,1024]{1,0:T(8,128)(2,1)}, u32[]{:S(2)}) copy-start(bf16[96,1024]{1,0:T(8,128)(2,1)} %copy-done.10) | copy-start | bytes 589828
  57.7 28.9 %collective-permute-start.8 = (bf16[96,1024]{1,0:T(8,128)(2,1)S(1)}, bf16[96,1024]{1,0:T(8,128)(2,1)S(1)}, u32[]{:S(2)}, u32[]{:S(2)}) collective-permute-start(bf16[96,1024]{1,0:T(8,128)(2,1)S(1)} %get-tuple-element.54), channel_id=1, source_target_pairs={{0,1},{1,2},{2,3},{3,0},{4,5},{5,6},{6,7},{7,4},{8,9},{9,10},{10,1... | collective-permute-start | bytes 589832 | tf_op jit(solution)/shard_map/ppermute | solution.py:38
  58.8 31.6 %collective-permute-start.7 = (bf16[96,1024]{1,0:T(8,128)(2,1)S(1)}, bf16[96,1024]{1,0:T(8,128)(2,1)S(1)}, u32[]{:S(2)}, u32[]{:S(2)}) collective-permute-start(bf16[96,1024]{1,0:T(8,128)(2,1)S(1)} %get-tuple-element.55), channel_id=1, source_target_pairs={{0,2},{1,3},{2,0},{3,1},{4,6},{5,7},{6,4},{7,5},{8,10},{9,11},{10,... | collective-permute-start | bytes 589832 | tf_op jit(solution)/shard_map/ppermute | solution.py:38
  62.1 29.8 %collective-permute-start.6 = (bf16[96,1024]{1,0:T(8,128)(2,1)S(1)}, bf16[96,1024]{1,0:T(8,128)(2,1)S(1)}, u32[]{:S(2)}, u32[]{:S(2)}) collective-permute-start(bf16[96,1024]{1,0:T(8,128)(2,1)S(1)} %get-tuple-element.56), channel_id=1, source_target_pairs={{0,3},{1,0},{2,1},{3,2},{4,7},{5,4},{6,5},{7,6},{8,11},{9,8},{10,9... | collective-permute-start | bytes 589832 | tf_op jit(solution)/shard_map/ppermute | solution.py:38
  83.2 3.2 %collective-permute-start.15 = (f32[4,128,384]{2,1,0:T(8,128)S(1)}, f32[4,128,384]{2,1,0:T(8,128)S(1)}, u32[]{:S(2)}, u32[]{:S(2)}) collective-permute-start(f32[4,128,384]{2,1,0:T(8,128)S(1)} %fusion.10), channel_id=1, source_target_pairs={{0,4},{4,0},{8,12},{12,8},{16,20},{20,16},{24,28},{28,24},{1,5},{5... | collective-permute-start | bytes 2359304 | tf_op jit(solution)/shard_map/ppermute | solution.py:66
  86.3 16.7 %collective-permute-start.14 = (bf16[96,1024]{1,0:T(8,128)(2,1)S(1)}, bf16[96,1024]{1,0:T(8,128)(2,1)S(1)}, u32[]{:S(2)}, u32[]{:S(2)}) collective-permute-start(bf16[96,1024]{1,0:T(8,128)(2,1)S(1)} %get-tuple-element.46), channel_id=1, source_target_pairs={{0,1},{1,2},{2,3},{3,0},{4,5},{5,6},{6,7},{7,4},{8,9},{9,10},{10,1... | collective-permute-start | bytes 589832 | tf_op jit(solution)/shard_map/ppermute | solution.py:38
  86.4 17.2 %collective-permute-start.13 = (bf16[96,1024]{1,0:T(8,128)(2,1)S(1)}, bf16[96,1024]{1,0:T(8,128)(2,1)S(1)}, u32[]{:S(2)}, u32[]{:S(2)}) collective-permute-start(bf16[96,1024]{1,0:T(8,128)(2,1)S(1)} %get-tuple-element.47), channel_id=1, source_target_pairs={{0,2},{1,3},{2,0},{3,1},{4,6},{5,7},{6,4},{7,5},{8,10},{9,11},{10,... | collective-permute-start | bytes 589832 | tf_op jit(solution)/shard_map/ppermute | solution.py:38
  86.6 17.0 %collective-permute-start.12 = (bf16[96,1024]{1,0:T(8,128)(2,1)S(1)}, bf16[96,1024]{1,0:T(8,128)(2,1)S(1)}, u32[]{:S(2)}, u32[]{:S(2)}) collective-permute-start(bf16[96,1024]{1,0:T(8,128)(2,1)S(1)} %get-tuple-element.48), channel_id=1, source_target_pairs={{0,3},{1,0},{2,1},{3,2},{4,7},{5,4},{6,5},{7,6},{8,11},{9,8},{10,9... | collective-permute-start | bytes 589832 | tf_op jit(solution)/shard_map/ppermute | solution.py:38
  90.4 11.0 %collective-permute-start.16 = (f32[2,128,384]{2,1,0:T(8,128)S(1)}, f32[2,128,384]{2,1,0:T(8,128)S(1)}, u32[]{:S(2)}, u32[]{:S(2)}) collective-permute-start(f32[2,128,384]{2,1,0:T(8,128)S(1)} %select_bitcast_fusion.4), channel_id=1, source_target_pairs={{0,8},{4,12},{8,0},{12,4},{16,24},{20,28},{24,16},{28,20},{1,9},{5... | collective-permute-start | bytes 1179656 | tf_op jit(solution)/shard_map/ppermute | solution.py:66
  101.5 6.0 %collective-permute-start.17 = (f32[1,128,384]{2,1,0:T(8,128)S(1)}, f32[1,128,384]{2,1,0:T(8,128)S(1)}, u32[]{:S(2)}, u32[]{:S(2)}) collective-permute-start(f32[1,128,384]{2,1,0:T(8,128)S(1)} %select_bitcast_fusion.7), channel_id=1, source_target_pairs={{0,16},{4,20},{8,24},{12,28},{16,0},{20,4},{24,8},{28,12},{1,17},{... | collective-permute-start | bytes 589832 | tf_op jit(solution)/shard_map/ppermute | solution.py:66

commit v6 on v4

--- a/solution.py
+++ b/solution.py
@@ -118,8 +118,10 @@
     gate_full = full[:, :, :ff_width]
     up_full = full[:, :, ff_width : 2 * ff_width]
     down_full = full[:, :, 2 * ff_width :]
-    recv_rows = shift_send([send_rows[s] for s in range(groups)], groups, 1)
-    recv_grads = shift_send([send_grads[s] for s in range(groups)], groups, 1)
+    both = jnp.stack([send_rows, send_grads], axis=1)
+    recv_both = shift_send([both[s] for s in range(groups)], groups, 1)
+    recv_rows = [b[0] for b in recv_both]
+    recv_grads = [b[1] for b in recv_both]
     gate_w = gate_full[0]
     up_w = up_full[0]
     down_w = down_full[0]

time: 89 us -> 116 us (1.30)
  the two profiles are of different devices: /device:TPU:0 before, /device:TPU:24 now
where the time goes in v6:
time: 116 us; the launch traced here: 115 us
  waiting for transfers between devices  61.3 us (53%)
  starting transfers between devices  31.9 us (28%)
  local copies, waits for them, and re-layouts  8.7 us (7%)
  matrix products  7.7 us (7%)
  other arithmetic  4.56 us (4%)
    ppermute x9, waiting for transfers between devices, shift_send(): got.append(lax.ppermute(blocks[step], 'expert', pairs))  36.8 us
    ppermute x9, starting transfers between devices, shift_send(): got.append(lax.ppermute(blocks[step], 'expert', pairs))  25.6 us
    ppermute x3, waiting for transfers between devices, all_gather_dp(): recv = lax.ppermute(work, 'dp', [(i, i ^ bit) for i in range(n_dp)])  16.4 us
    ppermute x3, waiting for transfers between devices, reduce_scatter_dp(): work = keep + lax.ppermute(give, 'dp', pairs)  8.09 us
    unnamed x12, local copies, waits for them, and re-layouts  4.19 us
    ppermute x3, starting transfers between devices, all_gather_dp(): recv = lax.ppermute(work, 'dp', [(i, i ^ bit) for i in range(n_dp)])  3.21 us
    ppermute x3, starting transfers between devices, reduce_scatter_dp(): work = keep + lax.ppermute(give, 'dp', pairs)  3.12 us
  transfers between devices with their start and end apart: 15, of which 7 were waited for; matrix products, arithmetic and copies ran while one was open for 10% of the time, Pallas kernels for 0%

profile of v6, /device:TPU:24, one launch (start us, length us, event | category | flops | bytes accessed | tf_op | source)
XLA Modules:
  0.0 115.2 jit_solution(9177368695946358809)
XLA Ops:
  0.6 0.9 constant_dynamic-update-slice_fusion.2
  1.6 0.9 constant_dynamic-update-slice_fusion.1
  2.5 0.9 constant_dynamic-update-slice_fusion
  3.4 1.6 %collective-permute-start.3 = (bf16[1,128,1152]{2,1,0:T(8,128)(2,1)S(1)}, bf16[1,128,1152]{2,1,0:T(8,128)(2,1)S(1)}, u32[]{:S(2)}, u32[]{:S(2)}) collective-permute-start(bf16[1,128,1152]{2,1,0:T(8,128)(2,1)S(1)} %constant_dynamic-update-slice_fusion), channel_id=1, source_target_pairs={{0,16},{4,20},{8,24},{12,28},{16,0},{20,4},{24,8},{28,12},{1,17},{... | collective-permute-start | bytes 884744 | tf_op jit(solution)/shard_map/ppermute | solution.py:47
  5.0 0.8 copy.22
  6.0 0.2 fusion.2
  6.5 0.8 copy.24
  7.4 0.1 fusion.23
  7.6 4.6 %collective-permute-done.3 = bf16[1,128,1152]{2,1,0:T(8,128)(2,1)S(1)} collective-permute-done((bf16[1,128,1152]{2,1,0:T(8,128)(2,1)S(1)}, bf16[1,128,1152]{2,1,0:T(8,128)(2,1)S(1)}, u32[]{:S(2)}, u32[]{:S(2)}) %collective-permute-start.3) | collective-permute-done | bytes 294944 | tf_op jit(solution)/shard_map/ppermute | solution.py:47
  12.4 1.6 %collective-permute-start.4 = (bf16[2,128,1152]{2,1,0:T(8,128)(2,1)S(1)}, bf16[2,128,1152]{2,1,0:T(8,128)(2,1)S(1)}, u32[]{:S(2)}, u32[]{:S(2)}) collective-permute-start(bf16[2,128,1152]{2,1,0:T(8,128)(2,1)S(1)} %maximum_bitcast_fusion), channel_id=1, source_target_pairs={{0,8},{4,12},{8,0},{12,4},{16,24},{20,28},{24,16},{28,20},{1,9},{5... | collective-permute-start | bytes 1769480 | tf_op jit(solution)/shard_map/ppermute | solution.py:47
  13.9 0.1 select_reduce_fusion
  14.1 0.4 convolution_convert_fusion
  14.5 0.4 multiply_convert_fusion
  14.9 11.7 %collective-permute-done.4 = bf16[2,128,1152]{2,1,0:T(8,128)(2,1)S(1)} collective-permute-done((bf16[2,128,1152]{2,1,0:T(8,128)(2,1)S(1)}, bf16[2,128,1152]{2,1,0:T(8,128)(2,1)S(1)}, u32[]{:S(2)}, u32[]{:S(2)}) %collective-permute-start.4) | collective-permute-done | bytes 589856 | tf_op jit(solution)/shard_map/ppermute | solution.py:47
  27.0 1.1 maximum_bitcast_fusion.2
  28.1 0.4 collective-permute-start.2
  28.5 0.4 collective-permute-start.1
  28.9 3.0 %collective-permute-start = (bf16[2,96,1024]{2,1,0:T(8,128)(2,1)}, bf16[2,96,1024]{2,1,0:T(8,128)(2,1)S(1)}, u32[]{:S(2)}, u32[]{:S(2)}) collective-permute-start(bf16[2,96,1024]{2,1,0:T(8,128)(2,1)} %get-tuple-element.41), channel_id=1, source_target_pairs={{0,1},{1,2},{2,3},{3,0},{4,5},{5,6},{6,7},{7,4},{8,9},{9,10},{10,1... | collective-permute-start | bytes 1179656 | tf_op jit(solution)/shard_map/ppermute | solution.py:38
  31.9 0.7 slice.147
  32.8 9.5 %collective-permute-done.2 = bf16[2,96,1024]{2,1,0:T(8,128)(2,1)} collective-permute-done((bf16[2,96,1024]{2,1,0:T(8,128)(2,1)}, bf16[2,96,1024]{2,1,0:T(8,128)(2,1)}, u32[]{:S(2)}, u32[]{:S(2)}) %collective-permute-start.2) | collective-permute-done | bytes 393248 | tf_op jit(solution)/shard_map/ppermute | solution.py:38
  42.3 1.0 slice_bitcast_fusion.9
  43.4 15.2 %collective-permute-done.1 = bf16[2,96,1024]{2,1,0:T(8,128)(2,1)} collective-permute-done((bf16[2,96,1024]{2,1,0:T(8,128)(2,1)}, bf16[2,96,1024]{2,1,0:T(8,128)(2,1)}, u32[]{:S(2)}, u32[]{:S(2)}) %collective-permute-start.1) | collective-permute-done | bytes 393248 | tf_op jit(solution)/shard_map/ppermute | solution.py:38
  58.6 1.0 slice_bitcast_fusion.10
  59.7 1.5 %select_bitcast_fusion.1 = (bf16[4,1,128,1152]{3,2,0,1:T(8,128)(2,1)S(1)}, bf16[4,1,128,1152]{3,2,0,1:T(8,128)(2,1)S(1)}) fusion(bf16[4,128,1152]{2,1,0:T(8,128)(2,1)} %collective-permute-done.5, pred[]{:T(512)S(6)} %eq.61, bf16[2,2,128,1152]{3,2,1,0:T(8,128)(2,1)S(1)} %pad_maximum_fusion.1), kind=kLoop, calls=%fused_computation.12 | loop fusion | flops 1179648 | bytes 4718593 | tf_op jit(solution)/shard_map/stack | solution.py:51
  61.2 0.2 pad_maximum_fusion
  61.5 0.2 copy.27
  61.7 0.7 copy-done.2
  62.4 0.6 fusion.14
  62.9 0.6 multiply_convert_fusion.3
  63.5 0.6 convolution_convert_fusion.1
  64.2 0.6 fusion.16
  64.7 0.7 fusion.25
  65.5 7.9 %collective-permute-start.8 = (bf16[96,1024]{1,0:T(8,128)(2,1)S(1)}, bf16[96,1024]{1,0:T(8,128)(2,1)S(1)}, u32[]{:S(2)}, u32[]{:S(2)}) collective-permute-start(bf16[96,1024]{1,0:T(8,128)(2,1)S(1)} %get-tuple-element.51), channel_id=1, source_target_pairs={{0,1},{1,2},{2,3},{3,0},{4,5},{5,6},{6,7},{7,4},{8,9},{9,10},{10,1... | collective-permute-start | bytes 589832 | tf_op jit(solution)/shard_map/ppermute | solution.py:38
  73.3 0.7 collective-permute-start.7
  74.2 0.7 fusion.13
  74.9 0.6 add_convert_fusion
  75.6 3.9 %collective-permute-start.11 = (bf16[96,1024]{1,0:T(8,128)(2,1)S(1)}, bf16[96,1024]{1,0:T(8,128)(2,1)S(1)}, u32[]{:S(2)}, u32[]{:S(2)}) collective-permute-start(bf16[96,1024]{1,0:T(8,128)(2,1)S(1)} %get-tuple-element.47), channel_id=1, source_target_pairs={{0,1},{1,2},{2,3},{3,0},{4,5},{5,6},{6,7},{7,4},{8,9},{9,10},{10,1... | collective-permute-start | bytes 589832 | tf_op jit(solution)/shard_map/ppermute | solution.py:38
  79.5 0.4 collective-permute-start.10
  80.0 8.9 %collective-permute-start.9 = (bf16[96,1024]{1,0:T(8,128)(2,1)S(1)}, bf16[96,1024]{1,0:T(8,128)(2,1)S(1)}, u32[]{:S(2)}, u32[]{:S(2)}) collective-permute-start(bf16[96,1024]{1,0:T(8,128)(2,1)S(1)} %get-tuple-element.49), channel_id=1, source_target_pairs={{0,3},{1,0},{2,1},{3,2},{4,7},{5,4},{6,5},{7,6},{8,11},{9,8},{10,9... | collective-permute-start | bytes 589832 | tf_op jit(solution)/shard_map/ppermute | solution.py:38
  88.9 12.1 %collective-permute-done.7 = bf16[96,1024]{1,0:T(8,128)(2,1)S(1)} collective-permute-done((bf16[96,1024]{1,0:T(8,128)(2,1)S(1)}, bf16[96,1024]{1,0:T(8,128)(2,1)S(1)}, u32[]{:S(2)}, u32[]{:S(2)}) %collective-permute-start.7) | collective-permute-done | bytes 196640 | tf_op jit(solution)/shard_map/ppermute | solution.py:38
  100.9 1.5 %collective-permute-start.13 = (f32[2,128,384]{2,1,0:T(8,128)S(1)}, f32[2,128,384]{2,1,0:T(8,128)S(1)}, u32[]{:S(2)}, u32[]{:S(2)}) collective-permute-start(f32[2,128,384]{2,1,0:T(8,128)S(1)} %select_bitcast_fusion.4), channel_id=1, source_target_pairs={{0,8},{4,12},{8,0},{12,4},{16,24},{20,28},{24,16},{28,20},{1,9},{5... | collective-permute-start | bytes 1179656 | tf_op jit(solution)/shard_map/ppermute | solution.py:66
  102.4 0.3 convolution_multiply_fusion
  102.8 1.0 fusion.1
  103.8 5.0 %collective-permute-done.13 = f32[2,128,384]{2,1,0:T(8,128)S(1)} collective-permute-done((f32[2,128,384]{2,1,0:T(8,128)S(1)}, f32[2,128,384]{2,1,0:T(8,128)S(1)}, u32[]{:S(2)}, u32[]{:S(2)}) %collective-permute-start.13) | collective-permute-done | bytes 393248 | tf_op jit(solution)/shard_map/ppermute | solution.py:66
  108.8 1.6 %collective-permute-start.14 = (f32[1,128,384]{2,1,0:T(8,128)S(1)}, f32[1,128,384]{2,1,0:T(8,128)S(1)}, u32[]{:S(2)}, u32[]{:S(2)}) collective-permute-start(f32[1,128,384]{2,1,0:T(8,128)S(1)} %select_bitcast_fusion.7), channel_id=1, source_target_pairs={{0,16},{4,20},{8,24},{12,28},{16,0},{20,4},{24,8},{28,12},{1,17},{... | collective-permute-start | bytes 589832 | tf_op jit(solution)/shard_map/ppermute | solution.py:66
  110.4 1.0 convolution_convert_fusion.2
  111.4 3.1 %collective-permute-done.14 = f32[1,128,384]{2,1,0:T(8,128)S(1)} collective-permute-done((f32[1,128,384]{2,1,0:T(8,128)S(1)}, f32[1,128,384]{2,1,0:T(8,128)S(1)}, u32[]{:S(2)}, u32[]{:S(2)}) %collective-permute-start.14) | collective-permute-done | bytes 196640 | tf_op jit(solution)/shard_map/ppermute | solution.py:66
  114.5 0.7 fusion.24
  (42 shorter events, 1.6 us)
Async XLA Ops:
  0.6 13.4 %copy-start = (bf16[128,1024]{1,0:T(8,128)(2,1)S(1)}, bf16[128,1024]{1,0:T(8,128)(2,1)}, u32[]{:S(2)}) copy-start(bf16[128,1024]{1,0:T(8,128)(2,1)} %param.13) | copy-start | bytes 786436
  3.4 8.8 %collective-permute-start.3 = (bf16[1,128,1152]{2,1,0:T(8,128)(2,1)S(1)}, bf16[1,128,1152]{2,1,0:T(8,128)(2,1)S(1)}, u32[]{:S(2)}, u32[]{:S(2)}) collective-permute-start(bf16[1,128,1152]{2,1,0:T(8,128)(2,1)S(1)} %constant_dynamic-update-slice_fusion), channel_id=1, source_target_pairs={{0,16},{4,20},{8,24},{12,28},{16,0},{20,4},{24,8},{28,12},{1,17},{... | collective-permute-start | bytes 884744 | tf_op jit(solution)/shard_map/ppermute | solution.py:47
  7.6 6.9 %copy-start.1 = (bf16[128,1024]{1,0:T(8,128)(2,1)S(1)}, bf16[128,1024]{1,0:T(8,128)(2,1)}, u32[]{:S(2)}) copy-start(bf16[128,1024]{1,0:T(8,128)(2,1)} %param.19) | copy-start | bytes 786436
  12.4 14.3 %collective-permute-start.4 = (bf16[2,128,1152]{2,1,0:T(8,128)(2,1)S(1)}, bf16[2,128,1152]{2,1,0:T(8,128)(2,1)S(1)}, u32[]{:S(2)}, u32[]{:S(2)}) collective-permute-start(bf16[2,128,1152]{2,1,0:T(8,128)(2,1)S(1)} %maximum_bitcast_fusion), channel_id=1, source_target_pairs={{0,8},{4,12},{8,0},{12,4},{16,24},{20,28},{24,16},{28,20},{1,9},{5... | collective-permute-start | bytes 1769480 | tf_op jit(solution)/shard_map/ppermute | solution.py:47
  26.9 5.0 %copy-start.3 = (f32[128,2]{0,1:T(2,128)S(1)}, f32[128,2]{0,1:T(2,128)}, u32[]{:S(2)}) copy-start(f32[128,2]{0,1:T(2,128)} %param.15) | copy-start | bytes 3076
  26.9 32.8 %collective-permute-start.5 = (bf16[4,128,1152]{2,1,0:T(8,128)(2,1)S(1)}, bf16[4,128,1152]{2,1,0:T(8,128)(2,1)}, u32[]{:S(2)}, u32[]{:S(2)}) collective-permute-start(bf16[4,128,1152]{2,1,0:T(8,128)(2,1)S(1)} %bitcast.118), channel_id=1, source_target_pairs={{0,4},{4,0},{8,12},{12,8},{16,20},{20,16},{24,28},{28,24},{1,5},{5... | collective-permute-start | bytes 3538952 | tf_op jit(solution)/shard_map/ppermute | solution.py:47
  28.1 14.2 %collective-permute-start.2 = (bf16[2,96,1024]{2,1,0:T(8,128)(2,1)}, bf16[2,96,1024]{2,1,0:T(8,128)(2,1)}, u32[]{:S(2)}, u32[]{:S(2)}) collective-permute-start(bf16[2,96,1024]{2,1,0:T(8,128)(2,1)} %get-tuple-element.43), channel_id=1, source_target_pairs={{0,3},{1,0},{2,1},{3,2},{4,7},{5,4},{6,5},{7,6},{8,11},{9,8},{10,9... | collective-permute-start | bytes 1179656 | tf_op jit(solution)/shard_map/ppermute | solution.py:38
  28.5 30.1 %collective-permute-start.1 = (bf16[2,96,1024]{2,1,0:T(8,128)(2,1)}, bf16[2,96,1024]{2,1,0:T(8,128)(2,1)}, u32[]{:S(2)}, u32[]{:S(2)}) collective-permute-start(bf16[2,96,1024]{2,1,0:T(8,128)(2,1)} %get-tuple-element.42), channel_id=1, source_target_pairs={{0,2},{1,3},{2,0},{3,1},{4,6},{5,7},{6,4},{7,5},{8,10},{9,11},{10,... | collective-permute-start | bytes 1179656 | tf_op jit(solution)/shard_map/ppermute | solution.py:38
  28.9 30.7 %collective-permute-start = (bf16[2,96,1024]{2,1,0:T(8,128)(2,1)}, bf16[2,96,1024]{2,1,0:T(8,128)(2,1)S(1)}, u32[]{:S(2)}, u32[]{:S(2)}) collective-permute-start(bf16[2,96,1024]{2,1,0:T(8,128)(2,1)} %get-tuple-element.41), channel_id=1, source_target_pairs={{0,1},{1,2},{2,3},{3,0},{4,5},{5,6},{6,7},{7,4},{8,9},{9,10},{10,1... | collective-permute-start | bytes 1179656 | tf_op jit(solution)/shard_map/ppermute | solution.py:38
  61.4 0.9 copy-start.2
  65.5 14.5 %collective-permute-start.8 = (bf16[96,1024]{1,0:T(8,128)(2,1)S(1)}, bf16[96,1024]{1,0:T(8,128)(2,1)S(1)}, u32[]{:S(2)}, u32[]{:S(2)}) collective-permute-start(bf16[96,1024]{1,0:T(8,128)(2,1)S(1)} %get-tuple-element.51), channel_id=1, source_target_pairs={{0,1},{1,2},{2,3},{3,0},{4,5},{5,6},{6,7},{7,4},{8,9},{9,10},{10,1... | collective-permute-start | bytes 589832 | tf_op jit(solution)/shard_map/ppermute | solution.py:38
  73.3 27.6 %collective-permute-start.7 = (bf16[96,1024]{1,0:T(8,128)(2,1)S(1)}, bf16[96,1024]{1,0:T(8,128)(2,1)S(1)}, u32[]{:S(2)}, u32[]{:S(2)}) collective-permute-start(bf16[96,1024]{1,0:T(8,128)(2,1)S(1)} %get-tuple-element.52), channel_id=1, source_target_pairs={{0,2},{1,3},{2,0},{3,1},{4,6},{5,7},{6,4},{7,5},{8,10},{9,11},{10,... | collective-permute-start | bytes 589832 | tf_op jit(solution)/shard_map/ppermute | solution.py:38
  74.1 28.3 %collective-permute-start.6 = (bf16[96,1024]{1,0:T(8,128)(2,1)S(1)}, bf16[96,1024]{1,0:T(8,128)(2,1)S(1)}, u32[]{:S(2)}, u32[]{:S(2)}) collective-permute-start(bf16[96,1024]{1,0:T(8,128)(2,1)S(1)} %get-tuple-element.53), channel_id=1, source_target_pairs={{0,3},{1,0},{2,1},{3,2},{4,7},{5,4},{6,5},{7,6},{8,11},{9,8},{10,9... | collective-permute-start | bytes 589832 | tf_op jit(solution)/shard_map/ppermute | solution.py:38
  74.2 5.3 %collective-permute-start.12 = (f32[4,128,384]{2,1,0:T(8,128)S(1)}, f32[4,128,384]{2,1,0:T(8,128)S(1)}, u32[]{:S(2)}, u32[]{:S(2)}) collective-permute-start(f32[4,128,384]{2,1,0:T(8,128)S(1)} %fusion.10), channel_id=1, source_target_pairs={{0,4},{4,0},{8,12},{12,8},{16,20},{20,16},{24,28},{28,24},{1,5},{5... | collective-permute-start | bytes 2359304 | tf_op jit(solution)/shard_map/ppermute | solution.py:66
  75.6 34.8 %collective-permute-start.11 = (bf16[96,1024]{1,0:T(8,128)(2,1)S(1)}, bf16[96,1024]{1,0:T(8,128)(2,1)S(1)}, u32[]{:S(2)}, u32[]{:S(2)}) collective-permute-start(bf16[96,1024]{1,0:T(8,128)(2,1)S(1)} %get-tuple-element.47), channel_id=1, source_target_pairs={{0,1},{1,2},{2,3},{3,0},{4,5},{5,6},{6,7},{7,4},{8,9},{9,10},{10,1... | collective-permute-start | bytes 589832 | tf_op jit(solution)/shard_map/ppermute | solution.py:38
  79.5 30.9 %collective-permute-start.10 = (bf16[96,1024]{1,0:T(8,128)(2,1)S(1)}, bf16[96,1024]{1,0:T(8,128)(2,1)S(1)}, u32[]{:S(2)}, u32[]{:S(2)}) collective-permute-start(bf16[96,1024]{1,0:T(8,128)(2,1)S(1)} %get-tuple-element.48), channel_id=1, source_target_pairs={{0,2},{1,3},{2,0},{3,1},{4,6},{5,7},{6,4},{7,5},{8,10},{9,11},{10,... | collective-permute-start | bytes 589832 | tf_op jit(solution)/shard_map/ppermute | solution.py:38
  80.0 30.4 %collective-permute-start.9 = (bf16[96,1024]{1,0:T(8,128)(2,1)S(1)}, bf16[96,1024]{1,0:T(8,128)(2,1)S(1)}, u32[]{:S(2)}, u32[]{:S(2)}) collective-permute-start(bf16[96,1024]{1,0:T(8,128)(2,1)S(1)} %get-tuple-element.49), channel_id=1, source_target_pairs={{0,3},{1,0},{2,1},{3,2},{4,7},{5,4},{6,5},{7,6},{8,11},{9,8},{10,9... | collective-permute-start | bytes 589832 | tf_op jit(solution)/shard_map/ppermute | solution.py:38
  100.9 7.8 %collective-permute-start.13 = (f32[2,128,384]{2,1,0:T(8,128)S(1)}, f32[2,128,384]{2,1,0:T(8,128)S(1)}, u32[]{:S(2)}, u32[]{:S(2)}) collective-permute-start(f32[2,128,384]{2,1,0:T(8,128)S(1)} %select_bitcast_fusion.4), channel_id=1, source_target_pairs={{0,8},{4,12},{8,0},{12,4},{16,24},{20,28},{24,16},{28,20},{1,9},{5... | collective-permute-start | bytes 1179656 | tf_op jit(solution)/shard_map/ppermute | solution.py:66
  108.8 5.7 %collective-permute-start.14 = (f32[1,128,384]{2,1,0:T(8,128)S(1)}, f32[1,128,384]{2,1,0:T(8,128)S(1)}, u32[]{:S(2)}, u32[]{:S(2)}) collective-permute-start(f32[1,128,384]{2,1,0:T(8,128)S(1)} %select_bitcast_fusion.7), channel_id=1, source_target_pairs={{0,16},{4,20},{8,24},{12,28},{16,0},{20,4},{24,8},{28,12},{1,17},{... | collective-permute-start | bytes 589832 | tf_op jit(solution)/shard_map/ppermute | solution.py:66

commit v7 on v4

--- a/solution.py
+++ b/solution.py
@@ -39,18 +39,32 @@
     return got
 
 
-def all_gather_dp(block, n_dp):
+def gather_bits(block, bits, n_dp):
     me = lax.axis_index("dp")
-    work = block[None]
-    bit = n_dp // 2
-    while bit >= 1:
+    work = block
+    for bit in bits:
         recv = lax.ppermute(work, "dp", [(i, i ^ bit) for i in range(n_dp)])
         upper = (me // bit) % 2 == 1
-        low = jnp.where(upper, recv, work)
-        high = jnp.where(upper, work, recv)
-        work = jnp.stack([low, high], axis=1).reshape((2 * work.shape[0],) + work.shape[1:])
-        bit //= 2
-    return work
+        work = jnp.stack([jnp.where(upper, recv, work), jnp.where(upper, work, recv)], axis=0)
+    axes = list(reversed(bits))
+    perm = sorted(range(len(bits)), key=lambda a: -axes[a])
+    work = jnp.transpose(work, perm + list(range(len(bits), work.ndim)))
+    return work.reshape((2 ** len(bits),) + block.shape)
+
+
+def all_gather_dp(block, n_dp):
+    bits = []
+    bit = 1
+    while bit < n_dp:
+        bits.append(bit)
+        bit *= 2
+    half = block.shape[-1] // 2
+    near = gather_bits(block, bits[:1], n_dp)
+    rest = bits[1:]
+    left = gather_bits(near[..., :half], rest, n_dp)
+    right = gather_bits(near[..., half:], rest[::-1], n_dp)
+    out_shape = (n_dp,) + block.shape[:-1] + (half,)
+    return jnp.concatenate([left.reshape(out_shape), right.reshape(out_shape)], axis=-1)
 
 
 def reduce_scatter_dp(pieces, n_dp):

time: 89 us -> 93 us (1.045)
  starting transfers between devices: 31.6 us -> 28.3 us
  local copies, waits for them, and re-layouts: 8.04 us -> 11.3 us
  other arithmetic: 3.01 us -> 4.81 us
  waiting for transfers between devices: 33.2 us -> 34.9 us
    ppermute x12, starting transfers between devices: 25 us -> 19.2 us  [shift_send(): got.append(lax.ppermute(blocks[step], 'expert', pairs))]
    ppermute x3 -> x5, waiting for transfers between devices: 12.2 us -> 14.9 us  [gather_bits(): recv = lax.ppermute(work, 'dp', [(i, i ^ bit) for i in range(n_dp)])]
    concatenate x1 -> x2, local copies, waits for them, and re-layouts: 0.91 us -> 2.54 us  [all_gather_dp(): jnp.concatenate([left.reshape(out_shape), right.reshape(out_shape)], axis...]
    ppermute x3 -> x5, starting transfers between devices: 4.91 us -> 6.28 us  [gather_bits(): recv = lax.ppermute(work, 'dp', [(i, i ^ bit) for i in range(n_dp)])]
    ppermute x3, waiting for transfers between devices: 12.4 us -> 11.1 us  [reduce_scatter_dp(): work = keep + lax.ppermute(give, 'dp', pairs)]
    transpose x0 -> x1, local copies, waits for them, and re-layouts: none -> 1.21 us  [gather_bits(): work = jnp.transpose(work, perm + list(range(len(bits), work.ndim)))]
    ppermute x3, starting transfers between devices: 1.65 us -> 2.86 us  [reduce_scatter_dp(): work = keep + lax.ppermute(give, 'dp', pairs)]
    transpose x0 -> x1, other arithmetic: none -> 1.17 us  [gather_bits(): work = jnp.transpose(work, perm + list(range(len(bits), work.ndim)))]
  transfers between devices with their start and end apart: 18 -> 20, of which waited for: 5 -> 7; matrix products, arithmetic and copies ran while one was open for 20% -> 26% of each run, Pallas kernels for 0% -> 0%
where the time goes in v7:
time: 93 us; the launch traced here: 92.6 us
  waiting for transfers between devices  34.9 us (38%)
  starting transfers between devices  28.3 us (30%)
  matrix products  12.1 us (13%)
  local copies, waits for them, and re-layouts  11.3 us (12%)
  other arithmetic  4.81 us (5%)
  between operations  1.16 us (1%)
    ppermute x12, starting transfers between devices, shift_send(): got.append(lax.ppermute(blocks[step], 'expert', pairs))  19.2 us
    ppermute x5, waiting for transfers between devices, gather_bits(): recv = lax.ppermute(work, 'dp', [(i, i ^ bit) for i in range(n_dp)])  14.9 us
    ppermute x3, waiting for transfers between devices, reduce_scatter_dp(): work = keep + lax.ppermute(give, 'dp', pairs)  11.1 us
    ppermute x12, waiting for transfers between devices, shift_send(): got.append(lax.ppermute(blocks[step], 'expert', pairs))  8.91 us
    ppermute x5, starting transfers between devices, gather_bits(): recv = lax.ppermute(work, 'dp', [(i, i ^ bit) for i in range(n_dp)])  6.28 us
    unnamed x19, local copies, waits for them, and re-layouts  4 us
    ppermute x3, starting transfers between devices, reduce_scatter_dp(): work = keep + lax.ppermute(give, 'dp', pairs)  2.86 us
    concatenate x2, local copies, waits for them, and re-layouts, all_gather_dp(): jnp.concatenate([left.reshape(out_shape), right.reshape(out_shape)], axis...  2.54 us
  transfers between devices with their start and end apart: 20, of which 7 were waited for; matrix products, arithmetic and copies ran while one was open for 26% of the time, Pallas kernels for 0%

profile of v7, /device:TPU:0, one launch (start us, length us, event | category | flops | bytes accessed | tf_op | source)
XLA Modules:
  0.0 92.6 jit_solution(18234640632219951220)
XLA Ops:
  0.6 1.1 %copy.35 = bf16[1,128,384]{1,2,0:T(8,128)(2,1)S(1)} copy(bf16[1,128,384]{2,1,0:T(8,128)(2,1)} %param.18) | data formatting | bytes 196608 | tf_op args[5]
  1.7 1.0 %copy.34 = bf16[1,128,384]{1,2,0:T(8,128)(2,1)S(1)} copy(bf16[1,128,384]{2,1,0:T(8,128)(2,1)} %param.17) | data formatting | bytes 196608 | tf_op args[4]
  2.7 1.0 %copy.33 = bf16[1,128,384]{1,2,0:T(8,128)(2,1)S(1)} copy(bf16[1,128,384]{2,1,0:T(8,128)(2,1)} %param.16) | data formatting | bytes 196608 | tf_op args[3]
  3.8 0.6 collective-permute-start.3
  4.3 0.8 copy.31
  5.9 0.4 convolution_convert_fusion
  6.3 0.8 fusion.48
  7.2 4.6 %collective-permute-start.2 = (bf16[96,1024]{1,0:T(8,128)(2,1)}, bf16[96,1024]{1,0:T(8,128)(2,1)}, u32[]{:S(2)}, u32[]{:S(2)}) collective-permute-start(bf16[96,1024]{1,0:T(8,128)(2,1)} %get-tuple-element.56), channel_id=1, source_target_pairs={{0,3},{1,0},{2,1},{3,2},{4,7},{5,4},{6,5},{7,6},{8,11},{9,8},{10,9... | collective-permute-start | bytes 589832 | tf_op jit(solution)/shard_map/ppermute | solution.py:38
  11.8 1.0 %collective-permute-start = (bf16[96,1024]{1,0:T(8,128)(2,1)}, bf16[96,1024]{1,0:T(8,128)(2,1)}, u32[]{:S(2)}, u32[]{:S(2)}) collective-permute-start(bf16[96,1024]{1,0:T(8,128)(2,1)} %get-tuple-element.58), channel_id=1, source_target_pairs={{0,1},{1,2},{2,3},{3,0},{4,5},{5,6},{6,7},{7,4},{8,9},{9,10},{10,1... | collective-permute-start | bytes 589832 | tf_op jit(solution)/shard_map/ppermute | solution.py:38
  13.3 1.6 %collective-permute-start.4 = (bf16[2,128,576]{1,2,0:T(8,128)(2,1)S(1)}, bf16[2,128,576]{1,2,0:T(8,128)(2,1)S(1)}, u32[]{:S(2)}, u32[]{:S(2)}) collective-permute-start(bf16[2,128,576]{1,2,0:T(8,128)(2,1)S(1)} %get-tuple-element.61), channel_id=1, source_target_pairs={{0,8},{4,12},{8,0},{12,4},{16,24},{20,28},{24,16},{28,20},{1,9},{5... | collective-permute-start | bytes 884744 | tf_op jit(solution)/shard_map/ppermute | solution.py:46
  15.1 0.4 multiply_convert_fusion
  15.5 1.6 %collective-permute-start.6 = (bf16[2,128,576]{1,2,0:T(8,128)(2,1)S(1)}, bf16[2,128,576]{1,2,0:T(8,128)(2,1)S(1)}, u32[]{:S(2)}, u32[]{:S(2)}) collective-permute-start(bf16[2,128,576]{1,2,0:T(8,128)(2,1)S(1)} %get-tuple-element.62), channel_id=1, source_target_pairs={{0,16},{4,20},{8,24},{12,28},{16,0},{20,4},{24,8},{28,12},{1,17},{... | collective-permute-start | bytes 884744 | tf_op jit(solution)/shard_map/ppermute | solution.py:46
  17.1 4.8 %collective-permute-done.4 = bf16[2,128,576]{1,2,0:T(8,128)(2,1)S(1)} collective-permute-done((bf16[2,128,576]{1,2,0:T(8,128)(2,1)S(1)}, bf16[2,128,576]{1,2,0:T(8,128)(2,1)S(1)}, u32[]{:S(2)}, u32[]{:S(2)}) %collective-permute-start.4) | collective-permute-done | bytes 294944 | tf_op jit(solution)/shard_map/ppermute | solution.py:46
  22.0 1.6 %collective-permute-start.5 = (bf16[2,2,128,576]{2,3,1,0:T(8,128)(2,1)S(1)}, bf16[2,2,128,576]{2,3,1,0:T(8,128)(2,1)S(1)}, u32[]{:S(2)}, u32[]{:S(2)}) collective-permute-start(bf16[2,2,128,576]{2,3,1,0:T(8,128)(2,1)S(1)} %pad_maximum_fusion.5), channel_id=1, source_target_pairs={{0,16},{4,20},{8,24},{12,28},{16,0},{20,4},{24,8},{28,12},{1,17},{... | collective-permute-start | bytes 1769480 | tf_op jit(solution)/shard_map/ppermute | solution.py:46
  23.6 0.6 collective-permute-done.6
  24.3 1.0 %collective-permute-start.7 = (bf16[2,2,128,576]{2,3,1,0:T(8,128)(2,1)S(1)}, bf16[2,2,128,576]{2,3,1,0:T(8,128)(2,1)S(1)}, u32[]{:S(2)}, u32[]{:S(2)}) collective-permute-start(bf16[2,2,128,576]{2,3,1,0:T(8,128)(2,1)S(1)} %pad_maximum_fusion.6), channel_id=1, source_target_pairs={{0,8},{4,12},{8,0},{12,4},{16,24},{20,28},{24,16},{28,20},{1,9},{5... | collective-permute-start | bytes 1769480 | tf_op jit(solution)/shard_map/ppermute | solution.py:46
  25.3 0.8 convert_reduce_fusion
  26.0 0.9 fusion.46
  26.9 9.6 %collective-permute-done.5 = bf16[2,2,128,576]{2,3,1,0:T(8,128)(2,1)S(1)} collective-permute-done((bf16[2,2,128,576]{2,3,1,0:T(8,128)(2,1)S(1)}, bf16[2,2,128,576]{2,3,1,0:T(8,128)(2,1)S(1)}, u32[]{:S(2)}, u32[]{:S(2)}) %collective-permute-start.5) | collective-permute-done | bytes 589856 | tf_op jit(solution)/shard_map/ppermute | solution.py:46
  36.5 3.1 %collective-permute-start.13 = (bf16[96,1024]{1,0:T(8,128)(2,1)}, bf16[96,1024]{1,0:T(8,128)(2,1)}, u32[]{:S(2)}, u32[]{:S(2)}) collective-permute-start(bf16[96,1024]{1,0:T(8,128)(2,1)} %get-tuple-element.48), channel_id=1, source_target_pairs={{0,3},{1,0},{2,1},{3,2},{4,7},{5,4},{6,5},{7,6},{8,11},{9,8},{10,9... | collective-permute-start | bytes 589832 | tf_op jit(solution)/shard_map/ppermute | solution.py:38
  39.7 0.9 collective-permute-start.12
  40.6 0.9 %select_bitcast_fusion.1 = (bf16[1,2,2,128,576]{3,4,2,1,0:T(8,128)(2,1)S(1)}, bf16[1,2,2,128,576]{3,4,2,1,0:T(8,128)(2,1)}) fusion(bf16[2,2,128,576]{2,3,1,0:T(8,128)(2,1)S(1)} %collective-permute-done.7, pred[]{:T(512)S(6)} %eq.63, bf16[1,2,128,576]{2,3,1,0:T(8,128)(2,1)S(1)} %get-tuple-element.64, bf16[1,2,128,576]{2,3,1,0:T(8,128)(2,1)S(1)} %get-tuple-element.63), kind=kLoop, calls=%fused_computation.43 | loop fusion | flops 884736 | bytes 2359297 | tf_op jit(solution)/shard_map/stack | solution.py:48
  41.6 1.2 %copy.36 = bf16[2,2,2,128,576]{3,2,1,0,4:T(2,128)(2,1)S(1)} copy(bf16[2,2,2,128,576]{3,4,2,1,0:T(8,128)(2,1)S(1)} %pad_maximum_fusion) | data formatting | bytes 2359296 | tf_op jit(solution)/shard_map/stack | solution.py:48
  42.9 0.9 concatenate.25
  43.7 1.2 %maximum_bitcast_fusion = bf16[2,2,2,128,576]{3,4,2,0,1:T(8,128)(2,1)S(1)} fusion(bf16[1,2,2,128,576]{3,4,2,1,0:T(8,128)(2,1)} %get-tuple-element.42, bf16[1,2,2,128,576]{3,4,2,1,0:T(8,128)(2,1)S(1)} %get-tuple-element.41), kind=kLoop, calls=%fused_computation.10 | loop fusion | flops 589824 | bytes 2359296 | tf_op jit(solution)/shard_map/transpose | solution.py:51
  44.9 1.2 %copy.37 = bf16[2,2,2,128,576]{3,2,1,0,4:T(2,128)(2,1)S(1)} copy(bf16[2,2,2,128,576]{3,4,2,0,1:T(8,128)(2,1)S(1)} %maximum_bitcast_fusion) | data formatting | bytes 2359296 | tf_op jit(solution)/shard_map/transpose | solution.py:51
  46.1 1.7 %concatenate.26 = bf16[1,1024,576]{1,2,0:T(8,128)(2,1)} reshape(bf16[2,2,2,128,576]{3,2,1,0,4:T(2,128)(2,1)S(1)} %copy.37) | data formatting | bytes 2359296 | tf_op jit(solution)/shard_map/concatenate | solution.py:67
  47.8 1.2 %collective-permute-start.11 = (bf16[96,1024]{1,0:T(8,128)(2,1)S(1)}, bf16[96,1024]{1,0:T(8,128)(2,1)S(1)}, u32[]{:S(2)}, u32[]{:S(2)}) collective-permute-start(bf16[96,1024]{1,0:T(8,128)(2,1)S(1)} %copy-done.4), channel_id=1, source_target_pairs={{0,1},{1,2},{2,3},{3,0},{4,5},{5,6},{6,7},{7,4},{8,9},{9,10},{10,1... | collective-permute-start | bytes 589832 | tf_op jit(solution)/shard_map/ppermute | solution.py:38
  49.1 1.8 %fusion.15 = f32[384,384]{1,0:T(8,128)S(1)} fusion(bf16[1,1024,576]{1,2,0:T(8,128)(2,1)S(1)} %concatenate.25, bf16[96,1024]{1,0:T(8,128)(2,1)} %collective-permute-done.2, bf16[96,1024]{1,0:T(8,128)(2,1)} %collective-permute-done.1, bf16[96,1024]{1,0:T(8,128)(2,1)} %collective-permute-done, bf16[96,1024]{1,0:T(8,128)(2,1)S(1)} %get-tuple-element.55), kind=kOutput, calls=%fused_computation.33 | convolution fusion | flops 305135616 | bytes 2162688 | tf_op jit(solution)/shard_map/dot_general | solution.py:11
  50.9 1.7 %multiply_convert_fusion.3 = (bf16[384,384]{1,0:T(8,128)(2,1)S(1)}, f32[384,384]{1,0:T(8,128)S(1)}) fusion(f32[384,384]{1,0:T(8,128)S(1)} %fusion.15, bf16[1,1024,576]{1,2,0:T(8,128)(2,1)S(1)} %copy-done.1, bf16[1,1024,576]{1,2,0:T(8,128)(2,1)S(1)} %concatenate.25, bf16[96,1024]{1,0:T(8,128)(2,1)} %collective-permute-done.2, ...), kind=kOutput, calls=%fused_computation.41 | convolution fusion | flops 307593216 | bytes 4620288 | tf_op jit(solution)/shard_map/dot_general | solution.py:12
  52.6 0.6 convolution_convert_fusion.1
  53.3 1.5 %collective-permute-start.10 = (bf16[96,1024]{1,0:T(8,128)(2,1)S(1)}, bf16[96,1024]{1,0:T(8,128)(2,1)S(1)}, u32[]{:S(2)}, u32[]{:S(2)}) collective-permute-start(bf16[96,1024]{1,0:T(8,128)(2,1)S(1)} %get-tuple-element.52), channel_id=1, source_target_pairs={{0,1},{1,2},{2,3},{3,0},{4,5},{5,6},{6,7},{7,4},{8,9},{9,10},{10,1... | collective-permute-start | bytes 589832 | tf_op jit(solution)/shard_map/ppermute | solution.py:38
  54.8 1.7 %collective-permute-start.9 = (bf16[96,1024]{1,0:T(8,128)(2,1)S(1)}, bf16[96,1024]{1,0:T(8,128)(2,1)S(1)}, u32[]{:S(2)}, u32[]{:S(2)}) collective-permute-start(bf16[96,1024]{1,0:T(8,128)(2,1)S(1)} %get-tuple-element.53), channel_id=1, source_target_pairs={{0,2},{1,3},{2,0},{3,1},{4,6},{5,7},{6,4},{7,5},{8,10},{9,11},{10,... | collective-permute-start | bytes 589832 | tf_op jit(solution)/shard_map/ppermute | solution.py:38
  56.5 1.2 %collective-permute-start.8 = (bf16[96,1024]{1,0:T(8,128)(2,1)S(1)}, bf16[96,1024]{1,0:T(8,128)(2,1)S(1)}, u32[]{:S(2)}, u32[]{:S(2)}) collective-permute-start(bf16[96,1024]{1,0:T(8,128)(2,1)S(1)} %get-tuple-element.54), channel_id=1, source_target_pairs={{0,3},{1,0},{2,1},{3,2},{4,7},{5,4},{6,5},{7,6},{8,11},{9,8},{10,9... | collective-permute-start | bytes 589832 | tf_op jit(solution)/shard_map/ppermute | solution.py:38
  57.7 8.3 %collective-permute-done.12 = bf16[96,1024]{1,0:T(8,128)(2,1)} collective-permute-done((bf16[96,1024]{1,0:T(8,128)(2,1)}, bf16[96,1024]{1,0:T(8,128)(2,1)}, u32[]{:S(2)}, u32[]{:S(2)}) %collective-permute-start.12) | collective-permute-done | bytes 196640 | tf_op jit(solution)/shard_map/ppermute | solution.py:38
  66.0 1.7 %fusion.25 = f32[1024,384]{1,0:T(8,128)S(1)} fusion(bf16[384,384]{1,0:T(8,128)(2,1)S(1)} %get-tuple-element.71, bf16[96,1024]{1,0:T(8,128)(2,1)} %collective-permute-done.13, bf16[96,1024]{1,0:T(8,128)(2,1)} %collective-permute-done.12, bf16[96,1024]{1,0:T(8,128)(2,1)S(1)} %collective-permute-done.11, bf16[96,1024]{1,0:T(8,128)(2,1)S(1)} %copy-done.3), kind=kOutput, calls=%fused_computation.74 | convolution fusion | flops 305135616 | bytes 2654208 | tf_op jit(solution)/shard_map/dot_general | solution.py:144
  67.9 1.6 %fusion.16 = f32[384,384]{1,0:T(8,128)S(1)} fusion(bf16[1,1024,576]{1,2,0:T(8,128)(2,1)S(1)} %copy-done.1, bf16[96,1024]{1,0:T(8,128)(2,1)} %collective-permute-done.13, bf16[96,1024]{1,0:T(8,128)(2,1)} %collective-permute-done.12, bf16[96,1024]{1,0:T(8,128)(2,1)S(1)} %collective-permute-done.11, bf16[96,1024]{1,0:T(8,128)(2,1)S(1)} %copy-done.3), kind=kOutput, calls=%fused_computation.34 | convolution fusion | flops 305135616 | bytes 2162688 | tf_op jit(solution)/shard_map/dot_general | solution.py:22
  69.5 0.7 fusion.14
  70.2 0.6 add_convert_fusion
  71.2 3.8 %collective-permute-start.14 = (bf16[96,1024]{1,0:T(8,128)(2,1)S(1)}, bf16[96,1024]{1,0:T(8,128)(2,1)S(1)}, u32[]{:S(2)}, u32[]{:S(2)}) collective-permute-start(bf16[96,1024]{1,0:T(8,128)(2,1)S(1)} %get-tuple-element.46), channel_id=1, source_target_pairs={{0,3},{1,0},{2,1},{3,2},{4,7},{5,4},{6,5},{7,6},{8,11},{9,8},{10,9... | collective-permute-start | bytes 589832 | tf_op jit(solution)/shard_map/ppermute | solution.py:38
  74.9 1.2 %collective-permute-start.18 = (f32[2,128,384]{2,1,0:T(8,128)S(1)}, f32[2,128,384]{2,1,0:T(8,128)S(1)}, u32[]{:S(2)}, u32[]{:S(2)}) collective-permute-start(f32[2,128,384]{2,1,0:T(8,128)S(1)} %select_bitcast_fusion.4), channel_id=1, source_target_pairs={{0,8},{4,12},{8,0},{12,4},{16,24},{20,28},{24,16},{28,20},{1,9},{5... | collective-permute-start | bytes 1179656 | tf_op jit(solution)/shard_map/ppermute | solution.py:80
  76.5 1.0 %fusion.1 = bf16[128,1024]{1,0:T(8,128)(2,1)} fusion(f32[128,1024]{1,0:T(8,128)S(1)} %convolution_multiply_fusion, f32[128]{0:T(128)S(1)} %get-tuple-element.67, pred[128,2,384]{2,0,1:T(32,128)(4,1)S(1)} %get-tuple-element.70, bf16[96,1024]{1,0:T(8,128)(2,1)S(1)} %collective-permute-done.10, bf16[96,1024]{1,0:T(8,128)(2,1)S(1)} %collective-permute-done.9, ...), kind=kOutput, calls=%fused_computation.7 | convolution fusion | flops 104202240 | bytes 1622528 | tf_op jit(solution)/shard_map/dot_general | solution.py:153
  77.5 8.4 %collective-permute-done.18 = f32[2,128,384]{2,1,0:T(8,128)S(1)} collective-permute-done((f32[2,128,384]{2,1,0:T(8,128)S(1)}, f32[2,128,384]{2,1,0:T(8,128)S(1)}, u32[]{:S(2)}, u32[]{:S(2)}) %collective-permute-start.18) | collective-permute-done | bytes 393248 | tf_op jit(solution)/shard_map/ppermute | solution.py:80
  86.0 1.6 %collective-permute-start.19 = (f32[1,128,384]{2,1,0:T(8,128)S(1)}, f32[1,128,384]{2,1,0:T(8,128)S(1)}, u32[]{:S(2)}, u32[]{:S(2)}) collective-permute-start(f32[1,128,384]{2,1,0:T(8,128)S(1)} %select_bitcast_fusion.11), channel_id=1, source_target_pairs={{0,16},{4,20},{8,24},{12,28},{16,0},{20,4},{24,8},{28,12},{1,17},{... | collective-permute-start | bytes 589832 | tf_op jit(solution)/shard_map/ppermute | solution.py:80
  87.5 0.6 collective-permute-done.15
  88.1 1.0 %convolution_convert_fusion.2 = bf16[128,1024]{1,0:T(8,128)(2,1)} fusion(bf16[96,1024]{1,0:T(8,128)(2,1)S(1)} %collective-permute-done.16, bf16[96,1024]{1,0:T(8,128)(2,1)S(1)} %collective-permute-done.15, bf16[96,1024]{1,0:T(8,128)(2,1)S(1)} %collective-permute-done.14, bf16[96,1024]{1,0:T(8,128)(2,1)S(1)} %get-tuple-element.43, s32[128,384]{1,0:T(8,128)S(1)} %copy-done.5), kind=kOutput, calls=%fused_computation.8 | convolution fusion | flops 103989248 | bytes 1245184 | tf_op jit(solution)/shard_map/dot_general | solution.py:159
  89.2 2.7 %collective-permute-done.19 = f32[1,128,384]{2,1,0:T(8,128)S(1)} collective-permute-done((f32[1,128,384]{2,1,0:T(8,128)S(1)}, f32[1,128,384]{2,1,0:T(8,128)S(1)}, u32[]{:S(2)}, u32[]{:S(2)}) %collective-permute-start.19) | collective-permute-done | bytes 196640 | tf_op jit(solution)/shard_map/ppermute | solution.py:80
  91.9 0.7 fusion.24
  (62 shorter events, 2.7 us)
Async XLA Ops:
  0.6 5.3 %copy-start = (bf16[128,1024]{1,0:T(8,128)(2,1)S(1)}, bf16[128,1024]{1,0:T(8,128)(2,1)}, u32[]{:S(2)}) copy-start(bf16[128,1024]{1,0:T(8,128)(2,1)} %param.13) | copy-start | bytes 786436
  3.8 9.3 %collective-permute-start.3 = (bf16[128,1152]{0,1:T(8,128)(2,1)S(1)}, bf16[128,1152]{0,1:T(8,128)(2,1)S(1)}, u32[]{:S(2)}, u32[]{:S(2)}) collective-permute-start(bf16[128,1152]{0,1:T(8,128)(2,1)S(1)} %maximum_bitcast_fusion.1), channel_id=1, source_target_pairs={{0,4},{4,0},{8,12},{12,8},{16,20},{20,16},{24,28},{28,24},{1,5},{5... | collective-permute-start | bytes 884744 | tf_op jit(solution)/shard_map/ppermute | solution.py:46
  5.5 7.3 %copy-start.6 = (f32[128,2]{0,1:T(2,128)S(1)}, f32[128,2]{0,1:T(2,128)}, u32[]{:S(2)}) copy-start(f32[128,2]{0,1:T(2,128)} %param.15) | copy-start | bytes 3076
  7.2 7.9 %copy-start.2 = (bf16[128,1024]{1,0:T(8,128)(2,1)S(1)}, bf16[128,1024]{1,0:T(8,128)(2,1)}, u32[]{:S(2)}) copy-start(bf16[128,1024]{1,0:T(8,128)(2,1)} %param.19) | copy-start | bytes 786436
  7.2 40.7 %collective-permute-start.2 = (bf16[96,1024]{1,0:T(8,128)(2,1)}, bf16[96,1024]{1,0:T(8,128)(2,1)}, u32[]{:S(2)}, u32[]{:S(2)}) collective-permute-start(bf16[96,1024]{1,0:T(8,128)(2,1)} %get-tuple-element.56), channel_id=1, source_target_pairs={{0,3},{1,0},{2,1},{3,2},{4,7},{5,4},{6,5},{7,6},{8,11},{9,8},{10,9... | collective-permute-start | bytes 589832 | tf_op jit(solution)/shard_map/ppermute | solution.py:38
  11.8 37.3 %collective-permute-start.1 = (bf16[96,1024]{1,0:T(8,128)(2,1)}, bf16[96,1024]{1,0:T(8,128)(2,1)}, u32[]{:S(2)}, u32[]{:S(2)}) collective-permute-start(bf16[96,1024]{1,0:T(8,128)(2,1)} %get-tuple-element.57), channel_id=1, source_target_pairs={{0,2},{1,3},{2,0},{3,1},{4,6},{5,7},{6,4},{7,5},{8,10},{9,11},{10,... | collective-permute-start | bytes 589832 | tf_op jit(solution)/shard_map/ppermute | solution.py:38
  11.8 37.3 %collective-permute-start = (bf16[96,1024]{1,0:T(8,128)(2,1)}, bf16[96,1024]{1,0:T(8,128)(2,1)}, u32[]{:S(2)}, u32[]{:S(2)}) collective-permute-start(bf16[96,1024]{1,0:T(8,128)(2,1)} %get-tuple-element.58), channel_id=1, source_target_pairs={{0,1},{1,2},{2,3},{3,0},{4,5},{5,6},{6,7},{7,4},{8,9},{9,10},{10,1... | collective-permute-start | bytes 589832 | tf_op jit(solution)/shard_map/ppermute | solution.py:38
  13.3 8.6 %collective-permute-start.4 = (bf16[2,128,576]{1,2,0:T(8,128)(2,1)S(1)}, bf16[2,128,576]{1,2,0:T(8,128)(2,1)S(1)}, u32[]{:S(2)}, u32[]{:S(2)}) collective-permute-start(bf16[2,128,576]{1,2,0:T(8,128)(2,1)S(1)} %get-tuple-element.61), channel_id=1, source_target_pairs={{0,8},{4,12},{8,0},{12,4},{16,24},{20,28},{24,16},{28,20},{1,9},{5... | collective-permute-start | bytes 884744 | tf_op jit(solution)/shard_map/ppermute | solution.py:46
  15.5 8.6 %collective-permute-start.6 = (bf16[2,128,576]{1,2,0:T(8,128)(2,1)S(1)}, bf16[2,128,576]{1,2,0:T(8,128)(2,1)S(1)}, u32[]{:S(2)}, u32[]{:S(2)}) collective-permute-start(bf16[2,128,576]{1,2,0:T(8,128)(2,1)S(1)} %get-tuple-element.62), channel_id=1, source_target_pairs={{0,16},{4,20},{8,24},{12,28},{16,0},{20,4},{24,8},{28,12},{1,17},{... | collective-permute-start | bytes 884744 | tf_op jit(solution)/shard_map/ppermute | solution.py:46
  22.0 14.5 %collective-permute-start.5 = (bf16[2,2,128,576]{2,3,1,0:T(8,128)(2,1)S(1)}, bf16[2,2,128,576]{2,3,1,0:T(8,128)(2,1)S(1)}, u32[]{:S(2)}, u32[]{:S(2)}) collective-permute-start(bf16[2,2,128,576]{2,3,1,0:T(8,128)(2,1)S(1)} %pad_maximum_fusion.5), channel_id=1, source_target_pairs={{0,16},{4,20},{8,24},{12,28},{16,0},{20,4},{24,8},{28,12},{1,17},{... | collective-permute-start | bytes 1769480 | tf_op jit(solution)/shard_map/ppermute | solution.py:46
  24.3 15.4 %collective-permute-start.7 = (bf16[2,2,128,576]{2,3,1,0:T(8,128)(2,1)S(1)}, bf16[2,2,128,576]{2,3,1,0:T(8,128)(2,1)S(1)}, u32[]{:S(2)}, u32[]{:S(2)}) collective-permute-start(bf16[2,2,128,576]{2,3,1,0:T(8,128)(2,1)S(1)} %pad_maximum_fusion.6), channel_id=1, source_target_pairs={{0,8},{4,12},{8,0},{12,4},{16,24},{20,28},{24,16},{28,20},{1,9},{5... | collective-permute-start | bytes 1769480 | tf_op jit(solution)/shard_map/ppermute | solution.py:46
  36.5 20.0 %collective-permute-start.13 = (bf16[96,1024]{1,0:T(8,128)(2,1)}, bf16[96,1024]{1,0:T(8,128)(2,1)}, u32[]{:S(2)}, u32[]{:S(2)}) collective-permute-start(bf16[96,1024]{1,0:T(8,128)(2,1)} %get-tuple-element.48), channel_id=1, source_target_pairs={{0,3},{1,0},{2,1},{3,2},{4,7},{5,4},{6,5},{7,6},{8,11},{9,8},{10,9... | collective-permute-start | bytes 589832 | tf_op jit(solution)/shard_map/ppermute | solution.py:38
  39.7 26.3 %collective-permute-start.12 = (bf16[96,1024]{1,0:T(8,128)(2,1)}, bf16[96,1024]{1,0:T(8,128)(2,1)}, u32[]{:S(2)}, u32[]{:S(2)}) collective-permute-start(bf16[96,1024]{1,0:T(8,128)(2,1)} %get-tuple-element.49), channel_id=1, source_target_pairs={{0,2},{1,3},{2,0},{3,1},{4,6},{5,7},{6,4},{7,5},{8,10},{9,11},{10,... | collective-permute-start | bytes 589832 | tf_op jit(solution)/shard_map/ppermute | solution.py:38
  46.1 1.7 %copy-start.4 = (bf16[96,1024]{1,0:T(8,128)(2,1)S(1)}, bf16[96,1024]{1,0:T(8,128)(2,1)}, u32[]{:S(2)}) copy-start(bf16[96,1024]{1,0:T(8,128)(2,1)} %get-tuple-element.50) | copy-start | bytes 589828
  47.8 18.2 %collective-permute-start.11 = (bf16[96,1024]{1,0:T(8,128)(2,1)S(1)}, bf16[96,1024]{1,0:T(8,128)(2,1)S(1)}, u32[]{:S(2)}, u32[]{:S(2)}) collective-permute-start(bf16[96,1024]{1,0:T(8,128)(2,1)S(1)} %copy-done.4), channel_id=1, source_target_pairs={{0,1},{1,2},{2,3},{3,0},{4,5},{5,6},{6,7},{7,4},{8,9},{9,10},{10,1... | collective-permute-start | bytes 589832 | tf_op jit(solution)/shard_map/ppermute | solution.py:38
  49.1 1.8 %copy-start.1 = (bf16[1,1024,576]{1,2,0:T(8,128)(2,1)S(1)}, bf16[1,1024,576]{1,2,0:T(8,128)(2,1)}, u32[]{:S(2)}) copy-start(bf16[1,1024,576]{1,2,0:T(8,128)(2,1)} %concatenate.26) | copy-start | bytes 3538948
  52.6 13.4 %copy-start.3 = (bf16[96,1024]{1,0:T(8,128)(2,1)S(1)}, bf16[96,1024]{1,0:T(8,128)(2,1)}, u32[]{:S(2)}) copy-start(bf16[96,1024]{1,0:T(8,128)(2,1)} %get-tuple-element.47) | copy-start | bytes 589828
  53.3 17.9 %collective-permute-start.10 = (bf16[96,1024]{1,0:T(8,128)(2,1)S(1)}, bf16[96,1024]{1,0:T(8,128)(2,1)S(1)}, u32[]{:S(2)}, u32[]{:S(2)}) collective-permute-start(bf16[96,1024]{1,0:T(8,128)(2,1)S(1)} %get-tuple-element.52), channel_id=1, source_target_pairs={{0,1},{1,2},{2,3},{3,0},{4,5},{5,6},{6,7},{7,4},{8,9},{9,10},{10,1... | collective-permute-start | bytes 589832 | tf_op jit(solution)/shard_map/ppermute | solution.py:38
  54.8 20.2 %collective-permute-start.9 = (bf16[96,1024]{1,0:T(8,128)(2,1)S(1)}, bf16[96,1024]{1,0:T(8,128)(2,1)S(1)}, u32[]{:S(2)}, u32[]{:S(2)}) collective-permute-start(bf16[96,1024]{1,0:T(8,128)(2,1)S(1)} %get-tuple-element.53), channel_id=1, source_target_pairs={{0,2},{1,3},{2,0},{3,1},{4,6},{5,7},{6,4},{7,5},{8,10},{9,11},{10,... | collective-permute-start | bytes 589832 | tf_op jit(solution)/shard_map/ppermute | solution.py:38
  56.5 19.7 %collective-permute-start.8 = (bf16[96,1024]{1,0:T(8,128)(2,1)S(1)}, bf16[96,1024]{1,0:T(8,128)(2,1)S(1)}, u32[]{:S(2)}, u32[]{:S(2)}) collective-permute-start(bf16[96,1024]{1,0:T(8,128)(2,1)S(1)} %get-tuple-element.54), channel_id=1, source_target_pairs={{0,3},{1,0},{2,1},{3,2},{4,7},{5,4},{6,5},{7,6},{8,11},{9,8},{10,9... | collective-permute-start | bytes 589832 | tf_op jit(solution)/shard_map/ppermute | solution.py:38
  67.8 3.1 %collective-permute-start.17 = (f32[4,128,384]{2,1,0:T(8,128)S(1)}, f32[4,128,384]{2,1,0:T(8,128)S(1)}, u32[]{:S(2)}, u32[]{:S(2)}) collective-permute-start(f32[4,128,384]{2,1,0:T(8,128)S(1)} %fusion.11), channel_id=1, source_target_pairs={{0,4},{4,0},{8,12},{12,8},{16,20},{20,16},{24,28},{28,24},{1,5},{5... | collective-permute-start | bytes 2359304 | tf_op jit(solution)/shard_map/ppermute | solution.py:80
  70.9 16.7 %collective-permute-start.16 = (bf16[96,1024]{1,0:T(8,128)(2,1)S(1)}, bf16[96,1024]{1,0:T(8,128)(2,1)S(1)}, u32[]{:S(2)}, u32[]{:S(2)}) collective-permute-start(bf16[96,1024]{1,0:T(8,128)(2,1)S(1)} %get-tuple-element.44), channel_id=1, source_target_pairs={{0,1},{1,2},{2,3},{3,0},{4,5},{5,6},{6,7},{7,4},{8,9},{9,10},{10,1... | collective-permute-start | bytes 589832 | tf_op jit(solution)/shard_map/ppermute | solution.py:38
  70.9 17.2 %collective-permute-start.15 = (bf16[96,1024]{1,0:T(8,128)(2,1)S(1)}, bf16[96,1024]{1,0:T(8,128)(2,1)S(1)}, u32[]{:S(2)}, u32[]{:S(2)}) collective-permute-start(bf16[96,1024]{1,0:T(8,128)(2,1)S(1)} %get-tuple-element.45), channel_id=1, source_target_pairs={{0,2},{1,3},{2,0},{3,1},{4,6},{5,7},{6,4},{7,5},{8,10},{9,11},{10,... | collective-permute-start | bytes 589832 | tf_op jit(solution)/shard_map/ppermute | solution.py:38
  71.2 17.0 %collective-permute-start.14 = (bf16[96,1024]{1,0:T(8,128)(2,1)S(1)}, bf16[96,1024]{1,0:T(8,128)(2,1)S(1)}, u32[]{:S(2)}, u32[]{:S(2)}) collective-permute-start(bf16[96,1024]{1,0:T(8,128)(2,1)S(1)} %get-tuple-element.46), channel_id=1, source_target_pairs={{0,3},{1,0},{2,1},{3,2},{4,7},{5,4},{6,5},{7,6},{8,11},{9,8},{10,9... | collective-permute-start | bytes 589832 | tf_op jit(solution)/shard_map/ppermute | solution.py:38
  74.9 11.0 %collective-permute-start.18 = (f32[2,128,384]{2,1,0:T(8,128)S(1)}, f32[2,128,384]{2,1,0:T(8,128)S(1)}, u32[]{:S(2)}, u32[]{:S(2)}) collective-permute-start(f32[2,128,384]{2,1,0:T(8,128)S(1)} %select_bitcast_fusion.4), channel_id=1, source_target_pairs={{0,8},{4,12},{8,0},{12,4},{16,24},{20,28},{24,16},{28,20},{1,9},{5... | collective-permute-start | bytes 1179656 | tf_op jit(solution)/shard_map/ppermute | solution.py:80
  77.5 10.6 %copy-start.5 = (s32[128,384]{1,0:T(8,128)S(1)}, s32[128,384]{1,0:T(8,128)}, u32[]{:S(2)}) copy-start(s32[128,384]{1,0:T(8,128)} %convert_reduce_fusion) | copy-start | bytes 589828
  86.0 5.9 %collective-permute-start.19 = (f32[1,128,384]{2,1,0:T(8,128)S(1)}, f32[1,128,384]{2,1,0:T(8,128)S(1)}, u32[]{:S(2)}, u32[]{:S(2)}) collective-permute-start(f32[1,128,384]{2,1,0:T(8,128)S(1)} %select_bitcast_fusion.11), channel_id=1, source_target_pairs={{0,16},{4,20},{8,24},{12,28},{16,0},{20,4},{24,8},{28,12},{1,17},{... | collective-permute-start | bytes 589832 | tf_op jit(solution)/shard_map/ppermute | solution.py:80

commit v8 on v4

--- a/solution.py
+++ b/solution.py
@@ -53,19 +53,32 @@
     return work
 
 
+def halve_bits(work, axes, bits, n_dp):
+    me = lax.axis_index("dp")
+    axes = list(axes)
+    for bit in bits:
+        ax = axes.index(bit)
+        mine = (me // bit) % 2
+        keep = jnp.take(work, mine, axis=ax)
+        give = jnp.take(work, 1 - mine, axis=ax)
+        work = keep + lax.ppermute(give, "dp", [(i, i ^ bit) for i in range(n_dp)])
+        axes.pop(ax)
+    return work, axes
+
+
 def reduce_scatter_dp(pieces, n_dp):
-    me = lax.axis_index("dp")
-    work = pieces
-    bit = 1
-    while bit < n_dp:
-        halves = work.reshape((work.shape[0] // 2, 2) + work.shape[1:])
-        mine = (me // bit) % 2
-        keep = jnp.take(halves, mine, axis=1)
-        give = jnp.take(halves, 1 - mine, axis=1)
-        pairs = [(i, i ^ bit) for i in range(n_dp)]
-        work = keep + lax.ppermute(give, "dp", pairs)
-        bit *= 2
-    return work[0]
+    bits = []
+    bit = n_dp // 2
+    while bit >= 1:
+        bits.append(bit)
+        bit //= 2
+    work = pieces.reshape((2,) * len(bits) + pieces.shape[1:])
+    work, axes = halve_bits(work, bits, bits[-1:], n_dp)
+    rest = sorted(axes)
+    half = work.shape[-1] // 2
+    left, _ = halve_bits(work[..., :half], axes, rest, n_dp)
+    right, _ = halve_bits(work[..., half:], axes, rest[::-1], n_dp)
+    return jnp.concatenate([left, right], axis=-1)
 
 
 def local(tokens, expert_ids, routing, w_gate, w_up, w_down, grad_out):

time: 89 us -> 101 us (1.13); the launches traced: 88.6 us -> 99.5 us
  starting transfers between devices: 31.6 us -> 36.9 us
  waiting for transfers between devices: 33.2 us -> 38.3 us
    ppermute x12, waiting for transfers between devices: 8.49 us -> 16 us  [shift_send(): got.append(lax.ppermute(blocks[step], 'expert', pairs))]
    ppermute x3 -> x5, starting transfers between devices: 1.65 us -> 5.38 us  [halve_bits(): work = keep + lax.ppermute(give, 'dp', [(i, i ^ bit) for i in range(n_dp)])]
    ppermute x3 -> x5, waiting for transfers between devices: 12.4 us -> 10.1 us  [halve_bits(): work = keep + lax.ppermute(give, 'dp', [(i, i ^ bit) for i in range(n_dp)])]
    ppermute x12, starting transfers between devices: 25 us -> 26.6 us  [shift_send(): got.append(lax.ppermute(blocks[step], 'expert', pairs))]
  transfers between devices with their start and end apart: 18 -> 20, of which waited for: 5 -> 6; matrix products, arithmetic and copies ran while one was open for 20% -> 18% of each run, Pallas kernels for 0% -> 0%
where the time goes in v8:
time: 101 us; the launch traced here: 99.5 us
  waiting for transfers between devices  38.3 us (38%)
  starting transfers between devices  36.9 us (37%)
  matrix products  11.8 us (12%)
  local copies, waits for them, and re-layouts  8.26 us (8%)
  other arithmetic  3.18 us (3%)
  between operations  1.07 us (1%)
    ppermute x12, starting transfers between devices, shift_send(): got.append(lax.ppermute(blocks[step], 'expert', pairs))  26.6 us
    ppermute x12, waiting for transfers between devices, shift_send(): got.append(lax.ppermute(blocks[step], 'expert', pairs))  16 us
    ppermute x3, waiting for transfers between devices, all_gather_dp(): recv = lax.ppermute(work, 'dp', [(i, i ^ bit) for i in range(n_dp)])  12.2 us
    ppermute x5, waiting for transfers between devices, halve_bits(): work = keep + lax.ppermute(give, 'dp', [(i, i ^ bit) for i in range(n_dp)])  10.1 us
    ppermute x5, starting transfers between devices, halve_bits(): work = keep + lax.ppermute(give, 'dp', [(i, i ^ bit) for i in range(n_dp)])  5.38 us
    ppermute x3, starting transfers between devices, all_gather_dp(): recv = lax.ppermute(work, 'dp', [(i, i ^ bit) for i in range(n_dp)])  4.91 us
    unnamed x26, local copies, waits for them, and re-layouts  4.09 us
  transfers between devices with their start and end apart: 20, of which 6 were waited for; matrix products, arithmetic and copies ran while one was open for 18% of the time, Pallas kernels for 0%

profile of v8, /device:TPU:0, one launch (start us, length us, event | category | flops | bytes accessed | tf_op | source)
XLA Modules:
  0.0 99.5 jit_solution(2572419119438633634)
XLA Ops:
  0.6 0.9 constant_dynamic-update-slice_fusion.2
  1.6 0.9 constant_dynamic-update-slice_fusion.1
  2.5 0.9 constant_dynamic-update-slice_fusion
  3.4 3.1 %collective-permute-start.3 = (bf16[1,128,1152]{2,1,0:T(8,128)(2,1)S(1)}, bf16[1,128,1152]{2,1,0:T(8,128)(2,1)S(1)}, u32[]{:S(2)}, u32[]{:S(2)}) collective-permute-start(bf16[1,128,1152]{2,1,0:T(8,128)(2,1)S(1)} %constant_dynamic-update-slice_fusion), channel_id=1, source_target_pairs={{0,16},{4,20},{8,24},{12,28},{16,0},{20,4},{24,8},{28,12},{1,17},{... | collective-permute-start | bytes 884744 | tf_op jit(solution)/shard_map/ppermute | solution.py:47
  6.5 0.8 copy.22
  7.9 5.6 %collective-permute-done.3 = bf16[1,128,1152]{2,1,0:T(8,128)(2,1)S(1)} collective-permute-done((bf16[1,128,1152]{2,1,0:T(8,128)(2,1)S(1)}, bf16[1,128,1152]{2,1,0:T(8,128)(2,1)S(1)}, u32[]{:S(2)}, u32[]{:S(2)}) %collective-permute-start.3) | collective-permute-done | bytes 294944 | tf_op jit(solution)/shard_map/ppermute | solution.py:47
  13.7 1.8 %collective-permute-start.4 = (bf16[2,128,1152]{2,1,0:T(8,128)(2,1)S(1)}, bf16[2,128,1152]{2,1,0:T(8,128)(2,1)S(1)}, u32[]{:S(2)}, u32[]{:S(2)}) collective-permute-start(bf16[2,128,1152]{2,1,0:T(8,128)(2,1)S(1)} %maximum_bitcast_fusion), channel_id=1, source_target_pairs={{0,8},{4,12},{8,0},{12,4},{16,24},{20,28},{24,16},{28,20},{1,9},{5... | collective-permute-start | bytes 1769480 | tf_op jit(solution)/shard_map/ppermute | solution.py:47
  15.6 0.4 convolution_convert_fusion
  16.1 3.7 %collective-permute-start.2 = (bf16[96,1024]{1,0:T(8,128)(2,1)S(1)}, bf16[96,1024]{1,0:T(8,128)(2,1)}, u32[]{:S(2)}, u32[]{:S(2)}) collective-permute-start(bf16[96,1024]{1,0:T(8,128)(2,1)S(1)} %get-tuple-element.70), channel_id=1, source_target_pairs={{0,3},{1,0},{2,1},{3,2},{4,7},{5,4},{6,5},{7,6},{8,11},{9,8},{10,9... | collective-permute-start | bytes 589832 | tf_op jit(solution)/shard_map/ppermute | solution.py:38
  19.7 1.0 %collective-permute-start = (bf16[96,1024]{1,0:T(8,128)(2,1)S(1)}, bf16[96,1024]{1,0:T(8,128)(2,1)}, u32[]{:S(2)}, u32[]{:S(2)}) collective-permute-start(bf16[96,1024]{1,0:T(8,128)(2,1)S(1)} %get-tuple-element.72), channel_id=1, source_target_pairs={{0,1},{1,2},{2,3},{3,0},{4,5},{5,6},{6,7},{7,4},{8,9},{9,10},{10,1... | collective-permute-start | bytes 589832 | tf_op jit(solution)/shard_map/ppermute | solution.py:38
  20.9 0.7 broadcast_in_dim.57
  21.6 6.6 %collective-permute-done.4 = bf16[2,128,1152]{2,1,0:T(8,128)(2,1)S(1)} collective-permute-done((bf16[2,128,1152]{2,1,0:T(8,128)(2,1)S(1)}, bf16[2,128,1152]{2,1,0:T(8,128)(2,1)S(1)}, u32[]{:S(2)}, u32[]{:S(2)}) %collective-permute-start.4) | collective-permute-done | bytes 589856 | tf_op jit(solution)/shard_map/ppermute | solution.py:47
  28.6 0.4 copy-done.6
  29.3 0.4 multiply_convert_fusion
  29.8 0.9 fusion.43
  30.7 3.5 %collective-permute-start.11 = (bf16[96,1024]{1,0:T(8,128)(2,1)}, bf16[96,1024]{1,0:T(8,128)(2,1)}, u32[]{:S(2)}, u32[]{:S(2)}) collective-permute-start(bf16[96,1024]{1,0:T(8,128)(2,1)} %get-tuple-element.62), channel_id=1, source_target_pairs={{0,3},{1,0},{2,1},{3,2},{4,7},{5,4},{6,5},{7,6},{8,11},{9,8},{10,9... | collective-permute-start | bytes 589832 | tf_op jit(solution)/shard_map/ppermute | solution.py:38
  34.2 0.8 convert_reduce_fusion
  35.0 0.8 slice_bitcast_fusion.14
  35.8 0.3 select_bitcast_fusion.1
  36.1 0.2 pad_maximum_fusion
  36.3 0.2 copy.25
  36.6 0.7 copy-done.3
  37.2 1.0 %collective-permute-start.9 = (bf16[96,1024]{1,0:T(8,128)(2,1)S(1)}, bf16[96,1024]{1,0:T(8,128)(2,1)S(1)}, u32[]{:S(2)}, u32[]{:S(2)}) collective-permute-start(bf16[96,1024]{1,0:T(8,128)(2,1)S(1)} %copy-done.3), channel_id=1, source_target_pairs={{0,1},{1,2},{2,3},{3,0},{4,5},{5,6},{6,7},{7,4},{8,9},{9,10},{10,1... | collective-permute-start | bytes 589832 | tf_op jit(solution)/shard_map/ppermute | solution.py:38
  38.3 1.7 %fusion.14 = f32[384,384]{1,0:T(8,128)S(1)} fusion(bf16[1,1024,1152]{2,1,0:T(8,128)(2,1)S(1)} %bitcast.104, bf16[96,1024]{1,0:T(8,128)(2,1)} %collective-permute-done.2, bf16[96,1024]{1,0:T(8,128)(2,1)} %collective-permute-done.1, bf16[96,1024]{1,0:T(8,128)(2,1)} %collective-permute-done, bf16[96,1024]{1,0:T(8,128)(2,1)S(1)} %get-tuple-element.69), kind=kOutput, calls=%fused_computation.34 | convolution fusion | flops 305135616 | bytes 2162688 | tf_op jit(solution)/shard_map/dot_general | solution.py:11
  40.0 1.7 %multiply_convert_fusion.3 = (bf16[384,384]{1,0:T(8,128)(2,1)S(1)}, f32[384,384]{1,0:T(8,128)S(1)}) fusion(f32[384,384]{1,0:T(8,128)S(1)} %fusion.14, bf16[1,1024,1152]{2,1,0:T(8,128)(2,1)S(1)} %bitcast.105, bf16[96,1024]{1,0:T(8,128)(2,1)} %collective-permute-done.2, bf16[96,1024]{1,0:T(8,128)(2,1)} %collective-permute-done.1, ...), kind=kOutput, calls=%fused_computation.40 | convolution fusion | flops 306020352 | bytes 3047424 | tf_op jit(solution)/shard_map/dot_general | solution.py:12
  41.7 0.6 convolution_convert_fusion.1
  42.3 2.5 %collective-permute-start.8 = (bf16[96,1024]{1,0:T(8,128)(2,1)S(1)}, bf16[96,1024]{1,0:T(8,128)(2,1)S(1)}, u32[]{:S(2)}, u32[]{:S(2)}) collective-permute-start(bf16[96,1024]{1,0:T(8,128)(2,1)S(1)} %get-tuple-element.66), channel_id=1, source_target_pairs={{0,1},{1,2},{2,3},{3,0},{4,5},{5,6},{6,7},{7,4},{8,9},{9,10},{10,1... | collective-permute-start | bytes 589832 | tf_op jit(solution)/shard_map/ppermute | solution.py:38
  44.9 5.5 %collective-permute-start.7 = (bf16[96,1024]{1,0:T(8,128)(2,1)S(1)}, bf16[96,1024]{1,0:T(8,128)(2,1)S(1)}, u32[]{:S(2)}, u32[]{:S(2)}) collective-permute-start(bf16[96,1024]{1,0:T(8,128)(2,1)S(1)} %get-tuple-element.67), channel_id=1, source_target_pairs={{0,2},{1,3},{2,0},{3,1},{4,6},{5,7},{6,4},{7,5},{8,10},{9,11},{10,... | collective-permute-start | bytes 589832 | tf_op jit(solution)/shard_map/ppermute | solution.py:38
  50.4 2.8 %collective-permute-start.6 = (bf16[96,1024]{1,0:T(8,128)(2,1)S(1)}, bf16[96,1024]{1,0:T(8,128)(2,1)S(1)}, u32[]{:S(2)}, u32[]{:S(2)}) collective-permute-start(bf16[96,1024]{1,0:T(8,128)(2,1)S(1)} %get-tuple-element.68), channel_id=1, source_target_pairs={{0,3},{1,0},{2,1},{3,2},{4,7},{5,4},{6,5},{7,6},{8,11},{9,8},{10,9... | collective-permute-start | bytes 589832 | tf_op jit(solution)/shard_map/ppermute | solution.py:38
  53.2 8.5 %collective-permute-done.10 = bf16[96,1024]{1,0:T(8,128)(2,1)S(1)} collective-permute-done((bf16[96,1024]{1,0:T(8,128)(2,1)}, bf16[96,1024]{1,0:T(8,128)(2,1)S(1)}, u32[]{:S(2)}, u32[]{:S(2)}) %collective-permute-start.10) | collective-permute-done | bytes 196640 | tf_op jit(solution)/shard_map/ppermute | solution.py:38
  61.7 1.6 %fusion.22 = f32[1024,384]{1,0:T(8,128)S(1)} fusion(bf16[384,384]{1,0:T(8,128)(2,1)S(1)} %get-tuple-element.79, bf16[96,1024]{1,0:T(8,128)(2,1)} %collective-permute-done.11, bf16[96,1024]{1,0:T(8,128)(2,1)S(1)} %collective-permute-done.10, bf16[96,1024]{1,0:T(8,128)(2,1)S(1)} %collective-permute-done.9, bf16[96,1024]{1,0:T(8,128)(2,1)S(1)} %copy-done.2), kind=kOutput, calls=%fused_computation.63 | convolution fusion | flops 305135616 | bytes 2654208 | tf_op jit(solution)/shard_map/dot_general | solution.py:143
  63.5 1.5 %fusion.16 = f32[384,384]{1,0:T(8,128)S(1)} fusion(bf16[1,1024,1152]{2,1,0:T(8,128)(2,1)S(1)} %bitcast.107, bf16[96,1024]{1,0:T(8,128)(2,1)} %collective-permute-done.11, bf16[96,1024]{1,0:T(8,128)(2,1)S(1)} %collective-permute-done.10, bf16[96,1024]{1,0:T(8,128)(2,1)S(1)} %collective-permute-done.9, bf16[96,1024]{1,0:T(8,128)(2,1)S(1)} %copy-done.2), kind=kOutput, calls=%fused_computation.36 | convolution fusion | flops 305135616 | bytes 2162688 | tf_op jit(solution)/shard_map/dot_general | solution.py:22
  65.0 0.7 fusion.13
  65.7 0.6 add_convert_fusion
  66.4 1.9 %collective-permute-start.13 = (bf16[96,1024]{1,0:T(8,128)(2,1)S(1)}, bf16[96,1024]{1,0:T(8,128)(2,1)S(1)}, u32[]{:S(2)}, u32[]{:S(2)}) collective-permute-start(bf16[96,1024]{1,0:T(8,128)(2,1)S(1)} %get-tuple-element.59), channel_id=1, source_target_pairs={{0,2},{1,3},{2,0},{3,1},{4,6},{5,7},{6,4},{7,5},{8,10},{9,11},{10,... | collective-permute-start | bytes 589832 | tf_op jit(solution)/shard_map/ppermute | solution.py:38
  68.4 4.5 %collective-permute-start.12 = (bf16[96,1024]{1,0:T(8,128)(2,1)S(1)}, bf16[96,1024]{1,0:T(8,128)(2,1)S(1)}, u32[]{:S(2)}, u32[]{:S(2)}) collective-permute-start(bf16[96,1024]{1,0:T(8,128)(2,1)S(1)} %get-tuple-element.60), channel_id=1, source_target_pairs={{0,3},{1,0},{2,1},{3,2},{4,7},{5,4},{6,5},{7,6},{8,11},{9,8},{10,9... | collective-permute-start | bytes 589832 | tf_op jit(solution)/shard_map/ppermute | solution.py:38
  72.9 0.3 convolution_multiply_fusion
  73.2 1.0 %fusion.1 = bf16[128,1024]{1,0:T(8,128)(2,1)} fusion(f32[128,1024]{1,0:T(8,128)S(1)} %convolution_multiply_fusion, f32[128]{0:T(128)S(1)} %get-tuple-element.75, pred[128,2,384]{2,0,1:T(32,128)(4,1)S(1)} %get-tuple-element.78, bf16[96,1024]{1,0:T(8,128)(2,1)S(1)} %collective-permute-done.8, bf16[96,1024]{1,0:T(8,128)(2,1)S(1)} %collective-permute-done.7, ...), kind=kOutput, calls=%fused_computation.8 | convolution fusion | flops 104202240 | bytes 1622528 | tf_op jit(solution)/shard_map/dot_general | solution.py:152
  74.3 0.2 fusion.41
  74.6 1.6 %collective-permute-start.18 = (f32[2,128,192]{2,1,0:T(8,128)S(1)}, f32[2,128,192]{2,1,0:T(8,128)S(1)}, u32[]{:S(2)}, u32[]{:S(2)}) collective-permute-start(f32[2,128,192]{2,1,0:T(8,128)S(1)} %select_bitcast_fusion.6), channel_id=1, source_target_pairs={{0,16},{4,20},{8,24},{12,28},{16,0},{20,4},{24,8},{28,12},{1,17},{... | collective-permute-start | bytes 589832 | tf_op jit(solution)/shard_map/ppermute | solution.py:64
  76.2 7.5 %collective-permute-done.13 = bf16[96,1024]{1,0:T(8,128)(2,1)S(1)} collective-permute-done((bf16[96,1024]{1,0:T(8,128)(2,1)S(1)}, bf16[96,1024]{1,0:T(8,128)(2,1)S(1)}, u32[]{:S(2)}, u32[]{:S(2)}) %collective-permute-start.13) | collective-permute-done | bytes 196640 | tf_op jit(solution)/shard_map/ppermute | solution.py:38
  83.7 1.0 %convolution_convert_fusion.2 = bf16[128,1024]{1,0:T(8,128)(2,1)} fusion(bf16[96,1024]{1,0:T(8,128)(2,1)S(1)} %collective-permute-done.14, bf16[96,1024]{1,0:T(8,128)(2,1)S(1)} %collective-permute-done.13, bf16[96,1024]{1,0:T(8,128)(2,1)S(1)} %collective-permute-done.12, bf16[96,1024]{1,0:T(8,128)(2,1)S(1)} %get-tuple-element.57, ...), kind=kOutput, calls=%fused_computation.9 | convolution fusion | flops 103989248 | bytes 1245184 | tf_op jit(solution)/shard_map/dot_general | solution.py:158
  84.7 0.4 collective-permute-start.16
  85.2 1.7 %collective-permute-start.19 = (f32[128,192]{1,0:T(8,128)S(1)}, f32[128,192]{1,0:T(8,128)S(1)}, u32[]{:S(2)}, u32[]{:S(2)}) collective-permute-start(f32[128,192]{1,0:T(8,128)S(1)} %select_bitcast_fusion.8), channel_id=1, source_target_pairs={{0,8},{4,12},{8,0},{12,4},{16,24},{20,28},{24,16},{28,20},{1,9},{5... | collective-permute-start | bytes 294920 | tf_op jit(solution)/shard_map/ppermute | solution.py:64
  86.9 6.6 %collective-permute-done.16 = f32[2,128,192]{2,1,0:T(8,128)S(1)} collective-permute-done((f32[2,128,192]{2,1,0:T(8,128)S(1)}, f32[2,128,192]{2,1,0:T(8,128)S(1)}, u32[]{:S(2)}, u32[]{:S(2)}) %collective-permute-start.16) | collective-permute-done | bytes 196640 | tf_op jit(solution)/shard_map/ppermute | solution.py:64
  93.6 1.6 %collective-permute-start.17 = (f32[128,192]{1,0:T(8,128)S(1)}, f32[128,192]{1,0:T(8,128)S(1)}, u32[]{:S(2)}, u32[]{:S(2)}) collective-permute-start(f32[128,192]{1,0:T(8,128)S(1)} %select_bitcast_fusion.9), channel_id=1, source_target_pairs={{0,16},{4,20},{8,24},{12,28},{16,0},{20,4},{24,8},{28,12},{1,17},{... | collective-permute-start | bytes 294920 | tf_op jit(solution)/shard_map/ppermute | solution.py:64
  95.2 3.4 %collective-permute-done.17 = f32[128,192]{1,0:T(8,128)S(1)} collective-permute-done((f32[128,192]{1,0:T(8,128)S(1)}, f32[128,192]{1,0:T(8,128)S(1)}, u32[]{:S(2)}, u32[]{:S(2)}) %collective-permute-start.17) | collective-permute-done | bytes 98336 | tf_op jit(solution)/shard_map/ppermute | solution.py:64
  98.7 0.8 maximum_multiply_fusion
  (68 shorter events, 2.3 us)
Async XLA Ops:
  0.6 15.0 %copy-start = (bf16[128,1024]{1,0:T(8,128)(2,1)S(1)}, bf16[128,1024]{1,0:T(8,128)(2,1)}, u32[]{:S(2)}) copy-start(bf16[128,1024]{1,0:T(8,128)(2,1)} %param.15) | copy-start | bytes 786436
  3.4 10.1 %collective-permute-start.3 = (bf16[1,128,1152]{2,1,0:T(8,128)(2,1)S(1)}, bf16[1,128,1152]{2,1,0:T(8,128)(2,1)S(1)}, u32[]{:S(2)}, u32[]{:S(2)}) collective-permute-start(bf16[1,128,1152]{2,1,0:T(8,128)(2,1)S(1)} %constant_dynamic-update-slice_fusion), channel_id=1, source_target_pairs={{0,16},{4,20},{8,24},{12,28},{16,0},{20,4},{24,8},{28,12},{1,17},{... | collective-permute-start | bytes 884744 | tf_op jit(solution)/shard_map/ppermute | solution.py:47
  7.4 6.2 %copy-start.5 = (s32[256]{0:T(256)}, s32[256]{0:T(256)S(1)}, u32[]{:S(2)}) copy-start(s32[256]{0:T(256)S(1)} %sub.50) | copy-start | bytes 3076
  7.6 6.0 %copy-start.9 = (f32[256]{0:T(256)}, f32[256]{0:T(256)S(1)}, u32[]{:S(2)}) copy-start(f32[256]{0:T(256)S(1)} %fusion.2) | copy-start | bytes 3076
  7.9 7.7 %copy-start.4 = (s32[128,2]{0,1:T(2,128)}, s32[128,2]{0,1:T(2,128)S(1)}, u32[]{:S(2)}) copy-start(s32[128,2]{0,1:T(2,128)S(1)} %copy.23) | copy-start | bytes 3076
  13.6 7.1 %copy-start.7 = (f32[128,2]{0,1:T(2,128)S(1)}, f32[128,2]{0,1:T(2,128)}, u32[]{:S(2)}) copy-start(f32[128,2]{0,1:T(2,128)} %param.17) | copy-start | bytes 3076
  13.7 14.6 %collective-permute-start.4 = (bf16[2,128,1152]{2,1,0:T(8,128)(2,1)S(1)}, bf16[2,128,1152]{2,1,0:T(8,128)(2,1)S(1)}, u32[]{:S(2)}, u32[]{:S(2)}) collective-permute-start(bf16[2,128,1152]{2,1,0:T(8,128)(2,1)S(1)} %maximum_bitcast_fusion), channel_id=1, source_target_pairs={{0,8},{4,12},{8,0},{12,4},{16,24},{20,28},{24,16},{28,20},{1,9},{5... | collective-permute-start | bytes 1769480 | tf_op jit(solution)/shard_map/ppermute | solution.py:47
  16.1 20.5 %collective-permute-start.2 = (bf16[96,1024]{1,0:T(8,128)(2,1)S(1)}, bf16[96,1024]{1,0:T(8,128)(2,1)}, u32[]{:S(2)}, u32[]{:S(2)}) collective-permute-start(bf16[96,1024]{1,0:T(8,128)(2,1)S(1)} %get-tuple-element.70), channel_id=1, source_target_pairs={{0,3},{1,0},{2,1},{3,2},{4,7},{5,4},{6,5},{7,6},{8,11},{9,8},{10,9... | collective-permute-start | bytes 589832 | tf_op jit(solution)/shard_map/ppermute | solution.py:38
  19.7 18.5 %collective-permute-start.1 = (bf16[96,1024]{1,0:T(8,128)(2,1)S(1)}, bf16[96,1024]{1,0:T(8,128)(2,1)}, u32[]{:S(2)}, u32[]{:S(2)}) collective-permute-start(bf16[96,1024]{1,0:T(8,128)(2,1)S(1)} %get-tuple-element.71), channel_id=1, source_target_pairs={{0,2},{1,3},{2,0},{3,1},{4,6},{5,7},{6,4},{7,5},{8,10},{9,11},{10,... | collective-permute-start | bytes 589832 | tf_op jit(solution)/shard_map/ppermute | solution.py:38
  19.7 18.5 %collective-permute-start = (bf16[96,1024]{1,0:T(8,128)(2,1)S(1)}, bf16[96,1024]{1,0:T(8,128)(2,1)}, u32[]{:S(2)}, u32[]{:S(2)}) collective-permute-start(bf16[96,1024]{1,0:T(8,128)(2,1)S(1)} %get-tuple-element.72), channel_id=1, source_target_pairs={{0,1},{1,2},{2,3},{3,0},{4,5},{5,6},{6,7},{7,4},{8,9},{9,10},{10,1... | collective-permute-start | bytes 589832 | tf_op jit(solution)/shard_map/ppermute | solution.py:38
  28.3 0.7 copy-start.6
  28.4 0.7 copy-start.10
  28.4 0.7 copy-start.8
  28.4 1.0 copy-start.1
  28.5 7.2 %collective-permute-start.5 = (bf16[4,128,1152]{2,1,0:T(8,128)(2,1)S(1)}, bf16[4,128,1152]{2,1,0:T(8,128)(2,1)S(1)}, u32[]{:S(2)}, u32[]{:S(2)}) collective-permute-start(bf16[4,128,1152]{2,1,0:T(8,128)(2,1)S(1)} %bitcast.103), channel_id=1, source_target_pairs={{0,4},{4,0},{8,12},{12,8},{16,20},{20,16},{24,28},{28,24},{1,5},{5... | collective-permute-start | bytes 3538952 | tf_op jit(solution)/shard_map/ppermute | solution.py:47
  30.7 19.7 %collective-permute-start.11 = (bf16[96,1024]{1,0:T(8,128)(2,1)}, bf16[96,1024]{1,0:T(8,128)(2,1)}, u32[]{:S(2)}, u32[]{:S(2)}) collective-permute-start(bf16[96,1024]{1,0:T(8,128)(2,1)} %get-tuple-element.62), channel_id=1, source_target_pairs={{0,3},{1,0},{2,1},{3,2},{4,7},{5,4},{6,5},{7,6},{8,11},{9,8},{10,9... | collective-permute-start | bytes 589832 | tf_op jit(solution)/shard_map/ppermute | solution.py:38
  35.8 26.0 %collective-permute-start.10 = (bf16[96,1024]{1,0:T(8,128)(2,1)}, bf16[96,1024]{1,0:T(8,128)(2,1)S(1)}, u32[]{:S(2)}, u32[]{:S(2)}) collective-permute-start(bf16[96,1024]{1,0:T(8,128)(2,1)} %get-tuple-element.63), channel_id=1, source_target_pairs={{0,2},{1,3},{2,0},{3,1},{4,6},{5,7},{6,4},{7,5},{8,10},{9,11},{10,... | collective-permute-start | bytes 589832 | tf_op jit(solution)/shard_map/ppermute | solution.py:38
  36.3 0.9 copy-start.3
  37.2 24.5 %collective-permute-start.9 = (bf16[96,1024]{1,0:T(8,128)(2,1)S(1)}, bf16[96,1024]{1,0:T(8,128)(2,1)S(1)}, u32[]{:S(2)}, u32[]{:S(2)}) collective-permute-start(bf16[96,1024]{1,0:T(8,128)(2,1)S(1)} %copy-done.3), channel_id=1, source_target_pairs={{0,1},{1,2},{2,3},{3,0},{4,5},{5,6},{6,7},{7,4},{8,9},{9,10},{10,1... | collective-permute-start | bytes 589832 | tf_op jit(solution)/shard_map/ppermute | solution.py:38
  41.7 20.1 %copy-start.2 = (bf16[96,1024]{1,0:T(8,128)(2,1)S(1)}, bf16[96,1024]{1,0:T(8,128)(2,1)}, u32[]{:S(2)}) copy-start(bf16[96,1024]{1,0:T(8,128)(2,1)} %get-tuple-element.61) | copy-start | bytes 589828
  42.3 24.1 %collective-permute-start.8 = (bf16[96,1024]{1,0:T(8,128)(2,1)S(1)}, bf16[96,1024]{1,0:T(8,128)(2,1)S(1)}, u32[]{:S(2)}, u32[]{:S(2)}) collective-permute-start(bf16[96,1024]{1,0:T(8,128)(2,1)S(1)} %get-tuple-element.66), channel_id=1, source_target_pairs={{0,1},{1,2},{2,3},{3,0},{4,5},{5,6},{6,7},{7,4},{8,9},{9,10},{10,1... | collective-permute-start | bytes 589832 | tf_op jit(solution)/shard_map/ppermute | solution.py:38
  44.9 23.5 %collective-permute-start.7 = (bf16[96,1024]{1,0:T(8,128)(2,1)S(1)}, bf16[96,1024]{1,0:T(8,128)(2,1)S(1)}, u32[]{:S(2)}, u32[]{:S(2)}) collective-permute-start(bf16[96,1024]{1,0:T(8,128)(2,1)S(1)} %get-tuple-element.67), channel_id=1, source_target_pairs={{0,2},{1,3},{2,0},{3,1},{4,6},{5,7},{6,4},{7,5},{8,10},{9,11},{10,... | collective-permute-start | bytes 589832 | tf_op jit(solution)/shard_map/ppermute | solution.py:38
  50.4 22.5 %collective-permute-start.6 = (bf16[96,1024]{1,0:T(8,128)(2,1)S(1)}, bf16[96,1024]{1,0:T(8,128)(2,1)S(1)}, u32[]{:S(2)}, u32[]{:S(2)}) collective-permute-start(bf16[96,1024]{1,0:T(8,128)(2,1)S(1)} %get-tuple-element.68), channel_id=1, source_target_pairs={{0,3},{1,0},{2,1},{3,2},{4,7},{5,4},{6,5},{7,6},{8,11},{9,8},{10,9... | collective-permute-start | bytes 589832 | tf_op jit(solution)/shard_map/ppermute | solution.py:38
  63.4 10.8 %collective-permute-start.15 = (f32[2,2,128,384]{3,2,1,0:T(8,128)S(1)}, f32[2,2,128,384]{3,2,1,0:T(8,128)S(1)}, u32[]{:S(2)}, u32[]{:S(2)}) collective-permute-start(f32[2,2,128,384]{3,2,1,0:T(8,128)S(1)} %fusion.10), channel_id=1, source_target_pairs={{0,4},{4,0},{8,12},{12,8},{16,20},{20,16},{24,28},{28,24},{1,5},{5... | collective-permute-start | bytes 2359304 | tf_op jit(solution)/shard_map/ppermute | solution.py:64
  66.4 9.8 %collective-permute-start.14 = (bf16[96,1024]{1,0:T(8,128)(2,1)S(1)}, bf16[96,1024]{1,0:T(8,128)(2,1)S(1)}, u32[]{:S(2)}, u32[]{:S(2)}) collective-permute-start(bf16[96,1024]{1,0:T(8,128)(2,1)S(1)} %get-tuple-element.58), channel_id=1, source_target_pairs={{0,1},{1,2},{2,3},{3,0},{4,5},{5,6},{6,7},{7,4},{8,9},{9,10},{10,1... | collective-permute-start | bytes 589832 | tf_op jit(solution)/shard_map/ppermute | solution.py:38
  66.4 17.2 %collective-permute-start.13 = (bf16[96,1024]{1,0:T(8,128)(2,1)S(1)}, bf16[96,1024]{1,0:T(8,128)(2,1)S(1)}, u32[]{:S(2)}, u32[]{:S(2)}) collective-permute-start(bf16[96,1024]{1,0:T(8,128)(2,1)S(1)} %get-tuple-element.59), channel_id=1, source_target_pairs={{0,2},{1,3},{2,0},{3,1},{4,6},{5,7},{6,4},{7,5},{8,10},{9,11},{10,... | collective-permute-start | bytes 589832 | tf_op jit(solution)/shard_map/ppermute | solution.py:38
  68.4 15.3 %collective-permute-start.12 = (bf16[96,1024]{1,0:T(8,128)(2,1)S(1)}, bf16[96,1024]{1,0:T(8,128)(2,1)S(1)}, u32[]{:S(2)}, u32[]{:S(2)}) collective-permute-start(bf16[96,1024]{1,0:T(8,128)(2,1)S(1)} %get-tuple-element.60), channel_id=1, source_target_pairs={{0,3},{1,0},{2,1},{3,2},{4,7},{5,4},{6,5},{7,6},{8,11},{9,8},{10,9... | collective-permute-start | bytes 589832 | tf_op jit(solution)/shard_map/ppermute | solution.py:38
  74.6 10.6 %collective-permute-start.18 = (f32[2,128,192]{2,1,0:T(8,128)S(1)}, f32[2,128,192]{2,1,0:T(8,128)S(1)}, u32[]{:S(2)}, u32[]{:S(2)}) collective-permute-start(f32[2,128,192]{2,1,0:T(8,128)S(1)} %select_bitcast_fusion.6), channel_id=1, source_target_pairs={{0,16},{4,20},{8,24},{12,28},{16,0},{20,4},{24,8},{28,12},{1,17},{... | collective-permute-start | bytes 589832 | tf_op jit(solution)/shard_map/ppermute | solution.py:64
  84.7 8.9 %collective-permute-start.16 = (f32[2,128,192]{2,1,0:T(8,128)S(1)}, f32[2,128,192]{2,1,0:T(8,128)S(1)}, u32[]{:S(2)}, u32[]{:S(2)}) collective-permute-start(f32[2,128,192]{2,1,0:T(8,128)S(1)} %select_bitcast_fusion.7), channel_id=1, source_target_pairs={{0,8},{4,12},{8,0},{12,4},{16,24},{20,28},{24,16},{28,20},{1,9},{5... | collective-permute-start | bytes 589832 | tf_op jit(solution)/shard_map/ppermute | solution.py:64
  85.2 10.0 %collective-permute-start.19 = (f32[128,192]{1,0:T(8,128)S(1)}, f32[128,192]{1,0:T(8,128)S(1)}, u32[]{:S(2)}, u32[]{:S(2)}) collective-permute-start(f32[128,192]{1,0:T(8,128)S(1)} %select_bitcast_fusion.8), channel_id=1, source_target_pairs={{0,8},{4,12},{8,0},{12,4},{16,24},{20,28},{24,16},{28,20},{1,9},{5... | collective-permute-start | bytes 294920 | tf_op jit(solution)/shard_map/ppermute | solution.py:64
  93.6 5.0 %collective-permute-start.17 = (f32[128,192]{1,0:T(8,128)S(1)}, f32[128,192]{1,0:T(8,128)S(1)}, u32[]{:S(2)}, u32[]{:S(2)}) collective-permute-start(f32[128,192]{1,0:T(8,128)S(1)} %select_bitcast_fusion.9), channel_id=1, source_target_pairs={{0,16},{4,20},{8,24},{12,28},{16,0},{20,4},{24,8},{28,12},{1,17},{... | collective-permute-start | bytes 294920 | tf_op jit(solution)/shard_map/ppermute | solution.py:64

commit v9 on v4

--- a/solution.py
+++ b/solution.py
@@ -41,16 +41,22 @@
 
 def all_gather_dp(block, n_dp):
     me = lax.axis_index("dp")
-    work = block[None]
+    bits = []
     bit = n_dp // 2
     while bit >= 1:
+        bits.append(bit)
+        bit //= 2
+    if len(bits) >= 3:
+        bits[0], bits[1] = bits[1], bits[0]
+    work = block
+    for bit in bits:
         recv = lax.ppermute(work, "dp", [(i, i ^ bit) for i in range(n_dp)])
         upper = (me // bit) % 2 == 1
-        low = jnp.where(upper, recv, work)
-        high = jnp.where(upper, work, recv)
-        work = jnp.stack([low, high], axis=1).reshape((2 * work.shape[0],) + work.shape[1:])
-        bit //= 2
-    return work
+        work = jnp.stack([jnp.where(upper, recv, work), jnp.where(upper, work, recv)], axis=0)
+    axes = list(reversed(bits))
+    perm = sorted(range(len(bits)), key=lambda a: -axes[a])
+    work = jnp.transpose(work, perm + list(range(len(bits), work.ndim)))
+    return work.reshape((n_dp,) + block.shape)
 
 
 def reduce_scatter_dp(pieces, n_dp):

time: 89 us -> 87.6 us (0.984)
  starting transfers between devices: 31.6 us -> 26.1 us
  waiting for transfers between devices: 33.2 us -> 37.8 us
  local copies, waits for them, and re-layouts: 8.04 us -> 4.47 us
  other arithmetic: 3.01 us -> 6.09 us
    ppermute x12, starting transfers between devices: 25 us -> 18.1 us  [shift_send(): got.append(lax.ppermute(blocks[step], 'expert', pairs))]
    ppermute x12, waiting for transfers between devices: 8.49 us -> 14.7 us  [shift_send(): got.append(lax.ppermute(blocks[step], 'expert', pairs))]
    another operation x5 -> x7, other arithmetic: 0.85 us -> 3.99 us  [the longest x6 2.93 us: all_gather_dp(): jnp.stack([jnp.where(upper, recv, work), jnp.where(upper, work, recv)], a...]
    unnamed x26 -> x24, local copies, waits for them, and re-layouts: 4.09 us -> 1.62 us
    ppermute x3, waiting for transfers between devices: 12.4 us -> 10.9 us  [reduce_scatter_dp(): work = keep + lax.ppermute(give, 'dp', pairs)]
    ppermute x3, starting transfers between devices: 1.65 us -> 3.15 us  [reduce_scatter_dp(): work = keep + lax.ppermute(give, 'dp', pairs)]
    concatenate x1 -> x0, local copies, waits for them, and re-layouts: 0.91 us -> none  [local(): packed = jnp.concatenate([w_gate, w_up, w_down], axis=2)]
  transfers between devices with their start and end apart: 18 -> 18, of which waited for: 5 -> 6; matrix products, arithmetic and copies ran while one was open for 20% -> 21% of each run, Pallas kernels for 0% -> 0%
where the time goes in v9:
time: 87.6 us; the launch traced here: 87.3 us
  waiting for transfers between devices  37.8 us (43%)
  starting transfers between devices  26.1 us (30%)
  matrix products  11.8 us (13%)
  other arithmetic  6.09 us (7%)
  local copies, waits for them, and re-layouts  4.47 us (5%)
  between operations  1.05 us (1%)
    ppermute x12, starting transfers between devices, shift_send(): got.append(lax.ppermute(blocks[step], 'expert', pairs))  18.1 us
    ppermute x12, waiting for transfers between devices, shift_send(): got.append(lax.ppermute(blocks[step], 'expert', pairs))  14.7 us
    ppermute x3, waiting for transfers between devices, all_gather_dp(): recv = lax.ppermute(work, 'dp', [(i, i ^ bit) for i in range(n_dp)])  12.2 us
    ppermute x3, waiting for transfers between devices, reduce_scatter_dp(): work = keep + lax.ppermute(give, 'dp', pairs)  10.9 us
    ppermute x3, starting transfers between devices, all_gather_dp(): recv = lax.ppermute(work, 'dp', [(i, i ^ bit) for i in range(n_dp)])  4.87 us
    ppermute x3, starting transfers between devices, reduce_scatter_dp(): work = keep + lax.ppermute(give, 'dp', pairs)  3.15 us
    another operation x6, other arithmetic, all_gather_dp(): jnp.stack([jnp.where(upper, recv, work), jnp.where(upper, work, recv)], a...  2.93 us
  transfers between devices with their start and end apart: 18, of which 6 were waited for; matrix products, arithmetic and copies ran while one was open for 21% of the time, Pallas kernels for 0%

profile of v9, /device:TPU:0, one launch (start us, length us, event | category | flops | bytes accessed | tf_op | source)
XLA Modules:
  0.0 87.3 jit_solution(1260684459591776536)
XLA Ops:
  0.6 1.1 %maximum_bitcast_fusion = bf16[128,1152]{1,0:T(8,128)(2,1)S(1)} fusion(bf16[1,128,384]{2,1,0:T(8,128)(2,1)} %param.18, bf16[1,128,384]{2,1,0:T(8,128)(2,1)} %param.17, bf16[1,128,384]{2,1,0:T(8,128)(2,1)} %param.16), kind=kLoop, calls=%fused_computation.53 | loop fusion | flops 884736 | bytes 589824 | tf_op jit(solution)/shard_map/reshape;transpose | solution.py:121
  1.7 3.0 %collective-permute-start.3 = (bf16[128,1152]{1,0:T(8,128)(2,1)S(1)}, bf16[128,1152]{1,0:T(8,128)(2,1)S(1)}, u32[]{:S(2)}, u32[]{:S(2)}) collective-permute-start(bf16[128,1152]{1,0:T(8,128)(2,1)S(1)} %maximum_bitcast_fusion), channel_id=1, source_target_pairs={{0,8},{4,12},{8,0},{12,4},{16,24},{20,28},{24,16},{28,20},{1,9},{5... | collective-permute-start | bytes 884744 | tf_op jit(solution)/shard_map/ppermute | solution.py:53
  4.7 0.8 copy.19
  5.5 0.1 sub.46
  5.7 0.2 fusion.2
  5.9 0.1 convert_element_type.57
  6.2 5.6 %collective-permute-done.3 = bf16[128,1152]{1,0:T(8,128)(2,1)S(1)} collective-permute-done((bf16[128,1152]{1,0:T(8,128)(2,1)S(1)}, bf16[128,1152]{1,0:T(8,128)(2,1)S(1)}, u32[]{:S(2)}, u32[]{:S(2)}) %collective-permute-start.3) | collective-permute-done | bytes 294944 | tf_op jit(solution)/shard_map/ppermute | solution.py:53
  11.7 1.1 %select_bitcast_fusion.6 = (bf16[1,128,1152]{2,1,0:T(8,128)(2,1)S(1)}, bf16[1,128,1152]{2,1,0:T(8,128)(2,1)S(1)}) fusion(bf16[128,1152]{1,0:T(8,128)(2,1)S(1)} %collective-permute-done.3, pred[]{:T(512)S(6)} %eq.60, bf16[1,128,384]{2,1,0:T(8,128)(2,1)} %param.18, bf16[1,128,384]{2,1,0:T(8,128)(2,1)} %param.17, bf16[1,128,384]{2,1,0:T(8,128)(2,1)} %param.16), kind=kLoop, calls=%fused_computation.57 | loop fusion | flops 1179648 | bytes 1179649 | tf_op jit(solution)/shard_map/stack | solution.py:55
  12.9 1.8 %collective-permute-start.4 = (bf16[2,128,1152]{2,1,0:T(8,128)(2,1)S(1)}, bf16[2,128,1152]{2,1,0:T(8,128)(2,1)S(1)}, u32[]{:S(2)}, u32[]{:S(2)}) collective-permute-start(bf16[2,128,1152]{2,1,0:T(8,128)(2,1)S(1)} %pad_maximum_fusion.5), channel_id=1, source_target_pairs={{0,16},{4,20},{8,24},{12,28},{16,0},{20,4},{24,8},{28,12},{1,17},{... | collective-permute-start | bytes 1769480 | tf_op jit(solution)/shard_map/ppermute | solution.py:53
  14.8 0.1 fusion.22
  14.9 0.4 convolution_convert_fusion
  15.4 3.7 %collective-permute-start.2 = (bf16[96,1024]{1,0:T(8,128)(2,1)S(1)}, bf16[96,1024]{1,0:T(8,128)(2,1)}, u32[]{:S(2)}, u32[]{:S(2)}) collective-permute-start(bf16[96,1024]{1,0:T(8,128)(2,1)S(1)} %get-tuple-element.56), channel_id=1, source_target_pairs={{0,3},{1,0},{2,1},{3,2},{4,7},{5,4},{6,5},{7,6},{8,11},{9,8},{10,9... | collective-permute-start | bytes 589832 | tf_op jit(solution)/shard_map/ppermute | solution.py:38
  19.1 1.0 %collective-permute-start = (bf16[96,1024]{1,0:T(8,128)(2,1)S(1)}, bf16[96,1024]{1,0:T(8,128)(2,1)}, u32[]{:S(2)}, u32[]{:S(2)}) collective-permute-start(bf16[96,1024]{1,0:T(8,128)(2,1)S(1)} %get-tuple-element.58), channel_id=1, source_target_pairs={{0,1},{1,2},{2,3},{3,0},{4,5},{5,6},{6,7},{7,4},{8,9},{9,10},{10,1... | collective-permute-start | bytes 589832 | tf_op jit(solution)/shard_map/ppermute | solution.py:38
  20.2 0.7 broadcast_in_dim.48
  20.9 6.6 %collective-permute-done.4 = bf16[2,128,1152]{2,1,0:T(8,128)(2,1)S(1)} collective-permute-done((bf16[2,128,1152]{2,1,0:T(8,128)(2,1)S(1)}, bf16[2,128,1152]{2,1,0:T(8,128)(2,1)S(1)}, u32[]{:S(2)}, u32[]{:S(2)}) %collective-permute-start.4) | collective-permute-done | bytes 589856 | tf_op jit(solution)/shard_map/ppermute | solution.py:53
  27.5 0.1 select_bitcast_fusion.3
  27.7 1.2 %pad_maximum_fusion.1 = bf16[2,2,128,1152]{3,2,1,0:T(8,128)(2,1)} fusion(bf16[1,2,128,1152]{3,2,1,0:T(8,128)(2,1)S(1)} %get-tuple-element.42, bf16[1,2,128,1152]{3,2,1,0:T(8,128)(2,1)S(1)} %get-tuple-element.41), kind=kLoop, calls=%fused_computation.10 | loop fusion | flops 589824 | bytes 2359296 | tf_op jit(solution)/shard_map/stack | solution.py:55
  28.9 0.1 select_reduce_fusion
  29.0 0.4 multiply_convert_fusion
  29.5 0.9 %fusion.42 = (bf16[96,1024]{1,0:T(8,128)(2,1)}, bf16[96,1024]{1,0:T(8,128)(2,1)}, bf16[96,1024]{1,0:T(8,128)(2,1)}, bf16[96,1024]{1,0:T(8,128)(2,1)}) fusion(bf16[384,1024]{1,0:T(8,128)(2,1)S(1)} %multiply_convert_fusion), kind=kLoop, calls=%fused_computation.94 | loop fusion | bytes 1572864 | tf_op jit(solution)/shard_map/slice | solution.py:128
  30.4 3.6 %collective-permute-start.11 = (bf16[96,1024]{1,0:T(8,128)(2,1)}, bf16[96,1024]{1,0:T(8,128)(2,1)}, u32[]{:S(2)}, u32[]{:S(2)}) collective-permute-start(bf16[96,1024]{1,0:T(8,128)(2,1)} %get-tuple-element.48), channel_id=1, source_target_pairs={{0,3},{1,0},{2,1},{3,2},{4,7},{5,4},{6,5},{7,6},{8,11},{9,8},{10,9... | collective-permute-start | bytes 589832 | tf_op jit(solution)/shard_map/ppermute | solution.py:38
  33.9 0.8 convert_reduce_fusion
  34.7 0.8 slice_bitcast_fusion.14
  35.5 0.2 select_bitcast_fusion.1
  35.7 0.2 pad_maximum_fusion
  36.0 0.7 copy-done.3
  36.7 1.0 %collective-permute-start.9 = (bf16[96,1024]{1,0:T(8,128)(2,1)S(1)}, bf16[96,1024]{1,0:T(8,128)(2,1)S(1)}, u32[]{:S(2)}, u32[]{:S(2)}) collective-permute-start(bf16[96,1024]{1,0:T(8,128)(2,1)S(1)} %copy-done.3), channel_id=1, source_target_pairs={{0,1},{1,2},{2,3},{3,0},{4,5},{5,6},{6,7},{7,4},{8,9},{9,10},{10,1... | collective-permute-start | bytes 589832 | tf_op jit(solution)/shard_map/ppermute | solution.py:38
  37.7 1.7 %fusion.14 = f32[384,384]{1,0:T(8,128)S(1)} fusion(bf16[1,1024,1152]{2,1,0:T(8,128)(2,1)S(1)} %bitcast.97, bf16[96,1024]{1,0:T(8,128)(2,1)} %collective-permute-done.2, bf16[96,1024]{1,0:T(8,128)(2,1)} %collective-permute-done.1, bf16[96,1024]{1,0:T(8,128)(2,1)} %collective-permute-done, bf16[96,1024]{1,0:T(8,128)(2,1)S(1)} %get-tuple-element.55), kind=kOutput, calls=%fused_computation.34 | convolution fusion | flops 305135616 | bytes 2162688 | tf_op jit(solution)/shard_map/dot_general | solution.py:11
  39.4 1.7 %multiply_convert_fusion.3 = (bf16[384,384]{1,0:T(8,128)(2,1)S(1)}, f32[384,384]{1,0:T(8,128)S(1)}) fusion(f32[384,384]{1,0:T(8,128)S(1)} %fusion.14, bf16[1,1024,1152]{2,1,0:T(8,128)(2,1)S(1)} %bitcast.98, bf16[96,1024]{1,0:T(8,128)(2,1)} %collective-permute-done.2, bf16[96,1024]{1,0:T(8,128)(2,1)} %collective-permute-done.1, ...), kind=kOutput, calls=%fused_computation.40 | convolution fusion | flops 306020352 | bytes 3047424 | tf_op jit(solution)/shard_map/dot_general | solution.py:12
  41.1 0.6 convolution_convert_fusion.1
  41.8 2.5 %collective-permute-start.8 = (bf16[96,1024]{1,0:T(8,128)(2,1)S(1)}, bf16[96,1024]{1,0:T(8,128)(2,1)S(1)}, u32[]{:S(2)}, u32[]{:S(2)}) collective-permute-start(bf16[96,1024]{1,0:T(8,128)(2,1)S(1)} %get-tuple-element.52), channel_id=1, source_target_pairs={{0,1},{1,2},{2,3},{3,0},{4,5},{5,6},{6,7},{7,4},{8,9},{9,10},{10,1... | collective-permute-start | bytes 589832 | tf_op jit(solution)/shard_map/ppermute | solution.py:38
  44.3 0.9 %collective-permute-start.7 = (bf16[96,1024]{1,0:T(8,128)(2,1)S(1)}, bf16[96,1024]{1,0:T(8,128)(2,1)S(1)}, u32[]{:S(2)}, u32[]{:S(2)}) collective-permute-start(bf16[96,1024]{1,0:T(8,128)(2,1)S(1)} %get-tuple-element.53), channel_id=1, source_target_pairs={{0,2},{1,3},{2,0},{3,1},{4,6},{5,7},{6,4},{7,5},{8,10},{9,11},{10,... | collective-permute-start | bytes 589832 | tf_op jit(solution)/shard_map/ppermute | solution.py:38
  45.2 1.5 %collective-permute-start.6 = (bf16[96,1024]{1,0:T(8,128)(2,1)S(1)}, bf16[96,1024]{1,0:T(8,128)(2,1)S(1)}, u32[]{:S(2)}, u32[]{:S(2)}) collective-permute-start(bf16[96,1024]{1,0:T(8,128)(2,1)S(1)} %get-tuple-element.54), channel_id=1, source_target_pairs={{0,3},{1,0},{2,1},{3,2},{4,7},{5,4},{6,5},{7,6},{8,11},{9,8},{10,9... | collective-permute-start | bytes 589832 | tf_op jit(solution)/shard_map/ppermute | solution.py:38
  46.7 14.1 %collective-permute-done.10 = bf16[96,1024]{1,0:T(8,128)(2,1)S(1)} collective-permute-done((bf16[96,1024]{1,0:T(8,128)(2,1)}, bf16[96,1024]{1,0:T(8,128)(2,1)S(1)}, u32[]{:S(2)}, u32[]{:S(2)}) %collective-permute-start.10) | collective-permute-done | bytes 196640 | tf_op jit(solution)/shard_map/ppermute | solution.py:38
  60.9 1.6 %fusion.24 = f32[1024,384]{1,0:T(8,128)S(1)} fusion(bf16[384,384]{1,0:T(8,128)(2,1)S(1)} %get-tuple-element.65, bf16[96,1024]{1,0:T(8,128)(2,1)} %collective-permute-done.11, bf16[96,1024]{1,0:T(8,128)(2,1)S(1)} %collective-permute-done.10, bf16[96,1024]{1,0:T(8,128)(2,1)S(1)} %collective-permute-done.9, bf16[96,1024]{1,0:T(8,128)(2,1)S(1)} %copy-done.2), kind=kOutput, calls=%fused_computation.65 | convolution fusion | flops 305135616 | bytes 2654208 | tf_op jit(solution)/shard_map/dot_general | solution.py:136
  62.7 1.5 %fusion.16 = f32[384,384]{1,0:T(8,128)S(1)} fusion(bf16[1,1024,1152]{2,1,0:T(8,128)(2,1)S(1)} %bitcast.100, bf16[96,1024]{1,0:T(8,128)(2,1)} %collective-permute-done.11, bf16[96,1024]{1,0:T(8,128)(2,1)S(1)} %collective-permute-done.10, bf16[96,1024]{1,0:T(8,128)(2,1)S(1)} %collective-permute-done.9, bf16[96,1024]{1,0:T(8,128)(2,1)S(1)} %copy-done.2), kind=kOutput, calls=%fused_computation.36 | convolution fusion | flops 305135616 | bytes 2162688 | tf_op jit(solution)/shard_map/dot_general | solution.py:22
  64.2 0.7 fusion.13
  64.8 0.6 add_convert_fusion
  65.8 3.8 %collective-permute-start.12 = (bf16[96,1024]{1,0:T(8,128)(2,1)S(1)}, bf16[96,1024]{1,0:T(8,128)(2,1)S(1)}, u32[]{:S(2)}, u32[]{:S(2)}) collective-permute-start(bf16[96,1024]{1,0:T(8,128)(2,1)S(1)} %get-tuple-element.46), channel_id=1, source_target_pairs={{0,3},{1,0},{2,1},{3,2},{4,7},{5,4},{6,5},{7,6},{8,11},{9,8},{10,9... | collective-permute-start | bytes 589832 | tf_op jit(solution)/shard_map/ppermute | solution.py:38
  69.6 1.5 %collective-permute-start.16 = (f32[2,128,384]{2,1,0:T(8,128)S(1)}, f32[2,128,384]{2,1,0:T(8,128)S(1)}, u32[]{:S(2)}, u32[]{:S(2)}) collective-permute-start(f32[2,128,384]{2,1,0:T(8,128)S(1)} %select_bitcast_fusion.4), channel_id=1, source_target_pairs={{0,8},{4,12},{8,0},{12,4},{16,24},{20,28},{24,16},{28,20},{1,9},{5... | collective-permute-start | bytes 1179656 | tf_op jit(solution)/shard_map/ppermute | solution.py:72
  71.1 0.3 convolution_multiply_fusion
  71.4 1.0 %fusion.1 = bf16[128,1024]{1,0:T(8,128)(2,1)} fusion(f32[128,1024]{1,0:T(8,128)S(1)} %convolution_multiply_fusion, f32[128]{0:T(128)S(1)} %get-tuple-element.61, pred[128,2,384]{2,0,1:T(32,128)(4,1)S(1)} %get-tuple-element.64, bf16[96,1024]{1,0:T(8,128)(2,1)S(1)} %collective-permute-done.8, bf16[96,1024]{1,0:T(8,128)(2,1)S(1)} %collective-permute-done.7, ...), kind=kOutput, calls=%fused_computation.8 | convolution fusion | flops 104202240 | bytes 1622528 | tf_op jit(solution)/shard_map/dot_general | solution.py:145
  72.5 8.1 %collective-permute-done.16 = f32[2,128,384]{2,1,0:T(8,128)S(1)} collective-permute-done((f32[2,128,384]{2,1,0:T(8,128)S(1)}, f32[2,128,384]{2,1,0:T(8,128)S(1)}, u32[]{:S(2)}, u32[]{:S(2)}) %collective-permute-start.16) | collective-permute-done | bytes 393248 | tf_op jit(solution)/shard_map/ppermute | solution.py:72
  80.6 1.6 %collective-permute-start.17 = (f32[1,128,384]{2,1,0:T(8,128)S(1)}, f32[1,128,384]{2,1,0:T(8,128)S(1)}, u32[]{:S(2)}, u32[]{:S(2)}) collective-permute-start(f32[1,128,384]{2,1,0:T(8,128)S(1)} %select_bitcast_fusion.7), channel_id=1, source_target_pairs={{0,16},{4,20},{8,24},{12,28},{16,0},{20,4},{24,8},{28,12},{1,17},{... | collective-permute-start | bytes 589832 | tf_op jit(solution)/shard_map/ppermute | solution.py:72
  82.2 0.6 collective-permute-done.13
  82.8 1.0 %convolution_convert_fusion.2 = bf16[128,1024]{1,0:T(8,128)(2,1)} fusion(bf16[96,1024]{1,0:T(8,128)(2,1)S(1)} %collective-permute-done.14, bf16[96,1024]{1,0:T(8,128)(2,1)S(1)} %collective-permute-done.13, bf16[96,1024]{1,0:T(8,128)(2,1)S(1)} %collective-permute-done.12, bf16[96,1024]{1,0:T(8,128)(2,1)S(1)} %get-tuple-element.43, ...), kind=kOutput, calls=%fused_computation.9 | convolution fusion | flops 103989248 | bytes 1245184 | tf_op jit(solution)/shard_map/dot_general | solution.py:151
  83.8 2.8 %collective-permute-done.17 = f32[1,128,384]{2,1,0:T(8,128)S(1)} collective-permute-done((f32[1,128,384]{2,1,0:T(8,128)S(1)}, f32[1,128,384]{2,1,0:T(8,128)S(1)}, u32[]{:S(2)}, u32[]{:S(2)}) %collective-permute-start.17) | collective-permute-done | bytes 196640 | tf_op jit(solution)/shard_map/ppermute | solution.py:72
  86.6 0.7 fusion.23
  (55 shorter events, 1.0 us)
Async XLA Ops:
  0.6 14.3 %copy-start = (bf16[128,1024]{1,0:T(8,128)(2,1)S(1)}, bf16[128,1024]{1,0:T(8,128)(2,1)}, u32[]{:S(2)}) copy-start(bf16[128,1024]{1,0:T(8,128)(2,1)} %param.13) | copy-start | bytes 786436
  1.7 10.0 %collective-permute-start.3 = (bf16[128,1152]{1,0:T(8,128)(2,1)S(1)}, bf16[128,1152]{1,0:T(8,128)(2,1)S(1)}, u32[]{:S(2)}, u32[]{:S(2)}) collective-permute-start(bf16[128,1152]{1,0:T(8,128)(2,1)S(1)} %maximum_bitcast_fusion), channel_id=1, source_target_pairs={{0,8},{4,12},{8,0},{12,4},{16,24},{20,28},{24,16},{28,20},{1,9},{5... | collective-permute-start | bytes 884744 | tf_op jit(solution)/shard_map/ppermute | solution.py:53
  5.7 7.2 %copy-start.5 = (s32[256]{0:T(256)}, s32[256]{0:T(256)S(1)}, u32[]{:S(2)}) copy-start(s32[256]{0:T(256)S(1)} %sub.46) | copy-start | bytes 3076
  5.9 7.0 %copy-start.9 = (f32[256]{0:T(256)}, f32[256]{0:T(256)S(1)}, u32[]{:S(2)}) copy-start(f32[256]{0:T(256)S(1)} %fusion.2) | copy-start | bytes 3076
  6.2 8.8 %copy-start.4 = (s32[128,2]{0,1:T(2,128)}, s32[128,2]{0,1:T(2,128)S(1)}, u32[]{:S(2)}) copy-start(s32[128,2]{0,1:T(2,128)S(1)} %copy.20) | copy-start | bytes 3076
  12.9 7.2 %copy-start.7 = (f32[128,2]{0,1:T(2,128)S(1)}, f32[128,2]{0,1:T(2,128)}, u32[]{:S(2)}) copy-start(f32[128,2]{0,1:T(2,128)} %param.15) | copy-start | bytes 3076
  12.9 14.6 %collective-permute-start.4 = (bf16[2,128,1152]{2,1,0:T(8,128)(2,1)S(1)}, bf16[2,128,1152]{2,1,0:T(8,128)(2,1)S(1)}, u32[]{:S(2)}, u32[]{:S(2)}) collective-permute-start(bf16[2,128,1152]{2,1,0:T(8,128)(2,1)S(1)} %pad_maximum_fusion.5), channel_id=1, source_target_pairs={{0,16},{4,20},{8,24},{12,28},{16,0},{20,4},{24,8},{28,12},{1,17},{... | collective-permute-start | bytes 1769480 | tf_op jit(solution)/shard_map/ppermute | solution.py:53
  15.4 20.6 %collective-permute-start.2 = (bf16[96,1024]{1,0:T(8,128)(2,1)S(1)}, bf16[96,1024]{1,0:T(8,128)(2,1)}, u32[]{:S(2)}, u32[]{:S(2)}) collective-permute-start(bf16[96,1024]{1,0:T(8,128)(2,1)S(1)} %get-tuple-element.56), channel_id=1, source_target_pairs={{0,3},{1,0},{2,1},{3,2},{4,7},{5,4},{6,5},{7,6},{8,11},{9,8},{10,9... | collective-permute-start | bytes 589832 | tf_op jit(solution)/shard_map/ppermute | solution.py:38
  19.1 18.6 %collective-permute-start.1 = (bf16[96,1024]{1,0:T(8,128)(2,1)S(1)}, bf16[96,1024]{1,0:T(8,128)(2,1)}, u32[]{:S(2)}, u32[]{:S(2)}) collective-permute-start(bf16[96,1024]{1,0:T(8,128)(2,1)S(1)} %get-tuple-element.57), channel_id=1, source_target_pairs={{0,2},{1,3},{2,0},{3,1},{4,6},{5,7},{6,4},{7,5},{8,10},{9,11},{10,... | collective-permute-start | bytes 589832 | tf_op jit(solution)/shard_map/ppermute | solution.py:38
  19.1 18.6 %collective-permute-start = (bf16[96,1024]{1,0:T(8,128)(2,1)S(1)}, bf16[96,1024]{1,0:T(8,128)(2,1)}, u32[]{:S(2)}, u32[]{:S(2)}) collective-permute-start(bf16[96,1024]{1,0:T(8,128)(2,1)S(1)} %get-tuple-element.58), channel_id=1, source_target_pairs={{0,1},{1,2},{2,3},{3,0},{4,5},{5,6},{6,7},{7,4},{8,9},{9,10},{10,1... | collective-permute-start | bytes 589832 | tf_op jit(solution)/shard_map/ppermute | solution.py:38
  27.6 1.2 %copy-start.6 = (s32[256]{0:T(256)S(1)}, s32[256]{0:T(256)}, u32[]{:S(2)}) copy-start(s32[256]{0:T(256)} %copy-done.5) | copy-start | bytes 3076
  27.6 1.2 %copy-start.10 = (f32[256]{0:T(256)S(1)}, f32[256]{0:T(256)}, u32[]{:S(2)}) copy-start(f32[256]{0:T(256)} %copy-done.9) | copy-start | bytes 3076
  27.7 1.2 %copy-start.8 = (f32[256]{0:T(256)S(1)}, f32[256]{0:T(256)}, u32[]{:S(2)}) copy-start(f32[256]{0:T(256)} %broadcast_in_dim.48) | copy-start | bytes 3076
  27.7 1.4 %copy-start.1 = (bf16[128,1024]{1,0:T(8,128)(2,1)S(1)}, bf16[128,1024]{1,0:T(8,128)(2,1)}, u32[]{:S(2)}) copy-start(bf16[128,1024]{1,0:T(8,128)(2,1)} %param.19) | copy-start | bytes 786436
  28.8 6.6 %collective-permute-start.5 = (bf16[2,2,128,1152]{3,2,1,0:T(8,128)(2,1)}, bf16[2,2,128,1152]{3,2,1,0:T(8,128)(2,1)S(1)}, u32[]{:S(2)}, u32[]{:S(2)}) collective-permute-start(bf16[2,2,128,1152]{3,2,1,0:T(8,128)(2,1)} %pad_maximum_fusion.1), channel_id=1, source_target_pairs={{0,4},{4,0},{8,12},{12,8},{16,20},{20,16},{24,28},{28,24},{1,5},{5... | collective-permute-start | bytes 3538952 | tf_op jit(solution)/shard_map/ppermute | solution.py:53
  30.4 14.9 %collective-permute-start.11 = (bf16[96,1024]{1,0:T(8,128)(2,1)}, bf16[96,1024]{1,0:T(8,128)(2,1)}, u32[]{:S(2)}, u32[]{:S(2)}) collective-permute-start(bf16[96,1024]{1,0:T(8,128)(2,1)} %get-tuple-element.48), channel_id=1, source_target_pairs={{0,3},{1,0},{2,1},{3,2},{4,7},{5,4},{6,5},{7,6},{8,11},{9,8},{10,9... | collective-permute-start | bytes 589832 | tf_op jit(solution)/shard_map/ppermute | solution.py:38
  35.5 25.4 %collective-permute-start.10 = (bf16[96,1024]{1,0:T(8,128)(2,1)}, bf16[96,1024]{1,0:T(8,128)(2,1)S(1)}, u32[]{:S(2)}, u32[]{:S(2)}) collective-permute-start(bf16[96,1024]{1,0:T(8,128)(2,1)} %get-tuple-element.49), channel_id=1, source_target_pairs={{0,2},{1,3},{2,0},{3,1},{4,6},{5,7},{6,4},{7,5},{8,10},{9,11},{10,... | collective-permute-start | bytes 589832 | tf_op jit(solution)/shard_map/ppermute | solution.py:38
  35.7 0.9 %copy-start.3 = (bf16[96,1024]{1,0:T(8,128)(2,1)S(1)}, bf16[96,1024]{1,0:T(8,128)(2,1)}, u32[]{:S(2)}) copy-start(bf16[96,1024]{1,0:T(8,128)(2,1)} %get-tuple-element.50) | copy-start | bytes 589828
  36.7 24.2 %collective-permute-start.9 = (bf16[96,1024]{1,0:T(8,128)(2,1)S(1)}, bf16[96,1024]{1,0:T(8,128)(2,1)S(1)}, u32[]{:S(2)}, u32[]{:S(2)}) collective-permute-start(bf16[96,1024]{1,0:T(8,128)(2,1)S(1)} %copy-done.3), channel_id=1, source_target_pairs={{0,1},{1,2},{2,3},{3,0},{4,5},{5,6},{6,7},{7,4},{8,9},{9,10},{10,1... | collective-permute-start | bytes 589832 | tf_op jit(solution)/shard_map/ppermute | solution.py:38
  41.1 19.8 %copy-start.2 = (bf16[96,1024]{1,0:T(8,128)(2,1)S(1)}, bf16[96,1024]{1,0:T(8,128)(2,1)}, u32[]{:S(2)}) copy-start(bf16[96,1024]{1,0:T(8,128)(2,1)} %get-tuple-element.47) | copy-start | bytes 589828
  41.8 24.1 %collective-permute-start.8 = (bf16[96,1024]{1,0:T(8,128)(2,1)S(1)}, bf16[96,1024]{1,0:T(8,128)(2,1)S(1)}, u32[]{:S(2)}, u32[]{:S(2)}) collective-permute-start(bf16[96,1024]{1,0:T(8,128)(2,1)S(1)} %get-tuple-element.52), channel_id=1, source_target_pairs={{0,1},{1,2},{2,3},{3,0},{4,5},{5,6},{6,7},{7,4},{8,9},{9,10},{10,1... | collective-permute-start | bytes 589832 | tf_op jit(solution)/shard_map/ppermute | solution.py:38
  44.3 25.3 %collective-permute-start.7 = (bf16[96,1024]{1,0:T(8,128)(2,1)S(1)}, bf16[96,1024]{1,0:T(8,128)(2,1)S(1)}, u32[]{:S(2)}, u32[]{:S(2)}) collective-permute-start(bf16[96,1024]{1,0:T(8,128)(2,1)S(1)} %get-tuple-element.53), channel_id=1, source_target_pairs={{0,2},{1,3},{2,0},{3,1},{4,6},{5,7},{6,4},{7,5},{8,10},{9,11},{10,... | collective-permute-start | bytes 589832 | tf_op jit(solution)/shard_map/ppermute | solution.py:38
  45.2 25.9 %collective-permute-start.6 = (bf16[96,1024]{1,0:T(8,128)(2,1)S(1)}, bf16[96,1024]{1,0:T(8,128)(2,1)S(1)}, u32[]{:S(2)}, u32[]{:S(2)}) collective-permute-start(bf16[96,1024]{1,0:T(8,128)(2,1)S(1)} %get-tuple-element.54), channel_id=1, source_target_pairs={{0,3},{1,0},{2,1},{3,2},{4,7},{5,4},{6,5},{7,6},{8,11},{9,8},{10,9... | collective-permute-start | bytes 589832 | tf_op jit(solution)/shard_map/ppermute | solution.py:38
  62.6 3.0 %collective-permute-start.15 = (f32[4,128,384]{2,1,0:T(8,128)S(1)}, f32[4,128,384]{2,1,0:T(8,128)S(1)}, u32[]{:S(2)}, u32[]{:S(2)}) collective-permute-start(f32[4,128,384]{2,1,0:T(8,128)S(1)} %fusion.10), channel_id=1, source_target_pairs={{0,4},{4,0},{8,12},{12,8},{16,20},{20,16},{24,28},{28,24},{1,5},{5... | collective-permute-start | bytes 2359304 | tf_op jit(solution)/shard_map/ppermute | solution.py:72
  65.5 16.7 %collective-permute-start.14 = (bf16[96,1024]{1,0:T(8,128)(2,1)S(1)}, bf16[96,1024]{1,0:T(8,128)(2,1)S(1)}, u32[]{:S(2)}, u32[]{:S(2)}) collective-permute-start(bf16[96,1024]{1,0:T(8,128)(2,1)S(1)} %get-tuple-element.44), channel_id=1, source_target_pairs={{0,1},{1,2},{2,3},{3,0},{4,5},{5,6},{6,7},{7,4},{8,9},{9,10},{10,1... | collective-permute-start | bytes 589832 | tf_op jit(solution)/shard_map/ppermute | solution.py:38
  65.6 17.2 %collective-permute-start.13 = (bf16[96,1024]{1,0:T(8,128)(2,1)S(1)}, bf16[96,1024]{1,0:T(8,128)(2,1)S(1)}, u32[]{:S(2)}, u32[]{:S(2)}) collective-permute-start(bf16[96,1024]{1,0:T(8,128)(2,1)S(1)} %get-tuple-element.45), channel_id=1, source_target_pairs={{0,2},{1,3},{2,0},{3,1},{4,6},{5,7},{6,4},{7,5},{8,10},{9,11},{10,... | collective-permute-start | bytes 589832 | tf_op jit(solution)/shard_map/ppermute | solution.py:38
  65.8 17.0 %collective-permute-start.12 = (bf16[96,1024]{1,0:T(8,128)(2,1)S(1)}, bf16[96,1024]{1,0:T(8,128)(2,1)S(1)}, u32[]{:S(2)}, u32[]{:S(2)}) collective-permute-start(bf16[96,1024]{1,0:T(8,128)(2,1)S(1)} %get-tuple-element.46), channel_id=1, source_target_pairs={{0,3},{1,0},{2,1},{3,2},{4,7},{5,4},{6,5},{7,6},{8,11},{9,8},{10,9... | collective-permute-start | bytes 589832 | tf_op jit(solution)/shard_map/ppermute | solution.py:38
  69.6 11.0 %collective-permute-start.16 = (f32[2,128,384]{2,1,0:T(8,128)S(1)}, f32[2,128,384]{2,1,0:T(8,128)S(1)}, u32[]{:S(2)}, u32[]{:S(2)}) collective-permute-start(f32[2,128,384]{2,1,0:T(8,128)S(1)} %select_bitcast_fusion.4), channel_id=1, source_target_pairs={{0,8},{4,12},{8,0},{12,4},{16,24},{20,28},{24,16},{28,20},{1,9},{5... | collective-permute-start | bytes 1179656 | tf_op jit(solution)/shard_map/ppermute | solution.py:72
  80.6 6.0 %collective-permute-start.17 = (f32[1,128,384]{2,1,0:T(8,128)S(1)}, f32[1,128,384]{2,1,0:T(8,128)S(1)}, u32[]{:S(2)}, u32[]{:S(2)}) collective-permute-start(f32[1,128,384]{2,1,0:T(8,128)S(1)} %select_bitcast_fusion.7), channel_id=1, source_target_pairs={{0,16},{4,20},{8,24},{12,28},{16,0},{20,4},{24,8},{28,12},{1,17},{... | collective-permute-start | bytes 589832 | tf_op jit(solution)/shard_map/ppermute | solution.py:72

commit v10 on v9

--- a/solution.py
+++ b/solution.py
@@ -39,7 +39,7 @@
     return got
 
 
-def all_gather_dp(block, n_dp):
+def all_gather_dp(block, n_dp, hold=None):
     me = lax.axis_index("dp")
     bits = []
     bit = n_dp // 2
@@ -49,7 +49,9 @@
     if len(bits) >= 3:
         bits[0], bits[1] = bits[1], bits[0]
     work = block
-    for bit in bits:
+    for step, bit in enumerate(bits):
+        if step == 1 and hold is not None:
+            work, _ = lax.optimization_barrier((work, hold))
         recv = lax.ppermute(work, "dp", [(i, i ^ bit) for i in range(n_dp)])
         upper = (me // bit) % 2 == 1
         work = jnp.stack([jnp.where(upper, recv, work), jnp.where(upper, work, recv)], axis=0)
@@ -119,7 +121,7 @@
     )
     packed = jnp.concatenate([w_gate, w_up, w_down], axis=2)
     packed = jnp.transpose(packed, (1, 0, 2)).reshape(shard_d, local_count * 3 * ff_width)
-    full = all_gather_dp(packed, n_dp).reshape(width, local_count * 3 * ff_width)
+    full = all_gather_dp(packed, n_dp, send_grads).reshape(width, local_count * 3 * ff_width)
     full = jnp.transpose(full.reshape(width, local_count, 3 * ff_width), (1, 0, 2))
     gate_full = full[:, :, :ff_width]
     up_full = full[:, :, ff_width : 2 * ff_width]

time: 87.6 us -> 87.6 us (level)
  no operation moved by 1% of the time
where the time goes in v10:
time: 87.6 us; the launch traced here: 87.3 us
  waiting for transfers between devices  37.8 us (43%)
  starting transfers between devices  26.1 us (30%)
  matrix products  11.8 us (13%)
  other arithmetic  6.08 us (7%)
  local copies, waits for them, and re-layouts  4.47 us (5%)
  between operations  1.05 us (1%)
    ppermute x12, starting transfers between devices, shift_send(): got.append(lax.ppermute(blocks[step], 'expert', pairs))  18.1 us
    ppermute x12, waiting for transfers between devices, shift_send(): got.append(lax.ppermute(blocks[step], 'expert', pairs))  14.7 us
    ppermute x3, waiting for transfers between devices, all_gather_dp(): recv = lax.ppermute(work, 'dp', [(i, i ^ bit) for i in range(n_dp)])  12.2 us
    ppermute x3, waiting for transfers between devices, reduce_scatter_dp(): work = keep + lax.ppermute(give, 'dp', pairs)  10.9 us
    ppermute x3, starting transfers between devices, all_gather_dp(): recv = lax.ppermute(work, 'dp', [(i, i ^ bit) for i in range(n_dp)])  4.87 us
    ppermute x3, starting transfers between devices, reduce_scatter_dp(): work = keep + lax.ppermute(give, 'dp', pairs)  3.15 us
    another operation x6, other arithmetic, all_gather_dp(): jnp.stack([jnp.where(upper, recv, work), jnp.where(upper, work, recv)], a...  2.92 us
  transfers between devices with their start and end apart: 18, of which 6 were waited for; matrix products, arithmetic and copies ran while one was open for 21% of the time, Pallas kernels for 0%

profile of v10, /device:TPU:0, one launch (start us, length us, event | category | flops | bytes accessed | tf_op | source)
XLA Modules:
  0.0 87.3 jit_solution(14601446134261698276)
XLA Ops:
  0.6 1.1 %maximum_bitcast_fusion = bf16[128,1152]{1,0:T(8,128)(2,1)S(1)} fusion(bf16[1,128,384]{2,1,0:T(8,128)(2,1)} %param.18, bf16[1,128,384]{2,1,0:T(8,128)(2,1)} %param.17, bf16[1,128,384]{2,1,0:T(8,128)(2,1)} %param.16), kind=kLoop, calls=%fused_computation.53 | loop fusion | flops 884736 | bytes 589824 | tf_op jit(solution)/shard_map/reshape;transpose | solution.py:123
  1.7 3.0 %collective-permute-start.3 = (bf16[128,1152]{1,0:T(8,128)(2,1)S(1)}, bf16[128,1152]{1,0:T(8,128)(2,1)S(1)}, u32[]{:S(2)}, u32[]{:S(2)}) collective-permute-start(bf16[128,1152]{1,0:T(8,128)(2,1)S(1)} %maximum_bitcast_fusion), channel_id=1, source_target_pairs={{0,8},{4,12},{8,0},{12,4},{16,24},{20,28},{24,16},{28,20},{1,9},{5... | collective-permute-start | bytes 884744 | tf_op jit(solution)/shard_map/ppermute | solution.py:55
  4.7 0.8 copy.19
  5.5 0.1 sub.46
  5.7 0.2 fusion.2
  5.9 0.1 convert_element_type.57
  6.2 5.6 %collective-permute-done.3 = bf16[128,1152]{1,0:T(8,128)(2,1)S(1)} collective-permute-done((bf16[128,1152]{1,0:T(8,128)(2,1)S(1)}, bf16[128,1152]{1,0:T(8,128)(2,1)S(1)}, u32[]{:S(2)}, u32[]{:S(2)}) %collective-permute-start.3) | collective-permute-done | bytes 294944 | tf_op jit(solution)/shard_map/ppermute | solution.py:55
  11.7 1.1 %select_bitcast_fusion.6 = (bf16[1,128,1152]{2,1,0:T(8,128)(2,1)S(1)}, bf16[1,128,1152]{2,1,0:T(8,128)(2,1)S(1)}) fusion(bf16[128,1152]{1,0:T(8,128)(2,1)S(1)} %collective-permute-done.3, pred[]{:T(512)S(6)} %eq.60, bf16[1,128,384]{2,1,0:T(8,128)(2,1)} %param.18, bf16[1,128,384]{2,1,0:T(8,128)(2,1)} %param.17, bf16[1,128,384]{2,1,0:T(8,128)(2,1)} %param.16), kind=kLoop, calls=%fused_computation.57 | loop fusion | flops 1179648 | bytes 1179649 | tf_op jit(solution)/shard_map/stack | solution.py:57
  12.9 1.8 %collective-permute-start.4 = (bf16[2,128,1152]{2,1,0:T(8,128)(2,1)S(1)}, bf16[2,128,1152]{2,1,0:T(8,128)(2,1)S(1)}, u32[]{:S(2)}, u32[]{:S(2)}) collective-permute-start(bf16[2,128,1152]{2,1,0:T(8,128)(2,1)S(1)} %pad_maximum_fusion.5), channel_id=1, source_target_pairs={{0,16},{4,20},{8,24},{12,28},{16,0},{20,4},{24,8},{28,12},{1,17},{... | collective-permute-start | bytes 1769480 | tf_op jit(solution)/shard_map/ppermute | solution.py:55
  14.8 0.1 fusion.22
  14.9 0.4 convolution_convert_fusion
  15.4 3.7 %collective-permute-start.2 = (bf16[96,1024]{1,0:T(8,128)(2,1)S(1)}, bf16[96,1024]{1,0:T(8,128)(2,1)}, u32[]{:S(2)}, u32[]{:S(2)}) collective-permute-start(bf16[96,1024]{1,0:T(8,128)(2,1)S(1)} %get-tuple-element.56), channel_id=1, source_target_pairs={{0,3},{1,0},{2,1},{3,2},{4,7},{5,4},{6,5},{7,6},{8,11},{9,8},{10,9... | collective-permute-start | bytes 589832 | tf_op jit(solution)/shard_map/ppermute | solution.py:38
  19.1 1.0 %collective-permute-start = (bf16[96,1024]{1,0:T(8,128)(2,1)S(1)}, bf16[96,1024]{1,0:T(8,128)(2,1)}, u32[]{:S(2)}, u32[]{:S(2)}) collective-permute-start(bf16[96,1024]{1,0:T(8,128)(2,1)S(1)} %get-tuple-element.58), channel_id=1, source_target_pairs={{0,1},{1,2},{2,3},{3,0},{4,5},{5,6},{6,7},{7,4},{8,9},{9,10},{10,1... | collective-permute-start | bytes 589832 | tf_op jit(solution)/shard_map/ppermute | solution.py:38
  20.1 0.1 copy.22
  20.2 0.7 broadcast_in_dim.48
  20.9 6.6 %collective-permute-done.4 = bf16[2,128,1152]{2,1,0:T(8,128)(2,1)S(1)} collective-permute-done((bf16[2,128,1152]{2,1,0:T(8,128)(2,1)S(1)}, bf16[2,128,1152]{2,1,0:T(8,128)(2,1)S(1)}, u32[]{:S(2)}, u32[]{:S(2)}) %collective-permute-start.4) | collective-permute-done | bytes 589856 | tf_op jit(solution)/shard_map/ppermute | solution.py:55
  27.7 1.2 %pad_maximum_fusion.1 = bf16[2,2,128,1152]{3,2,1,0:T(8,128)(2,1)} fusion(bf16[1,2,128,1152]{3,2,1,0:T(8,128)(2,1)S(1)} %get-tuple-element.42, bf16[1,2,128,1152]{3,2,1,0:T(8,128)(2,1)S(1)} %get-tuple-element.41), kind=kLoop, calls=%fused_computation.10 | loop fusion | flops 589824 | bytes 2359296 | tf_op jit(solution)/shard_map/stack | solution.py:57
  28.9 0.1 select_reduce_fusion
  29.0 0.4 multiply_convert_fusion
  29.5 0.9 %fusion.42 = (bf16[96,1024]{1,0:T(8,128)(2,1)}, bf16[96,1024]{1,0:T(8,128)(2,1)}, bf16[96,1024]{1,0:T(8,128)(2,1)}, bf16[96,1024]{1,0:T(8,128)(2,1)}) fusion(bf16[384,1024]{1,0:T(8,128)(2,1)S(1)} %multiply_convert_fusion), kind=kLoop, calls=%fused_computation.94 | loop fusion | bytes 1572864 | tf_op jit(solution)/shard_map/slice | solution.py:130
  30.3 3.6 %collective-permute-start.11 = (bf16[96,1024]{1,0:T(8,128)(2,1)}, bf16[96,1024]{1,0:T(8,128)(2,1)}, u32[]{:S(2)}, u32[]{:S(2)}) collective-permute-start(bf16[96,1024]{1,0:T(8,128)(2,1)} %get-tuple-element.48), channel_id=1, source_target_pairs={{0,3},{1,0},{2,1},{3,2},{4,7},{5,4},{6,5},{7,6},{8,11},{9,8},{10,9... | collective-permute-start | bytes 589832 | tf_op jit(solution)/shard_map/ppermute | solution.py:38
  33.9 0.8 convert_reduce_fusion
  34.7 0.8 slice_bitcast_fusion.14
  35.5 0.2 select_bitcast_fusion.1
  35.7 0.2 pad_maximum_fusion
  36.0 0.7 copy-done.3
  36.7 1.0 %collective-permute-start.9 = (bf16[96,1024]{1,0:T(8,128)(2,1)S(1)}, bf16[96,1024]{1,0:T(8,128)(2,1)S(1)}, u32[]{:S(2)}, u32[]{:S(2)}) collective-permute-start(bf16[96,1024]{1,0:T(8,128)(2,1)S(1)} %copy-done.3), channel_id=1, source_target_pairs={{0,1},{1,2},{2,3},{3,0},{4,5},{5,6},{6,7},{7,4},{8,9},{9,10},{10,1... | collective-permute-start | bytes 589832 | tf_op jit(solution)/shard_map/ppermute | solution.py:38
  37.7 1.7 %fusion.14 = f32[384,384]{1,0:T(8,128)S(1)} fusion(bf16[1,1024,1152]{2,1,0:T(8,128)(2,1)S(1)} %bitcast.97, bf16[96,1024]{1,0:T(8,128)(2,1)} %collective-permute-done.2, bf16[96,1024]{1,0:T(8,128)(2,1)} %collective-permute-done.1, bf16[96,1024]{1,0:T(8,128)(2,1)} %collective-permute-done, bf16[96,1024]{1,0:T(8,128)(2,1)S(1)} %get-tuple-element.55), kind=kOutput, calls=%fused_computation.34 | convolution fusion | flops 305135616 | bytes 2162688 | tf_op jit(solution)/shard_map/dot_general | solution.py:11
  39.4 1.7 %multiply_convert_fusion.3 = (bf16[384,384]{1,0:T(8,128)(2,1)S(1)}, f32[384,384]{1,0:T(8,128)S(1)}) fusion(f32[384,384]{1,0:T(8,128)S(1)} %fusion.14, bf16[1,1024,1152]{2,1,0:T(8,128)(2,1)S(1)} %bitcast.98, bf16[96,1024]{1,0:T(8,128)(2,1)} %collective-permute-done.2, bf16[96,1024]{1,0:T(8,128)(2,1)} %collective-permute-done.1, ...), kind=kOutput, calls=%fused_computation.40 | convolution fusion | flops 306020352 | bytes 3047424 | tf_op jit(solution)/shard_map/dot_general | solution.py:12
  41.1 0.6 convolution_convert_fusion.1
  41.8 2.5 %collective-permute-start.8 = (bf16[96,1024]{1,0:T(8,128)(2,1)S(1)}, bf16[96,1024]{1,0:T(8,128)(2,1)S(1)}, u32[]{:S(2)}, u32[]{:S(2)}) collective-permute-start(bf16[96,1024]{1,0:T(8,128)(2,1)S(1)} %get-tuple-element.52), channel_id=1, source_target_pairs={{0,1},{1,2},{2,3},{3,0},{4,5},{5,6},{6,7},{7,4},{8,9},{9,10},{10,1... | collective-permute-start | bytes 589832 | tf_op jit(solution)/shard_map/ppermute | solution.py:38
  44.3 0.9 %collective-permute-start.7 = (bf16[96,1024]{1,0:T(8,128)(2,1)S(1)}, bf16[96,1024]{1,0:T(8,128)(2,1)S(1)}, u32[]{:S(2)}, u32[]{:S(2)}) collective-permute-start(bf16[96,1024]{1,0:T(8,128)(2,1)S(1)} %get-tuple-element.53), channel_id=1, source_target_pairs={{0,2},{1,3},{2,0},{3,1},{4,6},{5,7},{6,4},{7,5},{8,10},{9,11},{10,... | collective-permute-start | bytes 589832 | tf_op jit(solution)/shard_map/ppermute | solution.py:38
  45.2 1.5 %collective-permute-start.6 = (bf16[96,1024]{1,0:T(8,128)(2,1)S(1)}, bf16[96,1024]{1,0:T(8,128)(2,1)S(1)}, u32[]{:S(2)}, u32[]{:S(2)}) collective-permute-start(bf16[96,1024]{1,0:T(8,128)(2,1)S(1)} %get-tuple-element.54), channel_id=1, source_target_pairs={{0,3},{1,0},{2,1},{3,2},{4,7},{5,4},{6,5},{7,6},{8,11},{9,8},{10,9... | collective-permute-start | bytes 589832 | tf_op jit(solution)/shard_map/ppermute | solution.py:38
  46.7 14.1 %collective-permute-done.10 = bf16[96,1024]{1,0:T(8,128)(2,1)S(1)} collective-permute-done((bf16[96,1024]{1,0:T(8,128)(2,1)}, bf16[96,1024]{1,0:T(8,128)(2,1)S(1)}, u32[]{:S(2)}, u32[]{:S(2)}) %collective-permute-start.10) | collective-permute-done | bytes 196640 | tf_op jit(solution)/shard_map/ppermute | solution.py:38
  60.9 1.6 %fusion.24 = f32[1024,384]{1,0:T(8,128)S(1)} fusion(bf16[384,384]{1,0:T(8,128)(2,1)S(1)} %get-tuple-element.65, bf16[96,1024]{1,0:T(8,128)(2,1)} %collective-permute-done.11, bf16[96,1024]{1,0:T(8,128)(2,1)S(1)} %collective-permute-done.10, bf16[96,1024]{1,0:T(8,128)(2,1)S(1)} %collective-permute-done.9, bf16[96,1024]{1,0:T(8,128)(2,1)S(1)} %copy-done.2), kind=kOutput, calls=%fused_computation.65 | convolution fusion | flops 305135616 | bytes 2654208 | tf_op jit(solution)/shard_map/dot_general | solution.py:138
  62.6 1.5 %fusion.16 = f32[384,384]{1,0:T(8,128)S(1)} fusion(bf16[1,1024,1152]{2,1,0:T(8,128)(2,1)S(1)} %bitcast.100, bf16[96,1024]{1,0:T(8,128)(2,1)} %collective-permute-done.11, bf16[96,1024]{1,0:T(8,128)(2,1)S(1)} %collective-permute-done.10, bf16[96,1024]{1,0:T(8,128)(2,1)S(1)} %collective-permute-done.9, bf16[96,1024]{1,0:T(8,128)(2,1)S(1)} %copy-done.2), kind=kOutput, calls=%fused_computation.36 | convolution fusion | flops 305135616 | bytes 2162688 | tf_op jit(solution)/shard_map/dot_general | solution.py:22
  64.2 0.7 fusion.13
  64.8 0.6 add_convert_fusion
  65.8 3.8 %collective-permute-start.12 = (bf16[96,1024]{1,0:T(8,128)(2,1)S(1)}, bf16[96,1024]{1,0:T(8,128)(2,1)S(1)}, u32[]{:S(2)}, u32[]{:S(2)}) collective-permute-start(bf16[96,1024]{1,0:T(8,128)(2,1)S(1)} %get-tuple-element.46), channel_id=1, source_target_pairs={{0,3},{1,0},{2,1},{3,2},{4,7},{5,4},{6,5},{7,6},{8,11},{9,8},{10,9... | collective-permute-start | bytes 589832 | tf_op jit(solution)/shard_map/ppermute | solution.py:38
  69.6 1.5 %collective-permute-start.16 = (f32[2,128,384]{2,1,0:T(8,128)S(1)}, f32[2,128,384]{2,1,0:T(8,128)S(1)}, u32[]{:S(2)}, u32[]{:S(2)}) collective-permute-start(f32[2,128,384]{2,1,0:T(8,128)S(1)} %select_bitcast_fusion.4), channel_id=1, source_target_pairs={{0,8},{4,12},{8,0},{12,4},{16,24},{20,28},{24,16},{28,20},{1,9},{5... | collective-permute-start | bytes 1179656 | tf_op jit(solution)/shard_map/ppermute | solution.py:74
  71.1 0.3 convolution_multiply_fusion
  71.4 1.0 %fusion.1 = bf16[128,1024]{1,0:T(8,128)(2,1)} fusion(f32[128,1024]{1,0:T(8,128)S(1)} %convolution_multiply_fusion, f32[128]{0:T(128)S(1)} %get-tuple-element.61, pred[128,2,384]{2,0,1:T(32,128)(4,1)S(1)} %get-tuple-element.64, bf16[96,1024]{1,0:T(8,128)(2,1)S(1)} %collective-permute-done.8, bf16[96,1024]{1,0:T(8,128)(2,1)S(1)} %collective-permute-done.7, ...), kind=kOutput, calls=%fused_computation.8 | convolution fusion | flops 104202240 | bytes 1622528 | tf_op jit(solution)/shard_map/dot_general | solution.py:147
  72.5 8.1 %collective-permute-done.16 = f32[2,128,384]{2,1,0:T(8,128)S(1)} collective-permute-done((f32[2,128,384]{2,1,0:T(8,128)S(1)}, f32[2,128,384]{2,1,0:T(8,128)S(1)}, u32[]{:S(2)}, u32[]{:S(2)}) %collective-permute-start.16) | collective-permute-done | bytes 393248 | tf_op jit(solution)/shard_map/ppermute | solution.py:74
  80.6 1.6 %collective-permute-start.17 = (f32[1,128,384]{2,1,0:T(8,128)S(1)}, f32[1,128,384]{2,1,0:T(8,128)S(1)}, u32[]{:S(2)}, u32[]{:S(2)}) collective-permute-start(f32[1,128,384]{2,1,0:T(8,128)S(1)} %select_bitcast_fusion.7), channel_id=1, source_target_pairs={{0,16},{4,20},{8,24},{12,28},{16,0},{20,4},{24,8},{28,12},{1,17},{... | collective-permute-start | bytes 589832 | tf_op jit(solution)/shard_map/ppermute | solution.py:74
  82.2 0.6 collective-permute-done.13
  82.8 1.0 %convolution_convert_fusion.2 = bf16[128,1024]{1,0:T(8,128)(2,1)} fusion(bf16[96,1024]{1,0:T(8,128)(2,1)S(1)} %collective-permute-done.14, bf16[96,1024]{1,0:T(8,128)(2,1)S(1)} %collective-permute-done.13, bf16[96,1024]{1,0:T(8,128)(2,1)S(1)} %collective-permute-done.12, bf16[96,1024]{1,0:T(8,128)(2,1)S(1)} %get-tuple-element.43, ...), kind=kOutput, calls=%fused_computation.9 | convolution fusion | flops 103989248 | bytes 1245184 | tf_op jit(solution)/shard_map/dot_general | solution.py:153
  83.8 2.8 %collective-permute-done.17 = f32[1,128,384]{2,1,0:T(8,128)S(1)} collective-permute-done((f32[1,128,384]{2,1,0:T(8,128)S(1)}, f32[1,128,384]{2,1,0:T(8,128)S(1)}, u32[]{:S(2)}, u32[]{:S(2)}) %collective-permute-start.17) | collective-permute-done | bytes 196640 | tf_op jit(solution)/shard_map/ppermute | solution.py:74
  86.6 0.7 fusion.23
  (55 shorter events, 1.0 us)
Async XLA Ops:
  0.6 14.3 %copy-start = (bf16[128,1024]{1,0:T(8,128)(2,1)S(1)}, bf16[128,1024]{1,0:T(8,128)(2,1)}, u32[]{:S(2)}) copy-start(bf16[128,1024]{1,0:T(8,128)(2,1)} %param.13) | copy-start | bytes 786436
  1.7 10.0 %collective-permute-start.3 = (bf16[128,1152]{1,0:T(8,128)(2,1)S(1)}, bf16[128,1152]{1,0:T(8,128)(2,1)S(1)}, u32[]{:S(2)}, u32[]{:S(2)}) collective-permute-start(bf16[128,1152]{1,0:T(8,128)(2,1)S(1)} %maximum_bitcast_fusion), channel_id=1, source_target_pairs={{0,8},{4,12},{8,0},{12,4},{16,24},{20,28},{24,16},{28,20},{1,9},{5... | collective-permute-start | bytes 884744 | tf_op jit(solution)/shard_map/ppermute | solution.py:55
  5.7 7.2 %copy-start.5 = (s32[256]{0:T(256)}, s32[256]{0:T(256)S(1)}, u32[]{:S(2)}) copy-start(s32[256]{0:T(256)S(1)} %sub.46) | copy-start | bytes 3076
  5.9 7.0 %copy-start.9 = (f32[256]{0:T(256)}, f32[256]{0:T(256)S(1)}, u32[]{:S(2)}) copy-start(f32[256]{0:T(256)S(1)} %fusion.2) | copy-start | bytes 3076
  6.2 8.8 %copy-start.4 = (s32[128,2]{0,1:T(2,128)}, s32[128,2]{0,1:T(2,128)S(1)}, u32[]{:S(2)}) copy-start(s32[128,2]{0,1:T(2,128)S(1)} %copy.20) | copy-start | bytes 3076
  12.9 7.2 %copy-start.7 = (f32[128,2]{0,1:T(2,128)S(1)}, f32[128,2]{0,1:T(2,128)}, u32[]{:S(2)}) copy-start(f32[128,2]{0,1:T(2,128)} %param.15) | copy-start | bytes 3076
  12.9 14.6 %collective-permute-start.4 = (bf16[2,128,1152]{2,1,0:T(8,128)(2,1)S(1)}, bf16[2,128,1152]{2,1,0:T(8,128)(2,1)S(1)}, u32[]{:S(2)}, u32[]{:S(2)}) collective-permute-start(bf16[2,128,1152]{2,1,0:T(8,128)(2,1)S(1)} %pad_maximum_fusion.5), channel_id=1, source_target_pairs={{0,16},{4,20},{8,24},{12,28},{16,0},{20,4},{24,8},{28,12},{1,17},{... | collective-permute-start | bytes 1769480 | tf_op jit(solution)/shard_map/ppermute | solution.py:55
  15.4 20.6 %collective-permute-start.2 = (bf16[96,1024]{1,0:T(8,128)(2,1)S(1)}, bf16[96,1024]{1,0:T(8,128)(2,1)}, u32[]{:S(2)}, u32[]{:S(2)}) collective-permute-start(bf16[96,1024]{1,0:T(8,128)(2,1)S(1)} %get-tuple-element.56), channel_id=1, source_target_pairs={{0,3},{1,0},{2,1},{3,2},{4,7},{5,4},{6,5},{7,6},{8,11},{9,8},{10,9... | collective-permute-start | bytes 589832 | tf_op jit(solution)/shard_map/ppermute | solution.py:38
  19.1 18.6 %collective-permute-start.1 = (bf16[96,1024]{1,0:T(8,128)(2,1)S(1)}, bf16[96,1024]{1,0:T(8,128)(2,1)}, u32[]{:S(2)}, u32[]{:S(2)}) collective-permute-start(bf16[96,1024]{1,0:T(8,128)(2,1)S(1)} %get-tuple-element.57), channel_id=1, source_target_pairs={{0,2},{1,3},{2,0},{3,1},{4,6},{5,7},{6,4},{7,5},{8,10},{9,11},{10,... | collective-permute-start | bytes 589832 | tf_op jit(solution)/shard_map/ppermute | solution.py:38
  19.1 18.6 %collective-permute-start = (bf16[96,1024]{1,0:T(8,128)(2,1)S(1)}, bf16[96,1024]{1,0:T(8,128)(2,1)}, u32[]{:S(2)}, u32[]{:S(2)}) collective-permute-start(bf16[96,1024]{1,0:T(8,128)(2,1)S(1)} %get-tuple-element.58), channel_id=1, source_target_pairs={{0,1},{1,2},{2,3},{3,0},{4,5},{5,6},{6,7},{7,4},{8,9},{9,10},{10,1... | collective-permute-start | bytes 589832 | tf_op jit(solution)/shard_map/ppermute | solution.py:38
  27.6 1.2 %copy-start.6 = (s32[256]{0:T(256)S(1)}, s32[256]{0:T(256)}, u32[]{:S(2)}) copy-start(s32[256]{0:T(256)} %copy-done.5) | copy-start | bytes 3076
  27.6 1.2 %copy-start.10 = (f32[256]{0:T(256)S(1)}, f32[256]{0:T(256)}, u32[]{:S(2)}) copy-start(f32[256]{0:T(256)} %copy-done.9) | copy-start | bytes 3076
  27.6 1.2 %copy-start.8 = (f32[256]{0:T(256)S(1)}, f32[256]{0:T(256)}, u32[]{:S(2)}) copy-start(f32[256]{0:T(256)} %broadcast_in_dim.48) | copy-start | bytes 3076
  27.6 1.4 %copy-start.1 = (bf16[128,1024]{1,0:T(8,128)(2,1)S(1)}, bf16[128,1024]{1,0:T(8,128)(2,1)}, u32[]{:S(2)}) copy-start(bf16[128,1024]{1,0:T(8,128)(2,1)} %param.19) | copy-start | bytes 786436
  28.8 6.6 %collective-permute-start.5 = (bf16[2,2,128,1152]{3,2,1,0:T(8,128)(2,1)}, bf16[2,2,128,1152]{3,2,1,0:T(8,128)(2,1)S(1)}, u32[]{:S(2)}, u32[]{:S(2)}) collective-permute-start(bf16[2,2,128,1152]{3,2,1,0:T(8,128)(2,1)} %pad_maximum_fusion.1), channel_id=1, source_target_pairs={{0,4},{4,0},{8,12},{12,8},{16,20},{20,16},{24,28},{28,24},{1,5},{5... | collective-permute-start | bytes 3538952 | tf_op jit(solution)/shard_map/ppermute | solution.py:55
  30.3 14.9 %collective-permute-start.11 = (bf16[96,1024]{1,0:T(8,128)(2,1)}, bf16[96,1024]{1,0:T(8,128)(2,1)}, u32[]{:S(2)}, u32[]{:S(2)}) collective-permute-start(bf16[96,1024]{1,0:T(8,128)(2,1)} %get-tuple-element.48), channel_id=1, source_target_pairs={{0,3},{1,0},{2,1},{3,2},{4,7},{5,4},{6,5},{7,6},{8,11},{9,8},{10,9... | collective-permute-start | bytes 589832 | tf_op jit(solution)/shard_map/ppermute | solution.py:38
  35.5 25.4 %collective-permute-start.10 = (bf16[96,1024]{1,0:T(8,128)(2,1)}, bf16[96,1024]{1,0:T(8,128)(2,1)S(1)}, u32[]{:S(2)}, u32[]{:S(2)}) collective-permute-start(bf16[96,1024]{1,0:T(8,128)(2,1)} %get-tuple-element.49), channel_id=1, source_target_pairs={{0,2},{1,3},{2,0},{3,1},{4,6},{5,7},{6,4},{7,5},{8,10},{9,11},{10,... | collective-permute-start | bytes 589832 | tf_op jit(solution)/shard_map/ppermute | solution.py:38
  35.7 0.9 %copy-start.3 = (bf16[96,1024]{1,0:T(8,128)(2,1)S(1)}, bf16[96,1024]{1,0:T(8,128)(2,1)}, u32[]{:S(2)}) copy-start(bf16[96,1024]{1,0:T(8,128)(2,1)} %get-tuple-element.50) | copy-start | bytes 589828
  36.7 24.2 %collective-permute-start.9 = (bf16[96,1024]{1,0:T(8,128)(2,1)S(1)}, bf16[96,1024]{1,0:T(8,128)(2,1)S(1)}, u32[]{:S(2)}, u32[]{:S(2)}) collective-permute-start(bf16[96,1024]{1,0:T(8,128)(2,1)S(1)} %copy-done.3), channel_id=1, source_target_pairs={{0,1},{1,2},{2,3},{3,0},{4,5},{5,6},{6,7},{7,4},{8,9},{9,10},{10,1... | collective-permute-start | bytes 589832 | tf_op jit(solution)/shard_map/ppermute | solution.py:38
  41.1 19.8 %copy-start.2 = (bf16[96,1024]{1,0:T(8,128)(2,1)S(1)}, bf16[96,1024]{1,0:T(8,128)(2,1)}, u32[]{:S(2)}) copy-start(bf16[96,1024]{1,0:T(8,128)(2,1)} %get-tuple-element.47) | copy-start | bytes 589828
  41.8 24.1 %collective-permute-start.8 = (bf16[96,1024]{1,0:T(8,128)(2,1)S(1)}, bf16[96,1024]{1,0:T(8,128)(2,1)S(1)}, u32[]{:S(2)}, u32[]{:S(2)}) collective-permute-start(bf16[96,1024]{1,0:T(8,128)(2,1)S(1)} %get-tuple-element.52), channel_id=1, source_target_pairs={{0,1},{1,2},{2,3},{3,0},{4,5},{5,6},{6,7},{7,4},{8,9},{9,10},{10,1... | collective-permute-start | bytes 589832 | tf_op jit(solution)/shard_map/ppermute | solution.py:38
  44.3 25.3 %collective-permute-start.7 = (bf16[96,1024]{1,0:T(8,128)(2,1)S(1)}, bf16[96,1024]{1,0:T(8,128)(2,1)S(1)}, u32[]{:S(2)}, u32[]{:S(2)}) collective-permute-start(bf16[96,1024]{1,0:T(8,128)(2,1)S(1)} %get-tuple-element.53), channel_id=1, source_target_pairs={{0,2},{1,3},{2,0},{3,1},{4,6},{5,7},{6,4},{7,5},{8,10},{9,11},{10,... | collective-permute-start | bytes 589832 | tf_op jit(solution)/shard_map/ppermute | solution.py:38
  45.2 25.9 %collective-permute-start.6 = (bf16[96,1024]{1,0:T(8,128)(2,1)S(1)}, bf16[96,1024]{1,0:T(8,128)(2,1)S(1)}, u32[]{:S(2)}, u32[]{:S(2)}) collective-permute-start(bf16[96,1024]{1,0:T(8,128)(2,1)S(1)} %get-tuple-element.54), channel_id=1, source_target_pairs={{0,3},{1,0},{2,1},{3,2},{4,7},{5,4},{6,5},{7,6},{8,11},{9,8},{10,9... | collective-permute-start | bytes 589832 | tf_op jit(solution)/shard_map/ppermute | solution.py:38
  62.6 3.0 %collective-permute-start.15 = (f32[4,128,384]{2,1,0:T(8,128)S(1)}, f32[4,128,384]{2,1,0:T(8,128)S(1)}, u32[]{:S(2)}, u32[]{:S(2)}) collective-permute-start(f32[4,128,384]{2,1,0:T(8,128)S(1)} %fusion.10), channel_id=1, source_target_pairs={{0,4},{4,0},{8,12},{12,8},{16,20},{20,16},{24,28},{28,24},{1,5},{5... | collective-permute-start | bytes 2359304 | tf_op jit(solution)/shard_map/ppermute | solution.py:74
  65.5 16.7 %collective-permute-start.14 = (bf16[96,1024]{1,0:T(8,128)(2,1)S(1)}, bf16[96,1024]{1,0:T(8,128)(2,1)S(1)}, u32[]{:S(2)}, u32[]{:S(2)}) collective-permute-start(bf16[96,1024]{1,0:T(8,128)(2,1)S(1)} %get-tuple-element.44), channel_id=1, source_target_pairs={{0,1},{1,2},{2,3},{3,0},{4,5},{5,6},{6,7},{7,4},{8,9},{9,10},{10,1... | collective-permute-start | bytes 589832 | tf_op jit(solution)/shard_map/ppermute | solution.py:38
  65.6 17.2 %collective-permute-start.13 = (bf16[96,1024]{1,0:T(8,128)(2,1)S(1)}, bf16[96,1024]{1,0:T(8,128)(2,1)S(1)}, u32[]{:S(2)}, u32[]{:S(2)}) collective-permute-start(bf16[96,1024]{1,0:T(8,128)(2,1)S(1)} %get-tuple-element.45), channel_id=1, source_target_pairs={{0,2},{1,3},{2,0},{3,1},{4,6},{5,7},{6,4},{7,5},{8,10},{9,11},{10,... | collective-permute-start | bytes 589832 | tf_op jit(solution)/shard_map/ppermute | solution.py:38
  65.8 17.0 %collective-permute-start.12 = (bf16[96,1024]{1,0:T(8,128)(2,1)S(1)}, bf16[96,1024]{1,0:T(8,128)(2,1)S(1)}, u32[]{:S(2)}, u32[]{:S(2)}) collective-permute-start(bf16[96,1024]{1,0:T(8,128)(2,1)S(1)} %get-tuple-element.46), channel_id=1, source_target_pairs={{0,3},{1,0},{2,1},{3,2},{4,7},{5,4},{6,5},{7,6},{8,11},{9,8},{10,9... | collective-permute-start | bytes 589832 | tf_op jit(solution)/shard_map/ppermute | solution.py:38
  69.6 11.0 %collective-permute-start.16 = (f32[2,128,384]{2,1,0:T(8,128)S(1)}, f32[2,128,384]{2,1,0:T(8,128)S(1)}, u32[]{:S(2)}, u32[]{:S(2)}) collective-permute-start(f32[2,128,384]{2,1,0:T(8,128)S(1)} %select_bitcast_fusion.4), channel_id=1, source_target_pairs={{0,8},{4,12},{8,0},{12,4},{16,24},{20,28},{24,16},{28,20},{1,9},{5... | collective-permute-start | bytes 1179656 | tf_op jit(solution)/shard_map/ppermute | solution.py:74
  80.6 6.0 %collective-permute-start.17 = (f32[1,128,384]{2,1,0:T(8,128)S(1)}, f32[1,128,384]{2,1,0:T(8,128)S(1)}, u32[]{:S(2)}, u32[]{:S(2)}) collective-permute-start(f32[1,128,384]{2,1,0:T(8,128)S(1)} %select_bitcast_fusion.7), channel_id=1, source_target_pairs={{0,16},{4,20},{8,24},{12,28},{16,0},{20,4},{24,8},{28,12},{1,17},{... | collective-permute-start | bytes 589832 | tf_op jit(solution)/shard_map/ppermute | solution.py:74

commit v11 on v9

--- a/solution.py
+++ b/solution.py
@@ -47,7 +47,7 @@
         bits.append(bit)
         bit //= 2
     if len(bits) >= 3:
-        bits[0], bits[1] = bits[1], bits[0]
+        bits = [bits[1], bits[-1]] + [bits[0]] + bits[2:-1]
     work = block
     for bit in bits:
         recv = lax.ppermute(work, "dp", [(i, i ^ bit) for i in range(n_dp)])

time: 87.6 us -> 101 us (1.15)
  waiting for transfers between devices: 37.8 us -> 50.9 us
  starting transfers between devices: 26.1 us -> 27.7 us
    ppermute x3, waiting for transfers between devices: 12.2 us -> 27.5 us  [all_gather_dp(): recv = lax.ppermute(work, 'dp', [(i, i ^ bit) for i in range(n_dp)])]
    ppermute x12, waiting for transfers between devices: 14.7 us -> 12.6 us  [shift_send(): got.append(lax.ppermute(blocks[step], 'expert', pairs))]
    ppermute x12, starting transfers between devices: 18.1 us -> 19.9 us  [shift_send(): got.append(lax.ppermute(blocks[step], 'expert', pairs))]
  transfers between devices with their start and end apart: 18 -> 18, of which waited for: 6 -> 6; matrix products, arithmetic and copies ran while one was open for 21% -> 17% of each run, Pallas kernels for 0% -> 0%
where the time goes in v11:
time: 101 us
  waiting for transfers between devices  50.9 us (50%)
  starting transfers between devices  27.7 us (27%)
  matrix products  11.8 us (12%)
  other arithmetic  5.41 us (5%)
  local copies, waits for them, and re-layouts  3.73 us (4%)
    ppermute x3, waiting for transfers between devices, all_gather_dp(): recv = lax.ppermute(work, 'dp', [(i, i ^ bit) for i in range(n_dp)])  27.5 us
    ppermute x12, starting transfers between devices, shift_send(): got.append(lax.ppermute(blocks[step], 'expert', pairs))  19.9 us
    ppermute x12, waiting for transfers between devices, shift_send(): got.append(lax.ppermute(blocks[step], 'expert', pairs))  12.6 us
    ppermute x3, waiting for transfers between devices, reduce_scatter_dp(): work = keep + lax.ppermute(give, 'dp', pairs)  10.9 us
    ppermute x3, starting transfers between devices, all_gather_dp(): recv = lax.ppermute(work, 'dp', [(i, i ^ bit) for i in range(n_dp)])  4.62 us
    ppermute x3, starting transfers between devices, reduce_scatter_dp(): work = keep + lax.ppermute(give, 'dp', pairs)  3.14 us
    another operation x6, other arithmetic, all_gather_dp(): jnp.stack([jnp.where(upper, recv, work), jnp.where(upper, work, recv)], a...  2.93 us
  transfers between devices with their start and end apart: 18, of which 6 were waited for; matrix products, arithmetic and copies ran while one was open for 17% of the time, Pallas kernels for 0%

profile of v11, /device:TPU:0, one launch (start us, length us, event | category | flops | bytes accessed | tf_op | source)
XLA Modules:
  0.0 100.6 jit_solution(8199922361032997840)
XLA Ops:
  0.6 1.1 %maximum_bitcast_fusion = bf16[128,1152]{1,0:T(8,128)(2,1)S(1)} fusion(bf16[1,128,384]{2,1,0:T(8,128)(2,1)} %param.18, bf16[1,128,384]{2,1,0:T(8,128)(2,1)} %param.17, bf16[1,128,384]{2,1,0:T(8,128)(2,1)} %param.16), kind=kLoop, calls=%fused_computation.53 | loop fusion | flops 884736 | bytes 589824 | tf_op jit(solution)/shard_map/reshape;transpose | solution.py:121
  1.7 3.0 %collective-permute-start.3 = (bf16[128,1152]{1,0:T(8,128)(2,1)S(1)}, bf16[128,1152]{1,0:T(8,128)(2,1)S(1)}, u32[]{:S(2)}, u32[]{:S(2)}) collective-permute-start(bf16[128,1152]{1,0:T(8,128)(2,1)S(1)} %maximum_bitcast_fusion), channel_id=1, source_target_pairs={{0,8},{4,12},{8,0},{12,4},{16,24},{20,28},{24,16},{28,20},{1,9},{5... | collective-permute-start | bytes 884744 | tf_op jit(solution)/shard_map/ppermute | solution.py:53
  4.7 0.8 copy.19
  5.5 0.1 sub.46
  5.7 0.2 fusion.2
  5.9 0.1 convert_element_type.57
  6.2 5.6 %collective-permute-done.3 = bf16[128,1152]{1,0:T(8,128)(2,1)S(1)} collective-permute-done((bf16[128,1152]{1,0:T(8,128)(2,1)S(1)}, bf16[128,1152]{1,0:T(8,128)(2,1)S(1)}, u32[]{:S(2)}, u32[]{:S(2)}) %collective-permute-start.3) | collective-permute-done | bytes 294944 | tf_op jit(solution)/shard_map/ppermute | solution.py:53
  11.7 1.1 %select_bitcast_fusion.6 = (bf16[1,128,1152]{2,1,0:T(8,128)(2,1)S(1)}, bf16[1,128,1152]{2,1,0:T(8,128)(2,1)S(1)}) fusion(bf16[128,1152]{1,0:T(8,128)(2,1)S(1)} %collective-permute-done.3, pred[]{:T(512)S(6)} %eq.60, bf16[1,128,384]{2,1,0:T(8,128)(2,1)} %param.18, bf16[1,128,384]{2,1,0:T(8,128)(2,1)} %param.17, bf16[1,128,384]{2,1,0:T(8,128)(2,1)} %param.16), kind=kLoop, calls=%fused_computation.57 | loop fusion | flops 1179648 | bytes 1179649 | tf_op jit(solution)/shard_map/stack | solution.py:55
  13.0 0.1 fusion.22
  13.2 0.4 convolution_convert_fusion
  13.6 0.8 fusion.44
  14.3 3.8 %collective-permute-start.2 = (bf16[96,1024]{1,0:T(8,128)(2,1)}, bf16[96,1024]{1,0:T(8,128)(2,1)}, u32[]{:S(2)}, u32[]{:S(2)}) collective-permute-start(bf16[96,1024]{1,0:T(8,128)(2,1)} %get-tuple-element.56), channel_id=1, source_target_pairs={{0,3},{1,0},{2,1},{3,2},{4,7},{5,4},{6,5},{7,6},{8,11},{9,8},{10,9... | collective-permute-start | bytes 589832 | tf_op jit(solution)/shard_map/ppermute | solution.py:38
  18.2 1.0 %collective-permute-start = (bf16[96,1024]{1,0:T(8,128)(2,1)S(1)}, bf16[96,1024]{1,0:T(8,128)(2,1)}, u32[]{:S(2)}, u32[]{:S(2)}) collective-permute-start(bf16[96,1024]{1,0:T(8,128)(2,1)S(1)} %get-tuple-element.58), channel_id=1, source_target_pairs={{0,1},{1,2},{2,3},{3,0},{4,5},{5,6},{6,7},{7,4},{8,9},{9,10},{10,1... | collective-permute-start | bytes 589832 | tf_op jit(solution)/shard_map/ppermute | solution.py:38
  19.2 0.1 copy.22
  19.3 0.1 broadcast_in_dim.48
  19.5 0.1 select_bitcast_fusion.3
  19.6 1.2 %pad_maximum_fusion.1 = bf16[2,2,128,1152]{3,2,0,1:T(8,128)(2,1)} fusion(bf16[1,2,128,1152]{3,2,0,1:T(8,128)(2,1)S(1)} %get-tuple-element.42, bf16[1,2,128,1152]{3,2,0,1:T(8,128)(2,1)S(1)} %get-tuple-element.41), kind=kLoop, calls=%fused_computation.10 | loop fusion | flops 589824 | bytes 2359296 | tf_op jit(solution)/shard_map/stack | solution.py:55
  20.8 1.5 %collective-permute-start.5 = (bf16[2,2,128,1152]{3,2,0,1:T(8,128)(2,1)}, bf16[2,2,128,1152]{3,2,0,1:T(8,128)(2,1)S(1)}, u32[]{:S(2)}, u32[]{:S(2)}) collective-permute-start(bf16[2,2,128,1152]{3,2,0,1:T(8,128)(2,1)} %pad_maximum_fusion.1), channel_id=1, source_target_pairs={{0,16},{4,20},{8,24},{12,28},{16,0},{20,4},{24,8},{28,12},{1,17},{... | collective-permute-start | bytes 3538952 | tf_op jit(solution)/shard_map/ppermute | solution.py:53
  22.3 0.1 select_reduce_fusion
  22.5 0.4 multiply_convert_fusion
  22.9 0.8 fusion.42
  23.7 2.8 %collective-permute-start.11 = (bf16[96,1024]{1,0:T(8,128)(2,1)}, bf16[96,1024]{1,0:T(8,128)(2,1)}, u32[]{:S(2)}, u32[]{:S(2)}) collective-permute-start(bf16[96,1024]{1,0:T(8,128)(2,1)} %get-tuple-element.48), channel_id=1, source_target_pairs={{0,3},{1,0},{2,1},{3,2},{4,7},{5,4},{6,5},{7,6},{8,11},{9,8},{10,9... | collective-permute-start | bytes 589832 | tf_op jit(solution)/shard_map/ppermute | solution.py:38
  26.6 21.9 %collective-permute-done.5 = bf16[2,2,128,1152]{3,2,0,1:T(8,128)(2,1)S(1)} collective-permute-done((bf16[2,2,128,1152]{3,2,0,1:T(8,128)(2,1)}, bf16[2,2,128,1152]{3,2,0,1:T(8,128)(2,1)S(1)}, u32[]{:S(2)}, u32[]{:S(2)}) %collective-permute-start.5) | collective-permute-done | bytes 1179680 | tf_op jit(solution)/shard_map/ppermute | solution.py:53
  48.5 2.2 %collective-permute-start.10 = (bf16[96,1024]{1,0:T(8,128)(2,1)}, bf16[96,1024]{1,0:T(8,128)(2,1)S(1)}, u32[]{:S(2)}, u32[]{:S(2)}) collective-permute-start(bf16[96,1024]{1,0:T(8,128)(2,1)} %get-tuple-element.49), channel_id=1, source_target_pairs={{0,2},{1,3},{2,0},{3,1},{4,6},{5,7},{6,4},{7,5},{8,10},{9,11},{10,... | collective-permute-start | bytes 589832 | tf_op jit(solution)/shard_map/ppermute | solution.py:38
  50.7 0.2 select_bitcast_fusion.1
  51.0 0.2 pad_maximum_fusion
  51.2 0.7 copy-done.2
  51.9 1.5 %collective-permute-start.9 = (bf16[96,1024]{1,0:T(8,128)(2,1)S(1)}, bf16[96,1024]{1,0:T(8,128)(2,1)S(1)}, u32[]{:S(2)}, u32[]{:S(2)}) collective-permute-start(bf16[96,1024]{1,0:T(8,128)(2,1)S(1)} %copy-done.2), channel_id=1, source_target_pairs={{0,1},{1,2},{2,3},{3,0},{4,5},{5,6},{6,7},{7,4},{8,9},{9,10},{10,1... | collective-permute-start | bytes 589832 | tf_op jit(solution)/shard_map/ppermute | solution.py:38
  53.4 1.7 %fusion.14 = f32[384,384]{1,0:T(8,128)S(1)} fusion(bf16[1,1024,1152]{2,1,0:T(8,128)(2,1)S(1)} %bitcast.97, bf16[96,1024]{1,0:T(8,128)(2,1)} %collective-permute-done.2, bf16[96,1024]{1,0:T(8,128)(2,1)} %collective-permute-done.1, bf16[96,1024]{1,0:T(8,128)(2,1)} %collective-permute-done, bf16[96,1024]{1,0:T(8,128)(2,1)S(1)} %get-tuple-element.55), kind=kOutput, calls=%fused_computation.34 | convolution fusion | flops 305135616 | bytes 2162688 | tf_op jit(solution)/shard_map/dot_general | solution.py:11
  55.1 1.7 %multiply_convert_fusion.3 = (bf16[384,384]{1,0:T(8,128)(2,1)S(1)}, f32[384,384]{1,0:T(8,128)S(1)}) fusion(f32[384,384]{1,0:T(8,128)S(1)} %fusion.14, bf16[1,1024,1152]{2,1,0:T(8,128)(2,1)S(1)} %bitcast.98, bf16[96,1024]{1,0:T(8,128)(2,1)} %collective-permute-done.2, bf16[96,1024]{1,0:T(8,128)(2,1)} %collective-permute-done.1, ...), kind=kOutput, calls=%fused_computation.40 | convolution fusion | flops 306020352 | bytes 3047424 | tf_op jit(solution)/shard_map/dot_general | solution.py:12
  56.8 0.6 convolution_convert_fusion.1
  57.5 2.9 %collective-permute-start.7 = (bf16[96,1024]{1,0:T(8,128)(2,1)S(1)}, bf16[96,1024]{1,0:T(8,128)(2,1)S(1)}, u32[]{:S(2)}, u32[]{:S(2)}) collective-permute-start(bf16[96,1024]{1,0:T(8,128)(2,1)S(1)} %get-tuple-element.53), channel_id=1, source_target_pairs={{0,2},{1,3},{2,0},{3,1},{4,6},{5,7},{6,4},{7,5},{8,10},{9,11},{10,... | collective-permute-start | bytes 589832 | tf_op jit(solution)/shard_map/ppermute | solution.py:38
  60.4 1.7 %collective-permute-start.6 = (bf16[96,1024]{1,0:T(8,128)(2,1)S(1)}, bf16[96,1024]{1,0:T(8,128)(2,1)S(1)}, u32[]{:S(2)}, u32[]{:S(2)}) collective-permute-start(bf16[96,1024]{1,0:T(8,128)(2,1)S(1)} %get-tuple-element.54), channel_id=1, source_target_pairs={{0,3},{1,0},{2,1},{3,2},{4,7},{5,4},{6,5},{7,6},{8,11},{9,8},{10,9... | collective-permute-start | bytes 589832 | tf_op jit(solution)/shard_map/ppermute | solution.py:38
  62.2 12.0 %collective-permute-done.10 = bf16[96,1024]{1,0:T(8,128)(2,1)S(1)} collective-permute-done((bf16[96,1024]{1,0:T(8,128)(2,1)}, bf16[96,1024]{1,0:T(8,128)(2,1)S(1)}, u32[]{:S(2)}, u32[]{:S(2)}) %collective-permute-start.10) | collective-permute-done | bytes 196640 | tf_op jit(solution)/shard_map/ppermute | solution.py:38
  74.1 1.6 %fusion.24 = f32[1024,384]{1,0:T(8,128)S(1)} fusion(bf16[384,384]{1,0:T(8,128)(2,1)S(1)} %get-tuple-element.65, bf16[96,1024]{1,0:T(8,128)(2,1)} %collective-permute-done.11, bf16[96,1024]{1,0:T(8,128)(2,1)S(1)} %collective-permute-done.10, bf16[96,1024]{1,0:T(8,128)(2,1)S(1)} %collective-permute-done.9, bf16[96,1024]{1,0:T(8,128)(2,1)S(1)} %get-tuple-element.47), kind=kOutput, calls=%fused_computation.65 | convolution fusion | flops 305135616 | bytes 2654208 | tf_op jit(solution)/shard_map/dot_general | solution.py:136
  75.9 1.5 %fusion.16 = f32[384,384]{1,0:T(8,128)S(1)} fusion(bf16[1,1024,1152]{2,1,0:T(8,128)(2,1)S(1)} %bitcast.100, bf16[96,1024]{1,0:T(8,128)(2,1)} %collective-permute-done.11, bf16[96,1024]{1,0:T(8,128)(2,1)S(1)} %collective-permute-done.10, bf16[96,1024]{1,0:T(8,128)(2,1)S(1)} %collective-permute-done.9, bf16[96,1024]{1,0:T(8,128)(2,1)S(1)} %get-tuple-element.47), kind=kOutput, calls=%fused_computation.36 | convolution fusion | flops 305135616 | bytes 2162688 | tf_op jit(solution)/shard_map/dot_general | solution.py:22
  77.4 0.7 fusion.13
  78.1 0.6 add_convert_fusion
  79.1 3.8 %collective-permute-start.12 = (bf16[96,1024]{1,0:T(8,128)(2,1)S(1)}, bf16[96,1024]{1,0:T(8,128)(2,1)S(1)}, u32[]{:S(2)}, u32[]{:S(2)}) collective-permute-start(bf16[96,1024]{1,0:T(8,128)(2,1)S(1)} %get-tuple-element.46), channel_id=1, source_target_pairs={{0,3},{1,0},{2,1},{3,2},{4,7},{5,4},{6,5},{7,6},{8,11},{9,8},{10,9... | collective-permute-start | bytes 589832 | tf_op jit(solution)/shard_map/ppermute | solution.py:38
  82.9 1.5 %collective-permute-start.16 = (f32[2,128,384]{2,1,0:T(8,128)S(1)}, f32[2,128,384]{2,1,0:T(8,128)S(1)}, u32[]{:S(2)}, u32[]{:S(2)}) collective-permute-start(f32[2,128,384]{2,1,0:T(8,128)S(1)} %select_bitcast_fusion.4), channel_id=1, source_target_pairs={{0,8},{4,12},{8,0},{12,4},{16,24},{20,28},{24,16},{28,20},{1,9},{5... | collective-permute-start | bytes 1179656 | tf_op jit(solution)/shard_map/ppermute | solution.py:72
  84.4 0.3 convolution_multiply_fusion
  84.7 1.0 %fusion.1 = bf16[128,1024]{1,0:T(8,128)(2,1)} fusion(f32[128,1024]{1,0:T(8,128)S(1)} %convolution_multiply_fusion, f32[128]{0:T(128)S(1)} %get-tuple-element.61, pred[128,2,384]{2,0,1:T(32,128)(4,1)S(1)} %get-tuple-element.64, bf16[96,1024]{1,0:T(8,128)(2,1)S(1)} %collective-permute-done.8, bf16[96,1024]{1,0:T(8,128)(2,1)S(1)} %collective-permute-done.7, ...), kind=kOutput, calls=%fused_computation.8 | convolution fusion | flops 104202240 | bytes 1622528 | tf_op jit(solution)/shard_map/dot_general | solution.py:145
  85.7 8.1 %collective-permute-done.16 = f32[2,128,384]{2,1,0:T(8,128)S(1)} collective-permute-done((f32[2,128,384]{2,1,0:T(8,128)S(1)}, f32[2,128,384]{2,1,0:T(8,128)S(1)}, u32[]{:S(2)}, u32[]{:S(2)}) %collective-permute-start.16) | collective-permute-done | bytes 393248 | tf_op jit(solution)/shard_map/ppermute | solution.py:72
  93.9 1.6 %collective-permute-start.17 = (f32[1,128,384]{2,1,0:T(8,128)S(1)}, f32[1,128,384]{2,1,0:T(8,128)S(1)}, u32[]{:S(2)}, u32[]{:S(2)}) collective-permute-start(f32[1,128,384]{2,1,0:T(8,128)S(1)} %select_bitcast_fusion.7), channel_id=1, source_target_pairs={{0,16},{4,20},{8,24},{12,28},{16,0},{20,4},{24,8},{28,12},{1,17},{... | collective-permute-start | bytes 589832 | tf_op jit(solution)/shard_map/ppermute | solution.py:72
  95.5 0.6 collective-permute-done.13
  96.1 1.0 %convolution_convert_fusion.2 = bf16[128,1024]{1,0:T(8,128)(2,1)} fusion(bf16[96,1024]{1,0:T(8,128)(2,1)S(1)} %collective-permute-done.14, bf16[96,1024]{1,0:T(8,128)(2,1)S(1)} %collective-permute-done.13, bf16[96,1024]{1,0:T(8,128)(2,1)S(1)} %collective-permute-done.12, bf16[96,1024]{1,0:T(8,128)(2,1)S(1)} %get-tuple-element.43, ...), kind=kOutput, calls=%fused_computation.9 | convolution fusion | flops 103989248 | bytes 1245184 | tf_op jit(solution)/shard_map/dot_general | solution.py:151
  97.1 2.8 %collective-permute-done.17 = f32[1,128,384]{2,1,0:T(8,128)S(1)} collective-permute-done((f32[1,128,384]{2,1,0:T(8,128)S(1)}, f32[1,128,384]{2,1,0:T(8,128)S(1)}, u32[]{:S(2)}, u32[]{:S(2)}) %collective-permute-start.17) | collective-permute-done | bytes 196640 | tf_op jit(solution)/shard_map/ppermute | solution.py:72
  99.9 0.7 fusion.23
  (41 shorter events, 1.0 us)
Async XLA Ops:
  0.6 12.5 %copy-start = (bf16[128,1024]{1,0:T(8,128)(2,1)S(1)}, bf16[128,1024]{1,0:T(8,128)(2,1)}, u32[]{:S(2)}) copy-start(bf16[128,1024]{1,0:T(8,128)(2,1)} %param.13) | copy-start | bytes 786436
  1.7 10.0 %collective-permute-start.3 = (bf16[128,1152]{1,0:T(8,128)(2,1)S(1)}, bf16[128,1152]{1,0:T(8,128)(2,1)S(1)}, u32[]{:S(2)}, u32[]{:S(2)}) collective-permute-start(bf16[128,1152]{1,0:T(8,128)(2,1)S(1)} %maximum_bitcast_fusion), channel_id=1, source_target_pairs={{0,8},{4,12},{8,0},{12,4},{16,24},{20,28},{24,16},{28,20},{1,9},{5... | collective-permute-start | bytes 884744 | tf_op jit(solution)/shard_map/ppermute | solution.py:53
  12.9 6.3 %copy-start.3 = (f32[128,2]{0,1:T(2,128)S(1)}, f32[128,2]{0,1:T(2,128)}, u32[]{:S(2)}) copy-start(f32[128,2]{0,1:T(2,128)} %param.15) | copy-start | bytes 3076
  12.9 6.5 %collective-permute-start.4 = (bf16[2,128,1152]{2,1,0:T(8,128)(2,1)S(1)}, bf16[2,128,1152]{2,1,0:T(8,128)(2,1)S(1)}, u32[]{:S(2)}, u32[]{:S(2)}) collective-permute-start(bf16[2,128,1152]{2,1,0:T(8,128)(2,1)S(1)} %pad_maximum_fusion.5), channel_id=1, source_target_pairs={{0,4},{4,0},{8,12},{12,8},{16,20},{20,16},{24,28},{28,24},{1,5},{5... | collective-permute-start | bytes 1769480 | tf_op jit(solution)/shard_map/ppermute | solution.py:53
  14.3 36.9 %collective-permute-start.2 = (bf16[96,1024]{1,0:T(8,128)(2,1)}, bf16[96,1024]{1,0:T(8,128)(2,1)}, u32[]{:S(2)}, u32[]{:S(2)}) collective-permute-start(bf16[96,1024]{1,0:T(8,128)(2,1)} %get-tuple-element.56), channel_id=1, source_target_pairs={{0,3},{1,0},{2,1},{3,2},{4,7},{5,4},{6,5},{7,6},{8,11},{9,8},{10,9... | collective-permute-start | bytes 589832 | tf_op jit(solution)/shard_map/ppermute | solution.py:38
  18.2 35.2 %collective-permute-start.1 = (bf16[96,1024]{1,0:T(8,128)(2,1)S(1)}, bf16[96,1024]{1,0:T(8,128)(2,1)}, u32[]{:S(2)}, u32[]{:S(2)}) collective-permute-start(bf16[96,1024]{1,0:T(8,128)(2,1)S(1)} %get-tuple-element.57), channel_id=1, source_target_pairs={{0,2},{1,3},{2,0},{3,1},{4,6},{5,7},{6,4},{7,5},{8,10},{9,11},{10,... | collective-permute-start | bytes 589832 | tf_op jit(solution)/shard_map/ppermute | solution.py:38
  18.2 35.2 %collective-permute-start = (bf16[96,1024]{1,0:T(8,128)(2,1)S(1)}, bf16[96,1024]{1,0:T(8,128)(2,1)}, u32[]{:S(2)}, u32[]{:S(2)}) collective-permute-start(bf16[96,1024]{1,0:T(8,128)(2,1)S(1)} %get-tuple-element.58), channel_id=1, source_target_pairs={{0,1},{1,2},{2,3},{3,0},{4,5},{5,6},{6,7},{7,4},{8,9},{9,10},{10,1... | collective-permute-start | bytes 589832 | tf_op jit(solution)/shard_map/ppermute | solution.py:38
  19.6 2.9 %copy-start.1 = (bf16[128,1024]{1,0:T(8,128)(2,1)S(1)}, bf16[128,1024]{1,0:T(8,128)(2,1)}, u32[]{:S(2)}) copy-start(bf16[128,1024]{1,0:T(8,128)(2,1)} %param.19) | copy-start | bytes 786436
  20.8 27.7 %collective-permute-start.5 = (bf16[2,2,128,1152]{3,2,0,1:T(8,128)(2,1)}, bf16[2,2,128,1152]{3,2,0,1:T(8,128)(2,1)S(1)}, u32[]{:S(2)}, u32[]{:S(2)}) collective-permute-start(bf16[2,2,128,1152]{3,2,0,1:T(8,128)(2,1)} %pad_maximum_fusion.1), channel_id=1, source_target_pairs={{0,16},{4,20},{8,24},{12,28},{16,0},{20,4},{24,8},{28,12},{1,17},{... | collective-permute-start | bytes 3538952 | tf_op jit(solution)/shard_map/ppermute | solution.py:53
  23.7 36.7 %collective-permute-start.11 = (bf16[96,1024]{1,0:T(8,128)(2,1)}, bf16[96,1024]{1,0:T(8,128)(2,1)}, u32[]{:S(2)}, u32[]{:S(2)}) collective-permute-start(bf16[96,1024]{1,0:T(8,128)(2,1)} %get-tuple-element.48), channel_id=1, source_target_pairs={{0,3},{1,0},{2,1},{3,2},{4,7},{5,4},{6,5},{7,6},{8,11},{9,8},{10,9... | collective-permute-start | bytes 589832 | tf_op jit(solution)/shard_map/ppermute | solution.py:38
  48.5 25.6 %collective-permute-start.10 = (bf16[96,1024]{1,0:T(8,128)(2,1)}, bf16[96,1024]{1,0:T(8,128)(2,1)S(1)}, u32[]{:S(2)}, u32[]{:S(2)}) collective-permute-start(bf16[96,1024]{1,0:T(8,128)(2,1)} %get-tuple-element.49), channel_id=1, source_target_pairs={{0,2},{1,3},{2,0},{3,1},{4,6},{5,7},{6,4},{7,5},{8,10},{9,11},{10,... | collective-permute-start | bytes 589832 | tf_op jit(solution)/shard_map/ppermute | solution.py:38
  51.0 0.9 copy-start.2
  51.9 22.3 %collective-permute-start.9 = (bf16[96,1024]{1,0:T(8,128)(2,1)S(1)}, bf16[96,1024]{1,0:T(8,128)(2,1)S(1)}, u32[]{:S(2)}, u32[]{:S(2)}) collective-permute-start(bf16[96,1024]{1,0:T(8,128)(2,1)S(1)} %copy-done.2), channel_id=1, source_target_pairs={{0,1},{1,2},{2,3},{3,0},{4,5},{5,6},{6,7},{7,4},{8,9},{9,10},{10,1... | collective-permute-start | bytes 589832 | tf_op jit(solution)/shard_map/ppermute | solution.py:38
  57.4 21.7 %collective-permute-start.8 = (bf16[96,1024]{1,0:T(8,128)(2,1)S(1)}, bf16[96,1024]{1,0:T(8,128)(2,1)S(1)}, u32[]{:S(2)}, u32[]{:S(2)}) collective-permute-start(bf16[96,1024]{1,0:T(8,128)(2,1)S(1)} %get-tuple-element.52), channel_id=1, source_target_pairs={{0,1},{1,2},{2,3},{3,0},{4,5},{5,6},{6,7},{7,4},{8,9},{9,10},{10,1... | collective-permute-start | bytes 589832 | tf_op jit(solution)/shard_map/ppermute | solution.py:38
  57.5 25.4 %collective-permute-start.7 = (bf16[96,1024]{1,0:T(8,128)(2,1)S(1)}, bf16[96,1024]{1,0:T(8,128)(2,1)S(1)}, u32[]{:S(2)}, u32[]{:S(2)}) collective-permute-start(bf16[96,1024]{1,0:T(8,128)(2,1)S(1)} %get-tuple-element.53), channel_id=1, source_target_pairs={{0,2},{1,3},{2,0},{3,1},{4,6},{5,7},{6,4},{7,5},{8,10},{9,11},{10,... | collective-permute-start | bytes 589832 | tf_op jit(solution)/shard_map/ppermute | solution.py:38
  60.4 23.9 %collective-permute-start.6 = (bf16[96,1024]{1,0:T(8,128)(2,1)S(1)}, bf16[96,1024]{1,0:T(8,128)(2,1)S(1)}, u32[]{:S(2)}, u32[]{:S(2)}) collective-permute-start(bf16[96,1024]{1,0:T(8,128)(2,1)S(1)} %get-tuple-element.54), channel_id=1, source_target_pairs={{0,3},{1,0},{2,1},{3,2},{4,7},{5,4},{6,5},{7,6},{8,11},{9,8},{10,9... | collective-permute-start | bytes 589832 | tf_op jit(solution)/shard_map/ppermute | solution.py:38
  75.8 3.0 %collective-permute-start.15 = (f32[4,128,384]{2,1,0:T(8,128)S(1)}, f32[4,128,384]{2,1,0:T(8,128)S(1)}, u32[]{:S(2)}, u32[]{:S(2)}) collective-permute-start(f32[4,128,384]{2,1,0:T(8,128)S(1)} %fusion.10), channel_id=1, source_target_pairs={{0,4},{4,0},{8,12},{12,8},{16,20},{20,16},{24,28},{28,24},{1,5},{5... | collective-permute-start | bytes 2359304 | tf_op jit(solution)/shard_map/ppermute | solution.py:72
  78.8 16.7 %collective-permute-start.14 = (bf16[96,1024]{1,0:T(8,128)(2,1)S(1)}, bf16[96,1024]{1,0:T(8,128)(2,1)S(1)}, u32[]{:S(2)}, u32[]{:S(2)}) collective-permute-start(bf16[96,1024]{1,0:T(8,128)(2,1)S(1)} %get-tuple-element.44), channel_id=1, source_target_pairs={{0,1},{1,2},{2,3},{3,0},{4,5},{5,6},{6,7},{7,4},{8,9},{9,10},{10,1... | collective-permute-start | bytes 589832 | tf_op jit(solution)/shard_map/ppermute | solution.py:38
  78.9 17.2 %collective-permute-start.13 = (bf16[96,1024]{1,0:T(8,128)(2,1)S(1)}, bf16[96,1024]{1,0:T(8,128)(2,1)S(1)}, u32[]{:S(2)}, u32[]{:S(2)}) collective-permute-start(bf16[96,1024]{1,0:T(8,128)(2,1)S(1)} %get-tuple-element.45), channel_id=1, source_target_pairs={{0,2},{1,3},{2,0},{3,1},{4,6},{5,7},{6,4},{7,5},{8,10},{9,11},{10,... | collective-permute-start | bytes 589832 | tf_op jit(solution)/shard_map/ppermute | solution.py:38
  79.1 17.0 %collective-permute-start.12 = (bf16[96,1024]{1,0:T(8,128)(2,1)S(1)}, bf16[96,1024]{1,0:T(8,128)(2,1)S(1)}, u32[]{:S(2)}, u32[]{:S(2)}) collective-permute-start(bf16[96,1024]{1,0:T(8,128)(2,1)S(1)} %get-tuple-element.46), channel_id=1, source_target_pairs={{0,3},{1,0},{2,1},{3,2},{4,7},{5,4},{6,5},{7,6},{8,11},{9,8},{10,9... | collective-permute-start | bytes 589832 | tf_op jit(solution)/shard_map/ppermute | solution.py:38
  82.9 11.0 %collective-permute-start.16 = (f32[2,128,384]{2,1,0:T(8,128)S(1)}, f32[2,128,384]{2,1,0:T(8,128)S(1)}, u32[]{:S(2)}, u32[]{:S(2)}) collective-permute-start(f32[2,128,384]{2,1,0:T(8,128)S(1)} %select_bitcast_fusion.4), channel_id=1, source_target_pairs={{0,8},{4,12},{8,0},{12,4},{16,24},{20,28},{24,16},{28,20},{1,9},{5... | collective-permute-start | bytes 1179656 | tf_op jit(solution)/shard_map/ppermute | solution.py:72
  93.9 6.0 %collective-permute-start.17 = (f32[1,128,384]{2,1,0:T(8,128)S(1)}, f32[1,128,384]{2,1,0:T(8,128)S(1)}, u32[]{:S(2)}, u32[]{:S(2)}) collective-permute-start(f32[1,128,384]{2,1,0:T(8,128)S(1)} %select_bitcast_fusion.7), channel_id=1, source_target_pairs={{0,16},{4,20},{8,24},{12,28},{16,0},{20,4},{24,8},{28,12},{1,17},{... | collective-permute-start | bytes 589832 | tf_op jit(solution)/shard_map/ppermute | solution.py:72

commit v12 on v9

--- a/solution.py
+++ b/solution.py
@@ -132,6 +132,7 @@
     x_rows = jnp.concatenate(recv_rows, axis=0)
     g_rows = jnp.concatenate(recv_grads, axis=0)
     gate_pre, up_pre, hidden, expert_out = forward_rows(x_rows, gate_w, up_w, down_w)
+    expert_out, g_rows = lax.optimization_barrier((expert_out, g_rows))
     pair_grad = backward_rows(g_rows, gate_pre, up_pre, gate_w, up_w, down_w)
     pieces = lax.dot_general(g_rows, hidden, contract_first, preferred_element_type=jnp.float32)
     block_rows = local_count * capacity

time: 87.6 us -> 111 us (1.27)
  the two profiles are of different devices: /device:TPU:0 before, /device:TPU:30 now
where the time goes in v12:
time: 111 us
  waiting for transfers between devices  58.5 us (53%)
  starting transfers between devices  31.8 us (29%)
  matrix products  9.57 us (9%)
  other arithmetic  7.21 us (6%)
  local copies, waits for them, and re-layouts  3.13 us (3%)
    ppermute x12, waiting for transfers between devices, shift_send(): got.append(lax.ppermute(blocks[step], 'expert', pairs))  30.4 us
    ppermute x12, starting transfers between devices, shift_send(): got.append(lax.ppermute(blocks[step], 'expert', pairs))  29.5 us
    ppermute x3, waiting for transfers between devices, all_gather_dp(): recv = lax.ppermute(work, 'dp', [(i, i ^ bit) for i in range(n_dp)])  18 us
    ppermute x3, waiting for transfers between devices, reduce_scatter_dp(): work = keep + lax.ppermute(give, 'dp', pairs)  10 us
    another operation x6, other arithmetic, all_gather_dp(): jnp.stack([jnp.where(upper, recv, work), jnp.where(upper, work, recv)], a...  2.93 us
  transfers between devices with their start and end apart: 18, of which 9 were waited for; matrix products, arithmetic and copies ran while one was open for 11% of the time, Pallas kernels for 0%

profile of v12, /device:TPU:30, one launch (start us, length us, event | category | flops | bytes accessed | tf_op | source)
XLA Modules:
  0.0 111.1 jit_solution(4850807603739856945)
XLA Ops:
  0.6 1.1 maximum_bitcast_fusion
  1.7 0.6 collective-permute-start.3
  2.3 0.8 copy.19
  3.3 0.2 fusion.2
  3.7 6.8 %collective-permute-done.3 = bf16[128,1152]{1,0:T(8,128)(2,1)S(1)} collective-permute-done((bf16[128,1152]{1,0:T(8,128)(2,1)S(1)}, bf16[128,1152]{1,0:T(8,128)(2,1)S(1)}, u32[]{:S(2)}, u32[]{:S(2)}) %collective-permute-start.3) | collective-permute-done | bytes 294944 | tf_op jit(solution)/shard_map/ppermute | solution.py:53
  10.5 1.1 select_bitcast_fusion.6
  11.7 0.6 collective-permute-start.4
  12.3 0.8 fusion.22
  13.1 0.4 convolution_convert_fusion
  13.5 0.8 fusion.41
  14.3 0.5 collective-permute-start.2
  14.7 11.2 %collective-permute-done.4 = bf16[2,128,1152]{2,1,0:T(8,128)(2,1)S(1)} collective-permute-done((bf16[2,128,1152]{2,1,0:T(8,128)(2,1)S(1)}, bf16[2,128,1152]{2,1,0:T(8,128)(2,1)S(1)}, u32[]{:S(2)}, u32[]{:S(2)}) %collective-permute-start.4) | collective-permute-done | bytes 589856 | tf_op jit(solution)/shard_map/ppermute | solution.py:53
  26.1 1.2 %pad_maximum_fusion.1 = bf16[2,2,128,1152]{3,2,1,0:T(8,128)(2,1)} fusion(bf16[1,2,128,1152]{3,2,1,0:T(8,128)(2,1)S(1)} %get-tuple-element.46, bf16[1,2,128,1152]{3,2,1,0:T(8,128)(2,1)S(1)} %get-tuple-element.45), kind=kLoop, calls=%fused_computation.10 | loop fusion | flops 589824 | bytes 2359296 | tf_op jit(solution)/shard_map/stack | solution.py:55
  27.4 0.1 broadcast_in_dim.48
  27.6 0.1 select_reduce_fusion
  27.7 0.4 multiply_convert_fusion
  28.1 0.8 fusion.40
  29.0 0.4 collective-permute-start.8
  29.4 0.3 collective-permute-start.7
  29.7 3.0 %collective-permute-start.6 = (bf16[96,1024]{1,0:T(8,128)(2,1)}, bf16[96,1024]{1,0:T(8,128)(2,1)}, u32[]{:S(2)}, u32[]{:S(2)}) collective-permute-start(bf16[96,1024]{1,0:T(8,128)(2,1)} %get-tuple-element.58), channel_id=1, source_target_pairs={{0,1},{1,2},{2,3},{3,0},{4,5},{5,6},{6,7},{7,4},{8,9},{9,10},{10,1... | collective-permute-start | bytes 589832 | tf_op jit(solution)/shard_map/ppermute | solution.py:38
  32.9 6.1 %collective-permute-done.8 = bf16[96,1024]{1,0:T(8,128)(2,1)} collective-permute-done((bf16[96,1024]{1,0:T(8,128)(2,1)}, bf16[96,1024]{1,0:T(8,128)(2,1)}, u32[]{:S(2)}, u32[]{:S(2)}) %collective-permute-start.8) | collective-permute-done | bytes 196640 | tf_op jit(solution)/shard_map/ppermute | solution.py:38
  39.0 8.3 %collective-permute-done.7 = bf16[96,1024]{1,0:T(8,128)(2,1)} collective-permute-done((bf16[96,1024]{1,0:T(8,128)(2,1)}, bf16[96,1024]{1,0:T(8,128)(2,1)}, u32[]{:S(2)}, u32[]{:S(2)}) %collective-permute-start.7) | collective-permute-done | bytes 196640 | tf_op jit(solution)/shard_map/ppermute | solution.py:38
  47.3 7.9 %collective-permute-start = (bf16[96,1024]{1,0:T(8,128)(2,1)S(1)}, bf16[96,1024]{1,0:T(8,128)(2,1)S(1)}, u32[]{:S(2)}, u32[]{:S(2)}) collective-permute-start(bf16[96,1024]{1,0:T(8,128)(2,1)S(1)} %get-tuple-element.62), channel_id=1, source_target_pairs={{0,1},{1,2},{2,3},{3,0},{4,5},{5,6},{6,7},{7,4},{8,9},{9,10},{10,1... | collective-permute-start | bytes 589832 | tf_op jit(solution)/shard_map/ppermute | solution.py:38
  55.1 1.2 %pad_maximum_fusion.3 = bf16[384,1024]{1,0:T(8,128)(2,1)S(1)} fusion(bf16[96,1024]{1,0:T(8,128)(2,1)} %collective-permute-done.8, bf16[96,1024]{1,0:T(8,128)(2,1)} %collective-permute-done.7, bf16[96,1024]{1,0:T(8,128)(2,1)} %collective-permute-done.6, bf16[96,1024]{1,0:T(8,128)(2,1)S(1)} %get-tuple-element.55), kind=kLoop, calls=%fused_computation.19 | loop fusion | flops 3145728 | bytes 1572864 | tf_op jit(solution)/shard_map/concatenate | solution.py:133
  56.3 0.2 select_bitcast_fusion.1
  56.6 0.2 pad_maximum_fusion
  56.8 2.6 %collective-permute-done.1 = bf16[96,1024]{1,0:T(8,128)(2,1)S(1)} collective-permute-done((bf16[96,1024]{1,0:T(8,128)(2,1)S(1)}, bf16[96,1024]{1,0:T(8,128)(2,1)S(1)}, u32[]{:S(2)}, u32[]{:S(2)}) %collective-permute-start.1) | collective-permute-done | bytes 196640 | tf_op jit(solution)/shard_map/ppermute | solution.py:38
  59.4 1.3 %collective-permute-done = bf16[96,1024]{1,0:T(8,128)(2,1)S(1)} collective-permute-done((bf16[96,1024]{1,0:T(8,128)(2,1)S(1)}, bf16[96,1024]{1,0:T(8,128)(2,1)S(1)}, u32[]{:S(2)}, u32[]{:S(2)}) %collective-permute-start) | collective-permute-done | bytes 196640 | tf_op jit(solution)/shard_map/ppermute | solution.py:38
  60.8 1.5 %fusion.14 = f32[384,384]{1,0:T(8,128)S(1)} fusion(bf16[1,1024,1152]{2,1,0:T(8,128)(2,1)S(1)} %bitcast.101, bf16[96,1024]{1,0:T(8,128)(2,1)} %collective-permute-done.2, bf16[96,1024]{1,0:T(8,128)(2,1)S(1)} %collective-permute-done.1, bf16[96,1024]{1,0:T(8,128)(2,1)S(1)} %collective-permute-done, bf16[96,1024]{1,0:T(8,128)(2,1)S(1)} %get-tuple-element.59), kind=kOutput, calls=%fused_computation.34 | convolution fusion | flops 305135616 | bytes 2162688 | tf_op jit(solution)/shard_map/dot_general | solution.py:11
  62.3 1.5 %multiply_convert_fusion.3 = (bf16[384,384]{1,0:T(8,128)(2,1)S(1)}, f32[384,384]{1,0:T(8,128)S(1)}) fusion(f32[384,384]{1,0:T(8,128)S(1)} %fusion.14, bf16[1,1024,1152]{2,1,0:T(8,128)(2,1)S(1)} %bitcast.102, bf16[96,1024]{1,0:T(8,128)(2,1)} %collective-permute-done.2, bf16[96,1024]{1,0:T(8,128)(2,1)S(1)} %collective-permute-done.1, ...), kind=kOutput, calls=%fused_computation.40 | convolution fusion | flops 306020352 | bytes 3047424 | tf_op jit(solution)/shard_map/dot_general | solution.py:12
  63.8 0.6 convolution_convert_fusion.1
  64.4 0.6 fusion.16
  65.0 0.7 fusion.42
  65.8 2.3 %collective-permute-start.11 = (bf16[96,1024]{1,0:T(8,128)(2,1)S(1)}, bf16[96,1024]{1,0:T(8,128)(2,1)S(1)}, u32[]{:S(2)}, u32[]{:S(2)}) collective-permute-start(bf16[96,1024]{1,0:T(8,128)(2,1)S(1)} %get-tuple-element.52), channel_id=1, source_target_pairs={{0,1},{1,2},{2,3},{3,0},{4,5},{5,6},{6,7},{7,4},{8,9},{9,10},{10,1... | collective-permute-start | bytes 589832 | tf_op jit(solution)/shard_map/ppermute | solution.py:38
  68.0 2.0 %collective-permute-start.10 = (bf16[96,1024]{1,0:T(8,128)(2,1)S(1)}, bf16[96,1024]{1,0:T(8,128)(2,1)S(1)}, u32[]{:S(2)}, u32[]{:S(2)}) collective-permute-start(bf16[96,1024]{1,0:T(8,128)(2,1)S(1)} %get-tuple-element.53), channel_id=1, source_target_pairs={{0,2},{1,3},{2,0},{3,1},{4,6},{5,7},{6,4},{7,5},{8,10},{9,11},{10,... | collective-permute-start | bytes 589832 | tf_op jit(solution)/shard_map/ppermute | solution.py:38
  70.1 0.7 fusion.13
  70.8 0.6 add_convert_fusion
  71.5 3.9 %collective-permute-start.14 = (bf16[96,1024]{1,0:T(8,128)(2,1)S(1)}, bf16[96,1024]{1,0:T(8,128)(2,1)S(1)}, u32[]{:S(2)}, u32[]{:S(2)}) collective-permute-start(bf16[96,1024]{1,0:T(8,128)(2,1)S(1)} %get-tuple-element.48), channel_id=1, source_target_pairs={{0,1},{1,2},{2,3},{3,0},{4,5},{5,6},{6,7},{7,4},{8,9},{9,10},{10,1... | collective-permute-start | bytes 589832 | tf_op jit(solution)/shard_map/ppermute | solution.py:38
  75.5 9.2 %collective-permute-start.12 = (bf16[96,1024]{1,0:T(8,128)(2,1)S(1)}, bf16[96,1024]{1,0:T(8,128)(2,1)S(1)}, u32[]{:S(2)}, u32[]{:S(2)}) collective-permute-start(bf16[96,1024]{1,0:T(8,128)(2,1)S(1)} %get-tuple-element.50), channel_id=1, source_target_pairs={{0,3},{1,0},{2,1},{3,2},{4,7},{5,4},{6,5},{7,6},{8,11},{9,8},{10,9... | collective-permute-start | bytes 589832 | tf_op jit(solution)/shard_map/ppermute | solution.py:38
  84.8 12.1 %collective-permute-done.10 = bf16[96,1024]{1,0:T(8,128)(2,1)S(1)} collective-permute-done((bf16[96,1024]{1,0:T(8,128)(2,1)S(1)}, bf16[96,1024]{1,0:T(8,128)(2,1)S(1)}, u32[]{:S(2)}, u32[]{:S(2)}) %collective-permute-start.10) | collective-permute-done | bytes 196640 | tf_op jit(solution)/shard_map/ppermute | solution.py:38
  96.9 0.5 collective-permute-start.16
  97.4 0.3 convolution_multiply_fusion
  97.7 1.0 fusion.1
  98.7 5.9 %collective-permute-done.16 = f32[2,128,384]{2,1,0:T(8,128)S(1)} collective-permute-done((f32[2,128,384]{2,1,0:T(8,128)S(1)}, f32[2,128,384]{2,1,0:T(8,128)S(1)}, u32[]{:S(2)}, u32[]{:S(2)}) %collective-permute-start.16) | collective-permute-done | bytes 393248 | tf_op jit(solution)/shard_map/ppermute | solution.py:72
  104.7 0.6 collective-permute-start.17
  105.3 1.0 convolution_convert_fusion.2
  106.3 4.1 %collective-permute-done.17 = f32[1,128,384]{2,1,0:T(8,128)S(1)} collective-permute-done((f32[1,128,384]{2,1,0:T(8,128)S(1)}, f32[1,128,384]{2,1,0:T(8,128)S(1)}, u32[]{:S(2)}, u32[]{:S(2)}) %collective-permute-start.17) | collective-permute-done | bytes 196640 | tf_op jit(solution)/shard_map/ppermute | solution.py:72
  110.4 0.7 fusion.23
  (44 shorter events, 1.3 us)
Async XLA Ops:
  0.6 12.4 %copy-start = (bf16[128,1024]{1,0:T(8,128)(2,1)S(1)}, bf16[128,1024]{1,0:T(8,128)(2,1)}, u32[]{:S(2)}) copy-start(bf16[128,1024]{1,0:T(8,128)(2,1)} %param.13) | copy-start | bytes 786436
  1.7 8.8 %collective-permute-start.3 = (bf16[128,1152]{1,0:T(8,128)(2,1)S(1)}, bf16[128,1152]{1,0:T(8,128)(2,1)S(1)}, u32[]{:S(2)}, u32[]{:S(2)}) collective-permute-start(bf16[128,1152]{1,0:T(8,128)(2,1)S(1)} %maximum_bitcast_fusion), channel_id=1, source_target_pairs={{0,8},{4,12},{8,0},{12,4},{16,24},{20,28},{24,16},{28,20},{1,9},{5... | collective-permute-start | bytes 884744 | tf_op jit(solution)/shard_map/ppermute | solution.py:53
  11.7 14.3 %collective-permute-start.4 = (bf16[2,128,1152]{2,1,0:T(8,128)(2,1)S(1)}, bf16[2,128,1152]{2,1,0:T(8,128)(2,1)S(1)}, u32[]{:S(2)}, u32[]{:S(2)}) collective-permute-start(bf16[2,128,1152]{2,1,0:T(8,128)(2,1)S(1)} %pad_maximum_fusion.5), channel_id=1, source_target_pairs={{0,16},{4,20},{8,24},{12,28},{16,0},{20,4},{24,8},{28,12},{1,17},{... | collective-permute-start | bytes 1769480 | tf_op jit(solution)/shard_map/ppermute | solution.py:53
  14.3 42.5 %collective-permute-start.2 = (bf16[96,1024]{1,0:T(8,128)(2,1)}, bf16[96,1024]{1,0:T(8,128)(2,1)}, u32[]{:S(2)}, u32[]{:S(2)}) collective-permute-start(bf16[96,1024]{1,0:T(8,128)(2,1)} %get-tuple-element.60), channel_id=1, source_target_pairs={{0,3},{1,0},{2,1},{3,2},{4,7},{5,4},{6,5},{7,6},{8,11},{9,8},{10,9... | collective-permute-start | bytes 589832 | tf_op jit(solution)/shard_map/ppermute | solution.py:38
  26.1 1.2 %copy-start.4 = (f32[128,2]{0,1:T(2,128)S(1)}, f32[128,2]{0,1:T(2,128)}, u32[]{:S(2)}) copy-start(f32[128,2]{0,1:T(2,128)} %param.15) | copy-start | bytes 3076
  26.1 1.6 %copy-start.1 = (bf16[128,1024]{1,0:T(8,128)(2,1)S(1)}, bf16[128,1024]{1,0:T(8,128)(2,1)}, u32[]{:S(2)}) copy-start(bf16[128,1024]{1,0:T(8,128)(2,1)} %param.19) | copy-start | bytes 786436
  27.3 29.0 %collective-permute-start.5 = (bf16[2,2,128,1152]{3,2,1,0:T(8,128)(2,1)}, bf16[2,2,128,1152]{3,2,1,0:T(8,128)(2,1)S(1)}, u32[]{:S(2)}, u32[]{:S(2)}) collective-permute-start(bf16[2,2,128,1152]{3,2,1,0:T(8,128)(2,1)} %pad_maximum_fusion.1), channel_id=1, source_target_pairs={{0,4},{4,0},{8,12},{12,8},{16,20},{20,16},{24,28},{28,24},{1,5},{5... | collective-permute-start | bytes 3538952 | tf_op jit(solution)/shard_map/ppermute | solution.py:53
  27.6 11.4 %copy-start.2 = (bf16[96,1024]{1,0:T(8,128)(2,1)S(1)}, bf16[96,1024]{1,0:T(8,128)(2,1)}, u32[]{:S(2)}) copy-start(bf16[96,1024]{1,0:T(8,128)(2,1)} %get-tuple-element.61) | copy-start | bytes 589828
  29.0 10.0 %collective-permute-start.8 = (bf16[96,1024]{1,0:T(8,128)(2,1)}, bf16[96,1024]{1,0:T(8,128)(2,1)}, u32[]{:S(2)}, u32[]{:S(2)}) collective-permute-start(bf16[96,1024]{1,0:T(8,128)(2,1)} %get-tuple-element.56), channel_id=1, source_target_pairs={{0,3},{1,0},{2,1},{3,2},{4,7},{5,4},{6,5},{7,6},{8,11},{9,8},{10,9... | collective-permute-start | bytes 589832 | tf_op jit(solution)/shard_map/ppermute | solution.py:38
  29.4 17.9 %collective-permute-start.7 = (bf16[96,1024]{1,0:T(8,128)(2,1)}, bf16[96,1024]{1,0:T(8,128)(2,1)}, u32[]{:S(2)}, u32[]{:S(2)}) collective-permute-start(bf16[96,1024]{1,0:T(8,128)(2,1)} %get-tuple-element.57), channel_id=1, source_target_pairs={{0,2},{1,3},{2,0},{3,1},{4,6},{5,7},{6,4},{7,5},{8,10},{9,11},{10,... | collective-permute-start | bytes 589832 | tf_op jit(solution)/shard_map/ppermute | solution.py:38
  29.7 25.4 %collective-permute-start.6 = (bf16[96,1024]{1,0:T(8,128)(2,1)}, bf16[96,1024]{1,0:T(8,128)(2,1)}, u32[]{:S(2)}, u32[]{:S(2)}) collective-permute-start(bf16[96,1024]{1,0:T(8,128)(2,1)} %get-tuple-element.58), channel_id=1, source_target_pairs={{0,1},{1,2},{2,3},{3,0},{4,5},{5,6},{6,7},{7,4},{8,9},{9,10},{10,1... | collective-permute-start | bytes 589832 | tf_op jit(solution)/shard_map/ppermute | solution.py:38
  39.0 20.4 %collective-permute-start.1 = (bf16[96,1024]{1,0:T(8,128)(2,1)S(1)}, bf16[96,1024]{1,0:T(8,128)(2,1)S(1)}, u32[]{:S(2)}, u32[]{:S(2)}) collective-permute-start(bf16[96,1024]{1,0:T(8,128)(2,1)S(1)} %copy-done.2), channel_id=1, source_target_pairs={{0,2},{1,3},{2,0},{3,1},{4,6},{5,7},{6,4},{7,5},{8,10},{9,11},{10,... | collective-permute-start | bytes 589832 | tf_op jit(solution)/shard_map/ppermute | solution.py:38
  47.3 13.5 %collective-permute-start = (bf16[96,1024]{1,0:T(8,128)(2,1)S(1)}, bf16[96,1024]{1,0:T(8,128)(2,1)S(1)}, u32[]{:S(2)}, u32[]{:S(2)}) collective-permute-start(bf16[96,1024]{1,0:T(8,128)(2,1)S(1)} %get-tuple-element.62), channel_id=1, source_target_pairs={{0,1},{1,2},{2,3},{3,0},{4,5},{5,6},{6,7},{7,4},{8,9},{9,10},{10,1... | collective-permute-start | bytes 589832 | tf_op jit(solution)/shard_map/ppermute | solution.py:38
  65.8 9.8 %collective-permute-start.11 = (bf16[96,1024]{1,0:T(8,128)(2,1)S(1)}, bf16[96,1024]{1,0:T(8,128)(2,1)S(1)}, u32[]{:S(2)}, u32[]{:S(2)}) collective-permute-start(bf16[96,1024]{1,0:T(8,128)(2,1)S(1)} %get-tuple-element.52), channel_id=1, source_target_pairs={{0,1},{1,2},{2,3},{3,0},{4,5},{5,6},{6,7},{7,4},{8,9},{9,10},{10,1... | collective-permute-start | bytes 589832 | tf_op jit(solution)/shard_map/ppermute | solution.py:38
  68.0 28.8 %collective-permute-start.10 = (bf16[96,1024]{1,0:T(8,128)(2,1)S(1)}, bf16[96,1024]{1,0:T(8,128)(2,1)S(1)}, u32[]{:S(2)}, u32[]{:S(2)}) collective-permute-start(bf16[96,1024]{1,0:T(8,128)(2,1)S(1)} %get-tuple-element.53), channel_id=1, source_target_pairs={{0,2},{1,3},{2,0},{3,1},{4,6},{5,7},{6,4},{7,5},{8,10},{9,11},{10,... | collective-permute-start | bytes 589832 | tf_op jit(solution)/shard_map/ppermute | solution.py:38
  70.0 27.4 %collective-permute-start.9 = (bf16[96,1024]{1,0:T(8,128)(2,1)S(1)}, bf16[96,1024]{1,0:T(8,128)(2,1)S(1)}, u32[]{:S(2)}, u32[]{:S(2)}) collective-permute-start(bf16[96,1024]{1,0:T(8,128)(2,1)S(1)} %get-tuple-element.54), channel_id=1, source_target_pairs={{0,3},{1,0},{2,1},{3,2},{4,7},{5,4},{6,5},{7,6},{8,11},{9,8},{10,9... | collective-permute-start | bytes 589832 | tf_op jit(solution)/shard_map/ppermute | solution.py:38
  70.1 5.3 %collective-permute-start.15 = (f32[4,128,384]{2,1,0:T(8,128)S(1)}, f32[4,128,384]{2,1,0:T(8,128)S(1)}, u32[]{:S(2)}, u32[]{:S(2)}) collective-permute-start(f32[4,128,384]{2,1,0:T(8,128)S(1)} %fusion.10), channel_id=1, source_target_pairs={{0,4},{4,0},{8,12},{12,8},{16,20},{20,16},{24,28},{28,24},{1,5},{5... | collective-permute-start | bytes 2359304 | tf_op jit(solution)/shard_map/ppermute | solution.py:72
  71.5 33.8 %collective-permute-start.14 = (bf16[96,1024]{1,0:T(8,128)(2,1)S(1)}, bf16[96,1024]{1,0:T(8,128)(2,1)S(1)}, u32[]{:S(2)}, u32[]{:S(2)}) collective-permute-start(bf16[96,1024]{1,0:T(8,128)(2,1)S(1)} %get-tuple-element.48), channel_id=1, source_target_pairs={{0,1},{1,2},{2,3},{3,0},{4,5},{5,6},{6,7},{7,4},{8,9},{9,10},{10,1... | collective-permute-start | bytes 589832 | tf_op jit(solution)/shard_map/ppermute | solution.py:38
  75.4 22.0 %copy-start.3 = (pred[128,2,384]{2,0,1:T(32,128)(4,1)S(1)}, pred[128,2,384]{2,0,1:T(32,128)(4,1)}, u32[]{:S(2)}) copy-start(pred[128,2,384]{2,0,1:T(32,128)(4,1)} %get-tuple-element.68) | copy-start | bytes 294916
  75.4 29.9 %collective-permute-start.13 = (bf16[96,1024]{1,0:T(8,128)(2,1)S(1)}, bf16[96,1024]{1,0:T(8,128)(2,1)S(1)}, u32[]{:S(2)}, u32[]{:S(2)}) collective-permute-start(bf16[96,1024]{1,0:T(8,128)(2,1)S(1)} %get-tuple-element.49), channel_id=1, source_target_pairs={{0,2},{1,3},{2,0},{3,1},{4,6},{5,7},{6,4},{7,5},{8,10},{9,11},{10,... | collective-permute-start | bytes 589832 | tf_op jit(solution)/shard_map/ppermute | solution.py:38
  75.5 29.7 %collective-permute-start.12 = (bf16[96,1024]{1,0:T(8,128)(2,1)S(1)}, bf16[96,1024]{1,0:T(8,128)(2,1)S(1)}, u32[]{:S(2)}, u32[]{:S(2)}) collective-permute-start(bf16[96,1024]{1,0:T(8,128)(2,1)S(1)} %get-tuple-element.50), channel_id=1, source_target_pairs={{0,3},{1,0},{2,1},{3,2},{4,7},{5,4},{6,5},{7,6},{8,11},{9,8},{10,9... | collective-permute-start | bytes 589832 | tf_op jit(solution)/shard_map/ppermute | solution.py:38
  96.9 7.8 %collective-permute-start.16 = (f32[2,128,384]{2,1,0:T(8,128)S(1)}, f32[2,128,384]{2,1,0:T(8,128)S(1)}, u32[]{:S(2)}, u32[]{:S(2)}) collective-permute-start(f32[2,128,384]{2,1,0:T(8,128)S(1)} %select_bitcast_fusion.4), channel_id=1, source_target_pairs={{0,8},{4,12},{8,0},{12,4},{16,24},{20,28},{24,16},{28,20},{1,9},{5... | collective-permute-start | bytes 1179656 | tf_op jit(solution)/shard_map/ppermute | solution.py:72
  104.7 5.7 %collective-permute-start.17 = (f32[1,128,384]{2,1,0:T(8,128)S(1)}, f32[1,128,384]{2,1,0:T(8,128)S(1)}, u32[]{:S(2)}, u32[]{:S(2)}) collective-permute-start(f32[1,128,384]{2,1,0:T(8,128)S(1)} %select_bitcast_fusion.7), channel_id=1, source_target_pairs={{0,16},{4,20},{8,24},{12,28},{16,0},{20,4},{24,8},{28,12},{1,17},{... | collective-permute-start | bytes 589832 | tf_op jit(solution)/shard_map/ppermute | solution.py:72

commit v13 on v9

--- a/solution.py
+++ b/solution.py
@@ -59,11 +59,13 @@
     return work.reshape((n_dp,) + block.shape)
 
 
-def reduce_scatter_dp(pieces, n_dp):
+def reduce_scatter_dp(pieces, n_dp, hold=None):
     me = lax.axis_index("dp")
     work = pieces
     bit = 1
     while bit < n_dp:
+        if bit == 2 and hold is not None:
+            work, hold = lax.optimization_barrier((work, hold))
         halves = work.reshape((work.shape[0] // 2, 2) + work.shape[1:])
         mine = (me // bit) % 2
         keep = jnp.take(halves, mine, axis=1)
@@ -71,7 +73,7 @@
         pairs = [(i, i ^ bit) for i in range(n_dp)]
         work = keep + lax.ppermute(give, "dp", pairs)
         bit *= 2
-    return work[0]
+    return work[0], hold
 
 
 def local(tokens, expert_ids, routing, w_gate, w_up, w_down, grad_out):
@@ -136,6 +138,7 @@
     pieces = lax.dot_general(g_rows, hidden, contract_first, preferred_element_type=jnp.float32)
     block_rows = local_count * capacity
     out_blocks = [expert_out[s * block_rows : (s + 1) * block_rows] for s in range(groups)]
+    summed, pair_grad = reduce_scatter_dp(pieces.reshape(n_dp, shard_d, ff_width), n_dp, pair_grad)
     grad_blocks = [pair_grad[s * block_rows : (s + 1) * block_rows] for s in range(groups)]
     back_out = jnp.concatenate(shift_send(out_blocks, groups, -1), axis=0)
     back_grad = jnp.concatenate(shift_send(grad_blocks, groups, -1), axis=0)
@@ -151,7 +154,6 @@
     token_grad = jnp.dot(
         gather_both, back_grad, preferred_element_type=jnp.float32
     ).astype(jnp.bfloat16)
-    summed = reduce_scatter_dp(pieces.reshape(n_dp, shard_d, ff_width), n_dp)
     down_grad = (summed / n_dp).reshape(local_count, shard_d, ff_width)
     return (output, token_grad, down_grad)
 

time: 87.6 us -> 116 us (1.32)
  waiting for transfers between devices: 37.8 us -> 58.3 us
  starting transfers between devices: 26.1 us -> 36.8 us
  local copies, waits for them, and re-layouts: 4.47 us -> 2.45 us
    ppermute x12, waiting for transfers between devices: 14.7 us -> 35.2 us  [shift_send(): got.append(lax.ppermute(blocks[step], 'expert', pairs))]
    ppermute x12, starting transfers between devices: 18.1 us -> 28.8 us  [shift_send(): got.append(lax.ppermute(blocks[step], 'expert', pairs))]
    ppermute x3, waiting for transfers between devices: 12.2 us -> 17.7 us  [all_gather_dp(): recv = lax.ppermute(work, 'dp', [(i, i ^ bit) for i in range(n_dp)])]
    ppermute x3, waiting for transfers between devices: 10.9 us -> 5.47 us  [reduce_scatter_dp(): work = keep + lax.ppermute(give, 'dp', pairs)]
  transfers between devices with their start and end apart: 18 -> 18, of which waited for: 6 -> 8; matrix products, arithmetic and copies ran while one was open for 21% -> 12% of each run, Pallas kernels for 0% -> 0%
where the time goes in v13:
time: 116 us
  waiting for transfers between devices  58.3 us (50%)
  starting transfers between devices  36.8 us (32%)
  matrix products  11.8 us (10%)
  other arithmetic  5.41 us (5%)
  local copies, waits for them, and re-layouts  2.45 us (2%)
    ppermute x12, waiting for transfers between devices, shift_send(): got.append(lax.ppermute(blocks[step], 'expert', pairs))  35.2 us
    ppermute x12, starting transfers between devices, shift_send(): got.append(lax.ppermute(blocks[step], 'expert', pairs))  28.8 us
    ppermute x3, waiting for transfers between devices, all_gather_dp(): recv = lax.ppermute(work, 'dp', [(i, i ^ bit) for i in range(n_dp)])  17.7 us
    ppermute x3, waiting for transfers between devices, reduce_scatter_dp(): work = keep + lax.ppermute(give, 'dp', pairs)  5.47 us
    ppermute x3, starting transfers between devices, all_gather_dp(): recv = lax.ppermute(work, 'dp', [(i, i ^ bit) for i in range(n_dp)])  4.87 us
    ppermute x3, starting transfers between devices, reduce_scatter_dp(): work = keep + lax.ppermute(give, 'dp', pairs)  3.15 us
    another operation x6, other arithmetic, all_gather_dp(): jnp.stack([jnp.where(upper, recv, work), jnp.where(upper, work, recv)], a...  2.93 us
  transfers between devices with their start and end apart: 18, of which 8 were waited for; matrix products, arithmetic and copies ran while one was open for 12% of the time, Pallas kernels for 0%

profile of v13, /device:TPU:0, one launch (start us, length us, event | category | flops | bytes accessed | tf_op | source)
XLA Modules:
  0.0 115.8 jit_solution(4445818787822334011)
XLA Ops:
  0.6 1.1 maximum_bitcast_fusion
  1.7 3.0 %collective-permute-start.3 = (bf16[128,1152]{1,0:T(8,128)(2,1)S(1)}, bf16[128,1152]{1,0:T(8,128)(2,1)S(1)}, u32[]{:S(2)}, u32[]{:S(2)}) collective-permute-start(bf16[128,1152]{1,0:T(8,128)(2,1)S(1)} %maximum_bitcast_fusion), channel_id=1, source_target_pairs={{0,8},{4,12},{8,0},{12,4},{16,24},{20,28},{24,16},{28,20},{1,9},{5... | collective-permute-start | bytes 884744 | tf_op jit(solution)/shard_map/ppermute | solution.py:53
  4.8 0.8 copy.19
  5.5 0.1 sub.46
  5.7 0.2 fusion.2
  5.9 0.1 convert_element_type.57
  6.1 5.7 %collective-permute-done.3 = bf16[128,1152]{1,0:T(8,128)(2,1)S(1)} collective-permute-done((bf16[128,1152]{1,0:T(8,128)(2,1)S(1)}, bf16[128,1152]{1,0:T(8,128)(2,1)S(1)}, u32[]{:S(2)}, u32[]{:S(2)}) %collective-permute-start.3) | collective-permute-done | bytes 294944 | tf_op jit(solution)/shard_map/ppermute | solution.py:53
  11.8 1.1 select_bitcast_fusion.6
  12.9 1.8 %collective-permute-start.4 = (bf16[2,128,1152]{2,1,0:T(8,128)(2,1)S(1)}, bf16[2,128,1152]{2,1,0:T(8,128)(2,1)S(1)}, u32[]{:S(2)}, u32[]{:S(2)}) collective-permute-start(bf16[2,128,1152]{2,1,0:T(8,128)(2,1)S(1)} %pad_maximum_fusion.5), channel_id=1, source_target_pairs={{0,16},{4,20},{8,24},{12,28},{16,0},{20,4},{24,8},{28,12},{1,17},{... | collective-permute-start | bytes 1769480 | tf_op jit(solution)/shard_map/ppermute | solution.py:53
  15.0 0.1 broadcast_in_dim.48
  15.2 0.1 select_reduce_fusion
  15.3 0.1 fusion.22
  15.5 12.0 %collective-permute-done.4 = bf16[2,128,1152]{2,1,0:T(8,128)(2,1)S(1)} collective-permute-done((bf16[2,128,1152]{2,1,0:T(8,128)(2,1)S(1)}, bf16[2,128,1152]{2,1,0:T(8,128)(2,1)S(1)}, u32[]{:S(2)}, u32[]{:S(2)}) %collective-permute-start.4) | collective-permute-done | bytes 589856 | tf_op jit(solution)/shard_map/ppermute | solution.py:53
  27.6 1.2 %pad_maximum_fusion.1 = bf16[2,2,128,1152]{3,2,1,0:T(8,128)(2,1)} fusion(bf16[1,2,128,1152]{3,2,1,0:T(8,128)(2,1)S(1)} %get-tuple-element.46, bf16[1,2,128,1152]{3,2,1,0:T(8,128)(2,1)S(1)} %get-tuple-element.45), kind=kLoop, calls=%fused_computation.10 | loop fusion | flops 589824 | bytes 2359296 | tf_op jit(solution)/shard_map/stack | solution.py:55
  28.8 0.4 multiply_convert_fusion
  29.3 2.6 %collective-permute-start.10 = (bf16[96,1024]{1,0:T(8,128)(2,1)S(1)}, bf16[96,1024]{1,0:T(8,128)(2,1)}, u32[]{:S(2)}, u32[]{:S(2)}) collective-permute-start(bf16[96,1024]{1,0:T(8,128)(2,1)S(1)} %get-tuple-element.53), channel_id=1, source_target_pairs={{0,2},{1,3},{2,0},{3,1},{4,6},{5,7},{6,4},{7,5},{8,10},{9,11},{10,... | collective-permute-start | bytes 589832 | tf_op jit(solution)/shard_map/ppermute | solution.py:38
  31.9 1.3 %collective-permute-start.11 = (bf16[96,1024]{1,0:T(8,128)(2,1)S(1)}, bf16[96,1024]{1,0:T(8,128)(2,1)}, u32[]{:S(2)}, u32[]{:S(2)}) collective-permute-start(bf16[96,1024]{1,0:T(8,128)(2,1)S(1)} %get-tuple-element.52), channel_id=1, source_target_pairs={{0,3},{1,0},{2,1},{3,2},{4,7},{5,4},{6,5},{7,6},{8,11},{9,8},{10,9... | collective-permute-start | bytes 589832 | tf_op jit(solution)/shard_map/ppermute | solution.py:38
  33.2 0.4 convolution_convert_fusion
  33.7 0.9 fusion.44
  34.5 0.7 collective-permute-start
  35.2 1.0 collective-permute-start.1
  36.4 3.0 %collective-permute-start.2 = (bf16[96,1024]{1,0:T(8,128)(2,1)}, bf16[96,1024]{1,0:T(8,128)(2,1)S(1)}, u32[]{:S(2)}, u32[]{:S(2)}) collective-permute-start(bf16[96,1024]{1,0:T(8,128)(2,1)} %get-tuple-element.60), channel_id=1, source_target_pairs={{0,3},{1,0},{2,1},{3,2},{4,7},{5,4},{6,5},{7,6},{8,11},{9,8},{10,9... | collective-permute-start | bytes 589832 | tf_op jit(solution)/shard_map/ppermute | solution.py:38
  39.3 0.2 select_bitcast_fusion.1
  39.6 0.2 pad_maximum_fusion
  39.9 7.8 %collective-permute-done = bf16[96,1024]{1,0:T(8,128)(2,1)} collective-permute-done((bf16[96,1024]{1,0:T(8,128)(2,1)}, bf16[96,1024]{1,0:T(8,128)(2,1)}, u32[]{:S(2)}, u32[]{:S(2)}) %collective-permute-start) | collective-permute-done | bytes 196640 | tf_op jit(solution)/shard_map/ppermute | solution.py:38
  47.7 11.8 %collective-permute-start.9 = (bf16[96,1024]{1,0:T(8,128)(2,1)S(1)}, bf16[96,1024]{1,0:T(8,128)(2,1)S(1)}, u32[]{:S(2)}, u32[]{:S(2)}) collective-permute-start(bf16[96,1024]{1,0:T(8,128)(2,1)S(1)} %get-tuple-element.54), channel_id=1, source_target_pairs={{0,1},{1,2},{2,3},{3,0},{4,5},{5,6},{6,7},{7,4},{8,9},{9,10},{10,1... | collective-permute-start | bytes 589832 | tf_op jit(solution)/shard_map/ppermute | solution.py:38
  59.4 4.0 %collective-permute-done.1 = bf16[96,1024]{1,0:T(8,128)(2,1)} collective-permute-done((bf16[96,1024]{1,0:T(8,128)(2,1)}, bf16[96,1024]{1,0:T(8,128)(2,1)}, u32[]{:S(2)}, u32[]{:S(2)}) %collective-permute-start.1) | collective-permute-done | bytes 196640 | tf_op jit(solution)/shard_map/ppermute | solution.py:38
  63.4 1.6 %fusion.14 = f32[384,384]{1,0:T(8,128)S(1)} fusion(bf16[1,1024,1152]{2,1,0:T(8,128)(2,1)S(1)} %bitcast.97, bf16[96,1024]{1,0:T(8,128)(2,1)S(1)} %collective-permute-done.2, bf16[96,1024]{1,0:T(8,128)(2,1)} %collective-permute-done.1, bf16[96,1024]{1,0:T(8,128)(2,1)} %collective-permute-done, bf16[96,1024]{1,0:T(8,128)(2,1)S(1)} %copy-done.2), kind=kOutput, calls=%fused_computation.34 | convolution fusion | flops 305135616 | bytes 2162688 | tf_op jit(solution)/shard_map/dot_general | solution.py:11
  65.0 1.6 %multiply_convert_fusion.3 = (bf16[384,384]{1,0:T(8,128)(2,1)S(1)}, f32[384,384]{1,0:T(8,128)S(1)}) fusion(f32[384,384]{1,0:T(8,128)S(1)} %fusion.14, bf16[1,1024,1152]{2,1,0:T(8,128)(2,1)S(1)} %bitcast.98, bf16[96,1024]{1,0:T(8,128)(2,1)S(1)} %collective-permute-done.2, bf16[96,1024]{1,0:T(8,128)(2,1)} %collective-permute-done.1, ...), kind=kOutput, calls=%fused_computation.40 | convolution fusion | flops 306020352 | bytes 3047424 | tf_op jit(solution)/shard_map/dot_general | solution.py:12
  66.7 0.6 convolution_convert_fusion.1
  67.3 1.7 %fusion.24 = f32[1024,384]{1,0:T(8,128)S(1)} fusion(bf16[384,384]{1,0:T(8,128)(2,1)S(1)} %get-tuple-element.69, bf16[96,1024]{1,0:T(8,128)(2,1)} %collective-permute-done.11, bf16[96,1024]{1,0:T(8,128)(2,1)} %collective-permute-done.10, bf16[96,1024]{1,0:T(8,128)(2,1)S(1)} %collective-permute-done.9, bf16[96,1024]{1,0:T(8,128)(2,1)S(1)} %get-tuple-element.51), kind=kOutput, calls=%fused_computation.65 | convolution fusion | flops 305135616 | bytes 2654208 | tf_op jit(solution)/shard_map/dot_general | solution.py:138
  69.2 3.3 %collective-permute-start.6 = (bf16[96,1024]{1,0:T(8,128)(2,1)S(1)}, bf16[96,1024]{1,0:T(8,128)(2,1)S(1)}, u32[]{:S(2)}, u32[]{:S(2)}) collective-permute-start(bf16[96,1024]{1,0:T(8,128)(2,1)S(1)} %get-tuple-element.58), channel_id=1, source_target_pairs={{0,3},{1,0},{2,1},{3,2},{4,7},{5,4},{6,5},{7,6},{8,11},{9,8},{10,9... | collective-permute-start | bytes 589832 | tf_op jit(solution)/shard_map/ppermute | solution.py:38
  72.6 2.4 %collective-permute-start.7 = (bf16[96,1024]{1,0:T(8,128)(2,1)S(1)}, bf16[96,1024]{1,0:T(8,128)(2,1)S(1)}, u32[]{:S(2)}, u32[]{:S(2)}) collective-permute-start(bf16[96,1024]{1,0:T(8,128)(2,1)S(1)} %get-tuple-element.57), channel_id=1, source_target_pairs={{0,2},{1,3},{2,0},{3,1},{4,6},{5,7},{6,4},{7,5},{8,10},{9,11},{10,... | collective-permute-start | bytes 589832 | tf_op jit(solution)/shard_map/ppermute | solution.py:38
  75.0 1.6 %fusion.16 = f32[384,384]{1,0:T(8,128)S(1)} fusion(bf16[1,1024,1152]{2,1,0:T(8,128)(2,1)S(1)} %bitcast.100, bf16[96,1024]{1,0:T(8,128)(2,1)} %collective-permute-done.11, bf16[96,1024]{1,0:T(8,128)(2,1)} %collective-permute-done.10, bf16[96,1024]{1,0:T(8,128)(2,1)S(1)} %collective-permute-done.9, bf16[96,1024]{1,0:T(8,128)(2,1)S(1)} %get-tuple-element.51), kind=kOutput, calls=%fused_computation.36 | convolution fusion | flops 305135616 | bytes 2162688 | tf_op jit(solution)/shard_map/dot_general | solution.py:22
  76.5 0.7 fusion.13
  77.2 0.6 add_convert_fusion
  77.9 1.2 %collective-permute-done.6 = bf16[96,1024]{1,0:T(8,128)(2,1)S(1)} collective-permute-done((bf16[96,1024]{1,0:T(8,128)(2,1)S(1)}, bf16[96,1024]{1,0:T(8,128)(2,1)S(1)}, u32[]{:S(2)}, u32[]{:S(2)}) %collective-permute-start.6) | collective-permute-done | bytes 196640 | tf_op jit(solution)/shard_map/ppermute | solution.py:38
  79.0 13.8 %collective-permute-done.7 = bf16[96,1024]{1,0:T(8,128)(2,1)S(1)} collective-permute-done((bf16[96,1024]{1,0:T(8,128)(2,1)S(1)}, bf16[96,1024]{1,0:T(8,128)(2,1)S(1)}, u32[]{:S(2)}, u32[]{:S(2)}) %collective-permute-start.7) | collective-permute-done | bytes 196640 | tf_op jit(solution)/shard_map/ppermute | solution.py:38
  92.9 0.3 convolution_multiply_fusion
  93.3 1.5 %collective-permute-start.16 = (f32[2,128,384]{2,1,0:T(8,128)S(1)}, f32[2,128,384]{2,1,0:T(8,128)S(1)}, u32[]{:S(2)}, u32[]{:S(2)}) collective-permute-start(f32[2,128,384]{2,1,0:T(8,128)S(1)} %select_bitcast_fusion.4), channel_id=1, source_target_pairs={{0,8},{4,12},{8,0},{12,4},{16,24},{20,28},{24,16},{28,20},{1,9},{5... | collective-permute-start | bytes 1179656 | tf_op jit(solution)/shard_map/ppermute | solution.py:74
  94.9 1.0 fusion.1
  96.0 0.6 collective-permute-start.14
  96.6 1.9 %collective-permute-start.15 = (bf16[96,1024]{1,0:T(8,128)(2,1)S(1)}, bf16[96,1024]{1,0:T(8,128)(2,1)S(1)}, u32[]{:S(2)}, u32[]{:S(2)}) collective-permute-start(bf16[96,1024]{1,0:T(8,128)(2,1)S(1)} %get-tuple-element.48), channel_id=1, source_target_pairs={{0,1},{1,2},{2,3},{3,0},{4,5},{5,6},{6,7},{7,4},{8,9},{9,10},{10,1... | collective-permute-start | bytes 589832 | tf_op jit(solution)/shard_map/ppermute | solution.py:38
  98.6 5.5 %collective-permute-done.16 = f32[2,128,384]{2,1,0:T(8,128)S(1)} collective-permute-done((f32[2,128,384]{2,1,0:T(8,128)S(1)}, f32[2,128,384]{2,1,0:T(8,128)S(1)}, u32[]{:S(2)}, u32[]{:S(2)}) %collective-permute-start.16) | collective-permute-done | bytes 393248 | tf_op jit(solution)/shard_map/ppermute | solution.py:74
  104.1 1.6 %collective-permute-start.17 = (f32[1,128,384]{2,1,0:T(8,128)S(1)}, f32[1,128,384]{2,1,0:T(8,128)S(1)}, u32[]{:S(2)}, u32[]{:S(2)}) collective-permute-start(f32[1,128,384]{2,1,0:T(8,128)S(1)} %select_bitcast_fusion.7), channel_id=1, source_target_pairs={{0,16},{4,20},{8,24},{12,28},{16,0},{20,4},{24,8},{28,12},{1,17},{... | collective-permute-start | bytes 589832 | tf_op jit(solution)/shard_map/ppermute | solution.py:74
  105.7 8.3 %collective-permute-done.14 = bf16[96,1024]{1,0:T(8,128)(2,1)S(1)} collective-permute-done((bf16[96,1024]{1,0:T(8,128)(2,1)S(1)}, bf16[96,1024]{1,0:T(8,128)(2,1)S(1)}, u32[]{:S(2)}, u32[]{:S(2)}) %collective-permute-start.14) | collective-permute-done | bytes 196640 | tf_op jit(solution)/shard_map/ppermute | solution.py:38
  114.0 1.0 convolution_convert_fusion.2
  115.1 0.7 fusion.23
  (41 shorter events, 1.2 us)
Async XLA Ops:
  0.6 28.2 %copy-start = (bf16[128,1024]{1,0:T(8,128)(2,1)S(1)}, bf16[128,1024]{1,0:T(8,128)(2,1)}, u32[]{:S(2)}) copy-start(bf16[128,1024]{1,0:T(8,128)(2,1)} %param.19) | copy-start | bytes 786436
  1.7 13.2 %copy-start.3 = (f32[128,2]{0,1:T(2,128)S(1)}, f32[128,2]{0,1:T(2,128)}, u32[]{:S(2)}) copy-start(f32[128,2]{0,1:T(2,128)} %param.15) | copy-start | bytes 3076
  1.7 10.0 %collective-permute-start.3 = (bf16[128,1152]{1,0:T(8,128)(2,1)S(1)}, bf16[128,1152]{1,0:T(8,128)(2,1)S(1)}, u32[]{:S(2)}, u32[]{:S(2)}) collective-permute-start(bf16[128,1152]{1,0:T(8,128)(2,1)S(1)} %maximum_bitcast_fusion), channel_id=1, source_target_pairs={{0,8},{4,12},{8,0},{12,4},{16,24},{20,28},{24,16},{28,20},{1,9},{5... | collective-permute-start | bytes 884744 | tf_op jit(solution)/shard_map/ppermute | solution.py:53
  12.9 14.6 %collective-permute-start.4 = (bf16[2,128,1152]{2,1,0:T(8,128)(2,1)S(1)}, bf16[2,128,1152]{2,1,0:T(8,128)(2,1)S(1)}, u32[]{:S(2)}, u32[]{:S(2)}) collective-permute-start(bf16[2,128,1152]{2,1,0:T(8,128)(2,1)S(1)} %pad_maximum_fusion.5), channel_id=1, source_target_pairs={{0,16},{4,20},{8,24},{12,28},{16,0},{20,4},{24,8},{28,12},{1,17},{... | collective-permute-start | bytes 1769480 | tf_op jit(solution)/shard_map/ppermute | solution.py:53
  28.8 4.5 %copy-start.1 = (bf16[128,1024]{1,0:T(8,128)(2,1)S(1)}, bf16[128,1024]{1,0:T(8,128)(2,1)}, u32[]{:S(2)}) copy-start(bf16[128,1024]{1,0:T(8,128)(2,1)} %param.13) | copy-start | bytes 786436
  28.8 7.6 %collective-permute-start.5 = (bf16[2,2,128,1152]{3,2,1,0:T(8,128)(2,1)}, bf16[2,2,128,1152]{3,2,1,0:T(8,128)(2,1)S(1)}, u32[]{:S(2)}, u32[]{:S(2)}) collective-permute-start(bf16[2,2,128,1152]{3,2,1,0:T(8,128)(2,1)} %pad_maximum_fusion.1), channel_id=1, source_target_pairs={{0,4},{4,0},{8,12},{12,8},{16,20},{20,16},{24,28},{28,24},{1,5},{5... | collective-permute-start | bytes 3538952 | tf_op jit(solution)/shard_map/ppermute | solution.py:53
  29.3 38.0 %collective-permute-start.10 = (bf16[96,1024]{1,0:T(8,128)(2,1)S(1)}, bf16[96,1024]{1,0:T(8,128)(2,1)}, u32[]{:S(2)}, u32[]{:S(2)}) collective-permute-start(bf16[96,1024]{1,0:T(8,128)(2,1)S(1)} %get-tuple-element.53), channel_id=1, source_target_pairs={{0,2},{1,3},{2,0},{3,1},{4,6},{5,7},{6,4},{7,5},{8,10},{9,11},{10,... | collective-permute-start | bytes 589832 | tf_op jit(solution)/shard_map/ppermute | solution.py:38
  31.9 35.4 %collective-permute-start.11 = (bf16[96,1024]{1,0:T(8,128)(2,1)S(1)}, bf16[96,1024]{1,0:T(8,128)(2,1)}, u32[]{:S(2)}, u32[]{:S(2)}) collective-permute-start(bf16[96,1024]{1,0:T(8,128)(2,1)S(1)} %get-tuple-element.52), channel_id=1, source_target_pairs={{0,3},{1,0},{2,1},{3,2},{4,7},{5,4},{6,5},{7,6},{8,11},{9,8},{10,9... | collective-permute-start | bytes 589832 | tf_op jit(solution)/shard_map/ppermute | solution.py:38
  34.5 13.1 %collective-permute-start = (bf16[96,1024]{1,0:T(8,128)(2,1)}, bf16[96,1024]{1,0:T(8,128)(2,1)}, u32[]{:S(2)}, u32[]{:S(2)}) collective-permute-start(bf16[96,1024]{1,0:T(8,128)(2,1)} %get-tuple-element.62), channel_id=1, source_target_pairs={{0,1},{1,2},{2,3},{3,0},{4,5},{5,6},{6,7},{7,4},{8,9},{9,10},{10,1... | collective-permute-start | bytes 589832 | tf_op jit(solution)/shard_map/ppermute | solution.py:38
  35.2 28.2 %collective-permute-start.1 = (bf16[96,1024]{1,0:T(8,128)(2,1)}, bf16[96,1024]{1,0:T(8,128)(2,1)}, u32[]{:S(2)}, u32[]{:S(2)}) collective-permute-start(bf16[96,1024]{1,0:T(8,128)(2,1)} %get-tuple-element.61), channel_id=1, source_target_pairs={{0,2},{1,3},{2,0},{3,1},{4,6},{5,7},{6,4},{7,5},{8,10},{9,11},{10,... | collective-permute-start | bytes 589832 | tf_op jit(solution)/shard_map/ppermute | solution.py:38
  36.4 27.1 %collective-permute-start.2 = (bf16[96,1024]{1,0:T(8,128)(2,1)}, bf16[96,1024]{1,0:T(8,128)(2,1)S(1)}, u32[]{:S(2)}, u32[]{:S(2)}) collective-permute-start(bf16[96,1024]{1,0:T(8,128)(2,1)} %get-tuple-element.60), channel_id=1, source_target_pairs={{0,3},{1,0},{2,1},{3,2},{4,7},{5,4},{6,5},{7,6},{8,11},{9,8},{10,9... | collective-permute-start | bytes 589832 | tf_op jit(solution)/shard_map/ppermute | solution.py:38
  39.6 23.8 %copy-start.2 = (bf16[96,1024]{1,0:T(8,128)(2,1)S(1)}, bf16[96,1024]{1,0:T(8,128)(2,1)}, u32[]{:S(2)}) copy-start(bf16[96,1024]{1,0:T(8,128)(2,1)} %get-tuple-element.59) | copy-start | bytes 589828
  47.7 19.6 %collective-permute-start.9 = (bf16[96,1024]{1,0:T(8,128)(2,1)S(1)}, bf16[96,1024]{1,0:T(8,128)(2,1)S(1)}, u32[]{:S(2)}, u32[]{:S(2)}) collective-permute-start(bf16[96,1024]{1,0:T(8,128)(2,1)S(1)} %get-tuple-element.54), channel_id=1, source_target_pairs={{0,1},{1,2},{2,3},{3,0},{4,5},{5,6},{6,7},{7,4},{8,9},{9,10},{10,1... | collective-permute-start | bytes 589832 | tf_op jit(solution)/shard_map/ppermute | solution.py:38
  69.1 24.1 %collective-permute-start.12 = (f32[4,128,384]{2,1,0:T(8,128)S(1)}, f32[4,128,384]{2,1,0:T(8,128)S(1)}, u32[]{:S(2)}, u32[]{:S(2)}) collective-permute-start(f32[4,128,384]{2,1,0:T(8,128)S(1)} %fusion.10), channel_id=1, source_target_pairs={{0,4},{4,0},{8,12},{12,8},{16,20},{20,16},{24,28},{28,24},{1,5},{5... | collective-permute-start | bytes 2359304 | tf_op jit(solution)/shard_map/ppermute | solution.py:74
  69.2 9.8 %collective-permute-start.6 = (bf16[96,1024]{1,0:T(8,128)(2,1)S(1)}, bf16[96,1024]{1,0:T(8,128)(2,1)S(1)}, u32[]{:S(2)}, u32[]{:S(2)}) collective-permute-start(bf16[96,1024]{1,0:T(8,128)(2,1)S(1)} %get-tuple-element.58), channel_id=1, source_target_pairs={{0,3},{1,0},{2,1},{3,2},{4,7},{5,4},{6,5},{7,6},{8,11},{9,8},{10,9... | collective-permute-start | bytes 589832 | tf_op jit(solution)/shard_map/ppermute | solution.py:38
  72.6 20.3 %collective-permute-start.7 = (bf16[96,1024]{1,0:T(8,128)(2,1)S(1)}, bf16[96,1024]{1,0:T(8,128)(2,1)S(1)}, u32[]{:S(2)}, u32[]{:S(2)}) collective-permute-start(bf16[96,1024]{1,0:T(8,128)(2,1)S(1)} %get-tuple-element.57), channel_id=1, source_target_pairs={{0,2},{1,3},{2,0},{3,1},{4,6},{5,7},{6,4},{7,5},{8,10},{9,11},{10,... | collective-permute-start | bytes 589832 | tf_op jit(solution)/shard_map/ppermute | solution.py:38
  74.9 17.9 %collective-permute-start.8 = (bf16[96,1024]{1,0:T(8,128)(2,1)S(1)}, bf16[96,1024]{1,0:T(8,128)(2,1)S(1)}, u32[]{:S(2)}, u32[]{:S(2)}) collective-permute-start(bf16[96,1024]{1,0:T(8,128)(2,1)S(1)} %get-tuple-element.56), channel_id=1, source_target_pairs={{0,1},{1,2},{2,3},{3,0},{4,5},{5,6},{6,7},{7,4},{8,9},{9,10},{10,1... | collective-permute-start | bytes 589832 | tf_op jit(solution)/shard_map/ppermute | solution.py:38
  93.3 10.7 %collective-permute-start.16 = (f32[2,128,384]{2,1,0:T(8,128)S(1)}, f32[2,128,384]{2,1,0:T(8,128)S(1)}, u32[]{:S(2)}, u32[]{:S(2)}) collective-permute-start(f32[2,128,384]{2,1,0:T(8,128)S(1)} %select_bitcast_fusion.4), channel_id=1, source_target_pairs={{0,8},{4,12},{8,0},{12,4},{16,24},{20,28},{24,16},{28,20},{1,9},{5... | collective-permute-start | bytes 1179656 | tf_op jit(solution)/shard_map/ppermute | solution.py:74
  95.9 9.8 %collective-permute-start.13 = (bf16[96,1024]{1,0:T(8,128)(2,1)S(1)}, bf16[96,1024]{1,0:T(8,128)(2,1)S(1)}, u32[]{:S(2)}, u32[]{:S(2)}) collective-permute-start(bf16[96,1024]{1,0:T(8,128)(2,1)S(1)} %get-tuple-element.50), channel_id=1, source_target_pairs={{0,3},{1,0},{2,1},{3,2},{4,7},{5,4},{6,5},{7,6},{8,11},{9,8},{10,9... | collective-permute-start | bytes 589832 | tf_op jit(solution)/shard_map/ppermute | solution.py:38
  96.0 18.0 %collective-permute-start.14 = (bf16[96,1024]{1,0:T(8,128)(2,1)S(1)}, bf16[96,1024]{1,0:T(8,128)(2,1)S(1)}, u32[]{:S(2)}, u32[]{:S(2)}) collective-permute-start(bf16[96,1024]{1,0:T(8,128)(2,1)S(1)} %get-tuple-element.49), channel_id=1, source_target_pairs={{0,2},{1,3},{2,0},{3,1},{4,6},{5,7},{6,4},{7,5},{8,10},{9,11},{10,... | collective-permute-start | bytes 589832 | tf_op jit(solution)/shard_map/ppermute | solution.py:38
  96.6 17.4 %collective-permute-start.15 = (bf16[96,1024]{1,0:T(8,128)(2,1)S(1)}, bf16[96,1024]{1,0:T(8,128)(2,1)S(1)}, u32[]{:S(2)}, u32[]{:S(2)}) collective-permute-start(bf16[96,1024]{1,0:T(8,128)(2,1)S(1)} %get-tuple-element.48), channel_id=1, source_target_pairs={{0,1},{1,2},{2,3},{3,0},{4,5},{5,6},{6,7},{7,4},{8,9},{9,10},{10,1... | collective-permute-start | bytes 589832 | tf_op jit(solution)/shard_map/ppermute | solution.py:38
  104.1 10.9 %collective-permute-start.17 = (f32[1,128,384]{2,1,0:T(8,128)S(1)}, f32[1,128,384]{2,1,0:T(8,128)S(1)}, u32[]{:S(2)}, u32[]{:S(2)}) collective-permute-start(f32[1,128,384]{2,1,0:T(8,128)S(1)} %select_bitcast_fusion.7), channel_id=1, source_target_pairs={{0,16},{4,20},{8,24},{12,28},{16,0},{20,4},{24,8},{28,12},{1,17},{... | collective-permute-start | bytes 589832 | tf_op jit(solution)/shard_map/ppermute | solution.py:74

commit v14 on v9

--- a/solution.py
+++ b/solution.py
@@ -61,17 +61,23 @@
 
 def reduce_scatter_dp(pieces, n_dp):
     me = lax.axis_index("dp")
-    work = pieces
-    bit = 1
-    while bit < n_dp:
-        halves = work.reshape((work.shape[0] // 2, 2) + work.shape[1:])
+    axes = []
+    bit = n_dp // 2
+    while bit >= 1:
+        axes.append(bit)
+        bit //= 2
+    order = sorted(axes)
+    if len(order) >= 3:
+        order = order[:1] + order[1:][::-1]
+    work = pieces.reshape((2,) * len(axes) + pieces.shape[1:])
+    for bit in order:
+        ax = axes.index(bit)
         mine = (me // bit) % 2
-        keep = jnp.take(halves, mine, axis=1)
-        give = jnp.take(halves, 1 - mine, axis=1)
-        pairs = [(i, i ^ bit) for i in range(n_dp)]
-        work = keep + lax.ppermute(give, "dp", pairs)
-        bit *= 2
-    return work[0]
+        keep = jnp.take(work, mine, axis=ax)
+        give = jnp.take(work, 1 - mine, axis=ax)
+        work = keep + lax.ppermute(give, "dp", [(i, i ^ bit) for i in range(n_dp)])
+        axes.pop(ax)
+    return work
 
 
 def local(tokens, expert_ids, routing, w_gate, w_up, w_down, grad_out):

time: 87.6 us -> 87.6 us (level)
  no operation moved by 1% of the time
where the time goes in v14:
time: 87.6 us; the launch traced here: 87.3 us
  waiting for transfers between devices  37.8 us (43%)
  starting transfers between devices  26.1 us (30%)
  matrix products  11.8 us (13%)
  other arithmetic  6.09 us (7%)
  local copies, waits for them, and re-layouts  4.47 us (5%)
  between operations  1.05 us (1%)
    ppermute x12, starting transfers between devices, shift_send(): got.append(lax.ppermute(blocks[step], 'expert', pairs))  18.1 us
    ppermute x12, waiting for transfers between devices, shift_send(): got.append(lax.ppermute(blocks[step], 'expert', pairs))  14.8 us
    ppermute x3, waiting for transfers between devices, all_gather_dp(): recv = lax.ppermute(work, 'dp', [(i, i ^ bit) for i in range(n_dp)])  12.2 us
    ppermute x3, waiting for transfers between devices, reduce_scatter_dp(): work = keep + lax.ppermute(give, 'dp', [(i, i ^ bit) for i in range(n_dp)])  10.8 us
    ppermute x3, starting transfers between devices, all_gather_dp(): recv = lax.ppermute(work, 'dp', [(i, i ^ bit) for i in range(n_dp)])  4.87 us
    ppermute x3, starting transfers between devices, reduce_scatter_dp(): work = keep + lax.ppermute(give, 'dp', [(i, i ^ bit) for i in range(n_dp)])  3.15 us
    another operation x6, other arithmetic, all_gather_dp(): jnp.stack([jnp.where(upper, recv, work), jnp.where(upper, work, recv)], a...  2.93 us
  transfers between devices with their start and end apart: 18, of which 6 were waited for; matrix products, arithmetic and copies ran while one was open for 21% of the time, Pallas kernels for 0%

profile of v14, /device:TPU:0, one launch (start us, length us, event | category | flops | bytes accessed | tf_op | source)
XLA Modules:
  0.0 87.3 jit_solution(797839644784775852)
XLA Ops:
  0.6 1.1 %maximum_bitcast_fusion = bf16[128,1152]{1,0:T(8,128)(2,1)S(1)} fusion(bf16[1,128,384]{2,1,0:T(8,128)(2,1)} %param.18, bf16[1,128,384]{2,1,0:T(8,128)(2,1)} %param.17, bf16[1,128,384]{2,1,0:T(8,128)(2,1)} %param.16), kind=kLoop, calls=%fused_computation.50 | loop fusion | flops 884736 | bytes 589824 | tf_op jit(solution)/shard_map/reshape;transpose | solution.py:127
  1.7 3.0 %collective-permute-start.3 = (bf16[128,1152]{1,0:T(8,128)(2,1)S(1)}, bf16[128,1152]{1,0:T(8,128)(2,1)S(1)}, u32[]{:S(2)}, u32[]{:S(2)}) collective-permute-start(bf16[128,1152]{1,0:T(8,128)(2,1)S(1)} %maximum_bitcast_fusion), channel_id=1, source_target_pairs={{0,8},{4,12},{8,0},{12,4},{16,24},{20,28},{24,16},{28,20},{1,9},{5... | collective-permute-start | bytes 884744 | tf_op jit(solution)/shard_map/ppermute | solution.py:53
  4.7 0.8 copy.19
  5.5 0.1 sub.46
  5.7 0.2 fusion.2
  5.9 0.1 convert_element_type.57
  6.2 5.6 %collective-permute-done.3 = bf16[128,1152]{1,0:T(8,128)(2,1)S(1)} collective-permute-done((bf16[128,1152]{1,0:T(8,128)(2,1)S(1)}, bf16[128,1152]{1,0:T(8,128)(2,1)S(1)}, u32[]{:S(2)}, u32[]{:S(2)}) %collective-permute-start.3) | collective-permute-done | bytes 294944 | tf_op jit(solution)/shard_map/ppermute | solution.py:53
  11.7 1.1 %select_bitcast_fusion.6 = (bf16[1,128,1152]{2,1,0:T(8,128)(2,1)S(1)}, bf16[1,128,1152]{2,1,0:T(8,128)(2,1)S(1)}) fusion(bf16[128,1152]{1,0:T(8,128)(2,1)S(1)} %collective-permute-done.3, pred[]{:T(512)S(6)} %eq.60, bf16[1,128,384]{2,1,0:T(8,128)(2,1)} %param.18, bf16[1,128,384]{2,1,0:T(8,128)(2,1)} %param.17, bf16[1,128,384]{2,1,0:T(8,128)(2,1)} %param.16), kind=kLoop, calls=%fused_computation.54 | loop fusion | flops 1179648 | bytes 1179649 | tf_op jit(solution)/shard_map/stack | solution.py:55
  12.9 1.8 %collective-permute-start.4 = (bf16[2,128,1152]{2,1,0:T(8,128)(2,1)S(1)}, bf16[2,128,1152]{2,1,0:T(8,128)(2,1)S(1)}, u32[]{:S(2)}, u32[]{:S(2)}) collective-permute-start(bf16[2,128,1152]{2,1,0:T(8,128)(2,1)S(1)} %pad_maximum_fusion.5), channel_id=1, source_target_pairs={{0,16},{4,20},{8,24},{12,28},{16,0},{20,4},{24,8},{28,12},{1,17},{... | collective-permute-start | bytes 1769480 | tf_op jit(solution)/shard_map/ppermute | solution.py:53
  14.8 0.1 fusion.19
  14.9 0.4 convolution_convert_fusion
  15.4 3.7 %collective-permute-start.2 = (bf16[96,1024]{1,0:T(8,128)(2,1)S(1)}, bf16[96,1024]{1,0:T(8,128)(2,1)}, u32[]{:S(2)}, u32[]{:S(2)}) collective-permute-start(bf16[96,1024]{1,0:T(8,128)(2,1)S(1)} %get-tuple-element.56), channel_id=1, source_target_pairs={{0,3},{1,0},{2,1},{3,2},{4,7},{5,4},{6,5},{7,6},{8,11},{9,8},{10,9... | collective-permute-start | bytes 589832 | tf_op jit(solution)/shard_map/ppermute | solution.py:38
  19.1 1.0 %collective-permute-start = (bf16[96,1024]{1,0:T(8,128)(2,1)S(1)}, bf16[96,1024]{1,0:T(8,128)(2,1)}, u32[]{:S(2)}, u32[]{:S(2)}) collective-permute-start(bf16[96,1024]{1,0:T(8,128)(2,1)S(1)} %get-tuple-element.58), channel_id=1, source_target_pairs={{0,1},{1,2},{2,3},{3,0},{4,5},{5,6},{6,7},{7,4},{8,9},{9,10},{10,1... | collective-permute-start | bytes 589832 | tf_op jit(solution)/shard_map/ppermute | solution.py:38
  20.2 0.7 broadcast_in_dim.48
  20.9 6.6 %collective-permute-done.4 = bf16[2,128,1152]{2,1,0:T(8,128)(2,1)S(1)} collective-permute-done((bf16[2,128,1152]{2,1,0:T(8,128)(2,1)S(1)}, bf16[2,128,1152]{2,1,0:T(8,128)(2,1)S(1)}, u32[]{:S(2)}, u32[]{:S(2)}) %collective-permute-start.4) | collective-permute-done | bytes 589856 | tf_op jit(solution)/shard_map/ppermute | solution.py:53
  27.5 0.1 select_bitcast_fusion.3
  27.7 1.2 %pad_maximum_fusion.1 = bf16[2,2,128,1152]{3,2,1,0:T(8,128)(2,1)} fusion(bf16[1,2,128,1152]{3,2,1,0:T(8,128)(2,1)S(1)} %get-tuple-element.42, bf16[1,2,128,1152]{3,2,1,0:T(8,128)(2,1)S(1)} %get-tuple-element.41), kind=kLoop, calls=%fused_computation.10 | loop fusion | flops 589824 | bytes 2359296 | tf_op jit(solution)/shard_map/stack | solution.py:55
  28.9 0.1 select_reduce_fusion
  29.0 0.4 multiply_convert_fusion
  29.5 0.9 %fusion.40 = (bf16[96,1024]{1,0:T(8,128)(2,1)}, bf16[96,1024]{1,0:T(8,128)(2,1)}, bf16[96,1024]{1,0:T(8,128)(2,1)}, bf16[96,1024]{1,0:T(8,128)(2,1)}) fusion(bf16[384,1024]{1,0:T(8,128)(2,1)S(1)} %multiply_convert_fusion), kind=kLoop, calls=%fused_computation.92 | loop fusion | bytes 1572864 | tf_op jit(solution)/shard_map/slice | solution.py:134
  30.4 3.6 %collective-permute-start.11 = (bf16[96,1024]{1,0:T(8,128)(2,1)}, bf16[96,1024]{1,0:T(8,128)(2,1)}, u32[]{:S(2)}, u32[]{:S(2)}) collective-permute-start(bf16[96,1024]{1,0:T(8,128)(2,1)} %get-tuple-element.48), channel_id=1, source_target_pairs={{0,3},{1,0},{2,1},{3,2},{4,7},{5,4},{6,5},{7,6},{8,11},{9,8},{10,9... | collective-permute-start | bytes 589832 | tf_op jit(solution)/shard_map/ppermute | solution.py:38
  33.9 0.8 convert_reduce_fusion
  34.7 0.8 slice_bitcast_fusion.14
  35.5 0.2 select_bitcast_fusion.1
  35.7 0.2 pad_maximum_fusion
  36.0 0.7 copy-done.3
  36.7 1.0 %collective-permute-start.9 = (bf16[96,1024]{1,0:T(8,128)(2,1)S(1)}, bf16[96,1024]{1,0:T(8,128)(2,1)S(1)}, u32[]{:S(2)}, u32[]{:S(2)}) collective-permute-start(bf16[96,1024]{1,0:T(8,128)(2,1)S(1)} %copy-done.3), channel_id=1, source_target_pairs={{0,1},{1,2},{2,3},{3,0},{4,5},{5,6},{6,7},{7,4},{8,9},{9,10},{10,1... | collective-permute-start | bytes 589832 | tf_op jit(solution)/shard_map/ppermute | solution.py:38
  37.7 1.7 %fusion.14 = f32[384,384]{1,0:T(8,128)S(1)} fusion(bf16[1,1024,1152]{2,1,0:T(8,128)(2,1)S(1)} %bitcast.84, bf16[96,1024]{1,0:T(8,128)(2,1)} %collective-permute-done.2, bf16[96,1024]{1,0:T(8,128)(2,1)} %collective-permute-done.1, bf16[96,1024]{1,0:T(8,128)(2,1)} %collective-permute-done, bf16[96,1024]{1,0:T(8,128)(2,1)S(1)} %get-tuple-element.55), kind=kOutput, calls=%fused_computation.34 | convolution fusion | flops 305135616 | bytes 2162688 | tf_op jit(solution)/shard_map/dot_general | solution.py:11
  39.4 1.7 %multiply_convert_fusion.3 = (bf16[384,384]{1,0:T(8,128)(2,1)S(1)}, f32[384,384]{1,0:T(8,128)S(1)}) fusion(f32[384,384]{1,0:T(8,128)S(1)} %fusion.14, bf16[1,1024,1152]{2,1,0:T(8,128)(2,1)S(1)} %bitcast.85, bf16[96,1024]{1,0:T(8,128)(2,1)} %collective-permute-done.2, bf16[96,1024]{1,0:T(8,128)(2,1)} %collective-permute-done.1, ...), kind=kOutput, calls=%fused_computation.40 | convolution fusion | flops 306020352 | bytes 3047424 | tf_op jit(solution)/shard_map/dot_general | solution.py:12
  41.1 0.6 convolution_convert_fusion.1
  41.8 2.5 %collective-permute-start.8 = (bf16[96,1024]{1,0:T(8,128)(2,1)S(1)}, bf16[96,1024]{1,0:T(8,128)(2,1)S(1)}, u32[]{:S(2)}, u32[]{:S(2)}) collective-permute-start(bf16[96,1024]{1,0:T(8,128)(2,1)S(1)} %get-tuple-element.52), channel_id=1, source_target_pairs={{0,1},{1,2},{2,3},{3,0},{4,5},{5,6},{6,7},{7,4},{8,9},{9,10},{10,1... | collective-permute-start | bytes 589832 | tf_op jit(solution)/shard_map/ppermute | solution.py:38
  44.3 0.9 %collective-permute-start.7 = (bf16[96,1024]{1,0:T(8,128)(2,1)S(1)}, bf16[96,1024]{1,0:T(8,128)(2,1)S(1)}, u32[]{:S(2)}, u32[]{:S(2)}) collective-permute-start(bf16[96,1024]{1,0:T(8,128)(2,1)S(1)} %get-tuple-element.53), channel_id=1, source_target_pairs={{0,2},{1,3},{2,0},{3,1},{4,6},{5,7},{6,4},{7,5},{8,10},{9,11},{10,... | collective-permute-start | bytes 589832 | tf_op jit(solution)/shard_map/ppermute | solution.py:38
  45.2 1.5 %collective-permute-start.6 = (bf16[96,1024]{1,0:T(8,128)(2,1)S(1)}, bf16[96,1024]{1,0:T(8,128)(2,1)S(1)}, u32[]{:S(2)}, u32[]{:S(2)}) collective-permute-start(bf16[96,1024]{1,0:T(8,128)(2,1)S(1)} %get-tuple-element.54), channel_id=1, source_target_pairs={{0,3},{1,0},{2,1},{3,2},{4,7},{5,4},{6,5},{7,6},{8,11},{9,8},{10,9... | collective-permute-start | bytes 589832 | tf_op jit(solution)/shard_map/ppermute | solution.py:38
  46.7 14.1 %collective-permute-done.10 = bf16[96,1024]{1,0:T(8,128)(2,1)S(1)} collective-permute-done((bf16[96,1024]{1,0:T(8,128)(2,1)}, bf16[96,1024]{1,0:T(8,128)(2,1)S(1)}, u32[]{:S(2)}, u32[]{:S(2)}) %collective-permute-start.10) | collective-permute-done | bytes 196640 | tf_op jit(solution)/shard_map/ppermute | solution.py:38
  60.9 1.6 %fusion.22 = f32[1024,384]{1,0:T(8,128)S(1)} fusion(bf16[384,384]{1,0:T(8,128)(2,1)S(1)} %get-tuple-element.65, bf16[96,1024]{1,0:T(8,128)(2,1)} %collective-permute-done.11, bf16[96,1024]{1,0:T(8,128)(2,1)S(1)} %collective-permute-done.10, bf16[96,1024]{1,0:T(8,128)(2,1)S(1)} %collective-permute-done.9, bf16[96,1024]{1,0:T(8,128)(2,1)S(1)} %copy-done.2), kind=kOutput, calls=%fused_computation.63 | convolution fusion | flops 305135616 | bytes 2654208 | tf_op jit(solution)/shard_map/dot_general | solution.py:142
  62.7 1.5 %fusion.16 = f32[384,384]{1,0:T(8,128)S(1)} fusion(bf16[1,1024,1152]{2,1,0:T(8,128)(2,1)S(1)} %bitcast.87, bf16[96,1024]{1,0:T(8,128)(2,1)} %collective-permute-done.11, bf16[96,1024]{1,0:T(8,128)(2,1)S(1)} %collective-permute-done.10, bf16[96,1024]{1,0:T(8,128)(2,1)S(1)} %collective-permute-done.9, bf16[96,1024]{1,0:T(8,128)(2,1)S(1)} %copy-done.2), kind=kOutput, calls=%fused_computation.36 | convolution fusion | flops 305135616 | bytes 2162688 | tf_op jit(solution)/shard_map/dot_general | solution.py:22
  64.2 0.7 fusion.13
  64.8 0.6 add_convert_fusion
  65.8 3.8 %collective-permute-start.12 = (bf16[96,1024]{1,0:T(8,128)(2,1)S(1)}, bf16[96,1024]{1,0:T(8,128)(2,1)S(1)}, u32[]{:S(2)}, u32[]{:S(2)}) collective-permute-start(bf16[96,1024]{1,0:T(8,128)(2,1)S(1)} %get-tuple-element.46), channel_id=1, source_target_pairs={{0,3},{1,0},{2,1},{3,2},{4,7},{5,4},{6,5},{7,6},{8,11},{9,8},{10,9... | collective-permute-start | bytes 589832 | tf_op jit(solution)/shard_map/ppermute | solution.py:38
  69.6 1.5 %collective-permute-start.16 = (f32[2,128,384]{2,1,0:T(8,128)S(1)}, f32[2,128,384]{2,1,0:T(8,128)S(1)}, u32[]{:S(2)}, u32[]{:S(2)}) collective-permute-start(f32[2,128,384]{2,1,0:T(8,128)S(1)} %select_bitcast_fusion.4), channel_id=1, source_target_pairs={{0,16},{4,20},{8,24},{12,28},{16,0},{20,4},{24,8},{28,12},{1,17},{... | collective-permute-start | bytes 1179656 | tf_op jit(solution)/shard_map/ppermute | solution.py:78
  71.1 0.3 convolution_multiply_fusion
  71.5 1.0 %fusion.1 = bf16[128,1024]{1,0:T(8,128)(2,1)} fusion(f32[128,1024]{1,0:T(8,128)S(1)} %convolution_multiply_fusion, f32[128]{0:T(128)S(1)} %get-tuple-element.61, pred[128,2,384]{2,0,1:T(32,128)(4,1)S(1)} %get-tuple-element.64, bf16[96,1024]{1,0:T(8,128)(2,1)S(1)} %collective-permute-done.8, bf16[96,1024]{1,0:T(8,128)(2,1)S(1)} %collective-permute-done.7, ...), kind=kOutput, calls=%fused_computation.8 | convolution fusion | flops 104202240 | bytes 1622528 | tf_op jit(solution)/shard_map/dot_general | solution.py:151
  72.5 8.1 %collective-permute-done.16 = f32[2,128,384]{2,1,0:T(8,128)S(1)} collective-permute-done((f32[2,128,384]{2,1,0:T(8,128)S(1)}, f32[2,128,384]{2,1,0:T(8,128)S(1)}, u32[]{:S(2)}, u32[]{:S(2)}) %collective-permute-start.16) | collective-permute-done | bytes 393248 | tf_op jit(solution)/shard_map/ppermute | solution.py:78
  80.6 1.6 %collective-permute-start.17 = (f32[128,384]{1,0:T(8,128)S(1)}, f32[128,384]{1,0:T(8,128)S(1)}, u32[]{:S(2)}, u32[]{:S(2)}) collective-permute-start(f32[128,384]{1,0:T(8,128)S(1)} %select_bitcast_fusion.7), channel_id=1, source_target_pairs={{0,8},{4,12},{8,0},{12,4},{16,24},{20,28},{24,16},{28,20},{1,9},{5... | collective-permute-start | bytes 589832 | tf_op jit(solution)/shard_map/ppermute | solution.py:78
  82.2 0.6 collective-permute-done.13
  82.8 1.0 %convolution_convert_fusion.2 = bf16[128,1024]{1,0:T(8,128)(2,1)} fusion(bf16[96,1024]{1,0:T(8,128)(2,1)S(1)} %collective-permute-done.14, bf16[96,1024]{1,0:T(8,128)(2,1)S(1)} %collective-permute-done.13, bf16[96,1024]{1,0:T(8,128)(2,1)S(1)} %collective-permute-done.12, bf16[96,1024]{1,0:T(8,128)(2,1)S(1)} %get-tuple-element.43, ...), kind=kOutput, calls=%fused_computation.9 | convolution fusion | flops 103989248 | bytes 1245184 | tf_op jit(solution)/shard_map/dot_general | solution.py:157
  83.8 2.8 %collective-permute-done.17 = f32[128,384]{1,0:T(8,128)S(1)} collective-permute-done((f32[128,384]{1,0:T(8,128)S(1)}, f32[128,384]{1,0:T(8,128)S(1)}, u32[]{:S(2)}, u32[]{:S(2)}) %collective-permute-start.17) | collective-permute-done | bytes 196640 | tf_op jit(solution)/shard_map/ppermute | solution.py:78
  86.6 0.7 fusion.21
  (55 shorter events, 1.0 us)
Async XLA Ops:
  0.6 14.3 %copy-start = (bf16[128,1024]{1,0:T(8,128)(2,1)S(1)}, bf16[128,1024]{1,0:T(8,128)(2,1)}, u32[]{:S(2)}) copy-start(bf16[128,1024]{1,0:T(8,128)(2,1)} %param.13) | copy-start | bytes 786436
  1.7 10.0 %collective-permute-start.3 = (bf16[128,1152]{1,0:T(8,128)(2,1)S(1)}, bf16[128,1152]{1,0:T(8,128)(2,1)S(1)}, u32[]{:S(2)}, u32[]{:S(2)}) collective-permute-start(bf16[128,1152]{1,0:T(8,128)(2,1)S(1)} %maximum_bitcast_fusion), channel_id=1, source_target_pairs={{0,8},{4,12},{8,0},{12,4},{16,24},{20,28},{24,16},{28,20},{1,9},{5... | collective-permute-start | bytes 884744 | tf_op jit(solution)/shard_map/ppermute | solution.py:53
  5.7 7.2 %copy-start.5 = (s32[256]{0:T(256)}, s32[256]{0:T(256)S(1)}, u32[]{:S(2)}) copy-start(s32[256]{0:T(256)S(1)} %sub.46) | copy-start | bytes 3076
  5.9 7.0 %copy-start.9 = (f32[256]{0:T(256)}, f32[256]{0:T(256)S(1)}, u32[]{:S(2)}) copy-start(f32[256]{0:T(256)S(1)} %fusion.2) | copy-start | bytes 3076
  6.2 8.8 %copy-start.4 = (s32[128,2]{0,1:T(2,128)}, s32[128,2]{0,1:T(2,128)S(1)}, u32[]{:S(2)}) copy-start(s32[128,2]{0,1:T(2,128)S(1)} %copy.20) | copy-start | bytes 3076
  12.9 7.2 %copy-start.7 = (f32[128,2]{0,1:T(2,128)S(1)}, f32[128,2]{0,1:T(2,128)}, u32[]{:S(2)}) copy-start(f32[128,2]{0,1:T(2,128)} %param.15) | copy-start | bytes 3076
  12.9 14.6 %collective-permute-start.4 = (bf16[2,128,1152]{2,1,0:T(8,128)(2,1)S(1)}, bf16[2,128,1152]{2,1,0:T(8,128)(2,1)S(1)}, u32[]{:S(2)}, u32[]{:S(2)}) collective-permute-start(bf16[2,128,1152]{2,1,0:T(8,128)(2,1)S(1)} %pad_maximum_fusion.5), channel_id=1, source_target_pairs={{0,16},{4,20},{8,24},{12,28},{16,0},{20,4},{24,8},{28,12},{1,17},{... | collective-permute-start | bytes 1769480 | tf_op jit(solution)/shard_map/ppermute | solution.py:53
  15.4 20.6 %collective-permute-start.2 = (bf16[96,1024]{1,0:T(8,128)(2,1)S(1)}, bf16[96,1024]{1,0:T(8,128)(2,1)}, u32[]{:S(2)}, u32[]{:S(2)}) collective-permute-start(bf16[96,1024]{1,0:T(8,128)(2,1)S(1)} %get-tuple-element.56), channel_id=1, source_target_pairs={{0,3},{1,0},{2,1},{3,2},{4,7},{5,4},{6,5},{7,6},{8,11},{9,8},{10,9... | collective-permute-start | bytes 589832 | tf_op jit(solution)/shard_map/ppermute | solution.py:38
  19.1 18.6 %collective-permute-start.1 = (bf16[96,1024]{1,0:T(8,128)(2,1)S(1)}, bf16[96,1024]{1,0:T(8,128)(2,1)}, u32[]{:S(2)}, u32[]{:S(2)}) collective-permute-start(bf16[96,1024]{1,0:T(8,128)(2,1)S(1)} %get-tuple-element.57), channel_id=1, source_target_pairs={{0,2},{1,3},{2,0},{3,1},{4,6},{5,7},{6,4},{7,5},{8,10},{9,11},{10,... | collective-permute-start | bytes 589832 | tf_op jit(solution)/shard_map/ppermute | solution.py:38
  19.1 18.6 %collective-permute-start = (bf16[96,1024]{1,0:T(8,128)(2,1)S(1)}, bf16[96,1024]{1,0:T(8,128)(2,1)}, u32[]{:S(2)}, u32[]{:S(2)}) collective-permute-start(bf16[96,1024]{1,0:T(8,128)(2,1)S(1)} %get-tuple-element.58), channel_id=1, source_target_pairs={{0,1},{1,2},{2,3},{3,0},{4,5},{5,6},{6,7},{7,4},{8,9},{9,10},{10,1... | collective-permute-start | bytes 589832 | tf_op jit(solution)/shard_map/ppermute | solution.py:38
  27.6 1.2 %copy-start.6 = (s32[256]{0:T(256)S(1)}, s32[256]{0:T(256)}, u32[]{:S(2)}) copy-start(s32[256]{0:T(256)} %copy-done.5) | copy-start | bytes 3076
  27.6 1.2 %copy-start.10 = (f32[256]{0:T(256)S(1)}, f32[256]{0:T(256)}, u32[]{:S(2)}) copy-start(f32[256]{0:T(256)} %copy-done.9) | copy-start | bytes 3076
  27.7 1.2 %copy-start.8 = (f32[256]{0:T(256)S(1)}, f32[256]{0:T(256)}, u32[]{:S(2)}) copy-start(f32[256]{0:T(256)} %broadcast_in_dim.48) | copy-start | bytes 3076
  27.7 1.4 %copy-start.1 = (bf16[128,1024]{1,0:T(8,128)(2,1)S(1)}, bf16[128,1024]{1,0:T(8,128)(2,1)}, u32[]{:S(2)}) copy-start(bf16[128,1024]{1,0:T(8,128)(2,1)} %param.19) | copy-start | bytes 786436
  28.8 6.6 %collective-permute-start.5 = (bf16[2,2,128,1152]{3,2,1,0:T(8,128)(2,1)}, bf16[2,2,128,1152]{3,2,1,0:T(8,128)(2,1)S(1)}, u32[]{:S(2)}, u32[]{:S(2)}) collective-permute-start(bf16[2,2,128,1152]{3,2,1,0:T(8,128)(2,1)} %pad_maximum_fusion.1), channel_id=1, source_target_pairs={{0,4},{4,0},{8,12},{12,8},{16,20},{20,16},{24,28},{28,24},{1,5},{5... | collective-permute-start | bytes 3538952 | tf_op jit(solution)/shard_map/ppermute | solution.py:53
  30.4 14.9 %collective-permute-start.11 = (bf16[96,1024]{1,0:T(8,128)(2,1)}, bf16[96,1024]{1,0:T(8,128)(2,1)}, u32[]{:S(2)}, u32[]{:S(2)}) collective-permute-start(bf16[96,1024]{1,0:T(8,128)(2,1)} %get-tuple-element.48), channel_id=1, source_target_pairs={{0,3},{1,0},{2,1},{3,2},{4,7},{5,4},{6,5},{7,6},{8,11},{9,8},{10,9... | collective-permute-start | bytes 589832 | tf_op jit(solution)/shard_map/ppermute | solution.py:38
  35.5 25.4 %collective-permute-start.10 = (bf16[96,1024]{1,0:T(8,128)(2,1)}, bf16[96,1024]{1,0:T(8,128)(2,1)S(1)}, u32[]{:S(2)}, u32[]{:S(2)}) collective-permute-start(bf16[96,1024]{1,0:T(8,128)(2,1)} %get-tuple-element.49), channel_id=1, source_target_pairs={{0,2},{1,3},{2,0},{3,1},{4,6},{5,7},{6,4},{7,5},{8,10},{9,11},{10,... | collective-permute-start | bytes 589832 | tf_op jit(solution)/shard_map/ppermute | solution.py:38
  35.7 0.9 %copy-start.3 = (bf16[96,1024]{1,0:T(8,128)(2,1)S(1)}, bf16[96,1024]{1,0:T(8,128)(2,1)}, u32[]{:S(2)}) copy-start(bf16[96,1024]{1,0:T(8,128)(2,1)} %get-tuple-element.50) | copy-start | bytes 589828
  36.7 24.2 %collective-permute-start.9 = (bf16[96,1024]{1,0:T(8,128)(2,1)S(1)}, bf16[96,1024]{1,0:T(8,128)(2,1)S(1)}, u32[]{:S(2)}, u32[]{:S(2)}) collective-permute-start(bf16[96,1024]{1,0:T(8,128)(2,1)S(1)} %copy-done.3), channel_id=1, source_target_pairs={{0,1},{1,2},{2,3},{3,0},{4,5},{5,6},{6,7},{7,4},{8,9},{9,10},{10,1... | collective-permute-start | bytes 589832 | tf_op jit(solution)/shard_map/ppermute | solution.py:38
  41.1 19.8 %copy-start.2 = (bf16[96,1024]{1,0:T(8,128)(2,1)S(1)}, bf16[96,1024]{1,0:T(8,128)(2,1)}, u32[]{:S(2)}) copy-start(bf16[96,1024]{1,0:T(8,128)(2,1)} %get-tuple-element.47) | copy-start | bytes 589828
  41.8 24.1 %collective-permute-start.8 = (bf16[96,1024]{1,0:T(8,128)(2,1)S(1)}, bf16[96,1024]{1,0:T(8,128)(2,1)S(1)}, u32[]{:S(2)}, u32[]{:S(2)}) collective-permute-start(bf16[96,1024]{1,0:T(8,128)(2,1)S(1)} %get-tuple-element.52), channel_id=1, source_target_pairs={{0,1},{1,2},{2,3},{3,0},{4,5},{5,6},{6,7},{7,4},{8,9},{9,10},{10,1... | collective-permute-start | bytes 589832 | tf_op jit(solution)/shard_map/ppermute | solution.py:38
  44.3 25.3 %collective-permute-start.7 = (bf16[96,1024]{1,0:T(8,128)(2,1)S(1)}, bf16[96,1024]{1,0:T(8,128)(2,1)S(1)}, u32[]{:S(2)}, u32[]{:S(2)}) collective-permute-start(bf16[96,1024]{1,0:T(8,128)(2,1)S(1)} %get-tuple-element.53), channel_id=1, source_target_pairs={{0,2},{1,3},{2,0},{3,1},{4,6},{5,7},{6,4},{7,5},{8,10},{9,11},{10,... | collective-permute-start | bytes 589832 | tf_op jit(solution)/shard_map/ppermute | solution.py:38
  45.2 25.9 %collective-permute-start.6 = (bf16[96,1024]{1,0:T(8,128)(2,1)S(1)}, bf16[96,1024]{1,0:T(8,128)(2,1)S(1)}, u32[]{:S(2)}, u32[]{:S(2)}) collective-permute-start(bf16[96,1024]{1,0:T(8,128)(2,1)S(1)} %get-tuple-element.54), channel_id=1, source_target_pairs={{0,3},{1,0},{2,1},{3,2},{4,7},{5,4},{6,5},{7,6},{8,11},{9,8},{10,9... | collective-permute-start | bytes 589832 | tf_op jit(solution)/shard_map/ppermute | solution.py:38
  62.6 3.0 %collective-permute-start.15 = (f32[2,2,128,384]{3,2,1,0:T(8,128)S(1)}, f32[2,2,128,384]{3,2,1,0:T(8,128)S(1)}, u32[]{:S(2)}, u32[]{:S(2)}) collective-permute-start(f32[2,2,128,384]{3,2,1,0:T(8,128)S(1)} %fusion.10), channel_id=1, source_target_pairs={{0,4},{4,0},{8,12},{12,8},{16,20},{20,16},{24,28},{28,24},{1,5},{5... | collective-permute-start | bytes 2359304 | tf_op jit(solution)/shard_map/ppermute | solution.py:78
  65.5 16.7 %collective-permute-start.14 = (bf16[96,1024]{1,0:T(8,128)(2,1)S(1)}, bf16[96,1024]{1,0:T(8,128)(2,1)S(1)}, u32[]{:S(2)}, u32[]{:S(2)}) collective-permute-start(bf16[96,1024]{1,0:T(8,128)(2,1)S(1)} %get-tuple-element.44), channel_id=1, source_target_pairs={{0,1},{1,2},{2,3},{3,0},{4,5},{5,6},{6,7},{7,4},{8,9},{9,10},{10,1... | collective-permute-start | bytes 589832 | tf_op jit(solution)/shard_map/ppermute | solution.py:38
  65.6 17.2 %collective-permute-start.13 = (bf16[96,1024]{1,0:T(8,128)(2,1)S(1)}, bf16[96,1024]{1,0:T(8,128)(2,1)S(1)}, u32[]{:S(2)}, u32[]{:S(2)}) collective-permute-start(bf16[96,1024]{1,0:T(8,128)(2,1)S(1)} %get-tuple-element.45), channel_id=1, source_target_pairs={{0,2},{1,3},{2,0},{3,1},{4,6},{5,7},{6,4},{7,5},{8,10},{9,11},{10,... | collective-permute-start | bytes 589832 | tf_op jit(solution)/shard_map/ppermute | solution.py:38
  65.8 17.0 %collective-permute-start.12 = (bf16[96,1024]{1,0:T(8,128)(2,1)S(1)}, bf16[96,1024]{1,0:T(8,128)(2,1)S(1)}, u32[]{:S(2)}, u32[]{:S(2)}) collective-permute-start(bf16[96,1024]{1,0:T(8,128)(2,1)S(1)} %get-tuple-element.46), channel_id=1, source_target_pairs={{0,3},{1,0},{2,1},{3,2},{4,7},{5,4},{6,5},{7,6},{8,11},{9,8},{10,9... | collective-permute-start | bytes 589832 | tf_op jit(solution)/shard_map/ppermute | solution.py:38
  69.6 11.0 %collective-permute-start.16 = (f32[2,128,384]{2,1,0:T(8,128)S(1)}, f32[2,128,384]{2,1,0:T(8,128)S(1)}, u32[]{:S(2)}, u32[]{:S(2)}) collective-permute-start(f32[2,128,384]{2,1,0:T(8,128)S(1)} %select_bitcast_fusion.4), channel_id=1, source_target_pairs={{0,16},{4,20},{8,24},{12,28},{16,0},{20,4},{24,8},{28,12},{1,17},{... | collective-permute-start | bytes 1179656 | tf_op jit(solution)/shard_map/ppermute | solution.py:78
  80.6 6.0 %collective-permute-start.17 = (f32[128,384]{1,0:T(8,128)S(1)}, f32[128,384]{1,0:T(8,128)S(1)}, u32[]{:S(2)}, u32[]{:S(2)}) collective-permute-start(f32[128,384]{1,0:T(8,128)S(1)} %select_bitcast_fusion.7), channel_id=1, source_target_pairs={{0,8},{4,12},{8,0},{12,4},{16,24},{20,28},{24,16},{28,20},{1,9},{5... | collective-permute-start | bytes 589832 | tf_op jit(solution)/shard_map/ppermute | solution.py:78

commit v15 on v14

--- a/solution.py
+++ b/solution.py
@@ -7,9 +7,11 @@
 contract_first = (((0,), (0,)), ((), ()))
 
 
-def forward_rows(row_data, gate_w, up_w, down_w):
-    gate_pre = jnp.dot(row_data, gate_w, preferred_element_type=jnp.float32)
-    up_pre = jnp.dot(row_data, up_w, preferred_element_type=jnp.float32)
+def forward_rows(row_data, gate_up_w, down_w):
+    ff_width = down_w.shape[1]
+    both = jnp.dot(row_data, gate_up_w, preferred_element_type=jnp.float32)
+    gate_pre = both[:, :ff_width]
+    up_pre = both[:, ff_width:]
     sigmoid_val = jax.nn.sigmoid(gate_pre)
     hidden = (gate_pre * sigmoid_val * up_pre).astype(jnp.bfloat16)
     expert_out = lax.dot_general(
@@ -18,15 +20,17 @@
     return (gate_pre, up_pre, hidden, expert_out)
 
 
-def backward_rows(grad_rows, gate_pre, up_pre, gate_w, up_w, down_w):
+def backward_rows(grad_rows, gate_pre, up_pre, gate_up_w, down_w):
     hidden_grad = jnp.dot(grad_rows, down_w, preferred_element_type=jnp.float32)
     sigmoid_val = jax.nn.sigmoid(gate_pre)
     slope_val = sigmoid_val * (1.0 + gate_pre * (1.0 - sigmoid_val))
     gate_grad = (hidden_grad * up_pre * slope_val).astype(jnp.bfloat16)
     up_grad = (hidden_grad * gate_pre * sigmoid_val).astype(jnp.bfloat16)
-    summed = lax.dot_general(gate_grad, gate_w, contract_last, preferred_element_type=jnp.float32)
-    summed = summed + lax.dot_general(
-        up_grad, up_w, contract_last, preferred_element_type=jnp.float32
+    summed = lax.dot_general(
+        jnp.concatenate([gate_grad, up_grad], axis=1),
+        gate_up_w,
+        contract_last,
+        preferred_element_type=jnp.float32,
     )
     return summed.astype(jnp.bfloat16)
 
@@ -127,18 +131,15 @@
     packed = jnp.transpose(packed, (1, 0, 2)).reshape(shard_d, local_count * 3 * ff_width)
     full = all_gather_dp(packed, n_dp).reshape(width, local_count * 3 * ff_width)
     full = jnp.transpose(full.reshape(width, local_count, 3 * ff_width), (1, 0, 2))
-    gate_full = full[:, :, :ff_width]
-    up_full = full[:, :, ff_width : 2 * ff_width]
     down_full = full[:, :, 2 * ff_width :]
     recv_rows = shift_send([send_rows[s] for s in range(groups)], groups, 1)
     recv_grads = shift_send([send_grads[s] for s in range(groups)], groups, 1)
-    gate_w = gate_full[0]
-    up_w = up_full[0]
+    gate_up_w = full[0, :, : 2 * ff_width]
     down_w = down_full[0]
     x_rows = jnp.concatenate(recv_rows, axis=0)
     g_rows = jnp.concatenate(recv_grads, axis=0)
-    gate_pre, up_pre, hidden, expert_out = forward_rows(x_rows, gate_w, up_w, down_w)
-    pair_grad = backward_rows(g_rows, gate_pre, up_pre, gate_w, up_w, down_w)
+    gate_pre, up_pre, hidden, expert_out = forward_rows(x_rows, gate_up_w, down_w)
+    pair_grad = backward_rows(g_rows, gate_pre, up_pre, gate_up_w, down_w)
     pieces = lax.dot_general(g_rows, hidden, contract_first, preferred_element_type=jnp.float32)
     block_rows = local_count * capacity
     out_blocks = [expert_out[s * block_rows : (s + 1) * block_rows] for s in range(groups)]

time: 87.6 us -> 101 us (1.15)
  the two profiles are of different devices: /device:TPU:0 before, /device:TPU:24 now
where the time goes in v15:
time: 101 us
  waiting for transfers between devices  45 us (45%)
  starting transfers between devices  33.9 us (34%)
  matrix products  10 us (10%)
  other arithmetic  6.08 us (6%)
  local copies, waits for them, and re-layouts  4.46 us (4%)
    ppermute x12, starting transfers between devices, shift_send(): got.append(lax.ppermute(blocks[step], 'expert', pairs))  27.7 us
    ppermute x12, waiting for transfers between devices, shift_send(): got.append(lax.ppermute(blocks[step], 'expert', pairs))  21.4 us
    ppermute x3, waiting for transfers between devices, all_gather_dp(): recv = lax.ppermute(work, 'dp', [(i, i ^ bit) for i in range(n_dp)])  13.2 us
    ppermute x3, waiting for transfers between devices, reduce_scatter_dp(): work = keep + lax.ppermute(give, 'dp', [(i, i ^ bit) for i in range(n_dp)])  10.5 us
    ppermute x3, starting transfers between devices, all_gather_dp(): recv = lax.ppermute(work, 'dp', [(i, i ^ bit) for i in range(n_dp)])  3.14 us
    ppermute x3, starting transfers between devices, reduce_scatter_dp(): work = keep + lax.ppermute(give, 'dp', [(i, i ^ bit) for i in range(n_dp)])  3.1 us
    another operation x6, other arithmetic, all_gather_dp(): jnp.stack([jnp.where(upper, recv, work), jnp.where(upper, work, recv)], a...  2.93 us
  transfers between devices with their start and end apart: 18, of which 7 were waited for; matrix products, arithmetic and copies ran while one was open for 13% of the time, Pallas kernels for 0%

profile of v15, /device:TPU:24, one launch (start us, length us, event | category | flops | bytes accessed | tf_op | source)
XLA Modules:
  0.0 100.6 jit_solution(485236273529370266)
XLA Ops:
  0.6 1.1 %maximum_bitcast_fusion = bf16[128,1152]{1,0:T(8,128)(2,1)S(1)} fusion(bf16[1,128,384]{2,1,0:T(8,128)(2,1)} %param.18, bf16[1,128,384]{2,1,0:T(8,128)(2,1)} %param.17, bf16[1,128,384]{2,1,0:T(8,128)(2,1)} %param.16), kind=kLoop, calls=%fused_computation.56 | loop fusion | flops 884736 | bytes 589824 | tf_op jit(solution)/shard_map/reshape;transpose | solution.py:131
  1.7 1.6 %collective-permute-start.3 = (bf16[128,1152]{1,0:T(8,128)(2,1)S(1)}, bf16[128,1152]{1,0:T(8,128)(2,1)S(1)}, u32[]{:S(2)}, u32[]{:S(2)}) collective-permute-start(bf16[128,1152]{1,0:T(8,128)(2,1)S(1)} %maximum_bitcast_fusion), channel_id=1, source_target_pairs={{0,8},{4,12},{8,0},{12,4},{16,24},{20,28},{24,16},{28,20},{1,9},{5... | collective-permute-start | bytes 884744 | tf_op jit(solution)/shard_map/ppermute | solution.py:57
  3.3 0.8 copy.23
  4.1 0.1 sub.46
  4.2 0.2 fusion.3
  4.4 0.1 convert_element_type.57
  4.7 5.8 %collective-permute-done.3 = bf16[128,1152]{1,0:T(8,128)(2,1)S(1)} collective-permute-done((bf16[128,1152]{1,0:T(8,128)(2,1)S(1)}, bf16[128,1152]{1,0:T(8,128)(2,1)S(1)}, u32[]{:S(2)}, u32[]{:S(2)}) %collective-permute-start.3) | collective-permute-done | bytes 294944 | tf_op jit(solution)/shard_map/ppermute | solution.py:57
  10.5 1.1 %select_bitcast_fusion.6 = (bf16[1,128,1152]{2,1,0:T(8,128)(2,1)S(1)}, bf16[1,128,1152]{2,1,0:T(8,128)(2,1)S(1)}) fusion(bf16[128,1152]{1,0:T(8,128)(2,1)S(1)} %collective-permute-done.3, pred[]{:T(512)S(6)} %eq.60, bf16[1,128,384]{2,1,0:T(8,128)(2,1)} %param.18, bf16[1,128,384]{2,1,0:T(8,128)(2,1)} %param.17, bf16[1,128,384]{2,1,0:T(8,128)(2,1)} %param.16), kind=kLoop, calls=%fused_computation.58 | loop fusion | flops 1179648 | bytes 1179649 | tf_op jit(solution)/shard_map/stack | solution.py:59
  11.7 1.6 %collective-permute-start.4 = (bf16[2,128,1152]{2,1,0:T(8,128)(2,1)S(1)}, bf16[2,128,1152]{2,1,0:T(8,128)(2,1)S(1)}, u32[]{:S(2)}, u32[]{:S(2)}) collective-permute-start(bf16[2,128,1152]{2,1,0:T(8,128)(2,1)S(1)} %pad_maximum_fusion.4), channel_id=1, source_target_pairs={{0,16},{4,20},{8,24},{12,28},{16,0},{20,4},{24,8},{28,12},{1,17},{... | collective-permute-start | bytes 1769480 | tf_op jit(solution)/shard_map/ppermute | solution.py:57
  13.3 0.1 fusion.25
  13.5 0.4 convolution_convert_fusion.1
  13.9 0.5 collective-permute-start.2
  14.5 0.3 collective-permute-start.1
  14.8 3.0 %collective-permute-start = (bf16[96,1024]{1,0:T(8,128)(2,1)S(1)}, bf16[96,1024]{1,0:T(8,128)(2,1)}, u32[]{:S(2)}, u32[]{:S(2)}) collective-permute-start(bf16[96,1024]{1,0:T(8,128)(2,1)S(1)} %get-tuple-element.61), channel_id=1, source_target_pairs={{0,1},{1,2},{2,3},{3,0},{4,5},{5,6},{6,7},{7,4},{8,9},{9,10},{10,1... | collective-permute-start | bytes 589832 | tf_op jit(solution)/shard_map/ppermute | solution.py:42
  17.9 0.7 broadcast_in_dim.48
  18.7 7.3 %collective-permute-done.4 = bf16[2,128,1152]{2,1,0:T(8,128)(2,1)S(1)} collective-permute-done((bf16[2,128,1152]{2,1,0:T(8,128)(2,1)S(1)}, bf16[2,128,1152]{2,1,0:T(8,128)(2,1)S(1)}, u32[]{:S(2)}, u32[]{:S(2)}) %collective-permute-start.4) | collective-permute-done | bytes 589856 | tf_op jit(solution)/shard_map/ppermute | solution.py:57
  26.2 1.2 %pad_maximum_fusion.1 = bf16[2,2,128,1152]{3,2,1,0:T(8,128)(2,1)} fusion(bf16[1,2,128,1152]{3,2,1,0:T(8,128)(2,1)S(1)} %get-tuple-element.45, bf16[1,2,128,1152]{3,2,1,0:T(8,128)(2,1)S(1)} %get-tuple-element.44), kind=kLoop, calls=%fused_computation.12 | loop fusion | flops 589824 | bytes 2359296 | tf_op jit(solution)/shard_map/stack | solution.py:59
  27.4 0.1 select_reduce_fusion
  27.5 0.4 multiply_convert_fusion
  28.0 0.9 fusion.44
  28.8 0.5 collective-permute-start.11
  29.3 0.8 convert_reduce_fusion
  30.1 0.8 slice_bitcast_fusion.11
  30.9 0.4 collective-permute-start.10
  31.2 0.2 select_bitcast_fusion.1
  31.5 0.2 pad_maximum_fusion
  31.7 0.7 copy-done.3
  32.4 3.0 %collective-permute-start.9 = (bf16[96,1024]{1,0:T(8,128)(2,1)S(1)}, bf16[96,1024]{1,0:T(8,128)(2,1)S(1)}, u32[]{:S(2)}, u32[]{:S(2)}) collective-permute-start(bf16[96,1024]{1,0:T(8,128)(2,1)S(1)} %copy-done.3), channel_id=1, source_target_pairs={{0,1},{1,2},{2,3},{3,0},{4,5},{5,6},{6,7},{7,4},{8,9},{9,10},{10,1... | collective-permute-start | bytes 589832 | tf_op jit(solution)/shard_map/ppermute | solution.py:42
  35.4 1.9 %fusion = f32[384,768]{1,0:T(8,128)S(1)} fusion(bf16[1,1024,1152]{2,1,0:T(8,128)(2,1)S(1)} %bitcast.80, bf16[96,1024]{1,0:T(8,128)(2,1)} %collective-permute-done.2, bf16[96,1024]{1,0:T(8,128)(2,1)} %collective-permute-done.1, bf16[96,1024]{1,0:T(8,128)(2,1)} %collective-permute-done, bf16[96,1024]{1,0:T(8,128)(2,1)S(1)} %get-tuple-element.58), kind=kOutput, calls=%fused_computation.6 | convolution fusion | flops 607125504 | bytes 3538944 | tf_op jit(solution)/shard_map/dot_general | solution.py:12
  37.4 1.5 %collective-permute-done.11 = bf16[96,1024]{1,0:T(8,128)(2,1)} collective-permute-done((bf16[96,1024]{1,0:T(8,128)(2,1)}, bf16[96,1024]{1,0:T(8,128)(2,1)}, u32[]{:S(2)}, u32[]{:S(2)}) %collective-permute-start.11) | collective-permute-done | bytes 196640 | tf_op jit(solution)/shard_map/ppermute | solution.py:42
  38.8 7.8 %collective-permute-done.10 = bf16[96,1024]{1,0:T(8,128)(2,1)S(1)} collective-permute-done((bf16[96,1024]{1,0:T(8,128)(2,1)}, bf16[96,1024]{1,0:T(8,128)(2,1)S(1)}, u32[]{:S(2)}, u32[]{:S(2)}) %collective-permute-start.10) | collective-permute-done | bytes 196640 | tf_op jit(solution)/shard_map/ppermute | solution.py:42
  46.7 1.7 %multiply_convert_fusion.2 = (bf16[384,384]{1,0:T(8,128)(2,1)S(1)}, bf16[384,384]{1,0:T(8,128)(2,1)S(1)}, bf16[384,384]{1,0:T(8,128)(2,1)S(1)}) fusion(f32[384,768]{1,0:T(8,128)S(1)} %fusion, bf16[1,1024,1152]{2,1,0:T(8,128)(2,1)S(1)} %bitcast.81, bf16[96,1024]{1,0:T(8,128)(2,1)} %collective-permute-done.11, ...), kind=kOutput, calls=%fused_computation.45 | convolution fusion | flops 307494912 | bytes 3637248 | tf_op jit(solution)/shard_map/dot_general | solution.py:24
  48.4 1.6 %fusion.28 = f32[1024,384]{1,0:T(8,128)S(1)} fusion(bf16[384,384]{1,0:T(8,128)(2,1)S(1)} %get-tuple-element.43, bf16[96,1024]{1,0:T(8,128)(2,1)} %collective-permute-done.11, bf16[96,1024]{1,0:T(8,128)(2,1)S(1)} %collective-permute-done.10, bf16[96,1024]{1,0:T(8,128)(2,1)S(1)} %collective-permute-done.9, bf16[96,1024]{1,0:T(8,128)(2,1)S(1)} %copy-done.2), kind=kOutput, calls=%fused_computation.67 | convolution fusion | flops 305135616 | bytes 2654208 | tf_op jit(solution)/shard_map/dot_general | solution.py:143
  50.1 0.6 convolution_convert_fusion.2
  50.8 4.2 %collective-permute-start.8 = (bf16[96,1024]{1,0:T(8,128)(2,1)S(1)}, bf16[96,1024]{1,0:T(8,128)(2,1)S(1)}, u32[]{:S(2)}, u32[]{:S(2)}) collective-permute-start(bf16[96,1024]{1,0:T(8,128)(2,1)S(1)} %get-tuple-element.55), channel_id=1, source_target_pairs={{0,1},{1,2},{2,3},{3,0},{4,5},{5,6},{6,7},{7,4},{8,9},{9,10},{10,1... | collective-permute-start | bytes 589832 | tf_op jit(solution)/shard_map/ppermute | solution.py:42
  55.0 2.1 %collective-permute-start.7 = (bf16[96,1024]{1,0:T(8,128)(2,1)S(1)}, bf16[96,1024]{1,0:T(8,128)(2,1)S(1)}, u32[]{:S(2)}, u32[]{:S(2)}) collective-permute-start(bf16[96,1024]{1,0:T(8,128)(2,1)S(1)} %get-tuple-element.56), channel_id=1, source_target_pairs={{0,2},{1,3},{2,0},{3,1},{4,6},{5,7},{6,4},{7,5},{8,10},{9,11},{10,... | collective-permute-start | bytes 589832 | tf_op jit(solution)/shard_map/ppermute | solution.py:42
  57.1 0.8 convolution_convert_fusion
  57.9 3.9 %collective-permute-start.14 = (bf16[96,1024]{1,0:T(8,128)(2,1)S(1)}, bf16[96,1024]{1,0:T(8,128)(2,1)S(1)}, u32[]{:S(2)}, u32[]{:S(2)}) collective-permute-start(bf16[96,1024]{1,0:T(8,128)(2,1)S(1)} %get-tuple-element.47), channel_id=1, source_target_pairs={{0,1},{1,2},{2,3},{3,0},{4,5},{5,6},{6,7},{7,4},{8,9},{9,10},{10,1... | collective-permute-start | bytes 589832 | tf_op jit(solution)/shard_map/ppermute | solution.py:42
  62.0 9.8 %collective-permute-start.12 = (bf16[96,1024]{1,0:T(8,128)(2,1)S(1)}, bf16[96,1024]{1,0:T(8,128)(2,1)S(1)}, u32[]{:S(2)}, u32[]{:S(2)}) collective-permute-start(bf16[96,1024]{1,0:T(8,128)(2,1)S(1)} %get-tuple-element.49), channel_id=1, source_target_pairs={{0,3},{1,0},{2,1},{3,2},{4,7},{5,4},{6,5},{7,6},{8,11},{9,8},{10,9... | collective-permute-start | bytes 589832 | tf_op jit(solution)/shard_map/ppermute | solution.py:42
  71.8 12.1 %collective-permute-done.7 = bf16[96,1024]{1,0:T(8,128)(2,1)S(1)} collective-permute-done((bf16[96,1024]{1,0:T(8,128)(2,1)S(1)}, bf16[96,1024]{1,0:T(8,128)(2,1)S(1)}, u32[]{:S(2)}, u32[]{:S(2)}) %collective-permute-start.7) | collective-permute-done | bytes 196640 | tf_op jit(solution)/shard_map/ppermute | solution.py:42
  83.9 1.5 %collective-permute-start.16 = (f32[2,128,384]{2,1,0:T(8,128)S(1)}, f32[2,128,384]{2,1,0:T(8,128)S(1)}, u32[]{:S(2)}, u32[]{:S(2)}) collective-permute-start(f32[2,128,384]{2,1,0:T(8,128)S(1)} %select_bitcast_fusion.4), channel_id=1, source_target_pairs={{0,16},{4,20},{8,24},{12,28},{16,0},{20,4},{24,8},{28,12},{1,17},{... | collective-permute-start | bytes 1179656 | tf_op jit(solution)/shard_map/ppermute | solution.py:82
  85.4 0.3 convolution_multiply_fusion
  85.7 1.0 %fusion.2 = bf16[128,1024]{1,0:T(8,128)(2,1)} fusion(f32[128,1024]{1,0:T(8,128)S(1)} %convolution_multiply_fusion, f32[128]{0:T(128)S(1)} %get-tuple-element.64, pred[128,2,384]{2,0,1:T(32,128)(4,1)S(1)} %get-tuple-element.67, bf16[96,1024]{1,0:T(8,128)(2,1)S(1)} %collective-permute-done.8, bf16[96,1024]{1,0:T(8,128)(2,1)S(1)} %collective-permute-done.7, ...), kind=kOutput, calls=%fused_computation.10 | convolution fusion | flops 104202240 | bytes 1622528 | tf_op jit(solution)/shard_map/dot_general | solution.py:152
  86.7 7.3 %collective-permute-done.16 = f32[2,128,384]{2,1,0:T(8,128)S(1)} collective-permute-done((f32[2,128,384]{2,1,0:T(8,128)S(1)}, f32[2,128,384]{2,1,0:T(8,128)S(1)}, u32[]{:S(2)}, u32[]{:S(2)}) %collective-permute-start.16) | collective-permute-done | bytes 393248 | tf_op jit(solution)/shard_map/ppermute | solution.py:82
  94.1 1.5 %collective-permute-start.17 = (f32[128,384]{1,0:T(8,128)S(1)}, f32[128,384]{1,0:T(8,128)S(1)}, u32[]{:S(2)}, u32[]{:S(2)}) collective-permute-start(f32[128,384]{1,0:T(8,128)S(1)} %select_bitcast_fusion.7), channel_id=1, source_target_pairs={{0,8},{4,12},{8,0},{12,4},{16,24},{20,28},{24,16},{28,20},{1,9},{5... | collective-permute-start | bytes 589832 | tf_op jit(solution)/shard_map/ppermute | solution.py:82
  95.6 1.0 %convolution_convert_fusion.3 = bf16[128,1024]{1,0:T(8,128)(2,1)} fusion(bf16[96,1024]{1,0:T(8,128)(2,1)S(1)} %collective-permute-done.14, bf16[96,1024]{1,0:T(8,128)(2,1)S(1)} %collective-permute-done.13, bf16[96,1024]{1,0:T(8,128)(2,1)S(1)} %collective-permute-done.12, bf16[96,1024]{1,0:T(8,128)(2,1)S(1)} %get-tuple-element.46, ...), kind=kOutput, calls=%fused_computation.11 | convolution fusion | flops 103989248 | bytes 1245184 | tf_op jit(solution)/shard_map/dot_general | solution.py:158
  96.7 3.2 %collective-permute-done.17 = f32[128,384]{1,0:T(8,128)S(1)} collective-permute-done((f32[128,384]{1,0:T(8,128)S(1)}, f32[128,384]{1,0:T(8,128)S(1)}, u32[]{:S(2)}, u32[]{:S(2)}) %collective-permute-start.17) | collective-permute-done | bytes 196640 | tf_op jit(solution)/shard_map/ppermute | solution.py:82
  99.8 0.7 fusion.27
  (53 shorter events, 1.0 us)
Async XLA Ops:
  0.6 12.8 %copy-start = (bf16[128,1024]{1,0:T(8,128)(2,1)S(1)}, bf16[128,1024]{1,0:T(8,128)(2,1)}, u32[]{:S(2)}) copy-start(bf16[128,1024]{1,0:T(8,128)(2,1)} %param.13) | copy-start | bytes 786436
  1.7 8.8 %collective-permute-start.3 = (bf16[128,1152]{1,0:T(8,128)(2,1)S(1)}, bf16[128,1152]{1,0:T(8,128)(2,1)S(1)}, u32[]{:S(2)}, u32[]{:S(2)}) collective-permute-start(bf16[128,1152]{1,0:T(8,128)(2,1)S(1)} %maximum_bitcast_fusion), channel_id=1, source_target_pairs={{0,8},{4,12},{8,0},{12,4},{16,24},{20,28},{24,16},{28,20},{1,9},{5... | collective-permute-start | bytes 884744 | tf_op jit(solution)/shard_map/ppermute | solution.py:57
  4.2 7.5 %copy-start.5 = (s32[256]{0:T(256)}, s32[256]{0:T(256)S(1)}, u32[]{:S(2)}) copy-start(s32[256]{0:T(256)S(1)} %sub.46) | copy-start | bytes 3076
  4.4 7.3 %copy-start.9 = (f32[256]{0:T(256)}, f32[256]{0:T(256)S(1)}, u32[]{:S(2)}) copy-start(f32[256]{0:T(256)S(1)} %fusion.3) | copy-start | bytes 3076
  4.7 8.8 %copy-start.4 = (s32[128,2]{0,1:T(2,128)}, s32[128,2]{0,1:T(2,128)S(1)}, u32[]{:S(2)}) copy-start(s32[128,2]{0,1:T(2,128)S(1)} %copy.24) | copy-start | bytes 3076
  11.7 6.1 %copy-start.7 = (f32[128,2]{0,1:T(2,128)S(1)}, f32[128,2]{0,1:T(2,128)}, u32[]{:S(2)}) copy-start(f32[128,2]{0,1:T(2,128)} %param.15) | copy-start | bytes 3076
  11.7 14.3 %collective-permute-start.4 = (bf16[2,128,1152]{2,1,0:T(8,128)(2,1)S(1)}, bf16[2,128,1152]{2,1,0:T(8,128)(2,1)S(1)}, u32[]{:S(2)}, u32[]{:S(2)}) collective-permute-start(bf16[2,128,1152]{2,1,0:T(8,128)(2,1)S(1)} %pad_maximum_fusion.4), channel_id=1, source_target_pairs={{0,16},{4,20},{8,24},{12,28},{16,0},{20,4},{24,8},{28,12},{1,17},{... | collective-permute-start | bytes 1769480 | tf_op jit(solution)/shard_map/ppermute | solution.py:57
  13.9 17.8 %collective-permute-start.2 = (bf16[96,1024]{1,0:T(8,128)(2,1)S(1)}, bf16[96,1024]{1,0:T(8,128)(2,1)}, u32[]{:S(2)}, u32[]{:S(2)}) collective-permute-start(bf16[96,1024]{1,0:T(8,128)(2,1)S(1)} %get-tuple-element.59), channel_id=1, source_target_pairs={{0,3},{1,0},{2,1},{3,2},{4,7},{5,4},{6,5},{7,6},{8,11},{9,8},{10,9... | collective-permute-start | bytes 589832 | tf_op jit(solution)/shard_map/ppermute | solution.py:42
  14.5 21.0 %collective-permute-start.1 = (bf16[96,1024]{1,0:T(8,128)(2,1)S(1)}, bf16[96,1024]{1,0:T(8,128)(2,1)}, u32[]{:S(2)}, u32[]{:S(2)}) collective-permute-start(bf16[96,1024]{1,0:T(8,128)(2,1)S(1)} %get-tuple-element.60), channel_id=1, source_target_pairs={{0,2},{1,3},{2,0},{3,1},{4,6},{5,7},{6,4},{7,5},{8,10},{9,11},{10,... | collective-permute-start | bytes 589832 | tf_op jit(solution)/shard_map/ppermute | solution.py:42
  14.8 20.6 %collective-permute-start = (bf16[96,1024]{1,0:T(8,128)(2,1)S(1)}, bf16[96,1024]{1,0:T(8,128)(2,1)}, u32[]{:S(2)}, u32[]{:S(2)}) collective-permute-start(bf16[96,1024]{1,0:T(8,128)(2,1)S(1)} %get-tuple-element.61), channel_id=1, source_target_pairs={{0,1},{1,2},{2,3},{3,0},{4,5},{5,6},{6,7},{7,4},{8,9},{9,10},{10,1... | collective-permute-start | bytes 589832 | tf_op jit(solution)/shard_map/ppermute | solution.py:42
  26.1 1.2 %copy-start.6 = (s32[256]{0:T(256)S(1)}, s32[256]{0:T(256)}, u32[]{:S(2)}) copy-start(s32[256]{0:T(256)} %copy-done.5) | copy-start | bytes 3076
  26.1 1.2 %copy-start.10 = (f32[256]{0:T(256)S(1)}, f32[256]{0:T(256)}, u32[]{:S(2)}) copy-start(f32[256]{0:T(256)} %copy-done.9) | copy-start | bytes 3076
  26.1 1.2 %copy-start.8 = (f32[256]{0:T(256)S(1)}, f32[256]{0:T(256)}, u32[]{:S(2)}) copy-start(f32[256]{0:T(256)} %broadcast_in_dim.48) | copy-start | bytes 3076
  26.2 1.4 %copy-start.1 = (bf16[128,1024]{1,0:T(8,128)(2,1)S(1)}, bf16[128,1024]{1,0:T(8,128)(2,1)}, u32[]{:S(2)}) copy-start(bf16[128,1024]{1,0:T(8,128)(2,1)} %param.19) | copy-start | bytes 786436
  27.3 3.5 %collective-permute-start.5 = (bf16[2,2,128,1152]{3,2,1,0:T(8,128)(2,1)}, bf16[2,2,128,1152]{3,2,1,0:T(8,128)(2,1)S(1)}, u32[]{:S(2)}, u32[]{:S(2)}) collective-permute-start(bf16[2,2,128,1152]{3,2,1,0:T(8,128)(2,1)} %pad_maximum_fusion.1), channel_id=1, source_target_pairs={{0,4},{4,0},{8,12},{12,8},{16,20},{20,16},{24,28},{28,24},{1,5},{5... | collective-permute-start | bytes 3538952 | tf_op jit(solution)/shard_map/ppermute | solution.py:57
  28.8 10.0 %collective-permute-start.11 = (bf16[96,1024]{1,0:T(8,128)(2,1)}, bf16[96,1024]{1,0:T(8,128)(2,1)}, u32[]{:S(2)}, u32[]{:S(2)}) collective-permute-start(bf16[96,1024]{1,0:T(8,128)(2,1)} %get-tuple-element.51), channel_id=1, source_target_pairs={{0,3},{1,0},{2,1},{3,2},{4,7},{5,4},{6,5},{7,6},{8,11},{9,8},{10,9... | collective-permute-start | bytes 589832 | tf_op jit(solution)/shard_map/ppermute | solution.py:42
  30.9 15.8 %collective-permute-start.10 = (bf16[96,1024]{1,0:T(8,128)(2,1)}, bf16[96,1024]{1,0:T(8,128)(2,1)S(1)}, u32[]{:S(2)}, u32[]{:S(2)}) collective-permute-start(bf16[96,1024]{1,0:T(8,128)(2,1)} %get-tuple-element.52), channel_id=1, source_target_pairs={{0,2},{1,3},{2,0},{3,1},{4,6},{5,7},{6,4},{7,5},{8,10},{9,11},{10,... | collective-permute-start | bytes 589832 | tf_op jit(solution)/shard_map/ppermute | solution.py:42
  31.5 0.9 copy-start.3
  32.4 14.3 %collective-permute-start.9 = (bf16[96,1024]{1,0:T(8,128)(2,1)S(1)}, bf16[96,1024]{1,0:T(8,128)(2,1)S(1)}, u32[]{:S(2)}, u32[]{:S(2)}) collective-permute-start(bf16[96,1024]{1,0:T(8,128)(2,1)S(1)} %copy-done.3), channel_id=1, source_target_pairs={{0,1},{1,2},{2,3},{3,0},{4,5},{5,6},{6,7},{7,4},{8,9},{9,10},{10,1... | collective-permute-start | bytes 589832 | tf_op jit(solution)/shard_map/ppermute | solution.py:42
  35.4 11.2 %copy-start.2 = (bf16[96,1024]{1,0:T(8,128)(2,1)S(1)}, bf16[96,1024]{1,0:T(8,128)(2,1)}, u32[]{:S(2)}) copy-start(bf16[96,1024]{1,0:T(8,128)(2,1)} %get-tuple-element.50) | copy-start | bytes 589828
  50.1 11.8 %collective-permute-start.15 = (f32[2,2,128,384]{3,2,1,0:T(8,128)S(1)}, f32[2,2,128,384]{3,2,1,0:T(8,128)S(1)}, u32[]{:S(2)}, u32[]{:S(2)}) collective-permute-start(f32[2,2,128,384]{3,2,1,0:T(8,128)S(1)} %fusion.18), channel_id=1, source_target_pairs={{0,4},{4,0},{8,12},{12,8},{16,20},{20,16},{24,28},{28,24},{1,5},{5... | collective-permute-start | bytes 2359304 | tf_op jit(solution)/shard_map/ppermute | solution.py:82
  50.8 11.1 %collective-permute-start.8 = (bf16[96,1024]{1,0:T(8,128)(2,1)S(1)}, bf16[96,1024]{1,0:T(8,128)(2,1)S(1)}, u32[]{:S(2)}, u32[]{:S(2)}) collective-permute-start(bf16[96,1024]{1,0:T(8,128)(2,1)S(1)} %get-tuple-element.55), channel_id=1, source_target_pairs={{0,1},{1,2},{2,3},{3,0},{4,5},{5,6},{6,7},{7,4},{8,9},{9,10},{10,1... | collective-permute-start | bytes 589832 | tf_op jit(solution)/shard_map/ppermute | solution.py:42
  55.0 28.9 %collective-permute-start.7 = (bf16[96,1024]{1,0:T(8,128)(2,1)S(1)}, bf16[96,1024]{1,0:T(8,128)(2,1)S(1)}, u32[]{:S(2)}, u32[]{:S(2)}) collective-permute-start(bf16[96,1024]{1,0:T(8,128)(2,1)S(1)} %get-tuple-element.56), channel_id=1, source_target_pairs={{0,2},{1,3},{2,0},{3,1},{4,6},{5,7},{6,4},{7,5},{8,10},{9,11},{10,... | collective-permute-start | bytes 589832 | tf_op jit(solution)/shard_map/ppermute | solution.py:42
  57.1 28.3 %collective-permute-start.6 = (bf16[96,1024]{1,0:T(8,128)(2,1)S(1)}, bf16[96,1024]{1,0:T(8,128)(2,1)S(1)}, u32[]{:S(2)}, u32[]{:S(2)}) collective-permute-start(bf16[96,1024]{1,0:T(8,128)(2,1)S(1)} %get-tuple-element.57), channel_id=1, source_target_pairs={{0,3},{1,0},{2,1},{3,2},{4,7},{5,4},{6,5},{7,6},{8,11},{9,8},{10,9... | collective-permute-start | bytes 589832 | tf_op jit(solution)/shard_map/ppermute | solution.py:42
  57.9 37.7 %collective-permute-start.14 = (bf16[96,1024]{1,0:T(8,128)(2,1)S(1)}, bf16[96,1024]{1,0:T(8,128)(2,1)S(1)}, u32[]{:S(2)}, u32[]{:S(2)}) collective-permute-start(bf16[96,1024]{1,0:T(8,128)(2,1)S(1)} %get-tuple-element.47), channel_id=1, source_target_pairs={{0,1},{1,2},{2,3},{3,0},{4,5},{5,6},{6,7},{7,4},{8,9},{9,10},{10,1... | collective-permute-start | bytes 589832 | tf_op jit(solution)/shard_map/ppermute | solution.py:42
  61.8 33.8 %collective-permute-start.13 = (bf16[96,1024]{1,0:T(8,128)(2,1)S(1)}, bf16[96,1024]{1,0:T(8,128)(2,1)S(1)}, u32[]{:S(2)}, u32[]{:S(2)}) collective-permute-start(bf16[96,1024]{1,0:T(8,128)(2,1)S(1)} %get-tuple-element.48), channel_id=1, source_target_pairs={{0,2},{1,3},{2,0},{3,1},{4,6},{5,7},{6,4},{7,5},{8,10},{9,11},{10,... | collective-permute-start | bytes 589832 | tf_op jit(solution)/shard_map/ppermute | solution.py:42
  62.0 33.7 %collective-permute-start.12 = (bf16[96,1024]{1,0:T(8,128)(2,1)S(1)}, bf16[96,1024]{1,0:T(8,128)(2,1)S(1)}, u32[]{:S(2)}, u32[]{:S(2)}) collective-permute-start(bf16[96,1024]{1,0:T(8,128)(2,1)S(1)} %get-tuple-element.49), channel_id=1, source_target_pairs={{0,3},{1,0},{2,1},{3,2},{4,7},{5,4},{6,5},{7,6},{8,11},{9,8},{10,9... | collective-permute-start | bytes 589832 | tf_op jit(solution)/shard_map/ppermute | solution.py:42
  83.9 10.2 %collective-permute-start.16 = (f32[2,128,384]{2,1,0:T(8,128)S(1)}, f32[2,128,384]{2,1,0:T(8,128)S(1)}, u32[]{:S(2)}, u32[]{:S(2)}) collective-permute-start(f32[2,128,384]{2,1,0:T(8,128)S(1)} %select_bitcast_fusion.4), channel_id=1, source_target_pairs={{0,16},{4,20},{8,24},{12,28},{16,0},{20,4},{24,8},{28,12},{1,17},{... | collective-permute-start | bytes 1179656 | tf_op jit(solution)/shard_map/ppermute | solution.py:82
  94.1 5.7 %collective-permute-start.17 = (f32[128,384]{1,0:T(8,128)S(1)}, f32[128,384]{1,0:T(8,128)S(1)}, u32[]{:S(2)}, u32[]{:S(2)}) collective-permute-start(f32[128,384]{1,0:T(8,128)S(1)} %select_bitcast_fusion.7), channel_id=1, source_target_pairs={{0,8},{4,12},{8,0},{12,4},{16,24},{20,28},{24,16},{28,20},{1,9},{5... | collective-permute-start | bytes 589832 | tf_op jit(solution)/shard_map/ppermute | solution.py:82
